TPU v7x, 512 devices: a whole 4x4x16 slice. The times are simulated.
512 devices in a mesh: seq: 64 (over z, y), tp: 4 (over x), dp: 2 (over core).
Axes of the slice: x: 4, y: 4, z: 16, core: 2. Of those that a mesh axis runs over, the one named last changes fastest.
Arguments:
- inputs: bfloat16 [16384, 1280], P(('dp', 'seq'), 'tp'), parts along dimension 0, may hold values from -6 to 6
- out_grads: bfloat16 [16384, 1280], P(('dp', 'seq'), 'tp'), parts along dimension 0, may hold values from -6 to 6
- norm_gain: float32 [1280], replicated, may hold values from 0.1 to 1.9
- w_query: bfloat16 [640, 1280], P('tp'), may hold values from -0.15625 to 0.15625
- w_key: bfloat16 [640, 1280], P('tp'), may hold values from -0.15625 to 0.15625
- w_value: bfloat16 [640, 1280], P('tp'), may hold values from -0.15625 to 0.15625
- w_output: bfloat16 [640, 1280], P('tp'), may hold values from -0.25 to 0.25
- query_scale: float32 [80], replicated, may hold values from -4 to 4
- offsets: int32 [64], replicated, may hold values from 0 to 63, each once
Outputs:
- input_grads: bfloat16 [16384, 1280], P(('dp', 'seq'), 'tp'), parts along dimension 0
There are 2 independent parts, one for each index of `dp`. A program takes and returns all parts, laid end to end along the dimension named above; an argument that names none is the same for every part. Nothing has to cross between parts.
Inputs may be any that keep to these rules, and one draw needn't show every extreme that they name: `offsets`: each number appears exactly once.
All inputs are finite; a program needn't handle non-finite values.
Results may differ from a plain program's by a relative error of at most 0.007.
The roundings to bfloat16 on the way count: a program that leaves them out, or rounds other values in their place, can miss the bound.
Values may be sent and summed in bfloat16 or wider, within the bound.
No kernel may reach another device: no remote copies, remote signals or barrier semaphores. Data moves between devices by JAX's collectives and lax.ppermute only.
A program may use at most 64 MiB of HBM per device.

v0:
```python
import math

import jax
import jax.numpy as jnp
from jax import lax
from jax.sharding import PartitionSpec as P

PIECE = 128


scale_base = 1.4426950408889634
masked_score = -1e30
norm_eps = 1e-06


def positions_of(offsets, first_row, piece_rows, block_len):
    row_index = first_row + lax.iota(jnp.int32, piece_rows)
    shard_ids = row_index // block_len
    one_hot = (shard_ids[:, None] == lax.iota(jnp.int32, offsets.shape[0])[None, :]).astype(
        jnp.int32
    )
    return jnp.sum(one_hot * offsets[None, :], axis=1) * block_len + row_index % block_len


def column_scale(query_scale, head_count):
    head_width = query_scale.shape[0]
    factor = scale_base / math.sqrt(head_width) * jax.nn.softplus(query_scale)
    return jnp.tile(factor, head_count)


def split_heads(values, head_count):
    return values.reshape(values.shape[0], head_count, values.shape[1] // head_count)


def over_blocks(running, pieces, step_fn):
    piece_rows = pieces[0].shape[0]
    block_size = math.gcd(piece_rows, 512)

    def visit_block(number, state_now):
        first_row = number * block_size
        block_parts = tuple(
            (lax.dynamic_slice_in_dim(piece, first_row, block_size, 0) for piece in pieces)
        )
        return step_fn(state_now, block_parts, first_row)

    return lax.fori_loop(0, piece_rows // block_size, visit_block, running)


def per_device(
    inputs, out_grads, norm_gain, w_query, w_key, w_value, w_output, query_scale, offsets
):
    row_count = inputs.shape[0]
    width_here = inputs.shape[1]
    head_width = query_scale.shape[0]
    heads_here = w_query.shape[0] // head_width
    contract = (((1,), (1,)), ((), ()))
    full_inputs, full_grads = (
        lax.all_gather(inputs, "tp", axis=1, tiled=True),
        lax.all_gather(out_grads, "tp", axis=1, tiled=True),
    )
    full_width = full_inputs.shape[1]
    widened = full_inputs.astype(jnp.float32)
    inverse = lax.rsqrt(jnp.mean(widened * widened, axis=1, keepdims=True) + norm_eps)
    normed = (widened * inverse * norm_gain[None, :]).astype(jnp.bfloat16)
    factor = column_scale(query_scale, heads_here)
    queries = (
        lax.dot_general(normed, w_query, contract, preferred_element_type=jnp.float32)
        * factor[None, :]
    ).astype(jnp.bfloat16)
    key_rows = lax.dot_general(normed, w_key, contract, preferred_element_type=jnp.float32).astype(
        jnp.bfloat16
    )
    values = lax.dot_general(normed, w_value, contract, preferred_element_type=jnp.float32).astype(
        jnp.bfloat16
    )
    head_grads = lax.dot_general(
        full_grads, w_output, contract, preferred_element_type=jnp.float32
    ).astype(jnp.bfloat16)
    seq_index = lax.axis_index("seq")
    own_positions = positions_of(offsets, seq_index * row_count, row_count, PIECE)
    query_heads = split_heads(queries, heads_here)
    grad_heads = split_heads(head_grads, heads_here)
    key_heads = split_heads(key_rows, heads_here)
    value_heads = split_heads(values, heads_here)

    def peak_step(running, block_parts, first_row):
        key_part = block_parts[0]
        key_place = positions_of(offsets, first_row, key_part.shape[0], PIECE)
        row_peak, summed = running
        raw_scores = jnp.einsum(
            "qhd,khd->hqk",
            query_heads,
            split_heads(key_part, heads_here),
            preferred_element_type=jnp.float32,
        )
        visible = key_place[None, None, :] <= own_positions[None, :, None]
        masked = jnp.where(visible, raw_scores, masked_score)
        fresh_peak = jnp.maximum(row_peak, jnp.max(masked, axis=2))
        fresh_terms = jnp.where(visible, jnp.exp(masked - fresh_peak[:, :, None]), 0.0)
        summed = summed * jnp.exp(row_peak - fresh_peak) + jnp.sum(fresh_terms, axis=2)
        return (fresh_peak, summed)

    def make_grad_step(log_total):

        def grad_step(running, block_parts, first_row):
            key_part, value_part = block_parts
            key_place = positions_of(offsets, first_row, key_part.shape[0], PIECE)
            row_delta, first_sum, second_sum = running
            key_heads_part = split_heads(key_part, heads_here)
            raw_scores = jnp.einsum(
                "qhd,khd->hqk", query_heads, key_heads_part, preferred_element_type=jnp.float32
            )
            visible = key_place[None, None, :] <= own_positions[None, :, None]
            attend = jnp.exp(jnp.where(visible, raw_scores - log_total[:, :, None], masked_score))
            grad_probs = jnp.einsum(
                "qhd,khd->hqk",
                grad_heads,
                split_heads(value_part, heads_here),
                preferred_element_type=jnp.float32,
            )
            weighted = attend * grad_probs
            row_delta = row_delta + jnp.sum(weighted, axis=2)
            first_sum = first_sum + jnp.einsum(
                "hqk,khd->hqd",
                weighted.astype(jnp.bfloat16),
                key_heads_part,
                preferred_element_type=jnp.float32,
            )
            second_sum = second_sum + jnp.einsum(
                "hqk,khd->hqd",
                attend.astype(jnp.bfloat16),
                key_heads_part,
                preferred_element_type=jnp.float32,
            )
            return (row_delta, first_sum, second_sum)

        return grad_step

    peak_start = (
        jnp.full((heads_here, row_count), masked_score, jnp.float32),
        jnp.zeros((heads_here, row_count), jnp.float32),
    )
    grad_start = (
        jnp.zeros((heads_here, row_count), jnp.float32),
        jnp.zeros((heads_here, row_count, head_width), jnp.float32),
        jnp.zeros((heads_here, row_count, head_width), jnp.float32),
    )
    row_peak, summed = over_blocks(
        peak_start, (lax.all_gather(key_rows, "seq", axis=0, tiled=True),), peak_step
    )
    log_total = row_peak + jnp.log(summed)
    grad_step = make_grad_step(log_total)
    row_delta, first_sum, second_sum = over_blocks(
        grad_start,
        (
            lax.all_gather(key_rows, "seq", axis=0, tiled=True),
            lax.all_gather(values, "seq", axis=0, tiled=True),
        ),
        grad_step,
    )
    query_grad = first_sum - row_delta[:, :, None] * second_sum
    query_grad = jnp.transpose(query_grad, (1, 0, 2)).reshape(row_count, heads_here * head_width)
    query_done = (query_grad * factor[None, :]).astype(jnp.bfloat16)
    log_all, delta_all = (
        lax.all_gather(log_total.T, "seq", axis=0, tiled=True),
        lax.all_gather(row_delta.T, "seq", axis=0, tiled=True),
    )

    def key_step(running, block_parts, first_row):
        query_part, grad_part = block_parts
        piece_rows = query_part.shape[0]
        query_place = positions_of(offsets, first_row, piece_rows, PIECE)
        log_part = lax.dynamic_slice_in_dim(log_all, first_row, piece_rows, 0).T
        delta_part = lax.dynamic_slice_in_dim(delta_all, first_row, piece_rows, 0).T
        key_grad, value_grad = running
        query_heads_part = split_heads(query_part, heads_here)
        grad_heads_part = split_heads(grad_part, heads_here)
        raw_scores = jnp.einsum(
            "qhd,khd->hqk", query_heads_part, key_heads, preferred_element_type=jnp.float32
        )
        visible = own_positions[None, None, :] <= query_place[None, :, None]
        attend = jnp.exp(jnp.where(visible, raw_scores - log_part[:, :, None], masked_score))
        grad_probs = jnp.einsum(
            "qhd,khd->hqk", grad_heads_part, value_heads, preferred_element_type=jnp.float32
        )
        score_grad = (attend * (grad_probs - delta_part[:, :, None])).astype(jnp.bfloat16)
        key_grad = key_grad + jnp.einsum(
            "hqk,qhd->khd", score_grad, query_heads_part, preferred_element_type=jnp.float32
        )
        value_grad = value_grad + jnp.einsum(
            "hqk,qhd->khd",
            attend.astype(jnp.bfloat16),
            grad_heads_part,
            preferred_element_type=jnp.float32,
        )
        return (key_grad, value_grad)

    key_start = (
        jnp.zeros((row_count, heads_here, head_width), jnp.float32),
        jnp.zeros((row_count, heads_here, head_width), jnp.float32),
    )
    key_grad, value_grad = over_blocks(
        key_start,
        (
            lax.all_gather(queries, "seq", axis=0, tiled=True),
            lax.all_gather(head_grads, "seq", axis=0, tiled=True),
        ),
        key_step,
    )
    key_done = key_grad.reshape(row_count, heads_here * head_width).astype(jnp.bfloat16)
    value_done = value_grad.reshape(row_count, heads_here * head_width).astype(jnp.bfloat16)
    back_sum = jnp.dot(query_done, w_query, preferred_element_type=jnp.float32)
    back_sum = back_sum + jnp.dot(key_done, w_key, preferred_element_type=jnp.float32)
    back_sum = back_sum + jnp.dot(value_done, w_value, preferred_element_type=jnp.float32)
    start_col = lax.axis_index("tp") * width_here
    total_back = lax.psum(back_sum, "tp")
    scaled = total_back * norm_gain[None, :]
    row_dot = jnp.sum(widened * scaled, axis=1, keepdims=True)
    branch = inverse * scaled - widened * inverse * inverse * inverse * row_dot / full_width
    result = out_grads.astype(jnp.float32) + lax.dynamic_slice_in_dim(
        branch, start_col, width_here, 1
    )
    return result.astype(jnp.bfloat16)


def solution(mesh):
    return jax.shard_map(
        per_device,
        mesh=mesh,
        in_specs=(
            P(("dp", "seq"), "tp"),
            P(("dp", "seq"), "tp"),
            P(),
            P("tp", None),
            P("tp", None),
            P("tp", None),
            P("tp", None),
            P(),
            P(),
        ),
        out_specs=P(("dp", "seq"), "tp"),
        check_vma=False,
    )
```

profile of v0, /device:TPU:24, one launch (start us, length us, event | category | flops | bytes accessed | tf_op | source)
XLA Modules:
  0.0 678.2 jit_solution(6673104376951234624)
XLA Ops:
  6.6 13.1 %all_gather.25 = bf16[128,1280]{0,1:T(8,128)(2,1)S(1)} all-gather(bf16[128,320]{0,1:T(8,128)(2,1)} %param.15), channel_id=1, replica_groups=mesh['seq'=64,'tp'=4,'dp'=2] {'tp'}, dimensions={1}, use_global_device_ids=true | all-gather | bytes 409600 | tf_op jit(solution)/shard_map/all_gather | solution.py:58
  19.9 2.1 convolution_convert_fusion.2
  22.0 2.1 convolution_convert_fusion.1
  25.4 12.4 %all_gather.28 = bf16[128,1280]{0,1:T(8,128)(2,1)S(1)} all-gather(bf16[128,320]{0,1:T(8,128)(2,1)S(1)} %copy-done.6), channel_id=1, replica_groups=mesh['seq'=64,'tp'=4,'dp'=2] {'tp'}, dimensions={1}, use_global_device_ids=true | all-gather | bytes 409600 | tf_op jit(solution)/shard_map/all_gather | solution.py:59
  39.0 125.2 %all-gather.5.cloned.1.call-done = bf16[8192,160]{0,1:T(8,128)(2,1)} async-done(((bf16[128,160]{0,1:T(8,128)(2,1)}), bf16[8192,160]{0,1:T(8,128)(2,1)}) %all-gather.5.cloned.1.call-update) | async-done | bytes 2621456 | tf_op jit(solution)/shard_map/all_gather | solution.py:156
  164.2 39.6 %while.56 = (s32[]{:T(128)}, f32[2,128]{1,0:T(2,128)S(1)}, f32[2,128]{1,0:T(2,128)S(1)}, s32[64]{0:T(128)S(1)}, s32[128]{0:T(128)S(1)}, /*index=5*/bf16[8192,160...) while((s32[]{:T(128)}, f32[2,128]{1,0:T(2,128)S(1)}, ...), condition=%wide.region_6.7_spmd.clone, body=%wide.region_2.6_spmd.clone.sunk | while | flops 21806852 | bytes 1804210 | solution.py:46
  165.4 1.1 fusion.103
  167.8 1.1 fusion.103
  170.3 1.1 fusion.103
  172.8 1.1 fusion.103
  175.3 1.1 fusion.103
  177.7 1.1 fusion.103
  180.2 1.1 fusion.103
  182.7 1.1 fusion.103
  185.2 1.1 fusion.103
  187.6 1.1 fusion.103
  190.1 1.1 fusion.103
  192.6 1.1 fusion.103
  195.1 1.1 fusion.103
  197.5 1.1 fusion.103
  200.0 1.1 fusion.103
  202.5 1.1 fusion.103
  203.8 97.4 %all-gather.7.cloned.1.call-done = bf16[8192,160]{0,1:T(8,128)(2,1)} async-done(((bf16[128,160]{0,1:T(8,128)(2,1)}), bf16[8192,160]{0,1:T(8,128)(2,1)}) %all-gather.7.cloned.1.call-update) | async-done | bytes 2621456 | tf_op jit(solution)/shard_map/all_gather | solution.py:157
  301.1 50.2 %while.57 = (s32[]{:T(128)}, f32[2,128]{1,0:T(2,128)S(1)}, f32[2,128,80]{1,2,0:T(8,128)S(1)}, f32[2,128,80]{1,2,0:T(8,128)S(1)}, s32[64]{0:T(128)S(1)}, /*index=...) while((s32[]{:T(128)}, f32[2,128]{1,0:T(2,128)S(1)}, ...), condition=%wide.region_10.11_spmd.clone, body=%wide.region_7.10_spmd.clone.sunk | while | flops 84933376 | bytes 3966931 | solution.py:46
  302.4 1.1 fusion.115
  305.6 1.1 fusion.115
  308.7 1.1 fusion.115
  311.9 1.1 fusion.115
  315.0 1.1 fusion.115
  318.1 1.1 fusion.115
  321.3 1.1 fusion.115
  324.4 1.1 fusion.115
  327.6 1.1 fusion.115
  330.7 1.1 fusion.115
  333.8 1.1 fusion.115
  337.0 1.1 fusion.115
  340.1 1.1 fusion.115
  343.2 1.1 fusion.115
  346.4 1.1 fusion.115
  349.5 1.1 fusion.115
  351.4 79.8 %all_gather.32 = f32[8192,2]{0,1:T(2,128)S(1)} all-gather(f32[128,2]{0,1:T(2,128)S(1)} %bitcast.134), channel_id=1, replica_groups=mesh['seq'=64,'tp'=4,'dp'=2] {'seq'}, dimensions={0}, use_global_device_ids=true | all-gather | bytes 66560 | tf_op jit(solution)/shard_map/all_gather | solution.py:166
  431.2 80.0 %all_gather.30 = f32[8192,2]{0,1:T(2,128)S(1)} all-gather(f32[128,2]{0,1:T(2,128)S(1)} %bitcast.133), channel_id=1, replica_groups=mesh['seq'=64,'tp'=4,'dp'=2] {'seq'}, dimensions={0}, use_global_device_ids=true | all-gather | bytes 66560 | tf_op jit(solution)/shard_map/all_gather | solution.py:165
  511.2 63.6 %all-gather.11.cloned.1.call-done = bf16[8192,160]{0,1:T(8,128)(2,1)} async-done(((bf16[128,160]{0,1:T(8,128)(2,1)}), bf16[8192,160]{0,1:T(8,128)(2,1)}) %all-gather.11.cloned.1.call-update) | async-done | bytes 2621456 | tf_op jit(solution)/shard_map/all_gather | solution.py:206
  574.8 37.7 %while.58 = (s32[]{:T(128)}, f32[128,2,80]{0,2,1:T(8,128)S(1)}, f32[128,2,80]{0,2,1:T(8,128)S(1)}, bf16[8192,160]{0,1:T(8,128)(2,1)}, s32[128]{0:T(128)S(1)}, /*...) while((s32[]{:T(128)}, f32[128,2,80]{0,2,1:T(8,128)S(1)}, ...), condition=%wide.region_13.14_spmd.clone, body=%wide.region_11.13_spmd.clone.sunk | while | flops 84933120 | bytes 3462102 | solution.py:46
  574.8 1.1 constant_dynamic-slice_fusion.10
  613.5 1.2 convolution_add_fusion.2
  614.8 54.9 %all-reduce.2.cloned.1.call-done = f32[128,1280]{0,1:T(8,128)} async-done(((f32[128,1280]{0,1:T(8,128)}), f32[128,1280]{0,1:T(8,128)}) %all-reduce.2.cloned.1.call-update) | async-done | bytes 655376 | tf_op jit(solution)/shard_map/psum | solution.py:216
  669.6 1.3 fusion.33
  (489 shorter events, 93.1 us)
Async XLA Ops:
  6.5 17.7 %copy-start = (bf16[160,1280]{1,0:T(8,128)(2,1)S(1)}, bf16[160,1280]{1,0:T(8,128)(2,1)}, u32[]{:S(2)}) copy-start(bf16[160,1280]{1,0:T(8,128)(2,1)} %param.18) | copy-start | bytes 1228804
  6.5 17.7 %copy-start.9 = (f32[1280]{0:T(1024)S(1)}, f32[1280]{0:T(1024)}, u32[]{:S(2)}) copy-start(f32[1280]{0:T(1024)} %param.17) | copy-start | bytes 15364
  6.5 17.6 %copy-start.10 = (f32[80]{0:T(128)S(1)}, f32[80]{0:T(128)}, u32[]{:S(2)}) copy-start(f32[80]{0:T(128)} %param.22) | copy-start | bytes 964
  6.5 18.9 %copy-start.6 = (bf16[128,320]{0,1:T(8,128)(2,1)S(1)}, bf16[128,320]{0,1:T(8,128)(2,1)}, u32[]{:S(2)}) copy-start(bf16[128,320]{0,1:T(8,128)(2,1)} %param.16) | copy-start | bytes 245764
  6.5 31.3 %copy-start.5 = (bf16[160,1280]{1,0:T(8,128)(2,1)S(1)}, bf16[160,1280]{1,0:T(8,128)(2,1)}, u32[]{:S(2)}) copy-start(bf16[160,1280]{1,0:T(8,128)(2,1)} %param.21) | copy-start | bytes 1228804
  6.5 32.3 %copy-start.7 = (s32[64]{0:T(128)S(1)}, s32[64]{0:T(128)}, u32[]{:S(2)}) copy-start(s32[64]{0:T(128)} %param.23) | copy-start | bytes 772
  6.6 157.6 %all-gather.5.cloned.1.call-start = ((), (), s32[]{:S(2)}) async-start(), calls=%async_computation | async-start | bytes 2662400 | tf_op jit(solution)/shard_map/all_gather | solution.py:156
  22.0 279.2 %all-gather.7.cloned.1.call-start = ((), (), s32[]{:S(2)}) async-start(), calls=%async_computation.1 | async-start | bytes 2662400 | tf_op jit(solution)/shard_map/all_gather | solution.py:157
  24.1 487.1 %all-gather.9.cloned.1.call-start = ((), (), s32[]{:S(2)}) async-start(), calls=%async_computation.2 | async-start | bytes 2662400 | tf_op jit(solution)/shard_map/all_gather | solution.py:205
  25.4 549.5 %all-gather.11.cloned.1.call-start = ((), (), s32[]{:S(2)}) async-start(), calls=%async_computation.3 | async-start | bytes 2662400 | tf_op jit(solution)/shard_map/all_gather | solution.py:206
  38.7 630.9 %all-reduce.2.cloned.1.call-start = ((), (), s32[]{:S(2)}) async-start(), calls=%async_computation.4 | async-start | bytes 1310720 | tf_op jit(solution)/shard_map/psum | solution.py:216
  164.2 137.0 %copy-start.1 = (bf16[128,160]{0,1:T(8,128)(2,1)S(1)}, bf16[128,160]{0,1:T(8,128)(2,1)}, u32[]{:S(2)}) copy-start(bf16[128,160]{0,1:T(8,128)(2,1)} %convolution_convert_fusion) | copy-start | bytes 122884
  301.1 273.7 %copy-start.2 = (bf16[128,160]{0,1:T(8,128)(2,1)S(1)}, bf16[128,160]{0,1:T(8,128)(2,1)}, u32[]{:S(2)}) copy-start(bf16[128,160]{0,1:T(8,128)(2,1)} %convolution_convert_fusion.1) | copy-start | bytes 122884
  301.1 273.7 %copy-start.8 = (bf16[128,160]{0,1:T(8,128)(2,1)S(1)}, bf16[128,160]{0,1:T(8,128)(2,1)}, u32[]{:S(2)}) copy-start(bf16[128,160]{0,1:T(8,128)(2,1)} %convolution_convert_fusion.2) | copy-start | bytes 122884
  574.8 38.2 %copy-start.3 = (bf16[160,1280]{1,0:T(8,128)(2,1)S(1)}, bf16[160,1280]{1,0:T(8,128)(2,1)}, u32[]{:S(2)}) copy-start(bf16[160,1280]{1,0:T(8,128)(2,1)} %param.19) | copy-start | bytes 1228804
  612.5 1.0 copy-start.4
Sparse Core Ops, SparseCore 0:
  22.1 142.0 all-gather.4
  167.1 134.0 all-gather.6
  304.1 134.0 all-gather.8
  440.9 133.9 all-gather.10
  614.9 54.7 all-reduce.1
where the time goes:
time: 682 us; the launch traced here: 678 us
  waiting for transfers between devices  341 us (50%)
  blocking collectives  185 us (27%)
  matrix products  69.4 us (10%)
  local copies, waits for them, and re-layouts  48.1 us (7%)
  other arithmetic  17.4 us (3%)
  between operations  13.4 us (2%)
    all_gather x1, waiting for transfers between devices, per_device(): lax.all_gather(key_rows, 'seq', axis=0, tiled=True)  125 us
    all_gather x1, waiting for transfers between devices, per_device(): lax.all_gather(values, 'seq', axis=0, tiled=True)  97.4 us
    all_gather x1, blocking collectives, per_device(): lax.all_gather(log_total.T, 'seq', axis=0, tiled=True)  80 us
    all_gather x1, blocking collectives, per_device(): lax.all_gather(row_delta.T, 'seq', axis=0, tiled=True)  79.8 us
    all_gather x1, waiting for transfers between devices, per_device(): lax.all_gather(head_grads, 'seq', axis=0, tiled=True)  63.6 us
    psum x1, waiting for transfers between devices, per_device(): total_back = lax.psum(back_sum, 'tp')  54.9 us
    dynamic_slice x48, local copies, waits for them, and re-layouts, visit_block(): lax.dynamic_slice_in_dim(piece, first_row, block_size, 0)  47.7 us
    dot_general x16, matrix products, peak_step(): jnp.einsum('qhd,khd->hqk', query_heads, split_heads(key_part, heads_here)...  17.2 us
  transfers between devices with their start and end apart: 5, of which 4 were waited for; matrix products, arithmetic and copies ran while one was open for 14% of the time, Pallas kernels for 0%

commit v1 on v0

v1 whole, which is shorter than its diff:
```python
import math

import jax
import jax.numpy as jnp
import numpy as np
from jax import lax
from jax.sharding import Mesh
from jax.sharding import PartitionSpec as P

PIECE = 128

scale_base = 1.4426950408889634
masked_score = -1e30
norm_eps = 1e-06


def column_scale(query_scale, head_count):
    head_width = query_scale.shape[0]
    factor = scale_base / math.sqrt(head_width) * jax.nn.softplus(query_scale)
    return jnp.tile(factor, head_count)


def block_positions(offsets, rows):
    return (offsets[:, None] * PIECE + lax.iota(jnp.int32, PIECE)[None, :]).reshape(rows)


def per_device(
    inputs, out_grads, norm_gain, w_query, w_key, w_value, w_output, query_scale, offsets
):
    row_count, width_here = inputs.shape
    head_width = query_scale.shape[0]
    heads_here = w_query.shape[0] // head_width
    cols = heads_here * head_width
    tp_size = lax.axis_size("tp")
    y_size = lax.axis_size("y")
    shards = offsets.shape[0]
    all_rows = shards * row_count
    contract = (((1,), (1,)), ((), ()))

    with jax.named_scope("gather_features"):
        both = jnp.concatenate([inputs, out_grads], axis=1)
        gathered = lax.all_gather(both, "tp", axis=1, tiled=True)
        gathered = gathered.reshape(row_count, tp_size, 2, width_here)
        full_inputs = gathered[:, :, 0, :].reshape(row_count, tp_size * width_here)
        full_grads = gathered[:, :, 1, :].reshape(row_count, tp_size * width_here)
    full_width = full_inputs.shape[1]

    with jax.named_scope("projections"):
        widened = full_inputs.astype(jnp.float32)
        inverse = lax.rsqrt(jnp.mean(widened * widened, axis=1, keepdims=True) + norm_eps)
        normed = (widened * inverse * norm_gain[None, :]).astype(jnp.bfloat16)
        factor = column_scale(query_scale, heads_here)
        queries = (
            lax.dot_general(normed, w_query, contract, preferred_element_type=jnp.float32)
            * factor[None, :]
        ).astype(jnp.bfloat16)
        keys = lax.dot_general(normed, w_key, contract, preferred_element_type=jnp.float32).astype(
            jnp.bfloat16
        )
        values = lax.dot_general(
            normed, w_value, contract, preferred_element_type=jnp.float32
        ).astype(jnp.bfloat16)
        head_grads = lax.dot_general(
            full_grads, w_output, contract, preferred_element_type=jnp.float32
        ).astype(jnp.bfloat16)

    with jax.named_scope("gather_sequence"):
        packed = jnp.concatenate([keys, values, queries, head_grads], axis=1)
        packed = lax.all_gather(packed, "y", axis=0, tiled=True)
        packed = lax.all_gather(packed, "z", axis=0, tiled=True)
        key_all = packed[:, 0 * cols : 1 * cols].reshape(all_rows, heads_here, head_width)
        value_all = packed[:, 1 * cols : 2 * cols].reshape(all_rows, heads_here, head_width)
        query_all = packed[:, 2 * cols : 3 * cols].reshape(all_rows, heads_here, head_width)
        grad_all = packed[:, 3 * cols : 4 * cols].reshape(all_rows, heads_here, head_width)

    seq_index = lax.axis_index("z") * y_size + lax.axis_index("y")
    positions = block_positions(offsets, all_rows)
    own_positions = offsets[seq_index] * PIECE + lax.iota(jnp.int32, row_count)

    query_heads = queries.reshape(row_count, heads_here, head_width)
    grad_heads = head_grads.reshape(row_count, heads_here, head_width)
    key_heads = keys.reshape(row_count, heads_here, head_width)
    value_heads = values.reshape(row_count, heads_here, head_width)

    with jax.named_scope("query_pass"):
        scores = jnp.einsum(
            "qhd,khd->hqk", query_heads, key_all, preferred_element_type=jnp.float32
        )
        visible = positions[None, None, :] <= own_positions[None, :, None]
        masked = jnp.where(visible, scores, masked_score)
        row_peak = jnp.max(masked, axis=2)
        summed = jnp.sum(jnp.where(visible, jnp.exp(masked - row_peak[:, :, None]), 0.0), axis=2)
        log_total = row_peak + jnp.log(summed)
        attend = jnp.exp(jnp.where(visible, scores - log_total[:, :, None], masked_score))
        grad_probs = jnp.einsum(
            "qhd,khd->hqk", grad_heads, value_all, preferred_element_type=jnp.float32
        )
        weighted = attend * grad_probs
        row_delta = jnp.sum(weighted, axis=2)
        first_sum = jnp.einsum(
            "hqk,khd->hqd",
            weighted.astype(jnp.bfloat16),
            key_all,
            preferred_element_type=jnp.float32,
        )
        second_sum = jnp.einsum(
            "hqk,khd->hqd", attend.astype(jnp.bfloat16), key_all, preferred_element_type=jnp.float32
        )
        query_grad = first_sum - row_delta[:, :, None] * second_sum
        query_grad = jnp.transpose(query_grad, (1, 0, 2)).reshape(row_count, cols)
        query_done = (query_grad * factor[None, :]).astype(jnp.bfloat16)

    with jax.named_scope("gather_row_stats"):
        stats = jnp.stack([log_total, row_delta], axis=0)
        sent = jnp.broadcast_to(stats[None], (shards,) + stats.shape)
        stats_all = lax.all_to_all(sent, ("z", "y"), 0, 0, tiled=False)
        log_all = jnp.transpose(stats_all[:, 0], (1, 0, 2)).reshape(heads_here, all_rows)
        delta_all = jnp.transpose(stats_all[:, 1], (1, 0, 2)).reshape(heads_here, all_rows)

    with jax.named_scope("key_pass"):
        scores_t = jnp.einsum(
            "khd,qhd->hkq", key_heads, query_all, preferred_element_type=jnp.float32
        )
        visible_t = own_positions[None, :, None] <= positions[None, None, :]
        attend_t = jnp.exp(
            jnp.where(visible_t, scores_t - log_all[:, None, :], masked_score)
        )
        grad_probs_t = jnp.einsum(
            "khd,qhd->hkq", value_heads, grad_all, preferred_element_type=jnp.float32
        )
        score_grad = (attend_t * (grad_probs_t - delta_all[:, None, :])).astype(jnp.bfloat16)
        key_grad = jnp.einsum(
            "hkq,qhd->khd", score_grad, query_all, preferred_element_type=jnp.float32
        )
        value_grad = jnp.einsum(
            "hkq,qhd->khd", attend_t.astype(jnp.bfloat16), grad_all, preferred_element_type=jnp.float32
        )
        key_done = key_grad.reshape(row_count, cols).astype(jnp.bfloat16)
        value_done = value_grad.reshape(row_count, cols).astype(jnp.bfloat16)

    with jax.named_scope("back_projection"):
        back_sum = jnp.dot(query_done, w_query, preferred_element_type=jnp.float32)
        back_sum = back_sum + jnp.dot(key_done, w_key, preferred_element_type=jnp.float32)
        back_sum = back_sum + jnp.dot(value_done, w_value, preferred_element_type=jnp.float32)
        scaled = back_sum * norm_gain[None, :]
        row_part = jnp.sum(widened * scaled, axis=1)
        chunks = scaled.reshape(row_count, tp_size, width_here).transpose(1, 0, 2)
        extra = jnp.zeros((tp_size, 1, width_here), jnp.float32)
        extra = extra.at[:, 0, :row_count].set(jnp.broadcast_to(row_part, (tp_size, row_count)))
        payload = jnp.concatenate([chunks, extra], axis=1)
        received = lax.all_to_all(payload, "tp", 0, 0, tiled=False)
        total = jnp.sum(received, axis=0)
        scaled_own = total[:row_count]
        row_dot = total[row_count, :row_count][:, None]

    with jax.named_scope("input_grads"):
        start_col = lax.axis_index("tp") * width_here
        own_inputs = inputs.astype(jnp.float32)
        branch = (
            inverse * scaled_own
            - own_inputs * inverse * inverse * inverse * row_dot / full_width
        )
        result = out_grads.astype(jnp.float32) + branch
    return result.astype(jnp.bfloat16)


def solution(mesh):
    seq_size = mesh.shape["seq"]
    devices = mesh.devices
    y_size = 4 if seq_size % 4 == 0 else 1
    split = Mesh(
        devices.reshape((seq_size // y_size, y_size) + devices.shape[1:]),
        ("z", "y", "tp", "dp"),
    )
    rows = P(("dp", "z", "y"), "tp")
    return jax.shard_map(
        per_device,
        mesh=split,
        in_specs=(
            rows,
            rows,
            P(),
            P("tp", None),
            P("tp", None),
            P("tp", None),
            P("tp", None),
            P(),
            P(),
        ),
        out_specs=rows,
        check_vma=False,
    )
```

time: 682 us -> 260 us (0.38)
  waiting for transfers between devices: 341 us -> 136 us
  blocking collectives: 185 us -> 45.1 us
  matrix products: 69.4 us -> 31.5 us
  local copies, waits for them, and re-layouts: 48.1 us -> 11.9 us
  starting transfers between devices: 0.21 us -> 12.5 us
  other arithmetic: 17.4 us -> 8.29 us
    all_gather x4 -> x1, waiting for transfers between devices: 286 us -> 125 us  [per_device(): packed = lax.all_gather(packed, 'z', axis=0, tiled=True)]
    all_gather x4 -> x2, blocking collectives: 185 us -> 30.3 us  [the longest x1 16.9 us: per_device(): packed = lax.all_gather(packed, 'y', axis=0, tiled=True)]
    psum x1 -> x0, waiting for transfers between devices: 54.9 us -> none  [per_device(): total_back = lax.psum(back_sum, 'tp')]
    dynamic_slice x48 -> x1, local copies, waits for them, and re-layouts: 47.7 us -> 0.64 us  [per_device(): own_positions = offsets[seq_index] * PIECE + lax.iota(jnp.int32, row_count)]
    dot_general x128 -> x7, matrix products: 61.4 us -> 26.5 us  [the longest x1 7.47 us: per_device(): jnp.einsum('hkq,qhd->khd', score_grad, query_all, preferred_element_type=...]
    all_to_all x0 -> x1, blocking collectives: none -> 14.7 us  [per_device(): received = lax.all_to_all(payload, 'tp', 0, 0, tiled=False)]
    all_to_all x0 -> x1, starting transfers between devices: none -> 12.5 us  [per_device(): stats_all = lax.all_to_all(sent, ('z', 'y'), 0, 0, tiled=False)]
    all_to_all x0 -> x1, waiting for transfers between devices: none -> 10.6 us  [per_device(): stats_all = lax.all_to_all(sent, ('z', 'y'), 0, 0, tiled=False)]
  transfers between devices with their start and end apart: 5 -> 2, of which waited for: 4 -> 2; matrix products, arithmetic and copies ran while one was open for 14% -> 3% of each run, Pallas kernels for 0% -> 0%
where the time goes in v1:
time: 260 us
  waiting for transfers between devices  136 us (52%)
  blocking collectives  45.1 us (17%)
  matrix products  31.5 us (12%)
  between operations  14.4 us (6%)
  starting transfers between devices  12.5 us (5%)
  local copies, waits for them, and re-layouts  11.9 us (5%)
  other arithmetic  8.29 us (3%)
    all_gather x1, waiting for transfers between devices, per_device(): packed = lax.all_gather(packed, 'z', axis=0, tiled=True)  125 us
    all_gather x1, blocking collectives, per_device(): packed = lax.all_gather(packed, 'y', axis=0, tiled=True)  16.9 us
    all_to_all x1, blocking collectives, per_device(): received = lax.all_to_all(payload, 'tp', 0, 0, tiled=False)  14.7 us
    all_gather x1, blocking collectives, per_device(): gathered = lax.all_gather(both, 'tp', axis=1, tiled=True)  13.4 us
    all_to_all x1, starting transfers between devices, per_device(): stats_all = lax.all_to_all(sent, ('z', 'y'), 0, 0, tiled=False)  12.5 us
    all_to_all x1, waiting for transfers between devices, per_device(): stats_all = lax.all_to_all(sent, ('z', 'y'), 0, 0, tiled=False)  10.6 us
    dot_general x1, matrix products, per_device(): jnp.einsum('hkq,qhd->khd', score_grad, query_all, preferred_element_type=...  7.47 us
    slice x1, local copies, waits for them, and re-layouts, per_device(): packed[:, 3 * cols:4 * cols].reshape(all_rows, heads_here, head_width)  6.19 us
  transfers between devices with their start and end apart: 2, of which 2 were waited for; matrix products, arithmetic and copies ran while one was open for 3% of the time, Pallas kernels for 0%

profile of v1, /device:TPU:24, one launch (start us, length us, event | category | flops | bytes accessed | tf_op | source)
XLA Modules:
  0.0 259.7 jit_solution(13433935919064924685)
XLA Ops:
  6.6 0.0 all-gather.2.cloned.1.call-start
  6.6 1.1 pad_maximum_fusion.1
  7.7 13.4 %all_gather.9 = bf16[128,2560]{0,1:T(8,128)(2,1)S(1)} all-gather(bf16[128,640]{0,1:T(8,128)(2,1)S(1)} %pad_maximum_fusion.1), channel_id=1, replica_groups=mesh['z'=16,'y'=4,'tp'=4,'dp'=2] {'tp'}, dimensions={1}, use_global_device_ids=true | all-gather | bytes 819200 | tf_op jit(solution)/shard_map/gather_features/all_gather | solution.py:42
  21.1 0.2 multiply_reduce_fusion.1
  21.2 0.1 fusion.37
  21.3 0.7 fusion.34
  22.0 0.1 mul.133
  22.1 0.2 copy.28
  22.3 0.1 multiply_convert_fusion
  22.5 0.3 convolution_convert_fusion.1
  22.8 0.3 convolution_convert_fusion.2
  23.1 0.3 convolution_convert_fusion
  23.3 0.0 copy-start.13
  23.3 0.3 fusion.28
  23.6 16.9 %all_gather.10 = bf16[512,640]{0,1:T(8,128)(2,1)} all-gather(bf16[128,640]{0,1:T(8,128)(2,1)S(1)} %pad_maximum_fusion.2), channel_id=1, replica_groups=mesh['z'=16,'y'=4,'tp'=4,'dp'=2] {'y'}, dimensions={0}, use_global_device_ids=true | all-gather | bytes 819200 | tf_op jit(solution)/shard_map/gather_sequence/all_gather | solution.py:69
  40.6 0.0 all-gather.2.cloned.1.call-update
  40.6 0.6 dynamic_slice.3
  41.9 0.1 add_bitcast_fusion
  42.0 2.7 %broadcast_compare_fusion = (pred[128,8192]{1,0:T(8,128)(4,1)}, pred[128,8192]{1,0:T(8,128)(4,1)}) fusion(s32[8192]{0:T(1024)S(1)} %add_bitcast_fusion, s32[128]{0:T(128)S(1)} %iota_add_fusion), kind=kLoop, calls=%fused_computation.22 | loop fusion | flops 2097152 | bytes 2130432 | tf_op jit(solution)/shard_map/key_pass/le | solution.py:124
  44.7 125.4 %all-gather.2.cloned.1.call-done = bf16[8192,640]{0,1:T(8,128)(2,1)} async-done(((bf16[512,640]{0,1:T(8,128)(2,1)}), bf16[8192,640]{0,1:T(8,128)(2,1)}) %all-gather.2.cloned.1.call-update) | async-done | bytes 10485776 | tf_op jit(solution)/shard_map/gather_sequence/all_gather | solution.py:70
  170.0 6.2 %fusion.36 = (bf16[8192,160]{0,1:T(8,128)(2,1)}, bf16[8192,160]{0,1:T(8,128)(2,1)}, bf16[8192,160]{0,1:T(8,128)(2,1)S(1)}, bf16[8192,160]{0,1:T(8,128)(2,1)S(1)}) fusion(bf16[8192,640]{0,1:T(8,128)(2,1)} %all-gather.2.cloned.1.call-done), kind=kLoop, calls=%fused_computation.58 | loop fusion | bytes 20971520 | tf_op jit(solution)/shard_map/gather_sequence/slice | solution.py:74
  176.2 1.8 select_reduce_fusion.1
  178.0 2.5 select_reduce_fusion
  180.5 4.8 %fusion.38 = (f32[2,128]{1,0:T(2,128)S(1)}, bf16[2,128,8192]{2,1,0:T(8,128)(2,1)}) fusion(bf16[128,2,80]{0,2,1:T(8,128)(2,1)S(1)} %bitcast.96, bf16[8192,2,80]{0,2,1:T(8,128)(2,1)S(1)} %bitcast.88, f32[2,128,8192]{2,1,0:T(8,128)S(1)} %get-tuple-element.28, f32[2,128]{1,0:T(2,128)S(1)} %log_add_fusion, pred[128,8192]{1,0:T(8,128)(4,1)S(1)} %copy-done.3), kind=kOutput, calls=%fused_computation.60 | convolution fusion | flops 346029824 | bytes 16295936 | tf_op jit(solution)/shard_map/query_pass/qhd,khd->hqk/dot_general | solution.py:95
  185.3 2.6 %fusion.25 = f32[128,2,80]{0,2,1:T(8,128)} fusion(bf16[8192,2,80]{0,2,1:T(8,128)(2,1)S(1)} %bitcast.80, f32[2,128,8192]{2,1,0:T(8,128)S(1)} %get-tuple-element.28, f32[2,128]{1,0:T(2,128)S(1)} %log_add_fusion, pred[128,8192]{1,0:T(8,128)(4,1)S(1)} %copy-done.3, f32[128,2]{0,1:T(2,128)S(1)} %bitcast.99), kind=kOutput, calls=%fused_computation.30 | convolution fusion | flops 341856256 | bytes 12142592 | tf_op jit(solution)/shard_map/query_pass/hqk,khd->hqd/dot_general | solution.py:106
  187.9 0.7 broadcast_in_dim.50
  188.6 12.5 %all-to-all-start = ((f32[64,2,2,128]{3,2,1,0:T(2,128)}), f32[64,2,2,128]{3,2,1,0:T(2,128)}, u32[]{:S(2)}, u32[]{:S(2)}) async-start(f32[64,2,2,128]{3,2,1,0:T(2,128)} %broadcast_in_dim.50), calls=%async_computation | async-start | bytes 262144 | tf_op jit(solution)/shard_map/gather_row_stats/all_to_all | solution.py:116
  201.0 0.0 copy-start.7
  201.1 3.8 %fusion.19 = f32[128,2,80]{0,2,1:T(8,128)S(1)} fusion(f32[128,2,80]{0,2,1:T(8,128)} %fusion.25, bf16[8192,2,80]{0,2,1:T(8,128)(2,1)S(1)} %bitcast.81, bf16[2,128,8192]{2,1,0:T(8,128)(2,1)} %get-tuple-element.30), kind=kOutput, calls=%fused_computation.27 | convolution fusion | flops 335564800 | bytes 6979584 | tf_op jit(solution)/shard_map/query_pass/hqk,khd->hqd/dot_general | solution.py:100
  204.8 0.1 fusion.33
  204.9 1.1 fusion.39
  206.1 10.6 %all-to-all-done = f32[64,2,2,128]{3,2,1,0:T(2,128)} async-done(((f32[64,2,2,128]{3,2,1,0:T(2,128)}), f32[64,2,2,128]{3,2,1,0:T(2,128)}, u32[]{:S(2)}, u32[]{:S(2)}) %all-to-all-start) | async-done | bytes 131104 | tf_op jit(solution)/shard_map/gather_row_stats/all_to_all | solution.py:116
  216.7 1.5 slice_bitcast_fusion
  218.2 4.5 %fusion.2 = f32[2,128,8192]{2,1,0:T(8,128)S(1)} fusion(bf16[128,2,80]{0,2,1:T(8,128)(2,1)S(1)} %bitcast.94, bf16[8192,2,80]{0,2,1:T(8,128)(2,1)} %bitcast.84, f32[2,8192]{1,0:T(2,128)S(1)} %get-tuple-element.24, pred[128,8192]{1,0:T(8,128)(4,1)} %get-tuple-element.25), kind=kOutput, calls=%fused_computation.4 | convolution fusion | flops 339738624 | bytes 12165120 | tf_op jit(solution)/shard_map/key_pass/khd,qhd->hkq/dot_general | solution.py:121
  222.8 1.6 fusion.30
  224.4 1.6 copy-done.1
  226.0 7.5 %fusion.29 = bf16[2,80,128]{2,1,0:T(8,128)(2,1)} fusion(bf16[8192,2,80]{0,2,1:T(8,128)(2,1)} %bitcast.85, f32[2,128,8192]{2,1,0:T(8,128)} %copy-done.1, bf16[128,2,80]{0,2,1:T(8,128)(2,1)S(1)} %bitcast.93, bf16[8192,2,80]{0,2,1:T(8,128)(2,1)S(1)} %bitcast.83, f32[2,8192]{1,0:T(2,128)} %get-tuple-element.23), kind=kOutput, calls=%fused_computation.32 | convolution fusion | flops 677400576 | bytes 13778944 | tf_op jit(solution)/shard_map/key_pass/hkq,qhd->khd/dot_general | solution.py:132
  233.4 1.4 convolution_add_fusion.1
  234.8 1.5 multiply_reduce_fusion
  236.3 0.2 copy.29
  236.5 0.1 scatter.8
  236.7 0.0 copy-start.11
  236.7 0.1 pad_maximum_fusion
  236.8 0.4 copy.31
  237.2 14.7 %all_to_all.10 = f32[4,129,320]{2,1,0:T(8,128)S(1)} all-to-all(f32[4,129,320]{2,1,0:T(8,128)S(1)} %copy.31), channel_id=1, replica_groups=mesh['z'=16,'y'=4,'tp'=4,'dp'=2] {'tp'}, dimensions={0} | all-to-all | bytes 1320960 | tf_op jit(solution)/shard_map/back_projection/all_to_all | solution.py:151
  252.0 0.1 reduce_sum.49
  252.0 0.1 copy.33
  252.2 0.7 add_convert_fusion
  (40 shorter events, 0.1 us)
Async XLA Ops:
  6.5 15.9 %copy-start = (bf16[160,1280]{1,0:T(8,128)(2,1)S(1)}, bf16[160,1280]{1,0:T(8,128)(2,1)}, u32[]{:S(2)}) copy-start(bf16[160,1280]{1,0:T(8,128)(2,1)} %param.16) | copy-start | bytes 1228804
  6.5 15.8 %copy-start.15 = (f32[1280]{0:T(1024)S(1)}, f32[1280]{0:T(1024)}, u32[]{:S(2)}) copy-start(f32[1280]{0:T(1024)} %param.13) | copy-start | bytes 15364
  6.5 16.2 %copy-start.5 = (bf16[160,1280]{1,0:T(8,128)(2,1)S(1)}, bf16[160,1280]{1,0:T(8,128)(2,1)}, u32[]{:S(2)}) copy-start(bf16[160,1280]{1,0:T(8,128)(2,1)} %param.15) | copy-start | bytes 1228804
  6.5 16.5 %copy-start.8 = (bf16[160,1280]{1,0:T(8,128)(2,1)S(1)}, bf16[160,1280]{1,0:T(8,128)(2,1)}, u32[]{:S(2)}) copy-start(bf16[160,1280]{1,0:T(8,128)(2,1)} %param.17) | copy-start | bytes 1228804
  6.5 16.8 %copy-start.6 = (bf16[160,1280]{1,0:T(8,128)(2,1)S(1)}, bf16[160,1280]{1,0:T(8,128)(2,1)}, u32[]{:S(2)}) copy-start(bf16[160,1280]{1,0:T(8,128)(2,1)} %param.14) | copy-start | bytes 1228804
  6.6 163.5 %all-gather.2.cloned.1.call-start = ((), (), s32[]{:S(2)}) async-start(), calls=%async_computation.2 | async-start | bytes 11141120 | tf_op jit(solution)/shard_map/gather_sequence/all_gather | solution.py:70
  21.2 19.4 %copy-start.16 = (s32[64]{0:T(128)S(1)}, s32[64]{0:T(128)}, u32[]{:S(2)}) copy-start(s32[64]{0:T(128)} %param.19) | copy-start | bytes 772
  22.3 22.3 %copy-start.4 = (f32[128,1280]{1,0:T(8,128)}, f32[128,1280]{1,0:T(8,128)S(1)}, u32[]{:S(2)}) copy-start(f32[128,1280]{1,0:T(8,128)S(1)} %copy.28) | copy-start | bytes 1966084
  23.0 21.6 %copy-start.9 = (bf16[128,160]{0,1:T(8,128)(2,1)}, bf16[128,160]{0,1:T(8,128)(2,1)S(1)}, u32[]{:S(2)}) copy-start(bf16[128,160]{0,1:T(8,128)(2,1)S(1)} %convolution_convert_fusion.2) | copy-start | bytes 122884
  23.3 21.3 %copy-start.13 = (bf16[128,160]{0,1:T(8,128)(2,1)}, bf16[128,160]{0,1:T(8,128)(2,1)S(1)}, u32[]{:S(2)}) copy-start(bf16[128,160]{0,1:T(8,128)(2,1)S(1)} %convolution_convert_fusion) | copy-start | bytes 122884
  170.0 6.2 %copy-start.3 = (pred[128,8192]{1,0:T(8,128)(4,1)S(1)}, pred[128,8192]{1,0:T(8,128)(4,1)}, u32[]{:S(2)}) copy-start(pred[128,8192]{1,0:T(8,128)(4,1)} %get-tuple-element.26) | copy-start | bytes 3145732
  178.0 2.5 copy-start.14
  188.6 28.1 %all-to-all-start = ((f32[64,2,2,128]{3,2,1,0:T(2,128)}), f32[64,2,2,128]{3,2,1,0:T(2,128)}, u32[]{:S(2)}, u32[]{:S(2)}) async-start(f32[64,2,2,128]{3,2,1,0:T(2,128)} %broadcast_in_dim.50), calls=%async_computation | async-start | bytes 262144 | tf_op jit(solution)/shard_map/gather_row_stats/all_to_all | solution.py:116
  201.0 3.9 %copy-start.7 = (bf16[160,1280]{1,0:T(8,128)(2,1)S(1)}, bf16[160,1280]{1,0:T(8,128)(2,1)}, u32[]{:S(2)}) copy-start(bf16[160,1280]{1,0:T(8,128)(2,1)} %param.14) | copy-start | bytes 1228804
  201.0 17.2 %copy-start.10 = (bf16[128,160]{0,1:T(8,128)(2,1)S(1)}, bf16[128,160]{0,1:T(8,128)(2,1)}, u32[]{:S(2)}) copy-start(bf16[128,160]{0,1:T(8,128)(2,1)} %copy-done.9) | copy-start | bytes 122884
  218.2 4.6 %copy-start.2 = (bf16[8192,160]{0,1:T(8,128)(2,1)S(1)}, bf16[8192,160]{0,1:T(8,128)(2,1)}, u32[]{:S(2)}) copy-start(bf16[8192,160]{0,1:T(8,128)(2,1)} %get-tuple-element.17) | copy-start | bytes 7864324
  222.8 3.2 %copy-start.1 = (f32[2,128,8192]{2,1,0:T(8,128)}, f32[2,128,8192]{2,1,0:T(8,128)S(1)}, u32[]{:S(2)}) copy-start(f32[2,128,8192]{2,1,0:T(8,128)S(1)} %fusion.2) | copy-start | bytes 25165828
  236.7 15.5 %copy-start.11 = (bf16[128,320]{0,1:T(8,128)(2,1)S(1)}, bf16[128,320]{0,1:T(8,128)(2,1)}, u32[]{:S(2)}) copy-start(bf16[128,320]{0,1:T(8,128)(2,1)} %param.11) | copy-start | bytes 245764
  236.7 15.5 %copy-start.12 = (bf16[128,320]{0,1:T(8,128)(2,1)S(1)}, bf16[128,320]{0,1:T(8,128)(2,1)}, u32[]{:S(2)}) copy-start(bf16[128,320]{0,1:T(8,128)(2,1)} %param.12) | copy-start | bytes 245764
Sparse Core Ops, SparseCore 0:
  40.7 129.2 all-gather.1

commit v2 on v1

--- a/solution.py
+++ b/solution.py
@@ -22,6 +22,32 @@
 
 def block_positions(offsets, rows):
     return (offsets[:, None] * PIECE + lax.iota(jnp.int32, PIECE)[None, :]).reshape(rows)
+
+
+def ring_steps(size):
+    return size // 2, (size - 1) // 2
+
+
+def two_rings(first, first_axis, first_size, second, second_axis, second_size):
+    results = []
+    state = []
+    for data, axis, size in ((first, first_axis, first_size), (second, second_axis, second_size)):
+        forward, backward = ring_steps(size)
+        pieces = [None] * size
+        pieces[0] = data
+        results.append(pieces)
+        state.append([data, data, axis, size, forward, backward])
+    for step in range(max(max(s[4], s[5]) for s in state)):
+        for pieces, entry in zip(results, state):
+            ahead, behind, axis, size, forward, backward = entry
+            if step < forward:
+                ahead = lax.ppermute(ahead, axis, [(i, (i + 1) % size) for i in range(size)])
+                pieces[size - 1 - step] = ahead
+            if step < backward:
+                behind = lax.ppermute(behind, axis, [(i, (i - 1) % size) for i in range(size)])
+                pieces[1 + step] = behind
+            entry[0], entry[1] = ahead, behind
+    return results
 
 
 def per_device(
@@ -64,17 +90,33 @@
             full_grads, w_output, contract, preferred_element_type=jnp.float32
         ).astype(jnp.bfloat16)
 
+    z_size = lax.axis_size("z")
+    z_index = lax.axis_index("z")
+    y_index = lax.axis_index("y")
+
     with jax.named_scope("gather_sequence"):
-        packed = jnp.concatenate([keys, values, queries, head_grads], axis=1)
-        packed = lax.all_gather(packed, "y", axis=0, tiled=True)
-        packed = lax.all_gather(packed, "z", axis=0, tiled=True)
-        key_all = packed[:, 0 * cols : 1 * cols].reshape(all_rows, heads_here, head_width)
-        value_all = packed[:, 1 * cols : 2 * cols].reshape(all_rows, heads_here, head_width)
-        query_all = packed[:, 2 * cols : 3 * cols].reshape(all_rows, heads_here, head_width)
-        grad_all = packed[:, 3 * cols : 4 * cols].reshape(all_rows, heads_here, head_width)
-
-    seq_index = lax.axis_index("z") * y_size + lax.axis_index("y")
-    positions = block_positions(offsets, all_rows)
+        kv = jnp.concatenate([keys, values], axis=1)
+        qg = jnp.concatenate([queries, head_grads], axis=1)
+        kv_y, qg_z = two_rings(kv, "y", y_size, qg, "z", z_size)
+        kv_y = jnp.concatenate(kv_y, axis=0)
+        qg_z = jnp.concatenate(qg_z, axis=0)
+        kv_all, qg_all = two_rings(kv_y, "z", z_size, qg_z, "y", y_size)
+        kv_all = jnp.concatenate(kv_all, axis=0)
+        qg_all = jnp.concatenate(qg_all, axis=0)
+        key_all = kv_all[:, :cols].reshape(all_rows, heads_here, head_width)
+        value_all = kv_all[:, cols:].reshape(all_rows, heads_here, head_width)
+        query_all = qg_all[:, :cols].reshape(all_rows, heads_here, head_width)
+        grad_all = qg_all[:, cols:].reshape(all_rows, heads_here, head_width)
+
+    rel_z = lax.iota(jnp.int32, z_size)
+    rel_y = lax.iota(jnp.int32, y_size)
+    abs_z = (z_index + rel_z) % z_size
+    abs_y = (y_index + rel_y) % y_size
+    kv_source = (abs_z[:, None] * y_size + abs_y[None, :]).reshape(shards)
+    qg_source = (abs_z[None, :] * y_size + abs_y[:, None]).reshape(shards)
+    key_positions = block_positions(offsets[kv_source], all_rows)
+    query_positions = block_positions(offsets[qg_source], all_rows)
+    seq_index = z_index * y_size + y_index
     own_positions = offsets[seq_index] * PIECE + lax.iota(jnp.int32, row_count)
 
     query_heads = queries.reshape(row_count, heads_here, head_width)
@@ -86,7 +128,7 @@
         scores = jnp.einsum(
             "qhd,khd->hqk", query_heads, key_all, preferred_element_type=jnp.float32
         )
-        visible = positions[None, None, :] <= own_positions[None, :, None]
+        visible = key_positions[None, None, :] <= own_positions[None, :, None]
         masked = jnp.where(visible, scores, masked_score)
         row_peak = jnp.max(masked, axis=2)
         summed = jnp.sum(jnp.where(visible, jnp.exp(masked - row_peak[:, :, None]), 0.0), axis=2)
@@ -114,6 +156,7 @@
         stats = jnp.stack([log_total, row_delta], axis=0)
         sent = jnp.broadcast_to(stats[None], (shards,) + stats.shape)
         stats_all = lax.all_to_all(sent, ("z", "y"), 0, 0, tiled=False)
+        stats_all = stats_all[qg_source]
         log_all = jnp.transpose(stats_all[:, 0], (1, 0, 2)).reshape(heads_here, all_rows)
         delta_all = jnp.transpose(stats_all[:, 1], (1, 0, 2)).reshape(heads_here, all_rows)
 
@@ -121,7 +164,7 @@
         scores_t = jnp.einsum(
             "khd,qhd->hkq", key_heads, query_all, preferred_element_type=jnp.float32
         )
-        visible_t = own_positions[None, :, None] <= positions[None, None, :]
+        visible_t = own_positions[None, :, None] <= query_positions[None, None, :]
         attend_t = jnp.exp(
             jnp.where(visible_t, scores_t - log_all[:, None, :], masked_score)
         )

time: 260 us -> 267 us (1.027)
  starting transfers between devices: 12.5 us -> 139 us
  waiting for transfers between devices: 136 us -> 19.5 us
  local copies, waits for them, and re-layouts: 11.9 us -> 32.3 us
  blocking collectives: 45.1 us -> 29.7 us
  between operations: 14.4 us -> 1.88 us
    ppermute x0 -> x36, starting transfers between devices: none -> 129 us  [the longest x16 84.7 us: two_rings(): lax.ppermute(behind, axis, [(i, (i - 1) % size) for i in range(size)])]
    all_gather x1 -> x0, waiting for transfers between devices: 125 us -> none  [per_device(): packed = lax.all_gather(packed, 'z', axis=0, tiled=True)]
    ppermute x0 -> x36, waiting for transfers between devices: none -> 19.5 us  [the longest x20 15.6 us: two_rings(): lax.ppermute(ahead, axis, [(i, (i + 1) % size) for i in range(size)])]
    all_gather x1 -> x0, blocking collectives: 16.9 us -> none  [per_device(): packed = lax.all_gather(packed, 'y', axis=0, tiled=True)]
    unnamed x35 -> x76, local copies, waits for them, and re-layouts: 1.77 us -> 16.1 us
    all_to_all x1, waiting for transfers between devices: 10.6 us -> 0.01 us  [per_device(): stats_all = lax.all_to_all(sent, ('z', 'y'), 0, 0, tiled=False)]
    gather x0 -> x3, local copies, waits for them, and re-layouts: none -> 3.82 us  [the longest x1 2.26 us: per_device(): stats_all = stats_all[qg_source]]
    concatenate x0 -> x3, local copies, waits for them, and re-layouts: none -> 3.28 us  [the longest x1 2.52 us: per_device(): qg_all = jnp.concatenate(qg_all, axis=0)]
  transfers between devices with their start and end apart: 2 -> 37, of which waited for: 2 -> 6; matrix products, arithmetic and copies ran while one was open for 3% -> 18% of each run, Pallas kernels for 0% -> 0%
where the time goes in v2:
time: 267 us; the launch traced here: 265 us
  starting transfers between devices  139 us (52%)
  matrix products  32.7 us (12%)
  local copies, waits for them, and re-layouts  32.3 us (12%)
  blocking collectives  29.7 us (11%)
  waiting for transfers between devices  19.5 us (7%)
  other arithmetic  9.64 us (4%)
    ppermute x16, starting transfers between devices, two_rings(): lax.ppermute(behind, axis, [(i, (i - 1) % size) for i in range(size)])  84.7 us
    ppermute x20, starting transfers between devices, two_rings(): lax.ppermute(ahead, axis, [(i, (i + 1) % size) for i in range(size)])  44.2 us
    all_to_all x1, blocking collectives, per_device(): received = lax.all_to_all(payload, 'tp', 0, 0, tiled=False)  16.3 us
    unnamed x76, local copies, waits for them, and re-layouts  16.1 us
    ppermute x20, waiting for transfers between devices, two_rings(): lax.ppermute(ahead, axis, [(i, (i + 1) % size) for i in range(size)])  15.6 us
    all_gather x1, blocking collectives, per_device(): gathered = lax.all_gather(both, 'tp', axis=1, tiled=True)  13.4 us
    all_to_all x1, starting transfers between devices, per_device(): stats_all = lax.all_to_all(sent, ('z', 'y'), 0, 0, tiled=False)  9.91 us
    dot_general x1, matrix products, per_device(): jnp.einsum('hkq,qhd->khd', score_grad, query_all, preferred_element_type=...  7.55 us
  transfers between devices with their start and end apart: 37, of which 6 were waited for; matrix products, arithmetic and copies ran while one was open for 18% of the time, Pallas kernels for 0%

profile of v2, /device:TPU:24, one launch (start us, length us, event | category | flops | bytes accessed | tf_op | source)
XLA Modules:
  0.0 264.5 jit_solution(3862074120216060168)
XLA Ops:
  1.1 13.4 %all_gather.3 = bf16[128,2560]{0,1:T(8,128)(2,1)S(1)} all-gather(bf16[128,640]{0,1:T(8,128)(2,1)S(1)} %pad_maximum_fusion.2), channel_id=1, replica_groups=mesh['z'=16,'y'=4,'tp'=4,'dp'=2] {'tp'}, dimensions={1}, use_global_device_ids=true | all-gather | bytes 819200 | tf_op jit(solution)/shard_map/gather_features/all_gather | solution.py:68
  17.1 2.6 collective-permute-start
  19.8 6.4 %collective-permute-start.1 = (bf16[128,320]{0,1:T(8,128)(2,1)S(1)}, bf16[128,320]{0,1:T(8,128)(2,1)S(1)}, u32[]{:S(2)}, u32[]{:S(2)}) collective-permute-start(bf16[128,320]{0,1:T(8,128)(2,1)S(1)} %get-tuple-element.58), channel_id=1, source_target_pairs={{0,8},{8,16},{16,24},{24,0},{1,9},{9,17},{17,25},{25,1},{2,10},{10... | collective-permute-start | bytes 245768 | tf_op jit(solution)/shard_map/gather_sequence/ppermute | solution.py:44
  27.6 9.4 %collective-permute-start.18 = (bf16[128,320]{0,1:T(8,128)(2,1)S(1)}, bf16[128,320]{0,1:T(8,128)(2,1)S(1)}, u32[]{:S(2)}, u32[]{:S(2)}) collective-permute-start(bf16[128,320]{0,1:T(8,128)(2,1)S(1)} %get-tuple-element.57), channel_id=1, source_target_pairs={{0,480},{32,0},{64,32},{96,64},{128,96},{160,128},{192,160},{224,1... | collective-permute-start | bytes 245768 | tf_op jit(solution)/shard_map/gather_sequence/ppermute | solution.py:47
  37.0 1.9 collective-permute-start.25
  42.5 2.1 collective-permute-start.2
  44.5 5.1 %collective-permute-start.19 = (bf16[128,320]{0,1:T(8,128)(2,1)S(1)}, bf16[128,320]{0,1:T(8,128)(2,1)S(1)}, u32[]{:S(2)}, u32[]{:S(2)}) collective-permute-start(bf16[128,320]{0,1:T(8,128)(2,1)S(1)} %collective-permute-done.18), channel_id=1, source_target_pairs={{0,480},{32,0},{64,32},{96,64},{128,96},{160,128},{192,160},{224,1... | collective-permute-start | bytes 245768 | tf_op jit(solution)/shard_map/gather_sequence/ppermute | solution.py:47
  49.7 1.9 collective-permute-start.26
  52.4 5.1 %collective-permute-start.3 = (bf16[512,320]{0,1:T(8,128)(2,1)S(1)}, bf16[512,320]{0,1:T(8,128)(2,1)S(1)}, u32[]{:S(2)}, u32[]{:S(2)}) collective-permute-start(bf16[512,320]{0,1:T(8,128)(2,1)S(1)} %pad_maximum_fusion.1), channel_id=1, source_target_pairs={{0,480},{32,0},{64,32},{96,64},{128,96},{160,128},{192,160},{224,1... | collective-permute-start | bytes 983048 | tf_op jit(solution)/shard_map/gather_sequence/ppermute | solution.py:47
  57.5 1.9 collective-permute-start.10
  59.5 5.1 %collective-permute-start.20 = (bf16[128,320]{0,1:T(8,128)(2,1)S(1)}, bf16[128,320]{0,1:T(8,128)(2,1)S(1)}, u32[]{:S(2)}, u32[]{:S(2)}) collective-permute-start(bf16[128,320]{0,1:T(8,128)(2,1)S(1)} %collective-permute-done.19), channel_id=1, source_target_pairs={{0,480},{32,0},{64,32},{96,64},{128,96},{160,128},{192,160},{224,1... | collective-permute-start | bytes 245768 | tf_op jit(solution)/shard_map/gather_sequence/ppermute | solution.py:47
  64.6 1.9 collective-permute-start.27
  67.3 5.1 %collective-permute-start.21 = (bf16[128,320]{0,1:T(8,128)(2,1)S(1)}, bf16[128,320]{0,1:T(8,128)(2,1)S(1)}, u32[]{:S(2)}, u32[]{:S(2)}) collective-permute-start(bf16[128,320]{0,1:T(8,128)(2,1)S(1)} %collective-permute-done.20), channel_id=1, source_target_pairs={{0,480},{32,0},{64,32},{96,64},{128,96},{160,128},{192,160},{224,1... | collective-permute-start | bytes 245768 | tf_op jit(solution)/shard_map/gather_sequence/ppermute | solution.py:47
  72.4 1.9 collective-permute-start.28
  75.0 5.1 %collective-permute-start.22 = (bf16[128,320]{0,1:T(8,128)(2,1)S(1)}, bf16[128,320]{0,1:T(8,128)(2,1)S(1)}, u32[]{:S(2)}, u32[]{:S(2)}) collective-permute-start(bf16[128,320]{0,1:T(8,128)(2,1)S(1)} %collective-permute-done.21), channel_id=1, source_target_pairs={{0,480},{32,0},{64,32},{96,64},{128,96},{160,128},{192,160},{224,1... | collective-permute-start | bytes 245768 | tf_op jit(solution)/shard_map/gather_sequence/ppermute | solution.py:47
  80.2 1.9 collective-permute-start.29
  82.8 5.1 %collective-permute-start.23 = (bf16[128,320]{0,1:T(8,128)(2,1)S(1)}, bf16[128,320]{0,1:T(8,128)(2,1)S(1)}, u32[]{:S(2)}, u32[]{:S(2)}) collective-permute-start(bf16[128,320]{0,1:T(8,128)(2,1)S(1)} %collective-permute-done.22), channel_id=1, source_target_pairs={{0,480},{32,0},{64,32},{96,64},{128,96},{160,128},{192,160},{224,1... | collective-permute-start | bytes 245768 | tf_op jit(solution)/shard_map/gather_sequence/ppermute | solution.py:47
  88.0 1.9 collective-permute-start.30
  90.6 5.1 %collective-permute-start.24 = (bf16[128,320]{0,1:T(8,128)(2,1)S(1)}, bf16[128,320]{0,1:T(8,128)(2,1)S(1)}, u32[]{:S(2)}, u32[]{:S(2)}) collective-permute-start(bf16[128,320]{0,1:T(8,128)(2,1)S(1)} %collective-permute-done.23), channel_id=1, source_target_pairs={{0,480},{32,0},{64,32},{96,64},{128,96},{160,128},{192,160},{224,1... | collective-permute-start | bytes 245768 | tf_op jit(solution)/shard_map/gather_sequence/ppermute | solution.py:47
  95.7 1.9 collective-permute-start.31
  98.4 5.1 %collective-permute-start.4 = (bf16[512,320]{0,1:T(8,128)(2,1)S(1)}, bf16[512,320]{0,1:T(8,128)(2,1)S(1)}, u32[]{:S(2)}, u32[]{:S(2)}) collective-permute-start(bf16[512,320]{0,1:T(8,128)(2,1)S(1)} %collective-permute-done.3), channel_id=1, source_target_pairs={{0,480},{32,0},{64,32},{96,64},{128,96},{160,128},{192,160},{224,1... | collective-permute-start | bytes 983048 | tf_op jit(solution)/shard_map/gather_sequence/ppermute | solution.py:47
  108.1 6.5 %collective-permute-done.32 = bf16[128,320]{0,1:T(8,128)(2,1)S(1)} collective-permute-done((bf16[128,320]{0,1:T(8,128)(2,1)S(1)}, bf16[128,320]{0,1:T(8,128)(2,1)S(1)}, u32[]{:S(2)}, u32[]{:S(2)}) %collective-permute-start.32) | collective-permute-done | bytes 81952 | tf_op jit(solution)/shard_map/gather_sequence/ppermute | solution.py:44
  120.1 5.1 %collective-permute-start.5 = (bf16[512,320]{0,1:T(8,128)(2,1)S(1)}, bf16[512,320]{0,1:T(8,128)(2,1)S(1)}, u32[]{:S(2)}, u32[]{:S(2)}) collective-permute-start(bf16[512,320]{0,1:T(8,128)(2,1)S(1)} %collective-permute-done.4), channel_id=1, source_target_pairs={{0,480},{32,0},{64,32},{96,64},{128,96},{160,128},{192,160},{224,1... | collective-permute-start | bytes 983048 | tf_op jit(solution)/shard_map/gather_sequence/ppermute | solution.py:47
  125.2 3.5 %collective-permute-done.12 = bf16[512,320]{0,1:T(8,128)(2,1)S(1)} collective-permute-done((bf16[512,320]{0,1:T(8,128)(2,1)S(1)}, bf16[512,320]{0,1:T(8,128)(2,1)S(1)}, u32[]{:S(2)}, u32[]{:S(2)}) %collective-permute-start.12) | collective-permute-done | bytes 327712 | tf_op jit(solution)/shard_map/gather_sequence/ppermute | solution.py:44
  132.7 4.9 %collective-permute-start.33 = (bf16[2048,320]{0,1:T(8,128)(2,1)}, bf16[2048,320]{0,1:T(8,128)(2,1)S(1)}, u32[]{:S(2)}, u32[]{:S(2)}) collective-permute-start(bf16[2048,320]{0,1:T(8,128)(2,1)} %get-tuple-element.25), channel_id=1, source_target_pairs={{0,24},{8,0},{16,8},{24,16},{1,25},{9,1},{17,9},{25,17},{2,26},{10... | collective-permute-start | bytes 3932168 | tf_op jit(solution)/shard_map/gather_sequence/ppermute | solution.py:47
  137.7 2.1 collective-permute-start.34
  139.8 5.1 %collective-permute-start.6 = (bf16[512,320]{0,1:T(8,128)(2,1)S(1)}, bf16[512,320]{0,1:T(8,128)(2,1)S(1)}, u32[]{:S(2)}, u32[]{:S(2)}) collective-permute-start(bf16[512,320]{0,1:T(8,128)(2,1)S(1)} %collective-permute-done.5), channel_id=1, source_target_pairs={{0,480},{32,0},{64,32},{96,64},{128,96},{160,128},{192,160},{224,1... | collective-permute-start | bytes 983048 | tf_op jit(solution)/shard_map/gather_sequence/ppermute | solution.py:47
  146.9 2.2 broadcast_compare_fusion
  150.2 5.6 %collective-permute-start.7 = (bf16[512,320]{0,1:T(8,128)(2,1)S(1)}, bf16[512,320]{0,1:T(8,128)(2,1)S(1)}, u32[]{:S(2)}, u32[]{:S(2)}) collective-permute-start(bf16[512,320]{0,1:T(8,128)(2,1)S(1)} %collective-permute-done.6), channel_id=1, source_target_pairs={{0,480},{32,0},{64,32},{96,64},{128,96},{160,128},{192,160},{224,1... | collective-permute-start | bytes 983048 | tf_op jit(solution)/shard_map/gather_sequence/ppermute | solution.py:47
  157.8 2.5 collective-permute-done.7
  160.3 5.6 %collective-permute-start.8 = (bf16[512,320]{0,1:T(8,128)(2,1)S(1)}, bf16[512,320]{0,1:T(8,128)(2,1)S(1)}, u32[]{:S(2)}, u32[]{:S(2)}) collective-permute-start(bf16[512,320]{0,1:T(8,128)(2,1)S(1)} %collective-permute-done.7), channel_id=1, source_target_pairs={{0,480},{32,0},{64,32},{96,64},{128,96},{160,128},{192,160},{224,1... | collective-permute-start | bytes 983048 | tf_op jit(solution)/shard_map/gather_sequence/ppermute | solution.py:47
  168.0 2.8 %collective-permute-start.35 = (bf16[2048,320]{0,1:T(8,128)(2,1)}, bf16[2048,320]{0,1:T(8,128)(2,1)}, u32[]{:S(2)}, u32[]{:S(2)}) collective-permute-start(bf16[2048,320]{0,1:T(8,128)(2,1)} %collective-permute-done.34), channel_id=1, source_target_pairs={{0,8},{8,16},{16,24},{24,0},{1,9},{9,17},{17,25},{25,1},{2,10},{10... | collective-permute-start | bytes 3932168 | tf_op jit(solution)/shard_map/gather_sequence/ppermute | solution.py:44
  170.8 5.3 %collective-permute-start.9 = (bf16[512,320]{0,1:T(8,128)(2,1)S(1)}, bf16[512,320]{0,1:T(8,128)(2,1)S(1)}, u32[]{:S(2)}, u32[]{:S(2)}) collective-permute-start(bf16[512,320]{0,1:T(8,128)(2,1)S(1)} %collective-permute-done.8), channel_id=1, source_target_pairs={{0,480},{32,0},{64,32},{96,64},{128,96},{160,128},{192,160},{224,1... | collective-permute-start | bytes 983048 | tf_op jit(solution)/shard_map/gather_sequence/ppermute | solution.py:47
  176.1 2.1 collective-permute-start.17
  180.7 5.6 %collective-permute-done.17 = bf16[512,320]{0,1:T(8,128)(2,1)S(1)} collective-permute-done((bf16[512,320]{0,1:T(8,128)(2,1)S(1)}, bf16[512,320]{0,1:T(8,128)(2,1)S(1)}, u32[]{:S(2)}, u32[]{:S(2)}) %collective-permute-start.17) | collective-permute-done | bytes 327712 | tf_op jit(solution)/shard_map/gather_sequence/ppermute | solution.py:44
  189.2 2.5 select_reduce_fusion
  191.7 4.8 %fusion.44 = (f32[2,128]{1,0:T(2,128)S(1)}, bf16[2,128,8192]{2,1,0:T(8,128)(2,1)}) fusion(bf16[128,2,80]{0,2,1:T(8,128)(2,1)S(1)} %bitcast.102, bf16[8192,2,80]{0,2,1:T(8,128)(2,1)S(1)} %bitcast.94, f32[2,128,8192]{2,1,0:T(8,128)S(1)} %get-tuple-element.63, f32[2,128]{1,0:T(2,128)S(1)} %log_add_fusion, pred[128,8192]{1,0:T(8,128)(4,1)S(1)} %get-tuple-element.61), kind=kOutput, calls=%fused_computation.139 | convolution fusion | flops 346029824 | bytes 16295936 | tf_op jit(solution)/shard_map/query_pass/qhd,khd->hqk/dot_general | solution.py:137
  196.5 2.6 fusion.25
  199.8 9.9 %all-to-all-start = ((f32[64,2,2,128]{3,2,1,0:T(2,128)}), f32[64,2,2,128]{3,2,1,0:T(2,128)}, u32[]{:S(2)}, u32[]{:S(2)}) async-start(f32[64,2,2,128]{3,2,1,0:T(2,128)} %broadcast_in_dim.59), calls=%async_computation | async-start | bytes 262144 | tf_op jit(solution)/shard_map/gather_row_stats/all_to_all | solution.py:158
  209.7 3.8 %fusion.19 = f32[128,2,80]{0,2,1:T(8,128)S(1)} fusion(f32[128,2,80]{0,2,1:T(8,128)} %fusion.25, bf16[8192,2,80]{0,2,1:T(8,128)(2,1)S(1)} %bitcast.87, bf16[2,128,8192]{2,1,0:T(8,128)(2,1)} %get-tuple-element.65), kind=kOutput, calls=%fused_computation.30 | convolution fusion | flops 335564800 | bytes 6979584 | tf_op jit(solution)/shard_map/query_pass/hqk,khd->hqd/dot_general | solution.py:142
  214.7 2.6 constant_dynamic-update-slice_fusion.36
  217.3 2.5 constant_dynamic-update-slice_fusion.35
  219.8 4.6 %fusion.41 = (bf16[8192,160]{0,1:T(8,128)(2,1)S(1)}, bf16[8192,160]{0,1:T(8,128)(2,1)}) fusion(bf16[8192,320]{0,1:T(8,128)(2,1)} %constant_dynamic-update-slice_fusion.35), kind=kLoop, calls=%fused_computation.136 | loop fusion | bytes 10485760 | tf_op jit(solution)/shard_map/gather_sequence/slice | solution.py:109
  224.4 2.3 gather_fusion.2
  228.2 4.4 %fusion.2 = f32[2,128,8192]{2,1,0:T(8,128)S(1)} fusion(bf16[128,2,80]{0,2,1:T(8,128)(2,1)S(1)} %bitcast.99, bf16[8192,2,80]{0,2,1:T(8,128)(2,1)} %bitcast.90, f32[2,8192]{1,0:T(2,128)S(1)} %get-tuple-element.24, pred[128,8192]{1,0:T(8,128)(4,1)} %get-tuple-element.60), kind=kOutput, calls=%fused_computation.7 | convolution fusion | flops 339738624 | bytes 12165120 | tf_op jit(solution)/shard_map/key_pass/khd,qhd->hkq/dot_general | solution.py:164
  232.6 2.8 %fusion.30 = bf16[2,80,128]{2,1,0:T(8,128)(2,1)} fusion(bf16[8192,2,80]{0,2,1:T(8,128)(2,1)S(1)} %bitcast.88, f32[2,128,8192]{2,1,0:T(8,128)S(1)} %fusion.2), kind=kOutput, calls=%fused_computation.36 | convolution fusion | flops 337661952 | bytes 11051008 | tf_op jit(solution)/shard_map/key_pass/hkq,qhd->khd/dot_general | solution.py:178
  235.9 7.5 %fusion.29 = bf16[2,80,128]{2,1,0:T(8,128)(2,1)} fusion(bf16[8192,2,80]{0,2,1:T(8,128)(2,1)} %bitcast.91, f32[2,128,8192]{2,1,0:T(8,128)} %copy-done.2, bf16[128,2,80]{0,2,1:T(8,128)(2,1)S(1)} %bitcast.98, bf16[8192,2,80]{0,2,1:T(8,128)(2,1)S(1)} %bitcast.89, f32[2,8192]{1,0:T(2,128)S(1)} %copy-done.14), kind=kOutput, calls=%fused_computation.35 | convolution fusion | flops 677400576 | bytes 13778944 | tf_op jit(solution)/shard_map/key_pass/hkq,qhd->khd/dot_general | solution.py:175
  247.3 16.3 %all_to_all.10 = f32[4,129,320]{2,1,0:T(8,128)S(1)} all-to-all(f32[4,129,320]{2,1,0:T(8,128)S(1)} %copy.31), channel_id=1, replica_groups=mesh['z'=16,'y'=4,'tp'=4,'dp'=2] {'tp'}, dimensions={0} | all-to-all | bytes 1320960 | tf_op jit(solution)/shard_map/back_projection/all_to_all | solution.py:194
  (169 shorter events, 47.0 us)
Async XLA Ops:
  0.0 26.2 %copy-start.20 = (f32[80]{0:T(128)S(1)}, f32[80]{0:T(128)}, u32[]{:S(2)}) copy-start(f32[80]{0:T(128)} %param.18) | copy-start | bytes 964
  0.0 26.3 %copy-start.6 = (bf16[160,1280]{1,0:T(8,128)(2,1)S(1)}, bf16[160,1280]{1,0:T(8,128)(2,1)}, u32[]{:S(2)}) copy-start(bf16[160,1280]{1,0:T(8,128)(2,1)} %param.14) | copy-start | bytes 1228804
  0.0 26.6 %copy-start.8 = (bf16[160,1280]{1,0:T(8,128)(2,1)S(1)}, bf16[160,1280]{1,0:T(8,128)(2,1)}, u32[]{:S(2)}) copy-start(bf16[160,1280]{1,0:T(8,128)(2,1)} %param.17) | copy-start | bytes 1228804
  0.0 39.3 %copy-start.1 = (s32[64]{0:T(128)S(1)}, s32[64]{0:T(128)}, u32[]{:S(2)}) copy-start(s32[64]{0:T(128)} %param.19) | copy-start | bytes 772
  15.0 134.1 %copy-start.3 = (f32[128,1280]{1,0:T(8,128)}, f32[128,1280]{1,0:T(8,128)S(1)}, u32[]{:S(2)}) copy-start(f32[128,1280]{1,0:T(8,128)S(1)} %copy.28) | copy-start | bytes 1966084
  17.1 35.2 %collective-permute-start = (bf16[128,320]{0,1:T(8,128)(2,1)S(1)}, bf16[128,320]{0,1:T(8,128)(2,1)S(1)}, u32[]{:S(2)}, u32[]{:S(2)}) collective-permute-start(bf16[128,320]{0,1:T(8,128)(2,1)S(1)} %get-tuple-element.58), channel_id=1, source_target_pairs={{0,24},{8,0},{16,8},{24,16},{1,25},{9,1},{17,9},{25,17},{2,26},{10... | collective-permute-start | bytes 245768 | tf_op jit(solution)/shard_map/gather_sequence/ppermute | solution.py:47
  19.8 22.7 %collective-permute-start.1 = (bf16[128,320]{0,1:T(8,128)(2,1)S(1)}, bf16[128,320]{0,1:T(8,128)(2,1)S(1)}, u32[]{:S(2)}, u32[]{:S(2)}) collective-permute-start(bf16[128,320]{0,1:T(8,128)(2,1)S(1)} %get-tuple-element.58), channel_id=1, source_target_pairs={{0,8},{8,16},{16,24},{24,0},{1,9},{9,17},{17,25},{25,1},{2,10},{10... | collective-permute-start | bytes 245768 | tf_op jit(solution)/shard_map/gather_sequence/ppermute | solution.py:44
  26.6 131.2 %copy-start.9 = (bf16[128,160]{0,1:T(8,128)(2,1)}, bf16[128,160]{0,1:T(8,128)(2,1)S(1)}, u32[]{:S(2)}) copy-start(bf16[128,160]{0,1:T(8,128)(2,1)S(1)} %fusion.28) | copy-start | bytes 122884
  26.9 25.5 %copy-start.15 = (bf16[128,160]{0,1:T(8,128)(2,1)}, bf16[128,160]{0,1:T(8,128)(2,1)S(1)}, u32[]{:S(2)}) copy-start(bf16[128,160]{0,1:T(8,128)(2,1)S(1)} %convolution_convert_fusion) | copy-start | bytes 122884
  27.6 16.9 %collective-permute-start.18 = (bf16[128,320]{0,1:T(8,128)(2,1)S(1)}, bf16[128,320]{0,1:T(8,128)(2,1)S(1)}, u32[]{:S(2)}, u32[]{:S(2)}) collective-permute-start(bf16[128,320]{0,1:T(8,128)(2,1)S(1)} %get-tuple-element.57), channel_id=1, source_target_pairs={{0,480},{32,0},{64,32},{96,64},{128,96},{160,128},{192,160},{224,1... | collective-permute-start | bytes 245768 | tf_op jit(solution)/shard_map/gather_sequence/ppermute | solution.py:47
  37.0 12.7 %collective-permute-start.25 = (bf16[128,320]{0,1:T(8,128)(2,1)S(1)}, bf16[128,320]{0,1:T(8,128)(2,1)S(1)}, u32[]{:S(2)}, u32[]{:S(2)}) collective-permute-start(bf16[128,320]{0,1:T(8,128)(2,1)S(1)} %get-tuple-element.57), channel_id=1, source_target_pairs={{0,32},{32,64},{64,96},{96,128},{128,160},{160,192},{192,224},{224... | collective-permute-start | bytes 245768 | tf_op jit(solution)/shard_map/gather_sequence/ppermute | solution.py:44
  41.6 107.6 %copy-start.4 = (bf16[8192,320]{0,1:T(8,128)(2,1)S(1)}, bf16[8192,320]{0,1:T(8,128)(2,1)}, u32[]{:S(2)}) copy-start(bf16[8192,320]{0,1:T(8,128)(2,1)} %get-tuple-element.59) | copy-start | bytes 15728644
  42.5 9.9 %collective-permute-start.2 = (bf16[128,320]{0,1:T(8,128)(2,1)S(1)}, bf16[128,320]{0,1:T(8,128)(2,1)S(1)}, u32[]{:S(2)}, u32[]{:S(2)}) collective-permute-start(bf16[128,320]{0,1:T(8,128)(2,1)S(1)} %collective-permute-done.1), channel_id=1, source_target_pairs={{0,8},{8,16},{16,24},{24,0},{1,9},{9,17},{17,25},{25,1},{2,10},{10... | collective-permute-start | bytes 245768 | tf_op jit(solution)/shard_map/gather_sequence/ppermute | solution.py:44
  44.5 14.9 %collective-permute-start.19 = (bf16[128,320]{0,1:T(8,128)(2,1)S(1)}, bf16[128,320]{0,1:T(8,128)(2,1)S(1)}, u32[]{:S(2)}, u32[]{:S(2)}) collective-permute-start(bf16[128,320]{0,1:T(8,128)(2,1)S(1)} %collective-permute-done.18), channel_id=1, source_target_pairs={{0,480},{32,0},{64,32},{96,64},{128,96},{160,128},{192,160},{224,1... | collective-permute-start | bytes 245768 | tf_op jit(solution)/shard_map/gather_sequence/ppermute | solution.py:47
  49.7 14.9 %collective-permute-start.26 = (bf16[128,320]{0,1:T(8,128)(2,1)S(1)}, bf16[128,320]{0,1:T(8,128)(2,1)S(1)}, u32[]{:S(2)}, u32[]{:S(2)}) collective-permute-start(bf16[128,320]{0,1:T(8,128)(2,1)S(1)} %collective-permute-done.25), channel_id=1, source_target_pairs={{0,32},{32,64},{64,96},{96,128},{128,160},{160,192},{192,224},{224... | collective-permute-start | bytes 245768 | tf_op jit(solution)/shard_map/gather_sequence/ppermute | solution.py:44
  52.3 80.4 %copy-start.11 = (bf16[128,320]{0,1:T(8,128)(2,1)}, bf16[128,320]{0,1:T(8,128)(2,1)S(1)}, u32[]{:S(2)}) copy-start(bf16[128,320]{0,1:T(8,128)(2,1)S(1)} %collective-permute-done) | copy-start | bytes 245764
  52.4 46.0 %collective-permute-start.3 = (bf16[512,320]{0,1:T(8,128)(2,1)S(1)}, bf16[512,320]{0,1:T(8,128)(2,1)S(1)}, u32[]{:S(2)}, u32[]{:S(2)}) collective-permute-start(bf16[512,320]{0,1:T(8,128)(2,1)S(1)} %pad_maximum_fusion.1), channel_id=1, source_target_pairs={{0,480},{32,0},{64,32},{96,64},{128,96},{160,128},{192,160},{224,1... | collective-permute-start | bytes 983048 | tf_op jit(solution)/shard_map/gather_sequence/ppermute | solution.py:47
  57.5 46.0 %collective-permute-start.10 = (bf16[512,320]{0,1:T(8,128)(2,1)S(1)}, bf16[512,320]{0,1:T(8,128)(2,1)S(1)}, u32[]{:S(2)}, u32[]{:S(2)}) collective-permute-start(bf16[512,320]{0,1:T(8,128)(2,1)S(1)} %pad_maximum_fusion.1), channel_id=1, source_target_pairs={{0,32},{32,64},{64,96},{96,128},{128,160},{160,192},{192,224},{224... | collective-permute-start | bytes 983048 | tf_op jit(solution)/shard_map/gather_sequence/ppermute | solution.py:44
  59.5 7.8 %collective-permute-start.20 = (bf16[128,320]{0,1:T(8,128)(2,1)S(1)}, bf16[128,320]{0,1:T(8,128)(2,1)S(1)}, u32[]{:S(2)}, u32[]{:S(2)}) collective-permute-start(bf16[128,320]{0,1:T(8,128)(2,1)S(1)} %collective-permute-done.19), channel_id=1, source_target_pairs={{0,480},{32,0},{64,32},{96,64},{128,96},{160,128},{192,160},{224,1... | collective-permute-start | bytes 245768 | tf_op jit(solution)/shard_map/gather_sequence/ppermute | solution.py:47
  64.6 7.8 %collective-permute-start.27 = (bf16[128,320]{0,1:T(8,128)(2,1)S(1)}, bf16[128,320]{0,1:T(8,128)(2,1)S(1)}, u32[]{:S(2)}, u32[]{:S(2)}) collective-permute-start(bf16[128,320]{0,1:T(8,128)(2,1)S(1)} %collective-permute-done.26), channel_id=1, source_target_pairs={{0,32},{32,64},{64,96},{96,128},{128,160},{160,192},{192,224},{224... | collective-permute-start | bytes 245768 | tf_op jit(solution)/shard_map/gather_sequence/ppermute | solution.py:44
  67.3 7.8 %collective-permute-start.21 = (bf16[128,320]{0,1:T(8,128)(2,1)S(1)}, bf16[128,320]{0,1:T(8,128)(2,1)S(1)}, u32[]{:S(2)}, u32[]{:S(2)}) collective-permute-start(bf16[128,320]{0,1:T(8,128)(2,1)S(1)} %collective-permute-done.20), channel_id=1, source_target_pairs={{0,480},{32,0},{64,32},{96,64},{128,96},{160,128},{192,160},{224,1... | collective-permute-start | bytes 245768 | tf_op jit(solution)/shard_map/gather_sequence/ppermute | solution.py:47
  72.4 7.8 %collective-permute-start.28 = (bf16[128,320]{0,1:T(8,128)(2,1)S(1)}, bf16[128,320]{0,1:T(8,128)(2,1)S(1)}, u32[]{:S(2)}, u32[]{:S(2)}) collective-permute-start(bf16[128,320]{0,1:T(8,128)(2,1)S(1)} %collective-permute-done.27), channel_id=1, source_target_pairs={{0,32},{32,64},{64,96},{96,128},{128,160},{160,192},{192,224},{224... | collective-permute-start | bytes 245768 | tf_op jit(solution)/shard_map/gather_sequence/ppermute | solution.py:44
  75.0 7.8 %collective-permute-start.22 = (bf16[128,320]{0,1:T(8,128)(2,1)S(1)}, bf16[128,320]{0,1:T(8,128)(2,1)S(1)}, u32[]{:S(2)}, u32[]{:S(2)}) collective-permute-start(bf16[128,320]{0,1:T(8,128)(2,1)S(1)} %collective-permute-done.21), channel_id=1, source_target_pairs={{0,480},{32,0},{64,32},{96,64},{128,96},{160,128},{192,160},{224,1... | collective-permute-start | bytes 245768 | tf_op jit(solution)/shard_map/gather_sequence/ppermute | solution.py:47
  80.2 7.8 %collective-permute-start.29 = (bf16[128,320]{0,1:T(8,128)(2,1)S(1)}, bf16[128,320]{0,1:T(8,128)(2,1)S(1)}, u32[]{:S(2)}, u32[]{:S(2)}) collective-permute-start(bf16[128,320]{0,1:T(8,128)(2,1)S(1)} %collective-permute-done.28), channel_id=1, source_target_pairs={{0,32},{32,64},{64,96},{96,128},{128,160},{160,192},{192,224},{224... | collective-permute-start | bytes 245768 | tf_op jit(solution)/shard_map/gather_sequence/ppermute | solution.py:44
  82.8 7.8 %collective-permute-start.23 = (bf16[128,320]{0,1:T(8,128)(2,1)S(1)}, bf16[128,320]{0,1:T(8,128)(2,1)S(1)}, u32[]{:S(2)}, u32[]{:S(2)}) collective-permute-start(bf16[128,320]{0,1:T(8,128)(2,1)S(1)} %collective-permute-done.22), channel_id=1, source_target_pairs={{0,480},{32,0},{64,32},{96,64},{128,96},{160,128},{192,160},{224,1... | collective-permute-start | bytes 245768 | tf_op jit(solution)/shard_map/gather_sequence/ppermute | solution.py:47
  88.0 7.8 %collective-permute-start.30 = (bf16[128,320]{0,1:T(8,128)(2,1)S(1)}, bf16[128,320]{0,1:T(8,128)(2,1)S(1)}, u32[]{:S(2)}, u32[]{:S(2)}) collective-permute-start(bf16[128,320]{0,1:T(8,128)(2,1)S(1)} %collective-permute-done.29), channel_id=1, source_target_pairs={{0,32},{32,64},{64,96},{96,128},{128,160},{160,192},{192,224},{224... | collective-permute-start | bytes 245768 | tf_op jit(solution)/shard_map/gather_sequence/ppermute | solution.py:44
  90.6 16.8 %collective-permute-start.24 = (bf16[128,320]{0,1:T(8,128)(2,1)S(1)}, bf16[128,320]{0,1:T(8,128)(2,1)S(1)}, u32[]{:S(2)}, u32[]{:S(2)}) collective-permute-start(bf16[128,320]{0,1:T(8,128)(2,1)S(1)} %collective-permute-done.23), channel_id=1, source_target_pairs={{0,480},{32,0},{64,32},{96,64},{128,96},{160,128},{192,160},{224,1... | collective-permute-start | bytes 245768 | tf_op jit(solution)/shard_map/gather_sequence/ppermute | solution.py:47
  95.7 9.7 %collective-permute-start.31 = (bf16[128,320]{0,1:T(8,128)(2,1)S(1)}, bf16[128,320]{0,1:T(8,128)(2,1)S(1)}, u32[]{:S(2)}, u32[]{:S(2)}) collective-permute-start(bf16[128,320]{0,1:T(8,128)(2,1)S(1)} %collective-permute-done.30), channel_id=1, source_target_pairs={{0,32},{32,64},{64,96},{96,128},{128,160},{160,192},{192,224},{224... | collective-permute-start | bytes 245768 | tf_op jit(solution)/shard_map/gather_sequence/ppermute | solution.py:44
  98.4 21.7 %collective-permute-start.4 = (bf16[512,320]{0,1:T(8,128)(2,1)S(1)}, bf16[512,320]{0,1:T(8,128)(2,1)S(1)}, u32[]{:S(2)}, u32[]{:S(2)}) collective-permute-start(bf16[512,320]{0,1:T(8,128)(2,1)S(1)} %collective-permute-done.3), channel_id=1, source_target_pairs={{0,480},{32,0},{64,32},{96,64},{128,96},{160,128},{192,160},{224,1... | collective-permute-start | bytes 983048 | tf_op jit(solution)/shard_map/gather_sequence/ppermute | solution.py:47
  103.5 12.4 %collective-permute-start.11 = (bf16[512,320]{0,1:T(8,128)(2,1)S(1)}, bf16[512,320]{0,1:T(8,128)(2,1)S(1)}, u32[]{:S(2)}, u32[]{:S(2)}) collective-permute-start(bf16[512,320]{0,1:T(8,128)(2,1)S(1)} %collective-permute-done.10), channel_id=1, source_target_pairs={{0,32},{32,64},{64,96},{96,128},{128,160},{160,192},{192,224},{224... | collective-permute-start | bytes 983048 | tf_op jit(solution)/shard_map/gather_sequence/ppermute | solution.py:44
  105.5 9.1 %collective-permute-start.32 = (bf16[128,320]{0,1:T(8,128)(2,1)S(1)}, bf16[128,320]{0,1:T(8,128)(2,1)S(1)}, u32[]{:S(2)}, u32[]{:S(2)}) collective-permute-start(bf16[128,320]{0,1:T(8,128)(2,1)S(1)} %collective-permute-done.31), channel_id=1, source_target_pairs={{0,32},{32,64},{64,96},{96,128},{128,160},{160,192},{192,224},{224... | collective-permute-start | bytes 245768 | tf_op jit(solution)/shard_map/gather_sequence/ppermute | solution.py:44
  116.0 12.7 %collective-permute-start.12 = (bf16[512,320]{0,1:T(8,128)(2,1)S(1)}, bf16[512,320]{0,1:T(8,128)(2,1)S(1)}, u32[]{:S(2)}, u32[]{:S(2)}) collective-permute-start(bf16[512,320]{0,1:T(8,128)(2,1)S(1)} %collective-permute-done.11), channel_id=1, source_target_pairs={{0,32},{32,64},{64,96},{96,128},{128,160},{160,192},{192,224},{224... | collective-permute-start | bytes 983048 | tf_op jit(solution)/shard_map/gather_sequence/ppermute | solution.py:44
  120.1 19.7 %collective-permute-start.5 = (bf16[512,320]{0,1:T(8,128)(2,1)S(1)}, bf16[512,320]{0,1:T(8,128)(2,1)S(1)}, u32[]{:S(2)}, u32[]{:S(2)}) collective-permute-start(bf16[512,320]{0,1:T(8,128)(2,1)S(1)} %collective-permute-done.4), channel_id=1, source_target_pairs={{0,480},{32,0},{64,32},{96,64},{128,96},{160,128},{192,160},{224,1... | collective-permute-start | bytes 983048 | tf_op jit(solution)/shard_map/gather_sequence/ppermute | solution.py:47
  128.7 16.3 %collective-permute-start.13 = (bf16[512,320]{0,1:T(8,128)(2,1)S(1)}, bf16[512,320]{0,1:T(8,128)(2,1)S(1)}, u32[]{:S(2)}, u32[]{:S(2)}) collective-permute-start(bf16[512,320]{0,1:T(8,128)(2,1)S(1)} %collective-permute-done.12), channel_id=1, source_target_pairs={{0,32},{32,64},{64,96},{96,128},{128,160},{160,192},{192,224},{224... | collective-permute-start | bytes 983048 | tf_op jit(solution)/shard_map/gather_sequence/ppermute | solution.py:44
  132.7 45.5 %collective-permute-start.33 = (bf16[2048,320]{0,1:T(8,128)(2,1)}, bf16[2048,320]{0,1:T(8,128)(2,1)S(1)}, u32[]{:S(2)}, u32[]{:S(2)}) collective-permute-start(bf16[2048,320]{0,1:T(8,128)(2,1)} %get-tuple-element.25), channel_id=1, source_target_pairs={{0,24},{8,0},{16,8},{24,16},{1,25},{9,1},{17,9},{25,17},{2,26},{10... | collective-permute-start | bytes 3932168 | tf_op jit(solution)/shard_map/gather_sequence/ppermute | solution.py:47
  137.7 30.4 %collective-permute-start.34 = (bf16[2048,320]{0,1:T(8,128)(2,1)}, bf16[2048,320]{0,1:T(8,128)(2,1)}, u32[]{:S(2)}, u32[]{:S(2)}) collective-permute-start(bf16[2048,320]{0,1:T(8,128)(2,1)} %get-tuple-element.25), channel_id=1, source_target_pairs={{0,8},{8,16},{16,24},{24,0},{1,9},{9,17},{17,25},{25,1},{2,10},{10... | collective-permute-start | bytes 3932168 | tf_op jit(solution)/shard_map/gather_sequence/ppermute | solution.py:44
  139.8 10.4 %collective-permute-start.6 = (bf16[512,320]{0,1:T(8,128)(2,1)S(1)}, bf16[512,320]{0,1:T(8,128)(2,1)S(1)}, u32[]{:S(2)}, u32[]{:S(2)}) collective-permute-start(bf16[512,320]{0,1:T(8,128)(2,1)S(1)} %collective-permute-done.5), channel_id=1, source_target_pairs={{0,480},{32,0},{64,32},{96,64},{128,96},{160,128},{192,160},{224,1... | collective-permute-start | bytes 983048 | tf_op jit(solution)/shard_map/gather_sequence/ppermute | solution.py:47
  145.0 10.8 %collective-permute-start.14 = (bf16[512,320]{0,1:T(8,128)(2,1)S(1)}, bf16[512,320]{0,1:T(8,128)(2,1)S(1)}, u32[]{:S(2)}, u32[]{:S(2)}) collective-permute-start(bf16[512,320]{0,1:T(8,128)(2,1)S(1)} %collective-permute-done.13), channel_id=1, source_target_pairs={{0,32},{32,64},{64,96},{96,128},{128,160},{160,192},{192,224},{224... | collective-permute-start | bytes 983048 | tf_op jit(solution)/shard_map/gather_sequence/ppermute | solution.py:44
  150.2 10.2 %collective-permute-start.7 = (bf16[512,320]{0,1:T(8,128)(2,1)S(1)}, bf16[512,320]{0,1:T(8,128)(2,1)S(1)}, u32[]{:S(2)}, u32[]{:S(2)}) collective-permute-start(bf16[512,320]{0,1:T(8,128)(2,1)S(1)} %collective-permute-done.6), channel_id=1, source_target_pairs={{0,480},{32,0},{64,32},{96,64},{128,96},{160,128},{192,160},{224,1... | collective-permute-start | bytes 983048 | tf_op jit(solution)/shard_map/gather_sequence/ppermute | solution.py:47
  155.8 10.2 %collective-permute-start.15 = (bf16[512,320]{0,1:T(8,128)(2,1)S(1)}, bf16[512,320]{0,1:T(8,128)(2,1)S(1)}, u32[]{:S(2)}, u32[]{:S(2)}) collective-permute-start(bf16[512,320]{0,1:T(8,128)(2,1)S(1)} %collective-permute-done.14), channel_id=1, source_target_pairs={{0,32},{32,64},{64,96},{96,128},{128,160},{160,192},{192,224},{224... | collective-permute-start | bytes 983048 | tf_op jit(solution)/shard_map/gather_sequence/ppermute | solution.py:44
  160.3 10.5 %collective-permute-start.8 = (bf16[512,320]{0,1:T(8,128)(2,1)S(1)}, bf16[512,320]{0,1:T(8,128)(2,1)S(1)}, u32[]{:S(2)}, u32[]{:S(2)}) collective-permute-start(bf16[512,320]{0,1:T(8,128)(2,1)S(1)} %collective-permute-done.7), channel_id=1, source_target_pairs={{0,480},{32,0},{64,32},{96,64},{128,96},{160,128},{192,160},{224,1... | collective-permute-start | bytes 983048 | tf_op jit(solution)/shard_map/gather_sequence/ppermute | solution.py:47
  166.0 10.2 %collective-permute-start.16 = (bf16[512,320]{0,1:T(8,128)(2,1)S(1)}, bf16[512,320]{0,1:T(8,128)(2,1)S(1)}, u32[]{:S(2)}, u32[]{:S(2)}) collective-permute-start(bf16[512,320]{0,1:T(8,128)(2,1)S(1)} %collective-permute-done.15), channel_id=1, source_target_pairs={{0,32},{32,64},{64,96},{96,128},{128,160},{160,192},{192,224},{224... | collective-permute-start | bytes 983048 | tf_op jit(solution)/shard_map/gather_sequence/ppermute | solution.py:44
  168.0 46.7 %collective-permute-start.35 = (bf16[2048,320]{0,1:T(8,128)(2,1)}, bf16[2048,320]{0,1:T(8,128)(2,1)}, u32[]{:S(2)}, u32[]{:S(2)}) collective-permute-start(bf16[2048,320]{0,1:T(8,128)(2,1)} %collective-permute-done.34), channel_id=1, source_target_pairs={{0,8},{8,16},{16,24},{24,0},{1,9},{9,17},{17,25},{25,1},{2,10},{10... | collective-permute-start | bytes 3932168 | tf_op jit(solution)/shard_map/gather_sequence/ppermute | solution.py:44
  170.8 9.9 %collective-permute-start.9 = (bf16[512,320]{0,1:T(8,128)(2,1)S(1)}, bf16[512,320]{0,1:T(8,128)(2,1)S(1)}, u32[]{:S(2)}, u32[]{:S(2)}) collective-permute-start(bf16[512,320]{0,1:T(8,128)(2,1)S(1)} %collective-permute-done.8), channel_id=1, source_target_pairs={{0,480},{32,0},{64,32},{96,64},{128,96},{160,128},{192,160},{224,1... | collective-permute-start | bytes 983048 | tf_op jit(solution)/shard_map/gather_sequence/ppermute | solution.py:47
  176.1 10.2 %collective-permute-start.17 = (bf16[512,320]{0,1:T(8,128)(2,1)S(1)}, bf16[512,320]{0,1:T(8,128)(2,1)S(1)}, u32[]{:S(2)}, u32[]{:S(2)}) collective-permute-start(bf16[512,320]{0,1:T(8,128)(2,1)S(1)} %collective-permute-done.16), channel_id=1, source_target_pairs={{0,32},{32,64},{64,96},{96,128},{128,160},{160,192},{192,224},{224... | collective-permute-start | bytes 983048 | tf_op jit(solution)/shard_map/gather_sequence/ppermute | solution.py:44
  199.8 24.6 %all-to-all-start = ((f32[64,2,2,128]{3,2,1,0:T(2,128)}), f32[64,2,2,128]{3,2,1,0:T(2,128)}, u32[]{:S(2)}, u32[]{:S(2)}) async-start(f32[64,2,2,128]{3,2,1,0:T(2,128)} %broadcast_in_dim.59), calls=%async_computation | async-start | bytes 262144 | tf_op jit(solution)/shard_map/gather_row_stats/all_to_all | solution.py:158
  246.3 17.5 %copy-start.12 = (bf16[128,320]{0,1:T(8,128)(2,1)S(1)}, bf16[128,320]{0,1:T(8,128)(2,1)}, u32[]{:S(2)}) copy-start(bf16[128,320]{0,1:T(8,128)(2,1)} %param.11) | copy-start | bytes 245764
  246.4 17.5 %copy-start.13 = (bf16[128,320]{0,1:T(8,128)(2,1)S(1)}, bf16[128,320]{0,1:T(8,128)(2,1)}, u32[]{:S(2)}) copy-start(bf16[128,320]{0,1:T(8,128)(2,1)} %param.12) | copy-start | bytes 245764
  (10 other events, 83.6 us)

commit v3 on v2

--- a/solution.py
+++ b/solution.py
@@ -28,26 +28,19 @@
     return size // 2, (size - 1) // 2
 
 
-def two_rings(first, first_axis, first_size, second, second_axis, second_size):
-    results = []
-    state = []
-    for data, axis, size in ((first, first_axis, first_size), (second, second_axis, second_size)):
-        forward, backward = ring_steps(size)
-        pieces = [None] * size
-        pieces[0] = data
-        results.append(pieces)
-        state.append([data, data, axis, size, forward, backward])
-    for step in range(max(max(s[4], s[5]) for s in state)):
-        for pieces, entry in zip(results, state):
-            ahead, behind, axis, size, forward, backward = entry
-            if step < forward:
-                ahead = lax.ppermute(ahead, axis, [(i, (i + 1) % size) for i in range(size)])
-                pieces[size - 1 - step] = ahead
-            if step < backward:
-                behind = lax.ppermute(behind, axis, [(i, (i - 1) % size) for i in range(size)])
-                pieces[1 + step] = behind
-            entry[0], entry[1] = ahead, behind
-    return results
+def ring_gather(data, axis, size):
+    forward, backward = ring_steps(size)
+    pieces = [None] * size
+    pieces[0] = data
+    ahead = behind = data
+    for step in range(max(forward, backward)):
+        if step < forward:
+            ahead = lax.ppermute(ahead, axis, [(i, (i + 1) % size) for i in range(size)])
+            pieces[size - 1 - step] = ahead
+        if step < backward:
+            behind = lax.ppermute(behind, axis, [(i, (i - 1) % size) for i in range(size)])
+            pieces[1 + step] = behind
+    return pieces
 
 
 def per_device(
@@ -97,12 +90,10 @@
     with jax.named_scope("gather_sequence"):
         kv = jnp.concatenate([keys, values], axis=1)
         qg = jnp.concatenate([queries, head_grads], axis=1)
-        kv_y, qg_z = two_rings(kv, "y", y_size, qg, "z", z_size)
-        kv_y = jnp.concatenate(kv_y, axis=0)
-        qg_z = jnp.concatenate(qg_z, axis=0)
-        kv_all, qg_all = two_rings(kv_y, "z", z_size, qg_z, "y", y_size)
-        kv_all = jnp.concatenate(kv_all, axis=0)
-        qg_all = jnp.concatenate(qg_all, axis=0)
+        kv_all = lax.all_gather(kv, "y", axis=0, tiled=True)
+        kv_all = lax.all_gather(kv_all, "z", axis=0, tiled=True)
+        qg_z = jnp.concatenate(ring_gather(qg, "z", z_size), axis=0)
+        qg_all = jnp.concatenate(ring_gather(qg_z, "y", y_size), axis=0)
         key_all = kv_all[:, :cols].reshape(all_rows, heads_here, head_width)
         value_all = kv_all[:, cols:].reshape(all_rows, heads_here, head_width)
         query_all = qg_all[:, :cols].reshape(all_rows, heads_here, head_width)
@@ -112,9 +103,8 @@
     rel_y = lax.iota(jnp.int32, y_size)
     abs_z = (z_index + rel_z) % z_size
     abs_y = (y_index + rel_y) % y_size
-    kv_source = (abs_z[:, None] * y_size + abs_y[None, :]).reshape(shards)
     qg_source = (abs_z[None, :] * y_size + abs_y[:, None]).reshape(shards)
-    key_positions = block_positions(offsets[kv_source], all_rows)
+    key_positions = block_positions(offsets, all_rows)
     query_positions = block_positions(offsets[qg_source], all_rows)
     seq_index = z_index * y_size + y_index
     own_positions = offsets[seq_index] * PIECE + lax.iota(jnp.int32, row_count)

time: 267 us -> 269 us (level)
  starting transfers between devices: 139 us -> 77.9 us
  waiting for transfers between devices: 19.5 us -> 62.2 us
  between operations: 1.88 us -> 14.6 us
  blocking collectives: 29.7 us -> 40.2 us
    ppermute x36 -> x18, starting transfers between devices: 129 us -> 67.2 us  [the longest x8 44.2 us: ring_gather(): lax.ppermute(behind, axis, [(i, (i - 1) % size) for i in range(size)])]
    ppermute x36 -> x18, waiting for transfers between devices: 19.5 us -> 53 us  [the longest x10 50.1 us: ring_gather(): lax.ppermute(ahead, axis, [(i, (i + 1) % size) for i in range(size)])]
    all_gather x0 -> x1, blocking collectives: none -> 14.6 us  [per_device(): kv_all = lax.all_gather(kv, 'y', axis=0, tiled=True)]
    all_to_all x1, waiting for transfers between devices: 0.01 us -> 9.24 us  [per_device(): stats_all = lax.all_to_all(sent, ('z', 'y'), 0, 0, tiled=False)]
    all_to_all x1, blocking collectives: 16.3 us -> 12.1 us  [per_device(): received = lax.all_to_all(payload, 'tp', 0, 0, tiled=False)]
    unnamed x76 -> x55, local copies, waits for them, and re-layouts: 16.1 us -> 15.6 us
  transfers between devices with their start and end apart: 37 -> 20, of which waited for: 6 -> 15; matrix products, arithmetic and copies ran while one was open for 18% -> 11% of each run, Pallas kernels for 0% -> 0%
where the time goes in v3:
time: 269 us; the launch traced here: 267 us
  starting transfers between devices  77.9 us (29%)
  waiting for transfers between devices  62.2 us (23%)
  blocking collectives  40.2 us (15%)
  local copies, waits for them, and re-layouts  31.6 us (12%)
  matrix products  31.5 us (12%)
  between operations  14.6 us (5%)
  other arithmetic  8.47 us (3%)
    ppermute x10, waiting for transfers between devices, ring_gather(): lax.ppermute(ahead, axis, [(i, (i + 1) % size) for i in range(size)])  50.1 us
    ppermute x8, starting transfers between devices, ring_gather(): lax.ppermute(behind, axis, [(i, (i - 1) % size) for i in range(size)])  44.2 us
    ppermute x10, starting transfers between devices, ring_gather(): lax.ppermute(ahead, axis, [(i, (i + 1) % size) for i in range(size)])  22.9 us
    unnamed x55, local copies, waits for them, and re-layouts  15.6 us
    all_gather x1, blocking collectives, per_device(): kv_all = lax.all_gather(kv, 'y', axis=0, tiled=True)  14.6 us
    all_gather x1, blocking collectives, per_device(): gathered = lax.all_gather(both, 'tp', axis=1, tiled=True)  13.5 us
    all_to_all x1, blocking collectives, per_device(): received = lax.all_to_all(payload, 'tp', 0, 0, tiled=False)  12.1 us
    all_to_all x1, starting transfers between devices, per_device(): stats_all = lax.all_to_all(sent, ('z', 'y'), 0, 0, tiled=False)  10.7 us
  transfers between devices with their start and end apart: 20, of which 15 were waited for; matrix products, arithmetic and copies ran while one was open for 11% of the time, Pallas kernels for 0%

profile of v3, /device:TPU:24, one launch (start us, length us, event | category | flops | bytes accessed | tf_op | source)
XLA Modules:
  0.0 266.6 jit_solution(12104290310467089872)
XLA Ops:
  7.6 13.5 %all_gather.9 = bf16[128,2560]{0,1:T(8,128)(2,1)S(1)} all-gather(bf16[128,640]{0,1:T(8,128)(2,1)S(1)} %pad_maximum_fusion.1), channel_id=1, replica_groups=mesh['z'=16,'y'=4,'tp'=4,'dp'=2] {'tp'}, dimensions={1}, use_global_device_ids=true | all-gather | bytes 819200 | tf_op jit(solution)/shard_map/gather_features/all_gather | solution.py:61
  23.2 14.6 %all_gather.10 = bf16[512,320]{0,1:T(8,128)(2,1)} all-gather(bf16[128,320]{0,1:T(8,128)(2,1)S(1)} %pad_maximum_fusion.2), channel_id=1, replica_groups=mesh['z'=16,'y'=4,'tp'=4,'dp'=2] {'y'}, dimensions={0}, use_global_device_ids=true | all-gather | bytes 409600 | tf_op jit(solution)/shard_map/gather_sequence/all_gather | solution.py:93
  39.2 8.9 %collective-permute-start = (bf16[128,320]{0,1:T(8,128)(2,1)S(1)}, bf16[128,320]{0,1:T(8,128)(2,1)S(1)}, u32[]{:S(2)}, u32[]{:S(2)}) collective-permute-start(bf16[128,320]{0,1:T(8,128)(2,1)S(1)} %get-tuple-element.57), channel_id=1, source_target_pairs={{0,480},{32,0},{64,32},{96,64},{128,96},{160,128},{192,160},{224,1... | collective-permute-start | bytes 245768 | tf_op jit(solution)/shard_map/gather_sequence/ppermute | solution.py:41
  48.1 1.9 collective-permute-start.7
  50.1 5.5 %collective-permute-start.1 = (bf16[128,320]{0,1:T(8,128)(2,1)S(1)}, bf16[128,320]{0,1:T(8,128)(2,1)S(1)}, u32[]{:S(2)}, u32[]{:S(2)}) collective-permute-start(bf16[128,320]{0,1:T(8,128)(2,1)S(1)} %collective-permute-done), channel_id=1, source_target_pairs={{0,480},{32,0},{64,32},{96,64},{128,96},{160,128},{192,160},{224,1... | collective-permute-start | bytes 245768 | tf_op jit(solution)/shard_map/gather_sequence/ppermute | solution.py:41
  55.6 1.9 collective-permute-start.8
  59.2 5.6 %collective-permute-start.2 = (bf16[128,320]{0,1:T(8,128)(2,1)S(1)}, bf16[128,320]{0,1:T(8,128)(2,1)S(1)}, u32[]{:S(2)}, u32[]{:S(2)}) collective-permute-start(bf16[128,320]{0,1:T(8,128)(2,1)S(1)} %collective-permute-done.1), channel_id=1, source_target_pairs={{0,480},{32,0},{64,32},{96,64},{128,96},{160,128},{192,160},{224,1... | collective-permute-start | bytes 245768 | tf_op jit(solution)/shard_map/gather_sequence/ppermute | solution.py:41
  64.9 1.9 collective-permute-start.9
  67.9 5.6 %collective-permute-start.3 = (bf16[128,320]{0,1:T(8,128)(2,1)S(1)}, bf16[128,320]{0,1:T(8,128)(2,1)S(1)}, u32[]{:S(2)}, u32[]{:S(2)}) collective-permute-start(bf16[128,320]{0,1:T(8,128)(2,1)S(1)} %collective-permute-done.2), channel_id=1, source_target_pairs={{0,480},{32,0},{64,32},{96,64},{128,96},{160,128},{192,160},{224,1... | collective-permute-start | bytes 245768 | tf_op jit(solution)/shard_map/gather_sequence/ppermute | solution.py:41
  73.5 1.2 collective-permute-done.9
  74.6 1.9 collective-permute-start.10
  77.5 5.6 %collective-permute-start.4 = (bf16[128,320]{0,1:T(8,128)(2,1)S(1)}, bf16[128,320]{0,1:T(8,128)(2,1)S(1)}, u32[]{:S(2)}, u32[]{:S(2)}) collective-permute-start(bf16[128,320]{0,1:T(8,128)(2,1)S(1)} %collective-permute-done.3), channel_id=1, source_target_pairs={{0,480},{32,0},{64,32},{96,64},{128,96},{160,128},{192,160},{224,1... | collective-permute-start | bytes 245768 | tf_op jit(solution)/shard_map/gather_sequence/ppermute | solution.py:41
  83.1 2.0 collective-permute-start.11
  86.4 5.6 %collective-permute-start.5 = (bf16[128,320]{0,1:T(8,128)(2,1)S(1)}, bf16[128,320]{0,1:T(8,128)(2,1)S(1)}, u32[]{:S(2)}, u32[]{:S(2)}) collective-permute-start(bf16[128,320]{0,1:T(8,128)(2,1)S(1)} %collective-permute-done.4), channel_id=1, source_target_pairs={{0,480},{32,0},{64,32},{96,64},{128,96},{160,128},{192,160},{224,1... | collective-permute-start | bytes 245768 | tf_op jit(solution)/shard_map/gather_sequence/ppermute | solution.py:41
  92.7 1.9 collective-permute-start.12
  95.9 5.6 %collective-permute-start.6 = (bf16[128,320]{0,1:T(8,128)(2,1)S(1)}, bf16[128,320]{0,1:T(8,128)(2,1)S(1)}, u32[]{:S(2)}, u32[]{:S(2)}) collective-permute-start(bf16[128,320]{0,1:T(8,128)(2,1)S(1)} %collective-permute-done.5), channel_id=1, source_target_pairs={{0,480},{32,0},{64,32},{96,64},{128,96},{160,128},{192,160},{224,1... | collective-permute-start | bytes 245768 | tf_op jit(solution)/shard_map/gather_sequence/ppermute | solution.py:41
  102.0 1.9 collective-permute-start.13
  104.6 6.3 %collective-permute-done.13 = bf16[128,320]{0,1:T(8,128)(2,1)S(1)} collective-permute-done((bf16[128,320]{0,1:T(8,128)(2,1)S(1)}, bf16[128,320]{0,1:T(8,128)(2,1)S(1)}, u32[]{:S(2)}, u32[]{:S(2)}) %collective-permute-start.13) | collective-permute-done | bytes 81952 | tf_op jit(solution)/shard_map/gather_sequence/ppermute | solution.py:38
  111.0 1.9 collective-permute-start.14
  113.6 6.2 %collective-permute-done.14 = bf16[128,320]{0,1:T(8,128)(2,1)S(1)} collective-permute-done((bf16[128,320]{0,1:T(8,128)(2,1)S(1)}, bf16[128,320]{0,1:T(8,128)(2,1)S(1)}, u32[]{:S(2)}, u32[]{:S(2)}) %collective-permute-start.14) | collective-permute-done | bytes 81952 | tf_op jit(solution)/shard_map/gather_sequence/ppermute | solution.py:38
  125.2 1.1 copy-done.17
  126.3 4.4 %collective-permute-start.16 = (bf16[2048,320]{0,1:T(8,128)(2,1)}, bf16[2048,320]{0,1:T(8,128)(2,1)S(1)}, u32[]{:S(2)}, u32[]{:S(2)}) collective-permute-start(bf16[2048,320]{0,1:T(8,128)(2,1)} %copy-done.17), channel_id=1, source_target_pairs={{0,8},{8,16},{16,24},{24,0},{1,9},{9,17},{17,25},{25,1},{2,10},{10... | collective-permute-start | bytes 3932168 | tf_op jit(solution)/shard_map/gather_sequence/ppermute | solution.py:38
  133.1 1.9 collective-permute-start.15
  135.0 20.9 %collective-permute-done.16 = bf16[2048,320]{0,1:T(8,128)(2,1)S(1)} collective-permute-done((bf16[2048,320]{0,1:T(8,128)(2,1)}, bf16[2048,320]{0,1:T(8,128)(2,1)S(1)}, u32[]{:S(2)}, u32[]{:S(2)}) %collective-permute-start.16) | collective-permute-done | bytes 1310752 | tf_op jit(solution)/shard_map/gather_sequence/ppermute | solution.py:38
  155.9 3.1 %collective-permute-start.17 = (bf16[2048,320]{0,1:T(8,128)(2,1)S(1)}, bf16[2048,320]{0,1:T(8,128)(2,1)S(1)}, u32[]{:S(2)}, u32[]{:S(2)}) collective-permute-start(bf16[2048,320]{0,1:T(8,128)(2,1)S(1)} %collective-permute-done.16), channel_id=1, source_target_pairs={{0,8},{8,16},{16,24},{24,0},{1,9},{9,17},{17,25},{25,1},{2,10},{10... | collective-permute-start | bytes 3932168 | tf_op jit(solution)/shard_map/gather_sequence/ppermute | solution.py:38
  159.1 2.7 %broadcast_compare_fusion = (pred[128,8192]{1,0:T(8,128)(4,1)}, pred[128,8192]{1,0:T(8,128)(4,1)}) fusion(s32[8192]{0:T(1024)S(1)} %get-tuple-element.66, s32[128]{0:T(128)S(1)} %iota_add_fusion, s32[8192]{0:T(1024)S(1)} %get-tuple-element.67), kind=kLoop, calls=%fused_computation.24 | loop fusion | flops 2097152 | bytes 2163200 | tf_op jit(solution)/shard_map/key_pass/le | solution.py:157
  161.8 1.2 constant_dynamic-update-slice_fusion.18
  162.9 14.1 %collective-permute-done.17 = bf16[2048,320]{0,1:T(8,128)(2,1)S(1)} collective-permute-done((bf16[2048,320]{0,1:T(8,128)(2,1)S(1)}, bf16[2048,320]{0,1:T(8,128)(2,1)S(1)}, u32[]{:S(2)}, u32[]{:S(2)}) %collective-permute-start.17) | collective-permute-done | bytes 1310752 | tf_op jit(solution)/shard_map/gather_sequence/ppermute | solution.py:38
  177.1 1.2 constant_dynamic-update-slice_fusion.17
  178.3 1.2 constant_dynamic-update-slice_fusion.16
  179.4 5.5 %fusion.40 = (bf16[8192,160]{0,1:T(8,128)(2,1)}, bf16[8192,160]{0,1:T(8,128)(2,1)}) fusion(bf16[8192,320]{0,1:T(8,128)(2,1)} %constant_dynamic-update-slice_fusion.16), kind=kLoop, calls=%fused_computation.111 | loop fusion | bytes 10485760 | tf_op jit(solution)/shard_map/gather_sequence/slice | solution.py:100
  184.9 3.1 %fusion.41 = (bf16[8192,160]{0,1:T(8,128)(2,1)S(1)}, bf16[8192,160]{0,1:T(8,128)(2,1)S(1)}) fusion(bf16[8192,320]{0,1:T(8,128)(2,1)} %all-gather.2.cloned.1.call-done), kind=kLoop, calls=%fused_computation.112 | loop fusion | bytes 10485760 | tf_op jit(solution)/shard_map/gather_sequence/slice | solution.py:98
  188.0 1.8 select_reduce_fusion.1
  189.8 2.5 select_reduce_fusion
  192.3 4.7 %fusion.43 = (f32[2,128]{1,0:T(2,128)S(1)}, bf16[2,128,8192]{2,1,0:T(8,128)(2,1)}) fusion(bf16[128,2,80]{0,2,1:T(8,128)(2,1)S(1)} %bitcast.100, bf16[8192,2,80]{0,2,1:T(8,128)(2,1)S(1)} %bitcast.92, f32[2,128,8192]{2,1,0:T(8,128)S(1)} %get-tuple-element.61, f32[2,128]{1,0:T(2,128)S(1)} %log_add_fusion, pred[128,8192]{1,0:T(8,128)(4,1)S(1)} %copy-done.4), kind=kOutput, calls=%fused_computation.114 | convolution fusion | flops 346029824 | bytes 16295936 | tf_op jit(solution)/shard_map/query_pass/qhd,khd->hqk/dot_general | solution.py:127
  197.0 2.6 fusion.25
  200.3 10.7 %all-to-all-start = ((f32[64,2,2,128]{3,2,1,0:T(2,128)}), f32[64,2,2,128]{3,2,1,0:T(2,128)}, u32[]{:S(2)}, u32[]{:S(2)}) async-start(f32[64,2,2,128]{3,2,1,0:T(2,128)} %broadcast_in_dim.56), calls=%async_computation | async-start | bytes 262144 | tf_op jit(solution)/shard_map/gather_row_stats/all_to_all | solution.py:148
  211.0 3.8 %fusion.19 = f32[128,2,80]{0,2,1:T(8,128)S(1)} fusion(f32[128,2,80]{0,2,1:T(8,128)} %fusion.25, bf16[8192,2,80]{0,2,1:T(8,128)(2,1)S(1)} %bitcast.85, bf16[2,128,8192]{2,1,0:T(8,128)(2,1)} %get-tuple-element.63), kind=kOutput, calls=%fused_computation.29 | convolution fusion | flops 335564800 | bytes 6979584 | tf_op jit(solution)/shard_map/query_pass/hqk,khd->hqd/dot_general | solution.py:132
  214.9 1.1 fusion.44
  216.0 9.2 %all-to-all-done = f32[64,2,2,128]{3,2,1,0:T(2,128)} async-done(((f32[64,2,2,128]{3,2,1,0:T(2,128)}), f32[64,2,2,128]{3,2,1,0:T(2,128)}, u32[]{:S(2)}, u32[]{:S(2)}) %all-to-all-start) | async-done | bytes 131104 | tf_op jit(solution)/shard_map/gather_row_stats/all_to_all | solution.py:148
  225.3 1.6 gather_fusion.1
  227.6 4.5 %fusion.2 = f32[2,128,8192]{2,1,0:T(8,128)S(1)} fusion(bf16[128,2,80]{0,2,1:T(8,128)(2,1)S(1)} %bitcast.98, bf16[8192,2,80]{0,2,1:T(8,128)(2,1)} %bitcast.88, f32[2,8192]{1,0:T(2,128)S(1)} %get-tuple-element.24, pred[128,8192]{1,0:T(8,128)(4,1)} %get-tuple-element.58), kind=kOutput, calls=%fused_computation.6 | convolution fusion | flops 339738624 | bytes 12165120 | tf_op jit(solution)/shard_map/key_pass/khd,qhd->hkq/dot_general | solution.py:154
  232.2 1.6 fusion.30
  233.8 1.7 copy-done.2
  235.4 7.5 %fusion.29 = bf16[2,80,128]{2,1,0:T(8,128)(2,1)} fusion(bf16[8192,2,80]{0,2,1:T(8,128)(2,1)} %bitcast.89, f32[2,128,8192]{2,1,0:T(8,128)} %copy-done.2, bf16[128,2,80]{0,2,1:T(8,128)(2,1)S(1)} %bitcast.97, bf16[8192,2,80]{0,2,1:T(8,128)(2,1)S(1)} %bitcast.87, f32[2,8192]{1,0:T(2,128)} %get-tuple-element.23), kind=kOutput, calls=%fused_computation.34 | convolution fusion | flops 677400576 | bytes 13778944 | tf_op jit(solution)/shard_map/key_pass/hkq,qhd->khd/dot_general | solution.py:165
  242.9 1.4 convolution_add_fusion.1
  244.3 1.5 multiply_reduce_fusion
  246.7 12.1 %all_to_all.10 = f32[4,129,320]{2,1,0:T(8,128)S(1)} all-to-all(f32[4,129,320]{2,1,0:T(8,128)S(1)} %copy.31), channel_id=1, replica_groups=mesh['z'=16,'y'=4,'tp'=4,'dp'=2] {'tp'}, dimensions={0} | all-to-all | bytes 1320960 | tf_op jit(solution)/shard_map/back_projection/all_to_all | solution.py:184
  (109 shorter events, 23.7 us)
Async XLA Ops:
  6.5 16.1 %copy-start = (bf16[160,1280]{1,0:T(8,128)(2,1)S(1)}, bf16[160,1280]{1,0:T(8,128)(2,1)}, u32[]{:S(2)}) copy-start(bf16[160,1280]{1,0:T(8,128)(2,1)} %param.16) | copy-start | bytes 1228804
  6.5 16.0 %copy-start.16 = (f32[1280]{0:T(1024)S(1)}, f32[1280]{0:T(1024)}, u32[]{:S(2)}) copy-start(f32[1280]{0:T(1024)} %param.13) | copy-start | bytes 15364
  6.5 16.4 %copy-start.6 = (bf16[160,1280]{1,0:T(8,128)(2,1)S(1)}, bf16[160,1280]{1,0:T(8,128)(2,1)}, u32[]{:S(2)}) copy-start(bf16[160,1280]{1,0:T(8,128)(2,1)} %param.15) | copy-start | bytes 1228804
  6.5 31.3 %copy-start.18 = (f32[80]{0:T(128)S(1)}, f32[80]{0:T(128)}, u32[]{:S(2)}) copy-start(f32[80]{0:T(128)} %param.18) | copy-start | bytes 964
  6.5 31.4 %copy-start.9 = (bf16[160,1280]{1,0:T(8,128)(2,1)S(1)}, bf16[160,1280]{1,0:T(8,128)(2,1)}, u32[]{:S(2)}) copy-start(bf16[160,1280]{1,0:T(8,128)(2,1)} %param.17) | copy-start | bytes 1228804
  6.5 178.4 %all-gather.2.cloned.1.call-start = ((), (), s32[]{:S(2)}) async-start(), calls=%async_computation.2 | async-start | bytes 5570560 | tf_op jit(solution)/shard_map/gather_sequence/all_gather | solution.py:94
  7.6 30.6 %copy-start.7 = (bf16[160,1280]{1,0:T(8,128)(2,1)S(1)}, bf16[160,1280]{1,0:T(8,128)(2,1)}, u32[]{:S(2)}) copy-start(bf16[160,1280]{1,0:T(8,128)(2,1)} %param.14) | copy-start | bytes 1228804
  21.7 0.8 copy-start.5
  22.6 108.3 %copy-start.1 = (s32[64]{0:T(128)S(1)}, s32[64]{0:T(128)}, u32[]{:S(2)}) copy-start(s32[64]{0:T(128)} %param.19) | copy-start | bytes 772
  23.2 14.7 %copy-start.10 = (bf16[128,160]{0,1:T(8,128)(2,1)}, bf16[128,160]{0,1:T(8,128)(2,1)S(1)}, u32[]{:S(2)}) copy-start(bf16[128,160]{0,1:T(8,128)(2,1)S(1)} %convolution_convert_fusion.2) | copy-start | bytes 122884
  38.2 124.7 %copy-start.14 = (bf16[128,160]{0,1:T(8,128)(2,1)}, bf16[128,160]{0,1:T(8,128)(2,1)S(1)}, u32[]{:S(2)}) copy-start(bf16[128,160]{0,1:T(8,128)(2,1)S(1)} %convolution_convert_fusion) | copy-start | bytes 122884
  39.2 10.9 %collective-permute-start = (bf16[128,320]{0,1:T(8,128)(2,1)S(1)}, bf16[128,320]{0,1:T(8,128)(2,1)S(1)}, u32[]{:S(2)}, u32[]{:S(2)}) collective-permute-start(bf16[128,320]{0,1:T(8,128)(2,1)S(1)} %get-tuple-element.57), channel_id=1, source_target_pairs={{0,480},{32,0},{64,32},{96,64},{128,96},{160,128},{192,160},{224,1... | collective-permute-start | bytes 245768 | tf_op jit(solution)/shard_map/gather_sequence/ppermute | solution.py:41
  48.1 7.5 %collective-permute-start.7 = (bf16[128,320]{0,1:T(8,128)(2,1)S(1)}, bf16[128,320]{0,1:T(8,128)(2,1)S(1)}, u32[]{:S(2)}, u32[]{:S(2)}) collective-permute-start(bf16[128,320]{0,1:T(8,128)(2,1)S(1)} %get-tuple-element.57), channel_id=1, source_target_pairs={{0,32},{32,64},{64,96},{96,128},{128,160},{160,192},{192,224},{224... | collective-permute-start | bytes 245768 | tf_op jit(solution)/shard_map/gather_sequence/ppermute | solution.py:38
  50.1 9.1 %collective-permute-start.1 = (bf16[128,320]{0,1:T(8,128)(2,1)S(1)}, bf16[128,320]{0,1:T(8,128)(2,1)S(1)}, u32[]{:S(2)}, u32[]{:S(2)}) collective-permute-start(bf16[128,320]{0,1:T(8,128)(2,1)S(1)} %collective-permute-done), channel_id=1, source_target_pairs={{0,480},{32,0},{64,32},{96,64},{128,96},{160,128},{192,160},{224,1... | collective-permute-start | bytes 245768 | tf_op jit(solution)/shard_map/gather_sequence/ppermute | solution.py:41
  55.6 9.3 %collective-permute-start.8 = (bf16[128,320]{0,1:T(8,128)(2,1)S(1)}, bf16[128,320]{0,1:T(8,128)(2,1)S(1)}, u32[]{:S(2)}, u32[]{:S(2)}) collective-permute-start(bf16[128,320]{0,1:T(8,128)(2,1)S(1)} %collective-permute-done.7), channel_id=1, source_target_pairs={{0,32},{32,64},{64,96},{96,128},{128,160},{160,192},{192,224},{224... | collective-permute-start | bytes 245768 | tf_op jit(solution)/shard_map/gather_sequence/ppermute | solution.py:38
  59.2 8.6 %collective-permute-start.2 = (bf16[128,320]{0,1:T(8,128)(2,1)S(1)}, bf16[128,320]{0,1:T(8,128)(2,1)S(1)}, u32[]{:S(2)}, u32[]{:S(2)}) collective-permute-start(bf16[128,320]{0,1:T(8,128)(2,1)S(1)} %collective-permute-done.1), channel_id=1, source_target_pairs={{0,480},{32,0},{64,32},{96,64},{128,96},{160,128},{192,160},{224,1... | collective-permute-start | bytes 245768 | tf_op jit(solution)/shard_map/gather_sequence/ppermute | solution.py:41
  64.9 9.7 %collective-permute-start.9 = (bf16[128,320]{0,1:T(8,128)(2,1)S(1)}, bf16[128,320]{0,1:T(8,128)(2,1)S(1)}, u32[]{:S(2)}, u32[]{:S(2)}) collective-permute-start(bf16[128,320]{0,1:T(8,128)(2,1)S(1)} %collective-permute-done.8), channel_id=1, source_target_pairs={{0,32},{32,64},{64,96},{96,128},{128,160},{160,192},{192,224},{224... | collective-permute-start | bytes 245768 | tf_op jit(solution)/shard_map/gather_sequence/ppermute | solution.py:38
  67.9 9.6 %collective-permute-start.3 = (bf16[128,320]{0,1:T(8,128)(2,1)S(1)}, bf16[128,320]{0,1:T(8,128)(2,1)S(1)}, u32[]{:S(2)}, u32[]{:S(2)}) collective-permute-start(bf16[128,320]{0,1:T(8,128)(2,1)S(1)} %collective-permute-done.2), channel_id=1, source_target_pairs={{0,480},{32,0},{64,32},{96,64},{128,96},{160,128},{192,160},{224,1... | collective-permute-start | bytes 245768 | tf_op jit(solution)/shard_map/gather_sequence/ppermute | solution.py:41
  74.6 8.4 %collective-permute-start.10 = (bf16[128,320]{0,1:T(8,128)(2,1)S(1)}, bf16[128,320]{0,1:T(8,128)(2,1)S(1)}, u32[]{:S(2)}, u32[]{:S(2)}) collective-permute-start(bf16[128,320]{0,1:T(8,128)(2,1)S(1)} %collective-permute-done.9), channel_id=1, source_target_pairs={{0,32},{32,64},{64,96},{96,128},{128,160},{160,192},{192,224},{224... | collective-permute-start | bytes 245768 | tf_op jit(solution)/shard_map/gather_sequence/ppermute | solution.py:38
  77.5 9.0 %collective-permute-start.4 = (bf16[128,320]{0,1:T(8,128)(2,1)S(1)}, bf16[128,320]{0,1:T(8,128)(2,1)S(1)}, u32[]{:S(2)}, u32[]{:S(2)}) collective-permute-start(bf16[128,320]{0,1:T(8,128)(2,1)S(1)} %collective-permute-done.3), channel_id=1, source_target_pairs={{0,480},{32,0},{64,32},{96,64},{128,96},{160,128},{192,160},{224,1... | collective-permute-start | bytes 245768 | tf_op jit(solution)/shard_map/gather_sequence/ppermute | solution.py:41
  83.1 9.7 %collective-permute-start.11 = (bf16[128,320]{0,1:T(8,128)(2,1)S(1)}, bf16[128,320]{0,1:T(8,128)(2,1)S(1)}, u32[]{:S(2)}, u32[]{:S(2)}) collective-permute-start(bf16[128,320]{0,1:T(8,128)(2,1)S(1)} %collective-permute-done.10), channel_id=1, source_target_pairs={{0,32},{32,64},{64,96},{96,128},{128,160},{160,192},{192,224},{224... | collective-permute-start | bytes 245768 | tf_op jit(solution)/shard_map/gather_sequence/ppermute | solution.py:38
  86.4 9.5 %collective-permute-start.5 = (bf16[128,320]{0,1:T(8,128)(2,1)S(1)}, bf16[128,320]{0,1:T(8,128)(2,1)S(1)}, u32[]{:S(2)}, u32[]{:S(2)}) collective-permute-start(bf16[128,320]{0,1:T(8,128)(2,1)S(1)} %collective-permute-done.4), channel_id=1, source_target_pairs={{0,480},{32,0},{64,32},{96,64},{128,96},{160,128},{192,160},{224,1... | collective-permute-start | bytes 245768 | tf_op jit(solution)/shard_map/gather_sequence/ppermute | solution.py:41
  92.7 9.3 %collective-permute-start.12 = (bf16[128,320]{0,1:T(8,128)(2,1)S(1)}, bf16[128,320]{0,1:T(8,128)(2,1)S(1)}, u32[]{:S(2)}, u32[]{:S(2)}) collective-permute-start(bf16[128,320]{0,1:T(8,128)(2,1)S(1)} %collective-permute-done.11), channel_id=1, source_target_pairs={{0,32},{32,64},{64,96},{96,128},{128,160},{160,192},{192,224},{224... | collective-permute-start | bytes 245768 | tf_op jit(solution)/shard_map/gather_sequence/ppermute | solution.py:38
  95.9 17.0 %collective-permute-start.6 = (bf16[128,320]{0,1:T(8,128)(2,1)S(1)}, bf16[128,320]{0,1:T(8,128)(2,1)S(1)}, u32[]{:S(2)}, u32[]{:S(2)}) collective-permute-start(bf16[128,320]{0,1:T(8,128)(2,1)S(1)} %collective-permute-done.5), channel_id=1, source_target_pairs={{0,480},{32,0},{64,32},{96,64},{128,96},{160,128},{192,160},{224,1... | collective-permute-start | bytes 245768 | tf_op jit(solution)/shard_map/gather_sequence/ppermute | solution.py:41
  102.0 8.9 %collective-permute-start.13 = (bf16[128,320]{0,1:T(8,128)(2,1)S(1)}, bf16[128,320]{0,1:T(8,128)(2,1)S(1)}, u32[]{:S(2)}, u32[]{:S(2)}) collective-permute-start(bf16[128,320]{0,1:T(8,128)(2,1)S(1)} %collective-permute-done.12), channel_id=1, source_target_pairs={{0,32},{32,64},{64,96},{96,128},{128,160},{160,192},{192,224},{224... | collective-permute-start | bytes 245768 | tf_op jit(solution)/shard_map/gather_sequence/ppermute | solution.py:38
  111.0 8.8 %collective-permute-start.14 = (bf16[128,320]{0,1:T(8,128)(2,1)S(1)}, bf16[128,320]{0,1:T(8,128)(2,1)S(1)}, u32[]{:S(2)}, u32[]{:S(2)}) collective-permute-start(bf16[128,320]{0,1:T(8,128)(2,1)S(1)} %collective-permute-done.13), channel_id=1, source_target_pairs={{0,32},{32,64},{64,96},{96,128},{128,160},{160,192},{192,224},{224... | collective-permute-start | bytes 245768 | tf_op jit(solution)/shard_map/gather_sequence/ppermute | solution.py:38
  125.2 1.1 copy-start.17
  126.3 29.6 %collective-permute-start.16 = (bf16[2048,320]{0,1:T(8,128)(2,1)}, bf16[2048,320]{0,1:T(8,128)(2,1)S(1)}, u32[]{:S(2)}, u32[]{:S(2)}) collective-permute-start(bf16[2048,320]{0,1:T(8,128)(2,1)} %copy-done.17), channel_id=1, source_target_pairs={{0,8},{8,16},{16,24},{24,0},{1,9},{9,17},{17,25},{25,1},{2,10},{10... | collective-permute-start | bytes 3932168 | tf_op jit(solution)/shard_map/gather_sequence/ppermute | solution.py:38
  133.1 28.7 %collective-permute-start.15 = (bf16[2048,320]{0,1:T(8,128)(2,1)}, bf16[2048,320]{0,1:T(8,128)(2,1)S(1)}, u32[]{:S(2)}, u32[]{:S(2)}) collective-permute-start(bf16[2048,320]{0,1:T(8,128)(2,1)} %copy-done.17), channel_id=1, source_target_pairs={{0,24},{8,0},{16,8},{24,16},{1,25},{9,1},{17,9},{25,17},{2,26},{10... | collective-permute-start | bytes 3932168 | tf_op jit(solution)/shard_map/gather_sequence/ppermute | solution.py:41
  155.9 21.1 %collective-permute-start.17 = (bf16[2048,320]{0,1:T(8,128)(2,1)S(1)}, bf16[2048,320]{0,1:T(8,128)(2,1)S(1)}, u32[]{:S(2)}, u32[]{:S(2)}) collective-permute-start(bf16[2048,320]{0,1:T(8,128)(2,1)S(1)} %collective-permute-done.16), channel_id=1, source_target_pairs={{0,8},{8,16},{16,24},{24,0},{1,9},{9,17},{17,25},{25,1},{2,10},{10... | collective-permute-start | bytes 3932168 | tf_op jit(solution)/shard_map/gather_sequence/ppermute | solution.py:38
  184.9 3.1 %copy-start.4 = (pred[128,8192]{1,0:T(8,128)(4,1)S(1)}, pred[128,8192]{1,0:T(8,128)(4,1)}, u32[]{:S(2)}) copy-start(pred[128,8192]{1,0:T(8,128)(4,1)} %get-tuple-element.59) | copy-start | bytes 3145732
  189.8 2.5 copy-start.15
  200.3 25.0 %all-to-all-start = ((f32[64,2,2,128]{3,2,1,0:T(2,128)}), f32[64,2,2,128]{3,2,1,0:T(2,128)}, u32[]{:S(2)}, u32[]{:S(2)}) async-start(f32[64,2,2,128]{3,2,1,0:T(2,128)} %broadcast_in_dim.56), calls=%async_computation | async-start | bytes 262144 | tf_op jit(solution)/shard_map/gather_row_stats/all_to_all | solution.py:148
  211.0 3.9 %copy-start.8 = (bf16[160,1280]{1,0:T(8,128)(2,1)S(1)}, bf16[160,1280]{1,0:T(8,128)(2,1)}, u32[]{:S(2)}) copy-start(bf16[160,1280]{1,0:T(8,128)(2,1)} %param.14) | copy-start | bytes 1228804
  211.0 16.6 %copy-start.11 = (bf16[128,160]{0,1:T(8,128)(2,1)S(1)}, bf16[128,160]{0,1:T(8,128)(2,1)}, u32[]{:S(2)}) copy-start(bf16[128,160]{0,1:T(8,128)(2,1)} %copy-done.10) | copy-start | bytes 122884
  227.6 4.6 %copy-start.3 = (bf16[8192,160]{0,1:T(8,128)(2,1)S(1)}, bf16[8192,160]{0,1:T(8,128)(2,1)}, u32[]{:S(2)}) copy-start(bf16[8192,160]{0,1:T(8,128)(2,1)} %get-tuple-element.17) | copy-start | bytes 7864324
  232.1 3.3 %copy-start.2 = (f32[2,128,8192]{2,1,0:T(8,128)}, f32[2,128,8192]{2,1,0:T(8,128)S(1)}, u32[]{:S(2)}) copy-start(f32[2,128,8192]{2,1,0:T(8,128)S(1)} %fusion.2) | copy-start | bytes 25165828
  246.1 12.9 %copy-start.12 = (bf16[128,320]{0,1:T(8,128)(2,1)S(1)}, bf16[128,320]{0,1:T(8,128)(2,1)}, u32[]{:S(2)}) copy-start(bf16[128,320]{0,1:T(8,128)(2,1)} %param.11) | copy-start | bytes 245764
  246.1 12.9 %copy-start.13 = (bf16[128,320]{0,1:T(8,128)(2,1)S(1)}, bf16[128,320]{0,1:T(8,128)(2,1)}, u32[]{:S(2)}) copy-start(bf16[128,320]{0,1:T(8,128)(2,1)} %param.12) | copy-start | bytes 245764
Sparse Core Ops, SparseCore 0:
  37.9 91.9 all-gather.1

commit v4 on v3

--- a/solution.py
+++ b/solution.py
@@ -28,18 +28,33 @@
     return size // 2, (size - 1) // 2
 
 
-def ring_gather(data, axis, size):
+def ring_gather(data, axis, size, split_far=False):
     forward, backward = ring_steps(size)
+    if split_far and size % 2 == 0 and size > 2:
+        backward = forward
+    half = data.shape[0] // 2
     pieces = [None] * size
     pieces[0] = data
     ahead = behind = data
+    far_parts = [None, None]
     for step in range(max(forward, backward)):
+        last = split_far and size % 2 == 0 and size > 2 and step == forward - 1
         if step < forward:
-            ahead = lax.ppermute(ahead, axis, [(i, (i + 1) % size) for i in range(size)])
-            pieces[size - 1 - step] = ahead
+            sent = ahead[:half] if last else ahead
+            ahead = lax.ppermute(sent, axis, [(i, (i + 1) % size) for i in range(size)])
+            if last:
+                far_parts[0] = ahead
+            else:
+                pieces[size - 1 - step] = ahead
         if step < backward:
-            behind = lax.ppermute(behind, axis, [(i, (i - 1) % size) for i in range(size)])
-            pieces[1 + step] = behind
+            sent = behind[half:] if last else behind
+            behind = lax.ppermute(sent, axis, [(i, (i - 1) % size) for i in range(size)])
+            if last:
+                far_parts[1] = behind
+            else:
+                pieces[1 + step] = behind
+    if far_parts[0] is not None:
+        pieces[size // 2] = jnp.concatenate(far_parts, axis=0)
     return pieces
 
 
@@ -93,7 +108,8 @@
         kv_all = lax.all_gather(kv, "y", axis=0, tiled=True)
         kv_all = lax.all_gather(kv_all, "z", axis=0, tiled=True)
         qg_z = jnp.concatenate(ring_gather(qg, "z", z_size), axis=0)
-        qg_all = jnp.concatenate(ring_gather(qg_z, "y", y_size), axis=0)
+        qg_z, kv_all = lax.optimization_barrier((qg_z, kv_all))
+        qg_all = jnp.concatenate(ring_gather(qg_z, "y", y_size, True), axis=0)
         key_all = kv_all[:, :cols].reshape(all_rows, heads_here, head_width)
         value_all = kv_all[:, cols:].reshape(all_rows, heads_here, head_width)
         query_all = qg_all[:, :cols].reshape(all_rows, heads_here, head_width)

time: 269 us -> 245 us (0.911)
  waiting for transfers between devices: 62.2 us -> 35.8 us
  local copies, waits for them, and re-layouts: 31.6 us -> 35.2 us
    ppermute x18 -> x19, waiting for transfers between devices: 53 us -> 28.2 us  [the longest x10 22.6 us: ring_gather(): ahead = lax.ppermute(sent, axis, [(i, (i + 1) % size) for i in range(size)])]
    all_to_all x1, waiting for transfers between devices: 9.24 us -> 6.49 us  [per_device(): stats_all = lax.all_to_all(sent, ('z', 'y'), 0, 0, tiled=False)]
    unnamed x55 -> x57, local copies, waits for them, and re-layouts: 15.6 us -> 18.1 us
    ppermute x18 -> x19, starting transfers between devices: 67.2 us -> 68.5 us  [the longest x9 44.8 us: ring_gather(): lax.ppermute(sent, axis, [(i, (i - 1) % size) for i in range(size)])]
  transfers between devices with their start and end apart: 20 -> 21, of which waited for: 15 -> 12; matrix products, arithmetic and copies ran while one was open for 11% -> 19% of each run, Pallas kernels for 0% -> 0%
where the time goes in v4:
time: 245 us; the launch traced here: 244 us
  starting transfers between devices  78.1 us (32%)
  blocking collectives  41.9 us (17%)
  waiting for transfers between devices  35.8 us (15%)
  local copies, waits for them, and re-layouts  35.2 us (14%)
  matrix products  29.4 us (12%)
  between operations  14.7 us (6%)
  other arithmetic  8.37 us (3%)
    ppermute x9, starting transfers between devices, ring_gather(): lax.ppermute(sent, axis, [(i, (i - 1) % size) for i in range(size)])  44.8 us
    ppermute x10, starting transfers between devices, ring_gather(): ahead = lax.ppermute(sent, axis, [(i, (i + 1) % size) for i in range(size)])  23.7 us
    ppermute x10, waiting for transfers between devices, ring_gather(): ahead = lax.ppermute(sent, axis, [(i, (i + 1) % size) for i in range(size)])  22.6 us
    unnamed x57, local copies, waits for them, and re-layouts  18.1 us
    all_gather x1, blocking collectives, per_device(): kv_all = lax.all_gather(kv, 'y', axis=0, tiled=True)  14.6 us
    all_to_all x1, blocking collectives, per_device(): received = lax.all_to_all(payload, 'tp', 0, 0, tiled=False)  13.9 us
    all_gather x1, blocking collectives, per_device(): gathered = lax.all_gather(both, 'tp', axis=1, tiled=True)  13.4 us
    all_to_all x1, starting transfers between devices, per_device(): stats_all = lax.all_to_all(sent, ('z', 'y'), 0, 0, tiled=False)  9.64 us
  transfers between devices with their start and end apart: 21, of which 12 were waited for; matrix products, arithmetic and copies ran while one was open for 19% of the time, Pallas kernels for 0%

profile of v4, /device:TPU:24, one launch (start us, length us, event | category | flops | bytes accessed | tf_op | source)
XLA Modules:
  0.0 243.5 jit_solution(10067607139152422488)
XLA Ops:
  7.5 13.4 %all_gather.9 = bf16[128,2560]{0,1:T(8,128)(2,1)S(1)} all-gather(bf16[128,640]{0,1:T(8,128)(2,1)S(1)} %pad_maximum_fusion.1), channel_id=1, replica_groups=mesh['z'=16,'y'=4,'tp'=4,'dp'=2] {'tp'}, dimensions={1}, use_global_device_ids=true | all-gather | bytes 819200 | tf_op jit(solution)/shard_map/gather_features/all_gather | solution.py:76
  22.2 14.6 %all_gather.10 = bf16[512,320]{0,1:T(8,128)(2,1)} all-gather(bf16[128,320]{0,1:T(8,128)(2,1)S(1)} %pad_maximum_fusion.3), channel_id=1, replica_groups=mesh['z'=16,'y'=4,'tp'=4,'dp'=2] {'y'}, dimensions={0}, use_global_device_ids=true | all-gather | bytes 409600 | tf_op jit(solution)/shard_map/gather_sequence/all_gather | solution.py:108
  38.2 8.9 %collective-permute-start = (bf16[128,320]{0,1:T(8,128)(2,1)S(1)}, bf16[128,320]{0,1:T(8,128)(2,1)S(1)}, u32[]{:S(2)}, u32[]{:S(2)}) collective-permute-start(bf16[128,320]{0,1:T(8,128)(2,1)S(1)} %get-tuple-element.29), channel_id=1, source_target_pairs={{0,480},{32,0},{64,32},{96,64},{128,96},{160,128},{192,160},{224,1... | collective-permute-start | bytes 245768 | tf_op jit(solution)/shard_map/gather_sequence/ppermute | solution.py:51
  47.1 1.9 collective-permute-start.7
  51.4 2.7 %broadcast_compare_fusion = (pred[128,8192]{1,0:T(8,128)(4,1)}, pred[128,8192]{1,0:T(8,128)(4,1)}) fusion(s32[8192]{0:T(1024)S(1)} %get-tuple-element.39, s32[128]{0:T(128)S(1)} %iota_add_fusion, s32[8192]{0:T(1024)S(1)} %get-tuple-element.40), kind=kLoop, calls=%fused_computation.24 | loop fusion | flops 2097152 | bytes 2163200 | tf_op jit(solution)/shard_map/key_pass/le | solution.py:173
  54.1 5.1 %collective-permute-start.1 = (bf16[128,320]{0,1:T(8,128)(2,1)S(1)}, bf16[128,320]{0,1:T(8,128)(2,1)S(1)}, u32[]{:S(2)}, u32[]{:S(2)}) collective-permute-start(bf16[128,320]{0,1:T(8,128)(2,1)S(1)} %collective-permute-done), channel_id=1, source_target_pairs={{0,480},{32,0},{64,32},{96,64},{128,96},{160,128},{192,160},{224,1... | collective-permute-start | bytes 245768 | tf_op jit(solution)/shard_map/gather_sequence/ppermute | solution.py:51
  59.2 1.9 collective-permute-start.8
  62.1 4.8 %collective-permute-start.2 = (bf16[128,320]{0,1:T(8,128)(2,1)S(1)}, bf16[128,320]{0,1:T(8,128)(2,1)S(1)}, u32[]{:S(2)}, u32[]{:S(2)}) collective-permute-start(bf16[128,320]{0,1:T(8,128)(2,1)S(1)} %collective-permute-done.1), channel_id=1, source_target_pairs={{0,480},{32,0},{64,32},{96,64},{128,96},{160,128},{192,160},{224,1... | collective-permute-start | bytes 245768 | tf_op jit(solution)/shard_map/gather_sequence/ppermute | solution.py:51
  66.9 1.5 collective-permute-done.8
  68.5 1.9 collective-permute-start.9
  71.0 5.1 %collective-permute-start.3 = (bf16[128,320]{0,1:T(8,128)(2,1)S(1)}, bf16[128,320]{0,1:T(8,128)(2,1)S(1)}, u32[]{:S(2)}, u32[]{:S(2)}) collective-permute-start(bf16[128,320]{0,1:T(8,128)(2,1)S(1)} %collective-permute-done.2), channel_id=1, source_target_pairs={{0,480},{32,0},{64,32},{96,64},{128,96},{160,128},{192,160},{224,1... | collective-permute-start | bytes 245768 | tf_op jit(solution)/shard_map/gather_sequence/ppermute | solution.py:51
  77.5 1.9 collective-permute-start.10
  80.1 5.4 %collective-permute-start.4 = (bf16[128,320]{0,1:T(8,128)(2,1)S(1)}, bf16[128,320]{0,1:T(8,128)(2,1)S(1)}, u32[]{:S(2)}, u32[]{:S(2)}) collective-permute-start(bf16[128,320]{0,1:T(8,128)(2,1)S(1)} %collective-permute-done.3), channel_id=1, source_target_pairs={{0,480},{32,0},{64,32},{96,64},{128,96},{160,128},{192,160},{224,1... | collective-permute-start | bytes 245768 | tf_op jit(solution)/shard_map/gather_sequence/ppermute | solution.py:51
  86.3 1.9 collective-permute-start.11
  88.9 5.3 %collective-permute-start.5 = (bf16[128,320]{0,1:T(8,128)(2,1)S(1)}, bf16[128,320]{0,1:T(8,128)(2,1)S(1)}, u32[]{:S(2)}, u32[]{:S(2)}) collective-permute-start(bf16[128,320]{0,1:T(8,128)(2,1)S(1)} %collective-permute-done.4), channel_id=1, source_target_pairs={{0,480},{32,0},{64,32},{96,64},{128,96},{160,128},{192,160},{224,1... | collective-permute-start | bytes 245768 | tf_op jit(solution)/shard_map/gather_sequence/ppermute | solution.py:51
  94.2 1.8 collective-permute-done.11
  96.0 1.9 collective-permute-start.12
  98.6 5.1 %collective-permute-start.6 = (bf16[128,320]{0,1:T(8,128)(2,1)S(1)}, bf16[128,320]{0,1:T(8,128)(2,1)S(1)}, u32[]{:S(2)}, u32[]{:S(2)}) collective-permute-start(bf16[128,320]{0,1:T(8,128)(2,1)S(1)} %collective-permute-done.5), channel_id=1, source_target_pairs={{0,480},{32,0},{64,32},{96,64},{128,96},{160,128},{192,160},{224,1... | collective-permute-start | bytes 245768 | tf_op jit(solution)/shard_map/gather_sequence/ppermute | solution.py:51
  103.8 2.1 collective-permute-done.12
  105.9 1.9 collective-permute-start.13
  108.5 6.4 %collective-permute-done.13 = bf16[128,320]{0,1:T(8,128)(2,1)S(1)} collective-permute-done((bf16[128,320]{0,1:T(8,128)(2,1)S(1)}, bf16[128,320]{0,1:T(8,128)(2,1)S(1)}, u32[]{:S(2)}, u32[]{:S(2)}) %collective-permute-start.13) | collective-permute-done | bytes 81952 | tf_op jit(solution)/shard_map/gather_sequence/ppermute | solution.py:44
  114.8 1.9 collective-permute-start.14
  117.4 6.0 %collective-permute-done.14 = bf16[128,320]{0,1:T(8,128)(2,1)S(1)} collective-permute-done((bf16[128,320]{0,1:T(8,128)(2,1)S(1)}, bf16[128,320]{0,1:T(8,128)(2,1)S(1)}, u32[]{:S(2)}, u32[]{:S(2)}) %collective-permute-start.14) | collective-permute-done | bytes 81952 | tf_op jit(solution)/shard_map/gather_sequence/ppermute | solution.py:44
  129.7 3.1 %collective-permute-start.15 = (bf16[2048,320]{0,1:T(8,128)(2,1)}, bf16[2048,320]{0,1:T(8,128)(2,1)}, u32[]{:S(2)}, u32[]{:S(2)}) collective-permute-start(bf16[2048,320]{0,1:T(8,128)(2,1)} %constant_dynamic-update-slice_fusion), channel_id=1, source_target_pairs={{0,24},{8,0},{16,8},{24,16},{1,25},{9,1},{17,9},{25,17},{2,26},{10... | collective-permute-start | bytes 3932168 | tf_op jit(solution)/shard_map/gather_sequence/ppermute | solution.py:51
  132.8 4.1 %collective-permute-start.16 = (bf16[2048,320]{0,1:T(8,128)(2,1)}, bf16[2048,320]{0,1:T(8,128)(2,1)}, u32[]{:S(2)}, u32[]{:S(2)}) collective-permute-start(bf16[2048,320]{0,1:T(8,128)(2,1)} %constant_dynamic-update-slice_fusion), channel_id=1, source_target_pairs={{0,8},{8,16},{16,24},{24,0},{1,9},{9,17},{17,25},{25,1},{2,10},{10... | collective-permute-start | bytes 3932168 | tf_op jit(solution)/shard_map/gather_sequence/ppermute | solution.py:44
  136.9 3.0 %fusion.41 = (bf16[8192,160]{0,1:T(8,128)(2,1)S(1)}, bf16[8192,160]{0,1:T(8,128)(2,1)S(1)}) fusion(bf16[8192,320]{0,1:T(8,128)(2,1)} %all-gather.2.cloned.1.call-done), kind=kLoop, calls=%fused_computation.98 | loop fusion | bytes 10485760 | tf_op jit(solution)/shard_map/gather_sequence/slice | solution.py:114
  139.9 1.8 select_reduce_fusion.1
  141.7 2.5 %select_reduce_fusion = f32[2,128]{1,0:T(2,128)S(1)} fusion(f32[2,128,8192]{2,1,0:T(8,128)S(1)} %get-tuple-element.34, f32[2,128]{1,0:T(2,128)S(1)} %get-tuple-element.33, pred[128,8192]{1,0:T(8,128)(4,1)S(1)} %copy-done.4), kind=kLoop, calls=%fused_computation.10 | loop fusion | flops 8388352 | bytes 9439232 | tf_op jit(solution)/shard_map/query_pass/reduce_sum | solution.py:140
  144.2 4.8 %fusion.43 = (f32[2,128]{1,0:T(2,128)S(1)}, bf16[2,128,8192]{2,1,0:T(8,128)(2,1)}) fusion(bf16[128,2,80]{0,2,1:T(8,128)(2,1)S(1)} %bitcast.100, bf16[8192,2,80]{0,2,1:T(8,128)(2,1)S(1)} %bitcast.92, f32[2,128,8192]{2,1,0:T(8,128)S(1)} %get-tuple-element.34, f32[2,128]{1,0:T(2,128)S(1)} %log_add_fusion, pred[128,8192]{1,0:T(8,128)(4,1)S(1)} %copy-done.4), kind=kOutput, calls=%fused_computation.100 | convolution fusion | flops 346029824 | bytes 16295936 | tf_op jit(solution)/shard_map/query_pass/qhd,khd->hqk/dot_general | solution.py:143
  149.0 2.6 %fusion.25 = f32[128,2,80]{0,2,1:T(8,128)} fusion(bf16[8192,2,80]{0,2,1:T(8,128)(2,1)S(1)} %bitcast.84, f32[2,128,8192]{2,1,0:T(8,128)S(1)} %get-tuple-element.34, f32[2,128]{1,0:T(2,128)S(1)} %log_add_fusion, pred[128,8192]{1,0:T(8,128)(4,1)S(1)} %copy-done.4, f32[128,2]{0,1:T(2,128)S(1)} %bitcast.103), kind=kOutput, calls=%fused_computation.32 | convolution fusion | flops 341856256 | bytes 12142592 | tf_op jit(solution)/shard_map/query_pass/hqk,khd->hqd/dot_general | solution.py:154
  152.3 9.6 %all-to-all-start = ((f32[64,2,2,128]{3,2,1,0:T(2,128)}), f32[64,2,2,128]{3,2,1,0:T(2,128)}, u32[]{:S(2)}, u32[]{:S(2)}) async-start(f32[64,2,2,128]{3,2,1,0:T(2,128)} %broadcast_in_dim.56), calls=%async_computation | async-start | bytes 262144 | tf_op jit(solution)/shard_map/gather_row_stats/all_to_all | solution.py:164
  161.9 3.8 %fusion.19 = f32[128,2,80]{0,2,1:T(8,128)S(1)} fusion(f32[128,2,80]{0,2,1:T(8,128)} %fusion.25, bf16[8192,2,80]{0,2,1:T(8,128)(2,1)S(1)} %bitcast.85, bf16[2,128,8192]{2,1,0:T(8,128)(2,1)} %get-tuple-element.36), kind=kOutput, calls=%fused_computation.29 | convolution fusion | flops 335564800 | bytes 6979584 | tf_op jit(solution)/shard_map/query_pass/hqk,khd->hqd/dot_general | solution.py:148
  166.9 2.6 %constant_dynamic-update-slice_fusion.20 = bf16[8192,320]{0,1:T(8,128)(2,1)} fusion(bf16[2048,320]{0,1:T(8,128)(2,1)} %constant_dynamic-update-slice_fusion), kind=kLoop, calls=%fused_computation.71 | loop fusion | bytes 2621440
  169.6 6.5 %all-to-all-done = f32[64,2,2,128]{3,2,1,0:T(2,128)} async-done(((f32[64,2,2,128]{3,2,1,0:T(2,128)}), f32[64,2,2,128]{3,2,1,0:T(2,128)}, u32[]{:S(2)}, u32[]{:S(2)}) %all-to-all-start) | async-done | bytes 131104 | tf_op jit(solution)/shard_map/gather_row_stats/all_to_all | solution.py:164
  176.0 1.6 gather_fusion.1
  178.8 4.3 %collective-permute-start.17 = (bf16[1024,320]{0,1:T(8,128)(2,1)S(1)}, bf16[1024,320]{0,1:T(8,128)(2,1)S(1)}, u32[]{:S(2)}, u32[]{:S(2)}) collective-permute-start(bf16[1024,320]{0,1:T(8,128)(2,1)S(1)} %slice.77), channel_id=1, source_target_pairs={{0,8},{8,16},{16,24},{24,0},{1,9},{9,17},{17,25},{25,1},{2,10},{10... | collective-permute-start | bytes 1966088 | tf_op jit(solution)/shard_map/gather_sequence/ppermute | solution.py:44
  184.3 1.9 collective-permute-start.18
  186.9 2.5 %constant_dynamic-update-slice_fusion.19 = bf16[8192,320]{0,1:T(8,128)(2,1)} fusion(bf16[8192,320]{0,1:T(8,128)(2,1)} %constant_dynamic-update-slice_fusion.20, bf16[2048,320]{0,1:T(8,128)(2,1)} %collective-permute-done.15), kind=kLoop, calls=%fused_computation.70 | loop fusion | bytes 2621440
  189.5 2.6 %collective-permute-done.17 = bf16[1024,320]{0,1:T(8,128)(2,1)S(1)} collective-permute-done((bf16[1024,320]{0,1:T(8,128)(2,1)S(1)}, bf16[1024,320]{0,1:T(8,128)(2,1)S(1)}, u32[]{:S(2)}, u32[]{:S(2)}) %collective-permute-start.17) | collective-permute-done | bytes 655392 | tf_op jit(solution)/shard_map/gather_sequence/ppermute | solution.py:44
  193.0 5.3 %collective-permute-done.18 = bf16[1024,320]{0,1:T(8,128)(2,1)S(1)} collective-permute-done((bf16[1024,320]{0,1:T(8,128)(2,1)S(1)}, bf16[1024,320]{0,1:T(8,128)(2,1)S(1)}, u32[]{:S(2)}, u32[]{:S(2)}) %collective-permute-start.18) | collective-permute-done | bytes 655392 | tf_op jit(solution)/shard_map/gather_sequence/ppermute | solution.py:51
  199.2 2.5 %constant_dynamic-update-slice_fusion.16 = bf16[8192,320]{0,1:T(8,128)(2,1)} fusion(bf16[8192,320]{0,1:T(8,128)(2,1)} %constant_dynamic-update-slice_fusion.17, bf16[2048,320]{0,1:T(8,128)(2,1)} %collective-permute-done.16), kind=kLoop, calls=%fused_computation.67 | loop fusion | bytes 2621440 | tf_op jit(solution)/shard_map/gather_sequence/concatenate | solution.py:112
  201.7 3.1 %fusion.40 = (bf16[8192,160]{0,1:T(8,128)(2,1)S(1)}, bf16[8192,160]{0,1:T(8,128)(2,1)S(1)}) fusion(bf16[8192,320]{0,1:T(8,128)(2,1)} %constant_dynamic-update-slice_fusion.16), kind=kLoop, calls=%fused_computation.97 | loop fusion | bytes 10485760 | tf_op jit(solution)/shard_map/gather_sequence/slice | solution.py:116
  204.9 2.4 %fusion.2 = f32[2,128,8192]{2,1,0:T(8,128)S(1)} fusion(bf16[128,2,80]{0,2,1:T(8,128)(2,1)S(1)} %bitcast.98, bf16[8192,2,80]{0,2,1:T(8,128)(2,1)S(1)} %bitcast.88, f32[2,8192]{1,0:T(2,128)S(1)} %get-tuple-element.28, pred[128,8192]{1,0:T(8,128)(4,1)S(1)} %copy-done.5), kind=kOutput, calls=%fused_computation.6 | convolution fusion | flops 339738624 | bytes 12165120 | tf_op jit(solution)/shard_map/key_pass/khd,qhd->hkq/dot_general | solution.py:170
  207.3 1.6 fusion.30
  208.9 1.7 copy-done.2
  210.6 7.5 %fusion.29 = bf16[2,80,128]{2,1,0:T(8,128)(2,1)} fusion(bf16[8192,2,80]{0,2,1:T(8,128)(2,1)} %bitcast.89, f32[2,128,8192]{2,1,0:T(8,128)} %copy-done.2, bf16[128,2,80]{0,2,1:T(8,128)(2,1)S(1)} %bitcast.97, bf16[8192,2,80]{0,2,1:T(8,128)(2,1)S(1)} %bitcast.87, f32[2,8192]{1,0:T(2,128)} %get-tuple-element.27), kind=kOutput, calls=%fused_computation.34 | convolution fusion | flops 677400576 | bytes 13778944 | tf_op jit(solution)/shard_map/key_pass/hkq,qhd->khd/dot_general | solution.py:181
  219.4 1.5 multiply_reduce_fusion
  221.8 13.9 %all_to_all.10 = f32[4,129,320]{2,1,0:T(8,128)S(1)} all-to-all(f32[4,129,320]{2,1,0:T(8,128)S(1)} %copy.31), channel_id=1, replica_groups=mesh['z'=16,'y'=4,'tp'=4,'dp'=2] {'tp'}, dimensions={0} | all-to-all | bytes 1320960 | tf_op jit(solution)/shard_map/back_projection/all_to_all | solution.py:200
  (115 shorter events, 28.6 us)
Async XLA Ops:
  6.5 15.1 %copy-start = (bf16[160,1280]{1,0:T(8,128)(2,1)S(1)}, bf16[160,1280]{1,0:T(8,128)(2,1)}, u32[]{:S(2)}) copy-start(bf16[160,1280]{1,0:T(8,128)(2,1)} %param.16) | copy-start | bytes 1228804
  6.5 15.0 %copy-start.17 = (f32[1280]{0:T(1024)S(1)}, f32[1280]{0:T(1024)}, u32[]{:S(2)}) copy-start(f32[1280]{0:T(1024)} %param.13) | copy-start | bytes 15364
  6.5 123.2 %all-gather.2.cloned.1.call-start = ((), (), s32[]{:S(2)}) async-start(), calls=%async_computation.2 | async-start | bytes 5570560 | tf_op jit(solution)/shard_map/gather_sequence/all_gather | solution.py:109
  20.9 1.0 copy-start.7
  21.0 15.8 %copy-start.18 = (f32[80]{0:T(128)S(1)}, f32[80]{0:T(128)}, u32[]{:S(2)}) copy-start(f32[80]{0:T(128)} %param.18) | copy-start | bytes 964
  21.0 15.9 %copy-start.10 = (bf16[160,1280]{1,0:T(8,128)(2,1)S(1)}, bf16[160,1280]{1,0:T(8,128)(2,1)}, u32[]{:S(2)}) copy-start(bf16[160,1280]{1,0:T(8,128)(2,1)} %param.17) | copy-start | bytes 1228804
  21.2 16.0 %copy-start.8 = (bf16[160,1280]{1,0:T(8,128)(2,1)S(1)}, bf16[160,1280]{1,0:T(8,128)(2,1)}, u32[]{:S(2)}) copy-start(bf16[160,1280]{1,0:T(8,128)(2,1)} %param.14) | copy-start | bytes 1228804
  21.5 16.7 %copy-start.6 = (f32[128,1280]{1,0:T(8,128)}, f32[128,1280]{1,0:T(8,128)S(1)}, u32[]{:S(2)}) copy-start(f32[128,1280]{1,0:T(8,128)S(1)} %copy.28) | copy-start | bytes 1966084
  21.5 27.7 %copy-start.1 = (s32[64]{0:T(128)S(1)}, s32[64]{0:T(128)}, u32[]{:S(2)}) copy-start(s32[64]{0:T(128)} %param.19) | copy-start | bytes 772
  22.2 14.7 %copy-start.11 = (bf16[128,160]{0,1:T(8,128)(2,1)}, bf16[128,160]{0,1:T(8,128)(2,1)S(1)}, u32[]{:S(2)}) copy-start(bf16[128,160]{0,1:T(8,128)(2,1)S(1)} %convolution_convert_fusion.2) | copy-start | bytes 122884
  37.2 87.5 %copy-start.15 = (bf16[128,160]{0,1:T(8,128)(2,1)}, bf16[128,160]{0,1:T(8,128)(2,1)S(1)}, u32[]{:S(2)}) copy-start(bf16[128,160]{0,1:T(8,128)(2,1)S(1)} %convolution_convert_fusion) | copy-start | bytes 122884
  38.2 15.9 %collective-permute-start = (bf16[128,320]{0,1:T(8,128)(2,1)S(1)}, bf16[128,320]{0,1:T(8,128)(2,1)S(1)}, u32[]{:S(2)}, u32[]{:S(2)}) collective-permute-start(bf16[128,320]{0,1:T(8,128)(2,1)S(1)} %get-tuple-element.29), channel_id=1, source_target_pairs={{0,480},{32,0},{64,32},{96,64},{128,96},{160,128},{192,160},{224,1... | collective-permute-start | bytes 245768 | tf_op jit(solution)/shard_map/gather_sequence/ppermute | solution.py:51
  47.1 12.1 %collective-permute-start.7 = (bf16[128,320]{0,1:T(8,128)(2,1)S(1)}, bf16[128,320]{0,1:T(8,128)(2,1)S(1)}, u32[]{:S(2)}, u32[]{:S(2)}) collective-permute-start(bf16[128,320]{0,1:T(8,128)(2,1)S(1)} %get-tuple-element.29), channel_id=1, source_target_pairs={{0,32},{32,64},{64,96},{96,128},{128,160},{160,192},{192,224},{224... | collective-permute-start | bytes 245768 | tf_op jit(solution)/shard_map/gather_sequence/ppermute | solution.py:44
  54.1 8.0 %collective-permute-start.1 = (bf16[128,320]{0,1:T(8,128)(2,1)S(1)}, bf16[128,320]{0,1:T(8,128)(2,1)S(1)}, u32[]{:S(2)}, u32[]{:S(2)}) collective-permute-start(bf16[128,320]{0,1:T(8,128)(2,1)S(1)} %collective-permute-done), channel_id=1, source_target_pairs={{0,480},{32,0},{64,32},{96,64},{128,96},{160,128},{192,160},{224,1... | collective-permute-start | bytes 245768 | tf_op jit(solution)/shard_map/gather_sequence/ppermute | solution.py:51
  59.2 9.3 %collective-permute-start.8 = (bf16[128,320]{0,1:T(8,128)(2,1)S(1)}, bf16[128,320]{0,1:T(8,128)(2,1)S(1)}, u32[]{:S(2)}, u32[]{:S(2)}) collective-permute-start(bf16[128,320]{0,1:T(8,128)(2,1)S(1)} %collective-permute-done.7), channel_id=1, source_target_pairs={{0,32},{32,64},{64,96},{96,128},{128,160},{160,192},{192,224},{224... | collective-permute-start | bytes 245768 | tf_op jit(solution)/shard_map/gather_sequence/ppermute | solution.py:44
  62.1 8.9 %collective-permute-start.2 = (bf16[128,320]{0,1:T(8,128)(2,1)S(1)}, bf16[128,320]{0,1:T(8,128)(2,1)S(1)}, u32[]{:S(2)}, u32[]{:S(2)}) collective-permute-start(bf16[128,320]{0,1:T(8,128)(2,1)S(1)} %collective-permute-done.1), channel_id=1, source_target_pairs={{0,480},{32,0},{64,32},{96,64},{128,96},{160,128},{192,160},{224,1... | collective-permute-start | bytes 245768 | tf_op jit(solution)/shard_map/gather_sequence/ppermute | solution.py:51
  68.5 9.0 %collective-permute-start.9 = (bf16[128,320]{0,1:T(8,128)(2,1)S(1)}, bf16[128,320]{0,1:T(8,128)(2,1)S(1)}, u32[]{:S(2)}, u32[]{:S(2)}) collective-permute-start(bf16[128,320]{0,1:T(8,128)(2,1)S(1)} %collective-permute-done.8), channel_id=1, source_target_pairs={{0,32},{32,64},{64,96},{96,128},{128,160},{160,192},{192,224},{224... | collective-permute-start | bytes 245768 | tf_op jit(solution)/shard_map/gather_sequence/ppermute | solution.py:44
  71.0 9.0 %collective-permute-start.3 = (bf16[128,320]{0,1:T(8,128)(2,1)S(1)}, bf16[128,320]{0,1:T(8,128)(2,1)S(1)}, u32[]{:S(2)}, u32[]{:S(2)}) collective-permute-start(bf16[128,320]{0,1:T(8,128)(2,1)S(1)} %collective-permute-done.2), channel_id=1, source_target_pairs={{0,480},{32,0},{64,32},{96,64},{128,96},{160,128},{192,160},{224,1... | collective-permute-start | bytes 245768 | tf_op jit(solution)/shard_map/gather_sequence/ppermute | solution.py:51
  77.5 8.9 %collective-permute-start.10 = (bf16[128,320]{0,1:T(8,128)(2,1)S(1)}, bf16[128,320]{0,1:T(8,128)(2,1)S(1)}, u32[]{:S(2)}, u32[]{:S(2)}) collective-permute-start(bf16[128,320]{0,1:T(8,128)(2,1)S(1)} %collective-permute-done.9), channel_id=1, source_target_pairs={{0,32},{32,64},{64,96},{96,128},{128,160},{160,192},{192,224},{224... | collective-permute-start | bytes 245768 | tf_op jit(solution)/shard_map/gather_sequence/ppermute | solution.py:44
  80.1 8.9 %collective-permute-start.4 = (bf16[128,320]{0,1:T(8,128)(2,1)S(1)}, bf16[128,320]{0,1:T(8,128)(2,1)S(1)}, u32[]{:S(2)}, u32[]{:S(2)}) collective-permute-start(bf16[128,320]{0,1:T(8,128)(2,1)S(1)} %collective-permute-done.3), channel_id=1, source_target_pairs={{0,480},{32,0},{64,32},{96,64},{128,96},{160,128},{192,160},{224,1... | collective-permute-start | bytes 245768 | tf_op jit(solution)/shard_map/gather_sequence/ppermute | solution.py:51
  86.3 9.7 %collective-permute-start.11 = (bf16[128,320]{0,1:T(8,128)(2,1)S(1)}, bf16[128,320]{0,1:T(8,128)(2,1)S(1)}, u32[]{:S(2)}, u32[]{:S(2)}) collective-permute-start(bf16[128,320]{0,1:T(8,128)(2,1)S(1)} %collective-permute-done.10), channel_id=1, source_target_pairs={{0,32},{32,64},{64,96},{96,128},{128,160},{160,192},{192,224},{224... | collective-permute-start | bytes 245768 | tf_op jit(solution)/shard_map/gather_sequence/ppermute | solution.py:44
  88.9 9.7 %collective-permute-start.5 = (bf16[128,320]{0,1:T(8,128)(2,1)S(1)}, bf16[128,320]{0,1:T(8,128)(2,1)S(1)}, u32[]{:S(2)}, u32[]{:S(2)}) collective-permute-start(bf16[128,320]{0,1:T(8,128)(2,1)S(1)} %collective-permute-done.4), channel_id=1, source_target_pairs={{0,480},{32,0},{64,32},{96,64},{128,96},{160,128},{192,160},{224,1... | collective-permute-start | bytes 245768 | tf_op jit(solution)/shard_map/gather_sequence/ppermute | solution.py:51
  96.0 9.9 %collective-permute-start.12 = (bf16[128,320]{0,1:T(8,128)(2,1)S(1)}, bf16[128,320]{0,1:T(8,128)(2,1)S(1)}, u32[]{:S(2)}, u32[]{:S(2)}) collective-permute-start(bf16[128,320]{0,1:T(8,128)(2,1)S(1)} %collective-permute-done.11), channel_id=1, source_target_pairs={{0,32},{32,64},{64,96},{96,128},{128,160},{160,192},{192,224},{224... | collective-permute-start | bytes 245768 | tf_op jit(solution)/shard_map/gather_sequence/ppermute | solution.py:44
  98.6 18.1 %collective-permute-start.6 = (bf16[128,320]{0,1:T(8,128)(2,1)S(1)}, bf16[128,320]{0,1:T(8,128)(2,1)S(1)}, u32[]{:S(2)}, u32[]{:S(2)}) collective-permute-start(bf16[128,320]{0,1:T(8,128)(2,1)S(1)} %collective-permute-done.5), channel_id=1, source_target_pairs={{0,480},{32,0},{64,32},{96,64},{128,96},{160,128},{192,160},{224,1... | collective-permute-start | bytes 245768 | tf_op jit(solution)/shard_map/gather_sequence/ppermute | solution.py:51
  105.9 8.9 %collective-permute-start.13 = (bf16[128,320]{0,1:T(8,128)(2,1)S(1)}, bf16[128,320]{0,1:T(8,128)(2,1)S(1)}, u32[]{:S(2)}, u32[]{:S(2)}) collective-permute-start(bf16[128,320]{0,1:T(8,128)(2,1)S(1)} %collective-permute-done.12), channel_id=1, source_target_pairs={{0,32},{32,64},{64,96},{96,128},{128,160},{160,192},{192,224},{224... | collective-permute-start | bytes 245768 | tf_op jit(solution)/shard_map/gather_sequence/ppermute | solution.py:44
  114.8 8.6 %collective-permute-start.14 = (bf16[128,320]{0,1:T(8,128)(2,1)S(1)}, bf16[128,320]{0,1:T(8,128)(2,1)S(1)}, u32[]{:S(2)}, u32[]{:S(2)}) collective-permute-start(bf16[128,320]{0,1:T(8,128)(2,1)S(1)} %collective-permute-done.13), channel_id=1, source_target_pairs={{0,32},{32,64},{64,96},{96,128},{128,160},{160,192},{192,224},{224... | collective-permute-start | bytes 245768 | tf_op jit(solution)/shard_map/gather_sequence/ppermute | solution.py:44
  129.7 10.2 %copy-start.4 = (pred[128,8192]{1,0:T(8,128)(4,1)S(1)}, pred[128,8192]{1,0:T(8,128)(4,1)}, u32[]{:S(2)}) copy-start(pred[128,8192]{1,0:T(8,128)(4,1)} %get-tuple-element.32) | copy-start | bytes 3145732
  129.7 53.4 %collective-permute-start.15 = (bf16[2048,320]{0,1:T(8,128)(2,1)}, bf16[2048,320]{0,1:T(8,128)(2,1)}, u32[]{:S(2)}, u32[]{:S(2)}) collective-permute-start(bf16[2048,320]{0,1:T(8,128)(2,1)} %constant_dynamic-update-slice_fusion), channel_id=1, source_target_pairs={{0,24},{8,0},{16,8},{24,16},{1,25},{9,1},{17,9},{25,17},{2,26},{10... | collective-permute-start | bytes 3932168 | tf_op jit(solution)/shard_map/gather_sequence/ppermute | solution.py:51
  132.8 44.8 %collective-permute-start.16 = (bf16[2048,320]{0,1:T(8,128)(2,1)}, bf16[2048,320]{0,1:T(8,128)(2,1)}, u32[]{:S(2)}, u32[]{:S(2)}) collective-permute-start(bf16[2048,320]{0,1:T(8,128)(2,1)} %constant_dynamic-update-slice_fusion), channel_id=1, source_target_pairs={{0,8},{8,16},{16,24},{24,0},{1,9},{9,17},{17,25},{25,1},{2,10},{10... | collective-permute-start | bytes 3932168 | tf_op jit(solution)/shard_map/gather_sequence/ppermute | solution.py:44
  141.7 2.5 %copy-start.16 = (bf16[128,160]{0,1:T(8,128)(2,1)S(1)}, bf16[128,160]{0,1:T(8,128)(2,1)}, u32[]{:S(2)}) copy-start(bf16[128,160]{0,1:T(8,128)(2,1)} %copy-done.15) | copy-start | bytes 122884
  152.3 23.8 %all-to-all-start = ((f32[64,2,2,128]{3,2,1,0:T(2,128)}), f32[64,2,2,128]{3,2,1,0:T(2,128)}, u32[]{:S(2)}, u32[]{:S(2)}) async-start(f32[64,2,2,128]{3,2,1,0:T(2,128)} %broadcast_in_dim.56), calls=%async_computation | async-start | bytes 262144 | tf_op jit(solution)/shard_map/gather_row_stats/all_to_all | solution.py:164
  161.9 3.9 %copy-start.9 = (bf16[160,1280]{1,0:T(8,128)(2,1)S(1)}, bf16[160,1280]{1,0:T(8,128)(2,1)}, u32[]{:S(2)}) copy-start(bf16[160,1280]{1,0:T(8,128)(2,1)} %param.14) | copy-start | bytes 1228804
  178.8 13.2 %collective-permute-start.17 = (bf16[1024,320]{0,1:T(8,128)(2,1)S(1)}, bf16[1024,320]{0,1:T(8,128)(2,1)S(1)}, u32[]{:S(2)}, u32[]{:S(2)}) collective-permute-start(bf16[1024,320]{0,1:T(8,128)(2,1)S(1)} %slice.77), channel_id=1, source_target_pairs={{0,8},{8,16},{16,24},{24,0},{1,9},{9,17},{17,25},{25,1},{2,10},{10... | collective-permute-start | bytes 1966088 | tf_op jit(solution)/shard_map/gather_sequence/ppermute | solution.py:44
  184.3 13.9 %collective-permute-start.18 = (bf16[1024,320]{0,1:T(8,128)(2,1)S(1)}, bf16[1024,320]{0,1:T(8,128)(2,1)S(1)}, u32[]{:S(2)}, u32[]{:S(2)}) collective-permute-start(bf16[1024,320]{0,1:T(8,128)(2,1)S(1)} %slice.78), channel_id=1, source_target_pairs={{0,24},{8,0},{16,8},{24,16},{1,25},{9,1},{17,9},{25,17},{2,26},{10... | collective-permute-start | bytes 1966088 | tf_op jit(solution)/shard_map/gather_sequence/ppermute | solution.py:51
  201.7 3.1 %copy-start.5 = (pred[128,8192]{1,0:T(8,128)(4,1)S(1)}, pred[128,8192]{1,0:T(8,128)(4,1)}, u32[]{:S(2)}) copy-start(pred[128,8192]{1,0:T(8,128)(4,1)} %get-tuple-element.31) | copy-start | bytes 3145732
  201.7 3.1 %copy-start.12 = (bf16[128,160]{0,1:T(8,128)(2,1)S(1)}, bf16[128,160]{0,1:T(8,128)(2,1)}, u32[]{:S(2)}) copy-start(bf16[128,160]{0,1:T(8,128)(2,1)} %copy-done.11) | copy-start | bytes 122884
  204.8 2.5 %copy-start.3 = (bf16[8192,160]{0,1:T(8,128)(2,1)}, bf16[8192,160]{0,1:T(8,128)(2,1)S(1)}, u32[]{:S(2)}) copy-start(bf16[8192,160]{0,1:T(8,128)(2,1)S(1)} %get-tuple-element.22) | copy-start | bytes 7864324
  207.3 3.3 %copy-start.2 = (f32[2,128,8192]{2,1,0:T(8,128)}, f32[2,128,8192]{2,1,0:T(8,128)S(1)}, u32[]{:S(2)}) copy-start(f32[2,128,8192]{2,1,0:T(8,128)S(1)} %fusion.2) | copy-start | bytes 25165828
  221.4 14.6 %copy-start.13 = (bf16[128,320]{0,1:T(8,128)(2,1)S(1)}, bf16[128,320]{0,1:T(8,128)(2,1)}, u32[]{:S(2)}) copy-start(bf16[128,320]{0,1:T(8,128)(2,1)} %param.11) | copy-start | bytes 245764
  221.4 14.6 %copy-start.14 = (bf16[128,320]{0,1:T(8,128)(2,1)S(1)}, bf16[128,320]{0,1:T(8,128)(2,1)}, u32[]{:S(2)}) copy-start(bf16[128,320]{0,1:T(8,128)(2,1)} %param.12) | copy-start | bytes 245764
Sparse Core Ops, SparseCore 0:
  36.9 92.7 all-gather.1

commit v5 on v3

--- a/solution.py
+++ b/solution.py
@@ -26,6 +26,10 @@
 
 def ring_steps(size):
     return size // 2, (size - 1) // 2
+
+
+def shift(data, axis, size, step):
+    return lax.ppermute(data, axis, [(i, (i + step) % size) for i in range(size)])
 
 
 def ring_gather(data, axis, size):
@@ -35,12 +39,24 @@
     ahead = behind = data
     for step in range(max(forward, backward)):
         if step < forward:
-            ahead = lax.ppermute(ahead, axis, [(i, (i + 1) % size) for i in range(size)])
+            ahead = shift(ahead, axis, size, 1)
             pieces[size - 1 - step] = ahead
         if step < backward:
-            behind = lax.ppermute(behind, axis, [(i, (i - 1) % size) for i in range(size)])
+            behind = shift(behind, axis, size, -1)
             pieces[1 + step] = behind
     return pieces
+
+
+def ring4_first(data, axis):
+    return shift(data, axis, 4, 1), shift(data, axis, 4, -1)
+
+
+def ring4_last(data, ahead, behind, axis):
+    half = data.shape[0] // 2
+    far = jnp.concatenate(
+        [shift(ahead[:half], axis, 4, 1), shift(behind[half:], axis, 4, -1)], axis=0
+    )
+    return [data, behind, far, ahead]
 
 
 def per_device(
@@ -93,11 +109,10 @@
         kv_all = lax.all_gather(kv, "y", axis=0, tiled=True)
         kv_all = lax.all_gather(kv_all, "z", axis=0, tiled=True)
         qg_z = jnp.concatenate(ring_gather(qg, "z", z_size), axis=0)
-        qg_all = jnp.concatenate(ring_gather(qg_z, "y", y_size), axis=0)
+        qg_z, kv_all = lax.optimization_barrier((qg_z, kv_all))
+        qg_ahead, qg_behind = ring4_first(qg_z, "y")
         key_all = kv_all[:, :cols].reshape(all_rows, heads_here, head_width)
         value_all = kv_all[:, cols:].reshape(all_rows, heads_here, head_width)
-        query_all = qg_all[:, :cols].reshape(all_rows, heads_here, head_width)
-        grad_all = qg_all[:, cols:].reshape(all_rows, heads_here, head_width)
 
     rel_z = lax.iota(jnp.int32, z_size)
     rel_y = lax.iota(jnp.int32, y_size)
@@ -144,6 +159,10 @@
 
     with jax.named_scope("gather_row_stats"):
         stats = jnp.stack([log_total, row_delta], axis=0)
+        stats, qg_ahead, qg_behind = lax.optimization_barrier((stats, qg_ahead, qg_behind))
+        qg_all = jnp.concatenate(ring4_last(qg_z, qg_ahead, qg_behind, "y"), axis=0)
+        query_all = qg_all[:, :cols].reshape(all_rows, heads_here, head_width)
+        grad_all = qg_all[:, cols:].reshape(all_rows, heads_here, head_width)
         sent = jnp.broadcast_to(stats[None], (shards,) + stats.shape)
         stats_all = lax.all_to_all(sent, ("z", "y"), 0, 0, tiled=False)
         stats_all = stats_all[qg_source]

time: 269 us -> 245 us (0.911)
  waiting for transfers between devices: 62.2 us -> 45.8 us
  local copies, waits for them, and re-layouts: 31.6 us -> 26.5 us
  matrix products: 31.5 us -> 26.6 us
  blocking collectives: 40.2 us -> 44.2 us
    ppermute x18 -> x19, waiting for transfers between devices: 53 us -> 41 us  [shift(): lax.ppermute(data, axis, [(i, (i + step) % size) for i in range(size)])]
    all_to_all x1, waiting for transfers between devices: 9.24 us -> 0.01 us  [per_device(): stats_all = lax.all_to_all(sent, ('z', 'y'), 0, 0, tiled=False)]
    all_gather x1, waiting for transfers between devices: 0.01 us -> 4.81 us  [per_device(): kv_all = lax.all_gather(kv_all, 'z', axis=0, tiled=True)]
    all_to_all x1, blocking collectives: 12.1 us -> 16.2 us  [per_device(): received = lax.all_to_all(payload, 'tp', 0, 0, tiled=False)]
    unnamed x55, local copies, waits for them, and re-layouts: 15.6 us -> 11.7 us
    slice x0 -> x2, local copies, waits for them, and re-layouts: none -> 2.92 us  [the longest x1 1.96 us: ring4_last(): behind[half:]]
    ppermute x18 -> x19, starting transfers between devices: 67.2 us -> 67.9 us  [shift(): lax.ppermute(data, axis, [(i, (i + step) % size) for i in range(size)])]
  transfers between devices with their start and end apart: 20 -> 21, of which waited for: 15 -> 15; matrix products, arithmetic and copies ran while one was open for 11% -> 14% of each run, Pallas kernels for 0% -> 0%
where the time goes in v5:
time: 245 us; the launch traced here: 244 us
  starting transfers between devices  77.8 us (32%)
  waiting for transfers between devices  45.8 us (19%)
  blocking collectives  44.2 us (18%)
  matrix products  26.6 us (11%)
  local copies, waits for them, and re-layouts  26.5 us (11%)
  between operations  14.8 us (6%)
  other arithmetic  8.04 us (3%)
    ppermute x19, starting transfers between devices, shift(): lax.ppermute(data, axis, [(i, (i + step) % size) for i in range(size)])  67.9 us
    ppermute x19, waiting for transfers between devices, shift(): lax.ppermute(data, axis, [(i, (i + step) % size) for i in range(size)])  41 us
    all_to_all x1, blocking collectives, per_device(): received = lax.all_to_all(payload, 'tp', 0, 0, tiled=False)  16.2 us
    all_gather x1, blocking collectives, per_device(): kv_all = lax.all_gather(kv, 'y', axis=0, tiled=True)  14.5 us
    all_gather x1, blocking collectives, per_device(): gathered = lax.all_gather(both, 'tp', axis=1, tiled=True)  13.4 us
    unnamed x55, local copies, waits for them, and re-layouts  11.7 us
    all_to_all x1, starting transfers between devices, per_device(): stats_all = lax.all_to_all(sent, ('z', 'y'), 0, 0, tiled=False)  9.96 us
    dot_general x1, matrix products, per_device(): jnp.einsum('hkq,qhd->khd', score_grad, query_all, preferred_element_type=...  7.55 us
  transfers between devices with their start and end apart: 21, of which 15 were waited for; matrix products, arithmetic and copies ran while one was open for 14% of the time, Pallas kernels for 0%

profile of v5, /device:TPU:24, one launch (start us, length us, event | category | flops | bytes accessed | tf_op | source)
XLA Modules:
  0.0 243.7 jit_solution(14382193769921107248)
XLA Ops:
  7.5 13.4 %all_gather.9 = bf16[128,2560]{0,1:T(8,128)(2,1)S(1)} all-gather(bf16[128,640]{0,1:T(8,128)(2,1)S(1)} %pad_maximum_fusion.1), channel_id=1, replica_groups=mesh['z'=16,'y'=4,'tp'=4,'dp'=2] {'tp'}, dimensions={1}, use_global_device_ids=true | all-gather | bytes 819200 | tf_op jit(solution)/shard_map/gather_features/all_gather | solution.py:77
  22.8 14.5 %all_gather.10 = bf16[512,320]{0,1:T(8,128)(2,1)} all-gather(bf16[128,320]{0,1:T(8,128)(2,1)S(1)} %pad_maximum_fusion.3), channel_id=1, replica_groups=mesh['z'=16,'y'=4,'tp'=4,'dp'=2] {'y'}, dimensions={0}, use_global_device_ids=true | all-gather | bytes 409600 | tf_op jit(solution)/shard_map/gather_sequence/all_gather | solution.py:109
  38.7 8.9 %collective-permute-start = (bf16[128,320]{0,1:T(8,128)(2,1)}, bf16[128,320]{0,1:T(8,128)(2,1)}, u32[]{:S(2)}, u32[]{:S(2)}) collective-permute-start(bf16[128,320]{0,1:T(8,128)(2,1)} %get-tuple-element.35), channel_id=1, source_target_pairs={{0,480},{32,0},{64,32},{96,64},{128,96},{160,128},{192,160},{224,1... | collective-permute-start | bytes 245768 | tf_op jit(solution)/shard_map/gather_sequence/ppermute | solution.py:32
  47.7 1.9 collective-permute-start.7
  51.9 2.3 broadcast_compare_fusion
  54.3 5.1 %collective-permute-start.1 = (bf16[128,320]{0,1:T(8,128)(2,1)}, bf16[128,320]{0,1:T(8,128)(2,1)S(1)}, u32[]{:S(2)}, u32[]{:S(2)}) collective-permute-start(bf16[128,320]{0,1:T(8,128)(2,1)} %collective-permute-done), channel_id=1, source_target_pairs={{0,480},{32,0},{64,32},{96,64},{128,96},{160,128},{192,160},{224,1... | collective-permute-start | bytes 245768 | tf_op jit(solution)/shard_map/gather_sequence/ppermute | solution.py:32
  59.4 1.9 collective-permute-start.8
  62.5 4.9 %collective-permute-start.2 = (bf16[128,320]{0,1:T(8,128)(2,1)S(1)}, bf16[128,320]{0,1:T(8,128)(2,1)S(1)}, u32[]{:S(2)}, u32[]{:S(2)}) collective-permute-start(bf16[128,320]{0,1:T(8,128)(2,1)S(1)} %collective-permute-done.1), channel_id=1, source_target_pairs={{0,480},{32,0},{64,32},{96,64},{128,96},{160,128},{192,160},{224,1... | collective-permute-start | bytes 245768 | tf_op jit(solution)/shard_map/gather_sequence/ppermute | solution.py:32
  68.7 1.9 collective-permute-start.9
  71.1 5.6 %collective-permute-start.3 = (bf16[128,320]{0,1:T(8,128)(2,1)S(1)}, bf16[128,320]{0,1:T(8,128)(2,1)S(1)}, u32[]{:S(2)}, u32[]{:S(2)}) collective-permute-start(bf16[128,320]{0,1:T(8,128)(2,1)S(1)} %collective-permute-done.2), channel_id=1, source_target_pairs={{0,480},{32,0},{64,32},{96,64},{128,96},{160,128},{192,160},{224,1... | collective-permute-start | bytes 245768 | tf_op jit(solution)/shard_map/gather_sequence/ppermute | solution.py:32
  77.7 1.9 collective-permute-start.10
  80.3 5.6 %collective-permute-start.4 = (bf16[128,320]{0,1:T(8,128)(2,1)S(1)}, bf16[128,320]{0,1:T(8,128)(2,1)S(1)}, u32[]{:S(2)}, u32[]{:S(2)}) collective-permute-start(bf16[128,320]{0,1:T(8,128)(2,1)S(1)} %collective-permute-done.3), channel_id=1, source_target_pairs={{0,480},{32,0},{64,32},{96,64},{128,96},{160,128},{192,160},{224,1... | collective-permute-start | bytes 245768 | tf_op jit(solution)/shard_map/gather_sequence/ppermute | solution.py:32
  86.9 1.9 collective-permute-start.11
  88.9 5.2 %collective-permute-start.5 = (bf16[128,320]{0,1:T(8,128)(2,1)S(1)}, bf16[128,320]{0,1:T(8,128)(2,1)S(1)}, u32[]{:S(2)}, u32[]{:S(2)}) collective-permute-start(bf16[128,320]{0,1:T(8,128)(2,1)S(1)} %collective-permute-done.4), channel_id=1, source_target_pairs={{0,480},{32,0},{64,32},{96,64},{128,96},{160,128},{192,160},{224,1... | collective-permute-start | bytes 245768 | tf_op jit(solution)/shard_map/gather_sequence/ppermute | solution.py:32
  94.2 2.6 %collective-permute-done.11 = bf16[128,320]{0,1:T(8,128)(2,1)S(1)} collective-permute-done((bf16[128,320]{0,1:T(8,128)(2,1)S(1)}, bf16[128,320]{0,1:T(8,128)(2,1)S(1)}, u32[]{:S(2)}, u32[]{:S(2)}) %collective-permute-start.11) | collective-permute-done | bytes 81952 | tf_op jit(solution)/shard_map/gather_sequence/ppermute | solution.py:32
  96.7 1.9 collective-permute-start.12
  98.7 5.1 %collective-permute-start.6 = (bf16[128,320]{0,1:T(8,128)(2,1)S(1)}, bf16[128,320]{0,1:T(8,128)(2,1)S(1)}, u32[]{:S(2)}, u32[]{:S(2)}) collective-permute-start(bf16[128,320]{0,1:T(8,128)(2,1)S(1)} %collective-permute-done.5), channel_id=1, source_target_pairs={{0,480},{32,0},{64,32},{96,64},{128,96},{160,128},{192,160},{224,1... | collective-permute-start | bytes 245768 | tf_op jit(solution)/shard_map/gather_sequence/ppermute | solution.py:32
  103.8 2.4 collective-permute-done.12
  106.2 1.9 collective-permute-start.13
  108.2 7.5 %collective-permute-done.13 = bf16[128,320]{0,1:T(8,128)(2,1)S(1)} collective-permute-done((bf16[128,320]{0,1:T(8,128)(2,1)S(1)}, bf16[128,320]{0,1:T(8,128)(2,1)S(1)}, u32[]{:S(2)}, u32[]{:S(2)}) %collective-permute-start.13) | collective-permute-done | bytes 81952 | tf_op jit(solution)/shard_map/gather_sequence/ppermute | solution.py:32
  115.6 1.9 collective-permute-start.14
  117.6 6.4 %collective-permute-done.14 = bf16[128,320]{0,1:T(8,128)(2,1)S(1)} collective-permute-done((bf16[128,320]{0,1:T(8,128)(2,1)S(1)}, bf16[128,320]{0,1:T(8,128)(2,1)S(1)}, u32[]{:S(2)}, u32[]{:S(2)}) %collective-permute-start.14) | collective-permute-done | bytes 81952 | tf_op jit(solution)/shard_map/gather_sequence/ppermute | solution.py:32
  125.2 4.8 %all-gather.2.cloned.1.call-done = bf16[8192,320]{0,1:T(8,128)(2,1)} async-done(((bf16[512,320]{0,1:T(8,128)(2,1)}), bf16[8192,320]{0,1:T(8,128)(2,1)}) %all-gather.2.cloned.1.call-update) | async-done | bytes 5242896 | tf_op jit(solution)/shard_map/gather_sequence/all_gather | solution.py:110
  130.1 2.2 collective-permute-start.15
  132.2 3.8 %collective-permute-start.16 = (bf16[2048,320]{0,1:T(8,128)(2,1)}, bf16[2048,320]{0,1:T(8,128)(2,1)}, u32[]{:S(2)}, u32[]{:S(2)}) collective-permute-start(bf16[2048,320]{0,1:T(8,128)(2,1)} %copy-done.9), channel_id=1, source_target_pairs={{0,24},{8,0},{16,8},{24,16},{1,25},{9,1},{17,9},{25,17},{2,26},{10... | collective-permute-start | bytes 3932168 | tf_op jit(solution)/shard_map/gather_sequence/ppermute | solution.py:32
  136.1 3.0 %fusion.41 = (bf16[8192,160]{0,1:T(8,128)(2,1)S(1)}, bf16[8192,160]{0,1:T(8,128)(2,1)S(1)}) fusion(bf16[8192,320]{0,1:T(8,128)(2,1)} %all-gather.2.cloned.1.call-done), kind=kLoop, calls=%fused_computation.98 | loop fusion | bytes 10485760 | tf_op jit(solution)/shard_map/gather_sequence/slice | solution.py:115
  139.1 1.8 select_reduce_fusion.1
  140.9 2.5 %select_reduce_fusion = f32[2,128]{1,0:T(2,128)S(1)} fusion(f32[2,128,8192]{2,1,0:T(8,128)S(1)} %get-tuple-element.40, f32[2,128]{1,0:T(2,128)S(1)} %get-tuple-element.39, pred[128,8192]{1,0:T(8,128)(4,1)S(1)} %get-tuple-element.38), kind=kLoop, calls=%fused_computation.10 | loop fusion | flops 8388352 | bytes 9439232 | tf_op jit(solution)/shard_map/query_pass/reduce_sum | solution.py:139
  143.4 3.5 %fusion.43 = (f32[2,128]{1,0:T(2,128)S(1)}, bf16[2,128,8192]{2,1,0:T(8,128)(2,1)S(1)}) fusion(bf16[128,2,80]{0,2,1:T(8,128)(2,1)S(1)} %bitcast.100, bf16[8192,2,80]{0,2,1:T(8,128)(2,1)S(1)} %bitcast.92, f32[2,128,8192]{2,1,0:T(8,128)S(1)} %get-tuple-element.40, f32[2,128]{1,0:T(2,128)S(1)} %log_add_fusion, pred[128,8192]{1,0:T(8,128)(4,1)S(1)} %get-tuple-element.38), kind=kOutput, calls=%fused_computation.100 | convolution fusion | flops 346029824 | bytes 16295936 | tf_op jit(solution)/shard_map/query_pass/qhd,khd->hqk/dot_general | solution.py:142
  146.9 2.0 fusion.25
  148.8 1.5 fusion.19
  150.5 8.5 %collective-permute-done.15 = bf16[2048,320]{0,1:T(8,128)(2,1)S(1)} collective-permute-done((bf16[2048,320]{0,1:T(8,128)(2,1)}, bf16[2048,320]{0,1:T(8,128)(2,1)S(1)}, u32[]{:S(2)}, u32[]{:S(2)}) %collective-permute-start.15) | collective-permute-done | bytes 1310752 | tf_op jit(solution)/shard_map/gather_sequence/ppermute | solution.py:32
  159.0 3.6 %collective-permute-done.16 = bf16[2048,320]{0,1:T(8,128)(2,1)} collective-permute-done((bf16[2048,320]{0,1:T(8,128)(2,1)}, bf16[2048,320]{0,1:T(8,128)(2,1)}, u32[]{:S(2)}, u32[]{:S(2)}) %collective-permute-start.16) | collective-permute-done | bytes 1310752 | tf_op jit(solution)/shard_map/gather_sequence/ppermute | solution.py:32
  163.2 10.0 %all-to-all-start = ((f32[64,2,2,128]{3,2,1,0:T(2,128)}), f32[64,2,2,128]{3,2,1,0:T(2,128)S(1)}, u32[]{:S(2)}, u32[]{:S(2)}) async-start(f32[64,2,2,128]{3,2,1,0:T(2,128)} %broadcast_in_dim.56), calls=%async_computation | async-start | bytes 262144 | tf_op jit(solution)/shard_map/gather_row_stats/all_to_all | solution.py:167
  174.4 2.6 %constant_dynamic-update-slice_fusion.20 = bf16[8192,320]{0,1:T(8,128)(2,1)} fusion(bf16[2048,320]{0,1:T(8,128)(2,1)} %copy-done.9), kind=kLoop, calls=%fused_computation.71 | loop fusion | bytes 2621440
  177.9 2.3 collective-permute-start.17
  180.3 2.0 slice.64
  182.2 3.7 %collective-permute-start.18 = (bf16[1024,320]{0,1:T(8,128)(2,1)}, bf16[1024,320]{0,1:T(8,128)(2,1)S(1)}, u32[]{:S(2)}, u32[]{:S(2)}) collective-permute-start(bf16[1024,320]{0,1:T(8,128)(2,1)} %slice.64), channel_id=1, source_target_pairs={{0,24},{8,0},{16,8},{24,16},{1,25},{9,1},{17,9},{25,17},{2,26},{10... | collective-permute-start | bytes 1966088 | tf_op jit(solution)/shard_map/gather_row_stats/ppermute | solution.py:32
  185.9 2.6 %constant_dynamic-update-slice_fusion.19 = bf16[8192,320]{0,1:T(8,128)(2,1)} fusion(bf16[8192,320]{0,1:T(8,128)(2,1)} %constant_dynamic-update-slice_fusion.20, bf16[2048,320]{0,1:T(8,128)(2,1)} %collective-permute-done.16), kind=kLoop, calls=%fused_computation.70 | loop fusion | bytes 2621440
  189.9 2.6 %collective-permute-done.17 = bf16[1024,320]{0,1:T(8,128)(2,1)} collective-permute-done((bf16[1024,320]{0,1:T(8,128)(2,1)}, bf16[1024,320]{0,1:T(8,128)(2,1)}, u32[]{:S(2)}, u32[]{:S(2)}) %collective-permute-start.17) | collective-permute-done | bytes 655392 | tf_op jit(solution)/shard_map/gather_row_stats/ppermute | solution.py:32
  192.5 2.0 constant_dynamic-update-slice_fusion.18
  194.5 2.9 %collective-permute-done.18 = bf16[1024,320]{0,1:T(8,128)(2,1)S(1)} collective-permute-done((bf16[1024,320]{0,1:T(8,128)(2,1)}, bf16[1024,320]{0,1:T(8,128)(2,1)S(1)}, u32[]{:S(2)}, u32[]{:S(2)}) %collective-permute-start.18) | collective-permute-done | bytes 655392 | tf_op jit(solution)/shard_map/gather_row_stats/ppermute | solution.py:32
  199.5 3.1 %fusion.40 = (bf16[8192,160]{0,1:T(8,128)(2,1)S(1)}, bf16[8192,160]{0,1:T(8,128)(2,1)S(1)}) fusion(bf16[8192,320]{0,1:T(8,128)(2,1)} %constant_dynamic-update-slice_fusion.16), kind=kLoop, calls=%fused_computation.97 | loop fusion | bytes 10485760 | tf_op jit(solution)/shard_map/gather_row_stats/slice | solution.py:165
  202.6 2.4 %fusion.2 = f32[2,128,8192]{2,1,0:T(8,128)S(1)} fusion(bf16[128,2,80]{0,2,1:T(8,128)(2,1)S(1)} %bitcast.98, bf16[8192,2,80]{0,2,1:T(8,128)(2,1)S(1)} %bitcast.88, f32[2,8192]{1,0:T(2,128)S(1)} %get-tuple-element.34, pred[128,8192]{1,0:T(8,128)(4,1)S(1)} %copy-done.4), kind=kOutput, calls=%fused_computation.6 | convolution fusion | flops 339738624 | bytes 12165120 | tf_op jit(solution)/shard_map/key_pass/khd,qhd->hkq/dot_general | solution.py:173
  205.1 2.8 %fusion.30 = bf16[2,80,128]{2,1,0:T(8,128)(2,1)} fusion(bf16[8192,2,80]{0,2,1:T(8,128)(2,1)S(1)} %bitcast.86, f32[2,128,8192]{2,1,0:T(8,128)S(1)} %fusion.2), kind=kOutput, calls=%fused_computation.35 | convolution fusion | flops 337661952 | bytes 11051008 | tf_op jit(solution)/shard_map/key_pass/hkq,qhd->khd/dot_general | solution.py:187
  208.3 7.5 %fusion.29 = bf16[2,80,128]{2,1,0:T(8,128)(2,1)} fusion(bf16[8192,2,80]{0,2,1:T(8,128)(2,1)} %bitcast.89, f32[2,128,8192]{2,1,0:T(8,128)} %copy-done.2, bf16[128,2,80]{0,2,1:T(8,128)(2,1)S(1)} %bitcast.97, bf16[8192,2,80]{0,2,1:T(8,128)(2,1)S(1)} %bitcast.87, f32[2,8192]{1,0:T(2,128)S(1)} %copy-done.13), kind=kOutput, calls=%fused_computation.34 | convolution fusion | flops 677400576 | bytes 13778944 | tf_op jit(solution)/shard_map/key_pass/hkq,qhd->khd/dot_general | solution.py:184
  217.3 1.5 multiply_reduce_fusion
  219.7 16.2 %all_to_all.10 = f32[4,129,320]{2,1,0:T(8,128)S(1)} all-to-all(f32[4,129,320]{2,1,0:T(8,128)S(1)} %copy.31), channel_id=1, replica_groups=mesh['z'=16,'y'=4,'tp'=4,'dp'=2] {'tp'}, dimensions={0} | all-to-all | bytes 1320960 | tf_op jit(solution)/shard_map/back_projection/all_to_all | solution.py:203
  (113 shorter events, 22.8 us)
Async XLA Ops:
  6.5 15.7 %copy-start = (bf16[160,1280]{1,0:T(8,128)(2,1)S(1)}, bf16[160,1280]{1,0:T(8,128)(2,1)}, u32[]{:S(2)}) copy-start(bf16[160,1280]{1,0:T(8,128)(2,1)} %param.16) | copy-start | bytes 1228804
  6.5 15.6 %copy-start.14 = (f32[1280]{0:T(1024)S(1)}, f32[1280]{0:T(1024)}, u32[]{:S(2)}) copy-start(f32[1280]{0:T(1024)} %param.13) | copy-start | bytes 15364
  6.5 123.5 %all-gather.2.cloned.1.call-start = ((), (), s32[]{:S(2)}) async-start(), calls=%async_computation.2 | async-start | bytes 5570560 | tf_op jit(solution)/shard_map/gather_sequence/all_gather | solution.py:110
  20.9 1.6 copy-start.6
  21.0 16.4 %copy-start.17 = (f32[80]{0:T(128)S(1)}, f32[80]{0:T(128)}, u32[]{:S(2)}) copy-start(f32[80]{0:T(128)} %param.18) | copy-start | bytes 964
  21.0 16.5 %copy-start.10 = (bf16[160,1280]{1,0:T(8,128)(2,1)S(1)}, bf16[160,1280]{1,0:T(8,128)(2,1)}, u32[]{:S(2)}) copy-start(bf16[160,1280]{1,0:T(8,128)(2,1)} %param.17) | copy-start | bytes 1228804
  21.2 16.6 %copy-start.7 = (bf16[160,1280]{1,0:T(8,128)(2,1)S(1)}, bf16[160,1280]{1,0:T(8,128)(2,1)}, u32[]{:S(2)}) copy-start(bf16[160,1280]{1,0:T(8,128)(2,1)} %param.14) | copy-start | bytes 1228804
  21.5 17.3 %copy-start.5 = (f32[128,1280]{1,0:T(8,128)}, f32[128,1280]{1,0:T(8,128)S(1)}, u32[]{:S(2)}) copy-start(f32[128,1280]{1,0:T(8,128)S(1)} %copy.28) | copy-start | bytes 1966084
  21.5 0.6 copy-start.15
  22.1 27.7 %copy-start.1 = (s32[64]{0:T(128)S(1)}, s32[64]{0:T(128)}, u32[]{:S(2)}) copy-start(s32[64]{0:T(128)} %param.19) | copy-start | bytes 772
  38.7 15.5 %collective-permute-start = (bf16[128,320]{0,1:T(8,128)(2,1)}, bf16[128,320]{0,1:T(8,128)(2,1)}, u32[]{:S(2)}, u32[]{:S(2)}) collective-permute-start(bf16[128,320]{0,1:T(8,128)(2,1)} %get-tuple-element.35), channel_id=1, source_target_pairs={{0,480},{32,0},{64,32},{96,64},{128,96},{160,128},{192,160},{224,1... | collective-permute-start | bytes 245768 | tf_op jit(solution)/shard_map/gather_sequence/ppermute | solution.py:32
  47.7 11.7 %collective-permute-start.7 = (bf16[128,320]{0,1:T(8,128)(2,1)}, bf16[128,320]{0,1:T(8,128)(2,1)S(1)}, u32[]{:S(2)}, u32[]{:S(2)}) collective-permute-start(bf16[128,320]{0,1:T(8,128)(2,1)} %get-tuple-element.35), channel_id=1, source_target_pairs={{0,32},{32,64},{64,96},{96,128},{128,160},{160,192},{192,224},{224... | collective-permute-start | bytes 245768 | tf_op jit(solution)/shard_map/gather_sequence/ppermute | solution.py:32
  54.3 8.2 %collective-permute-start.1 = (bf16[128,320]{0,1:T(8,128)(2,1)}, bf16[128,320]{0,1:T(8,128)(2,1)S(1)}, u32[]{:S(2)}, u32[]{:S(2)}) collective-permute-start(bf16[128,320]{0,1:T(8,128)(2,1)} %collective-permute-done), channel_id=1, source_target_pairs={{0,480},{32,0},{64,32},{96,64},{128,96},{160,128},{192,160},{224,1... | collective-permute-start | bytes 245768 | tf_op jit(solution)/shard_map/gather_sequence/ppermute | solution.py:32
  59.4 9.3 %collective-permute-start.8 = (bf16[128,320]{0,1:T(8,128)(2,1)S(1)}, bf16[128,320]{0,1:T(8,128)(2,1)S(1)}, u32[]{:S(2)}, u32[]{:S(2)}) collective-permute-start(bf16[128,320]{0,1:T(8,128)(2,1)S(1)} %collective-permute-done.7), channel_id=1, source_target_pairs={{0,32},{32,64},{64,96},{96,128},{128,160},{160,192},{192,224},{224... | collective-permute-start | bytes 245768 | tf_op jit(solution)/shard_map/gather_sequence/ppermute | solution.py:32
  62.5 8.6 %collective-permute-start.2 = (bf16[128,320]{0,1:T(8,128)(2,1)S(1)}, bf16[128,320]{0,1:T(8,128)(2,1)S(1)}, u32[]{:S(2)}, u32[]{:S(2)}) collective-permute-start(bf16[128,320]{0,1:T(8,128)(2,1)S(1)} %collective-permute-done.1), channel_id=1, source_target_pairs={{0,480},{32,0},{64,32},{96,64},{128,96},{160,128},{192,160},{224,1... | collective-permute-start | bytes 245768 | tf_op jit(solution)/shard_map/gather_sequence/ppermute | solution.py:32
  68.7 9.0 %collective-permute-start.9 = (bf16[128,320]{0,1:T(8,128)(2,1)S(1)}, bf16[128,320]{0,1:T(8,128)(2,1)S(1)}, u32[]{:S(2)}, u32[]{:S(2)}) collective-permute-start(bf16[128,320]{0,1:T(8,128)(2,1)S(1)} %collective-permute-done.8), channel_id=1, source_target_pairs={{0,32},{32,64},{64,96},{96,128},{128,160},{160,192},{192,224},{224... | collective-permute-start | bytes 245768 | tf_op jit(solution)/shard_map/gather_sequence/ppermute | solution.py:32
  71.1 9.3 %collective-permute-start.3 = (bf16[128,320]{0,1:T(8,128)(2,1)S(1)}, bf16[128,320]{0,1:T(8,128)(2,1)S(1)}, u32[]{:S(2)}, u32[]{:S(2)}) collective-permute-start(bf16[128,320]{0,1:T(8,128)(2,1)S(1)} %collective-permute-done.2), channel_id=1, source_target_pairs={{0,480},{32,0},{64,32},{96,64},{128,96},{160,128},{192,160},{224,1... | collective-permute-start | bytes 245768 | tf_op jit(solution)/shard_map/gather_sequence/ppermute | solution.py:32
  77.7 9.2 %collective-permute-start.10 = (bf16[128,320]{0,1:T(8,128)(2,1)S(1)}, bf16[128,320]{0,1:T(8,128)(2,1)S(1)}, u32[]{:S(2)}, u32[]{:S(2)}) collective-permute-start(bf16[128,320]{0,1:T(8,128)(2,1)S(1)} %collective-permute-done.9), channel_id=1, source_target_pairs={{0,32},{32,64},{64,96},{96,128},{128,160},{160,192},{192,224},{224... | collective-permute-start | bytes 245768 | tf_op jit(solution)/shard_map/gather_sequence/ppermute | solution.py:32
  80.3 8.5 %collective-permute-start.4 = (bf16[128,320]{0,1:T(8,128)(2,1)S(1)}, bf16[128,320]{0,1:T(8,128)(2,1)S(1)}, u32[]{:S(2)}, u32[]{:S(2)}) collective-permute-start(bf16[128,320]{0,1:T(8,128)(2,1)S(1)} %collective-permute-done.3), channel_id=1, source_target_pairs={{0,480},{32,0},{64,32},{96,64},{128,96},{160,128},{192,160},{224,1... | collective-permute-start | bytes 245768 | tf_op jit(solution)/shard_map/gather_sequence/ppermute | solution.py:32
  86.9 9.8 %collective-permute-start.11 = (bf16[128,320]{0,1:T(8,128)(2,1)S(1)}, bf16[128,320]{0,1:T(8,128)(2,1)S(1)}, u32[]{:S(2)}, u32[]{:S(2)}) collective-permute-start(bf16[128,320]{0,1:T(8,128)(2,1)S(1)} %collective-permute-done.10), channel_id=1, source_target_pairs={{0,32},{32,64},{64,96},{96,128},{128,160},{160,192},{192,224},{224... | collective-permute-start | bytes 245768 | tf_op jit(solution)/shard_map/gather_sequence/ppermute | solution.py:32
  88.9 9.8 %collective-permute-start.5 = (bf16[128,320]{0,1:T(8,128)(2,1)S(1)}, bf16[128,320]{0,1:T(8,128)(2,1)S(1)}, u32[]{:S(2)}, u32[]{:S(2)}) collective-permute-start(bf16[128,320]{0,1:T(8,128)(2,1)S(1)} %collective-permute-done.4), channel_id=1, source_target_pairs={{0,480},{32,0},{64,32},{96,64},{128,96},{160,128},{192,160},{224,1... | collective-permute-start | bytes 245768 | tf_op jit(solution)/shard_map/gather_sequence/ppermute | solution.py:32
  96.7 9.5 %collective-permute-start.12 = (bf16[128,320]{0,1:T(8,128)(2,1)S(1)}, bf16[128,320]{0,1:T(8,128)(2,1)S(1)}, u32[]{:S(2)}, u32[]{:S(2)}) collective-permute-start(bf16[128,320]{0,1:T(8,128)(2,1)S(1)} %collective-permute-done.11), channel_id=1, source_target_pairs={{0,32},{32,64},{64,96},{96,128},{128,160},{160,192},{192,224},{224... | collective-permute-start | bytes 245768 | tf_op jit(solution)/shard_map/gather_sequence/ppermute | solution.py:32
  98.7 18.8 %collective-permute-start.6 = (bf16[128,320]{0,1:T(8,128)(2,1)S(1)}, bf16[128,320]{0,1:T(8,128)(2,1)S(1)}, u32[]{:S(2)}, u32[]{:S(2)}) collective-permute-start(bf16[128,320]{0,1:T(8,128)(2,1)S(1)} %collective-permute-done.5), channel_id=1, source_target_pairs={{0,480},{32,0},{64,32},{96,64},{128,96},{160,128},{192,160},{224,1... | collective-permute-start | bytes 245768 | tf_op jit(solution)/shard_map/gather_sequence/ppermute | solution.py:32
  106.2 9.4 %collective-permute-start.13 = (bf16[128,320]{0,1:T(8,128)(2,1)S(1)}, bf16[128,320]{0,1:T(8,128)(2,1)S(1)}, u32[]{:S(2)}, u32[]{:S(2)}) collective-permute-start(bf16[128,320]{0,1:T(8,128)(2,1)S(1)} %collective-permute-done.12), channel_id=1, source_target_pairs={{0,32},{32,64},{64,96},{96,128},{128,160},{160,192},{192,224},{224... | collective-permute-start | bytes 245768 | tf_op jit(solution)/shard_map/gather_sequence/ppermute | solution.py:32
  115.6 8.3 %collective-permute-start.14 = (bf16[128,320]{0,1:T(8,128)(2,1)S(1)}, bf16[128,320]{0,1:T(8,128)(2,1)S(1)}, u32[]{:S(2)}, u32[]{:S(2)}) collective-permute-start(bf16[128,320]{0,1:T(8,128)(2,1)S(1)} %collective-permute-done.13), channel_id=1, source_target_pairs={{0,32},{32,64},{64,96},{96,128},{128,160},{160,192},{192,224},{224... | collective-permute-start | bytes 245768 | tf_op jit(solution)/shard_map/gather_sequence/ppermute | solution.py:32
  124.2 1.1 copy-start.9
  130.1 28.9 %collective-permute-start.15 = (bf16[2048,320]{0,1:T(8,128)(2,1)}, bf16[2048,320]{0,1:T(8,128)(2,1)S(1)}, u32[]{:S(2)}, u32[]{:S(2)}) collective-permute-start(bf16[2048,320]{0,1:T(8,128)(2,1)} %copy-done.9), channel_id=1, source_target_pairs={{0,8},{8,16},{16,24},{24,0},{1,9},{9,17},{17,25},{25,1},{2,10},{10... | collective-permute-start | bytes 3932168 | tf_op jit(solution)/shard_map/gather_sequence/ppermute | solution.py:32
  132.2 30.3 %collective-permute-start.16 = (bf16[2048,320]{0,1:T(8,128)(2,1)}, bf16[2048,320]{0,1:T(8,128)(2,1)}, u32[]{:S(2)}, u32[]{:S(2)}) collective-permute-start(bf16[2048,320]{0,1:T(8,128)(2,1)} %copy-done.9), channel_id=1, source_target_pairs={{0,24},{8,0},{16,8},{24,16},{1,25},{9,1},{17,9},{25,17},{2,26},{10... | collective-permute-start | bytes 3932168 | tf_op jit(solution)/shard_map/gather_sequence/ppermute | solution.py:32
  148.8 24.4 %copy-start.8 = (bf16[160,1280]{1,0:T(8,128)(2,1)S(1)}, bf16[160,1280]{1,0:T(8,128)(2,1)}, u32[]{:S(2)}) copy-start(bf16[160,1280]{1,0:T(8,128)(2,1)} %param.14) | copy-start | bytes 1228804
  163.2 25.3 %all-to-all-start = ((f32[64,2,2,128]{3,2,1,0:T(2,128)}), f32[64,2,2,128]{3,2,1,0:T(2,128)S(1)}, u32[]{:S(2)}, u32[]{:S(2)}) async-start(f32[64,2,2,128]{3,2,1,0:T(2,128)} %broadcast_in_dim.56), calls=%async_computation | async-start | bytes 262144 | tf_op jit(solution)/shard_map/gather_row_stats/all_to_all | solution.py:167
  177.9 14.6 %collective-permute-start.17 = (bf16[1024,320]{0,1:T(8,128)(2,1)}, bf16[1024,320]{0,1:T(8,128)(2,1)}, u32[]{:S(2)}, u32[]{:S(2)}) collective-permute-start(bf16[1024,320]{0,1:T(8,128)(2,1)} %slice.63), channel_id=1, source_target_pairs={{0,8},{8,16},{16,24},{24,0},{1,9},{9,17},{17,25},{25,1},{2,10},{10... | collective-permute-start | bytes 1966088 | tf_op jit(solution)/shard_map/gather_row_stats/ppermute | solution.py:32
  182.2 15.1 %collective-permute-start.18 = (bf16[1024,320]{0,1:T(8,128)(2,1)}, bf16[1024,320]{0,1:T(8,128)(2,1)S(1)}, u32[]{:S(2)}, u32[]{:S(2)}) collective-permute-start(bf16[1024,320]{0,1:T(8,128)(2,1)} %slice.64), channel_id=1, source_target_pairs={{0,24},{8,0},{16,8},{24,16},{1,25},{9,1},{17,9},{25,17},{2,26},{10... | collective-permute-start | bytes 1966088 | tf_op jit(solution)/shard_map/gather_row_stats/ppermute | solution.py:32
  199.5 3.1 %copy-start.4 = (pred[128,8192]{1,0:T(8,128)(4,1)S(1)}, pred[128,8192]{1,0:T(8,128)(4,1)}, u32[]{:S(2)}) copy-start(pred[128,8192]{1,0:T(8,128)(4,1)} %get-tuple-element.37) | copy-start | bytes 3145732
  202.6 2.5 %copy-start.3 = (bf16[8192,160]{0,1:T(8,128)(2,1)}, bf16[8192,160]{0,1:T(8,128)(2,1)S(1)}, u32[]{:S(2)}) copy-start(bf16[8192,160]{0,1:T(8,128)(2,1)S(1)} %get-tuple-element.28) | copy-start | bytes 7864324
  205.1 3.3 %copy-start.2 = (f32[2,128,8192]{2,1,0:T(8,128)}, f32[2,128,8192]{2,1,0:T(8,128)S(1)}, u32[]{:S(2)}) copy-start(f32[2,128,8192]{2,1,0:T(8,128)S(1)} %fusion.2) | copy-start | bytes 25165828
  205.1 3.3 %copy-start.13 = (f32[2,8192]{1,0:T(2,128)S(1)}, f32[2,8192]{1,0:T(2,128)}, u32[]{:S(2)}) copy-start(f32[2,8192]{1,0:T(2,128)} %get-tuple-element.33) | copy-start | bytes 196612
  219.2 16.9 %copy-start.11 = (bf16[128,320]{0,1:T(8,128)(2,1)S(1)}, bf16[128,320]{0,1:T(8,128)(2,1)}, u32[]{:S(2)}) copy-start(bf16[128,320]{0,1:T(8,128)(2,1)} %param.11) | copy-start | bytes 245764
  219.2 16.9 %copy-start.12 = (bf16[128,320]{0,1:T(8,128)(2,1)S(1)}, bf16[128,320]{0,1:T(8,128)(2,1)}, u32[]{:S(2)}) copy-start(bf16[128,320]{0,1:T(8,128)(2,1)} %param.12) | copy-start | bytes 245764
  219.3 16.9 %copy-start.16 = (f32[128]{0:T(128)S(1)}, f32[128]{0:T(128)}, u32[]{:S(2)}) copy-start(f32[128]{0:T(128)} %copy-done.15) | copy-start | bytes 1540
Sparse Core Ops, SparseCore 0:
  37.5 92.4 all-gather.1

commit v6 on v5

--- a/solution.py
+++ b/solution.py
@@ -120,7 +120,6 @@
     abs_y = (y_index + rel_y) % y_size
     qg_source = (abs_z[None, :] * y_size + abs_y[:, None]).reshape(shards)
     key_positions = block_positions(offsets, all_rows)
-    query_positions = block_positions(offsets[qg_source], all_rows)
     seq_index = z_index * y_size + y_index
     own_positions = offsets[seq_index] * PIECE + lax.iota(jnp.int32, row_count)
 
@@ -160,33 +159,46 @@
     with jax.named_scope("gather_row_stats"):
         stats = jnp.stack([log_total, row_delta], axis=0)
         stats, qg_ahead, qg_behind = lax.optimization_barrier((stats, qg_ahead, qg_behind))
-        qg_all = jnp.concatenate(ring4_last(qg_z, qg_ahead, qg_behind, "y"), axis=0)
-        query_all = qg_all[:, :cols].reshape(all_rows, heads_here, head_width)
-        grad_all = qg_all[:, cols:].reshape(all_rows, heads_here, head_width)
+        qg_pieces = ring4_last(qg_z, qg_ahead, qg_behind, "y")
         sent = jnp.broadcast_to(stats[None], (shards,) + stats.shape)
         stats_all = lax.all_to_all(sent, ("z", "y"), 0, 0, tiled=False)
-        stats_all = stats_all[qg_source]
-        log_all = jnp.transpose(stats_all[:, 0], (1, 0, 2)).reshape(heads_here, all_rows)
-        delta_all = jnp.transpose(stats_all[:, 1], (1, 0, 2)).reshape(heads_here, all_rows)
 
     with jax.named_scope("key_pass"):
-        scores_t = jnp.einsum(
-            "khd,qhd->hkq", key_heads, query_all, preferred_element_type=jnp.float32
-        )
-        visible_t = own_positions[None, :, None] <= query_positions[None, None, :]
-        attend_t = jnp.exp(
-            jnp.where(visible_t, scores_t - log_all[:, None, :], masked_score)
-        )
-        grad_probs_t = jnp.einsum(
-            "khd,qhd->hkq", value_heads, grad_all, preferred_element_type=jnp.float32
-        )
-        score_grad = (attend_t * (grad_probs_t - delta_all[:, None, :])).astype(jnp.bfloat16)
-        key_grad = jnp.einsum(
-            "hkq,qhd->khd", score_grad, query_all, preferred_element_type=jnp.float32
-        )
-        value_grad = jnp.einsum(
-            "hkq,qhd->khd", attend_t.astype(jnp.bfloat16), grad_all, preferred_element_type=jnp.float32
-        )
+        piece_rows = qg_pieces[0].shape[0]
+        key_grad = jnp.zeros((row_count, heads_here, head_width), jnp.float32)
+        value_grad = jnp.zeros((row_count, heads_here, head_width), jnp.float32)
+        for ry, piece in enumerate(qg_pieces):
+            source = qg_source[ry * z_size : (ry + 1) * z_size]
+            query_part = piece[:, :cols].reshape(piece_rows, heads_here, head_width)
+            grad_part = piece[:, cols:].reshape(piece_rows, heads_here, head_width)
+            place = block_positions(offsets[source], piece_rows)
+            part_stats = stats_all[source]
+            log_part = jnp.transpose(part_stats[:, 0], (1, 0, 2)).reshape(heads_here, piece_rows)
+            delta_part = jnp.transpose(part_stats[:, 1], (1, 0, 2)).reshape(
+                heads_here, piece_rows
+            )
+            scores_t = jnp.einsum(
+                "khd,qhd->hkq", key_heads, query_part, preferred_element_type=jnp.float32
+            )
+            visible_t = own_positions[None, :, None] <= place[None, None, :]
+            attend_t = jnp.exp(
+                jnp.where(visible_t, scores_t - log_part[:, None, :], masked_score)
+            )
+            grad_probs_t = jnp.einsum(
+                "khd,qhd->hkq", value_heads, grad_part, preferred_element_type=jnp.float32
+            )
+            score_grad = (attend_t * (grad_probs_t - delta_part[:, None, :])).astype(
+                jnp.bfloat16
+            )
+            key_grad = key_grad + jnp.einsum(
+                "hkq,qhd->khd", score_grad, query_part, preferred_element_type=jnp.float32
+            )
+            value_grad = value_grad + jnp.einsum(
+                "hkq,qhd->khd",
+                attend_t.astype(jnp.bfloat16),
+                grad_part,
+                preferred_element_type=jnp.float32,
+            )
         key_done = key_grad.reshape(row_count, cols).astype(jnp.bfloat16)
         value_done = value_grad.reshape(row_count, cols).astype(jnp.bfloat16)
 

time: 245 us -> 244 us (level)
  waiting for transfers between devices: 45.8 us -> 34.9 us
  matrix products: 26.6 us -> 32.8 us
  local copies, waits for them, and re-layouts: 26.5 us -> 29 us
    ppermute x19, waiting for transfers between devices: 41 us -> 30 us  [shift(): lax.ppermute(data, axis, [(i, (i + step) % size) for i in range(size)])]
    dot_general x3 -> x12, matrix products: 12.8 us -> 18.9 us  [the longest x4 10.4 us: per_device(): jnp.einsum('hkq,qhd->khd', score_grad, query_part, preferred_element_type...]
    gather x2 -> x8, local copies, waits for them, and re-layouts: 1.49 us -> 6.16 us  [the longest x4 3.52 us: per_device(): part_stats = stats_all[source]]
    unnamed x55 -> x78, local copies, waits for them, and re-layouts: 11.7 us -> 7.37 us
    all_to_all x1, waiting for transfers between devices: 0.01 us -> 2.64 us  [per_device(): stats_all = lax.all_to_all(sent, ('z', 'y'), 0, 0, tiled=False)]
    all_gather x1, waiting for transfers between devices: 4.81 us -> 2.26 us  [per_device(): kv_all = lax.all_gather(kv_all, 'z', axis=0, tiled=True)]
  transfers between devices with their start and end apart: 21 -> 21, of which waited for: 15 -> 12; matrix products, arithmetic and copies ran while one was open for 14% -> 22% of each run, Pallas kernels for 0% -> 0%
where the time goes in v6:
time: 244 us; the launch traced here: 242 us
  starting transfers between devices  79.7 us (33%)
  blocking collectives  42.2 us (17%)
  waiting for transfers between devices  34.9 us (14%)
  matrix products  32.8 us (13%)
  local copies, waits for them, and re-layouts  29 us (12%)
  between operations  15 us (6%)
  other arithmetic  8.14 us (3%)
    ppermute x19, starting transfers between devices, shift(): lax.ppermute(data, axis, [(i, (i + step) % size) for i in range(size)])  69.4 us
    ppermute x19, waiting for transfers between devices, shift(): lax.ppermute(data, axis, [(i, (i + step) % size) for i in range(size)])  30 us
    all_gather x1, blocking collectives, per_device(): kv_all = lax.all_gather(kv, 'y', axis=0, tiled=True)  14.6 us
    all_to_all x1, blocking collectives, per_device(): received = lax.all_to_all(payload, 'tp', 0, 0, tiled=False)  14.3 us
    all_gather x1, blocking collectives, per_device(): gathered = lax.all_gather(both, 'tp', axis=1, tiled=True)  13.4 us
    dot_general x4, matrix products, per_device(): jnp.einsum('hkq,qhd->khd', score_grad, query_part, preferred_element_type...  10.4 us
    all_to_all x1, starting transfers between devices, per_device(): stats_all = lax.all_to_all(sent, ('z', 'y'), 0, 0, tiled=False)  10.3 us
    unnamed x78, local copies, waits for them, and re-layouts  7.37 us
  transfers between devices with their start and end apart: 21, of which 12 were waited for; matrix products, arithmetic and copies ran while one was open for 22% of the time, Pallas kernels for 0%

profile of v6, /device:TPU:24, one launch (start us, length us, event | category | flops | bytes accessed | tf_op | source)
XLA Modules:
  0.0 241.7 jit_solution(10379044547414494224)
XLA Ops:
  7.5 13.4 %all_gather.9 = bf16[128,2560]{0,1:T(8,128)(2,1)S(1)} all-gather(bf16[128,640]{0,1:T(8,128)(2,1)S(1)} %pad_maximum_fusion.1), channel_id=1, replica_groups=mesh['z'=16,'y'=4,'tp'=4,'dp'=2] {'tp'}, dimensions={1}, use_global_device_ids=true | all-gather | bytes 819200 | tf_op jit(solution)/shard_map/gather_features/all_gather | solution.py:77
  23.1 14.6 %all_gather.10 = bf16[512,320]{0,1:T(8,128)(2,1)} all-gather(bf16[128,320]{0,1:T(8,128)(2,1)S(1)} %pad_maximum_fusion.3), channel_id=1, replica_groups=mesh['z'=16,'y'=4,'tp'=4,'dp'=2] {'y'}, dimensions={0}, use_global_device_ids=true | all-gather | bytes 409600 | tf_op jit(solution)/shard_map/gather_sequence/all_gather | solution.py:109
  40.0 8.9 %collective-permute-start = (bf16[128,320]{0,1:T(8,128)(2,1)}, bf16[128,320]{0,1:T(8,128)(2,1)}, u32[]{:S(2)}, u32[]{:S(2)}) collective-permute-start(bf16[128,320]{0,1:T(8,128)(2,1)} %get-tuple-element.39), channel_id=1, source_target_pairs={{0,480},{32,0},{64,32},{96,64},{128,96},{160,128},{192,160},{224,1... | collective-permute-start | bytes 245768 | tf_op jit(solution)/shard_map/gather_sequence/ppermute | solution.py:32
  48.9 1.9 collective-permute-start.7
  57.5 5.1 %collective-permute-start.1 = (bf16[128,320]{0,1:T(8,128)(2,1)}, bf16[128,320]{0,1:T(8,128)(2,1)S(1)}, u32[]{:S(2)}, u32[]{:S(2)}) collective-permute-start(bf16[128,320]{0,1:T(8,128)(2,1)} %collective-permute-done), channel_id=1, source_target_pairs={{0,480},{32,0},{64,32},{96,64},{128,96},{160,128},{192,160},{224,1... | collective-permute-start | bytes 245768 | tf_op jit(solution)/shard_map/gather_sequence/ppermute | solution.py:32
  62.7 1.9 collective-permute-start.8
  66.4 5.5 %collective-permute-start.2 = (bf16[128,320]{0,1:T(8,128)(2,1)S(1)}, bf16[128,320]{0,1:T(8,128)(2,1)S(1)}, u32[]{:S(2)}, u32[]{:S(2)}) collective-permute-start(bf16[128,320]{0,1:T(8,128)(2,1)S(1)} %collective-permute-done.1), channel_id=1, source_target_pairs={{0,480},{32,0},{64,32},{96,64},{128,96},{160,128},{192,160},{224,1... | collective-permute-start | bytes 245768 | tf_op jit(solution)/shard_map/gather_sequence/ppermute | solution.py:32
  71.9 1.9 collective-permute-start.9
  75.3 5.6 %collective-permute-start.3 = (bf16[128,320]{0,1:T(8,128)(2,1)S(1)}, bf16[128,320]{0,1:T(8,128)(2,1)S(1)}, u32[]{:S(2)}, u32[]{:S(2)}) collective-permute-start(bf16[128,320]{0,1:T(8,128)(2,1)S(1)} %collective-permute-done.2), channel_id=1, source_target_pairs={{0,480},{32,0},{64,32},{96,64},{128,96},{160,128},{192,160},{224,1... | collective-permute-start | bytes 245768 | tf_op jit(solution)/shard_map/gather_sequence/ppermute | solution.py:32
  81.0 1.9 collective-permute-start.10
  82.9 1.8 collective-permute-done.3
  84.7 5.6 %collective-permute-start.4 = (bf16[128,320]{0,1:T(8,128)(2,1)S(1)}, bf16[128,320]{0,1:T(8,128)(2,1)S(1)}, u32[]{:S(2)}, u32[]{:S(2)}) collective-permute-start(bf16[128,320]{0,1:T(8,128)(2,1)S(1)} %collective-permute-done.3), channel_id=1, source_target_pairs={{0,480},{32,0},{64,32},{96,64},{128,96},{160,128},{192,160},{224,1... | collective-permute-start | bytes 245768 | tf_op jit(solution)/shard_map/gather_sequence/ppermute | solution.py:32
  90.4 1.9 collective-permute-start.11
  92.3 1.7 collective-permute-done.4
  94.0 5.6 %collective-permute-start.5 = (bf16[128,320]{0,1:T(8,128)(2,1)S(1)}, bf16[128,320]{0,1:T(8,128)(2,1)S(1)}, u32[]{:S(2)}, u32[]{:S(2)}) collective-permute-start(bf16[128,320]{0,1:T(8,128)(2,1)S(1)} %collective-permute-done.4), channel_id=1, source_target_pairs={{0,480},{32,0},{64,32},{96,64},{128,96},{160,128},{192,160},{224,1... | collective-permute-start | bytes 245768 | tf_op jit(solution)/shard_map/gather_sequence/ppermute | solution.py:32
  100.0 1.9 collective-permute-start.12
  102.0 1.8 collective-permute-done.5
  103.7 5.6 %collective-permute-start.6 = (bf16[128,320]{0,1:T(8,128)(2,1)S(1)}, bf16[128,320]{0,1:T(8,128)(2,1)S(1)}, u32[]{:S(2)}, u32[]{:S(2)}) collective-permute-start(bf16[128,320]{0,1:T(8,128)(2,1)S(1)} %collective-permute-done.5), channel_id=1, source_target_pairs={{0,480},{32,0},{64,32},{96,64},{128,96},{160,128},{192,160},{224,1... | collective-permute-start | bytes 245768 | tf_op jit(solution)/shard_map/gather_sequence/ppermute | solution.py:32
  109.4 1.9 collective-permute-start.13
  111.3 7.3 %collective-permute-done.13 = bf16[128,320]{0,1:T(8,128)(2,1)S(1)} collective-permute-done((bf16[128,320]{0,1:T(8,128)(2,1)S(1)}, bf16[128,320]{0,1:T(8,128)(2,1)S(1)}, u32[]{:S(2)}, u32[]{:S(2)}) %collective-permute-start.13) | collective-permute-done | bytes 81952 | tf_op jit(solution)/shard_map/gather_sequence/ppermute | solution.py:32
  118.6 1.9 collective-permute-start.14
  120.6 5.7 %collective-permute-done.14 = bf16[128,320]{0,1:T(8,128)(2,1)S(1)} collective-permute-done((bf16[128,320]{0,1:T(8,128)(2,1)S(1)}, bf16[128,320]{0,1:T(8,128)(2,1)S(1)}, u32[]{:S(2)}, u32[]{:S(2)}) %collective-permute-start.14) | collective-permute-done | bytes 81952 | tf_op jit(solution)/shard_map/gather_sequence/ppermute | solution.py:32
  128.5 2.3 all-gather.2.cloned.1.call-done
  130.7 2.8 %collective-permute-start.15 = (bf16[2048,320]{0,1:T(8,128)(2,1)}, bf16[2048,320]{0,1:T(8,128)(2,1)S(1)}, u32[]{:S(2)}, u32[]{:S(2)}) collective-permute-start(bf16[2048,320]{0,1:T(8,128)(2,1)} %copy-done.11), channel_id=1, source_target_pairs={{0,8},{8,16},{16,24},{24,0},{1,9},{9,17},{17,25},{25,1},{2,10},{10... | collective-permute-start | bytes 3932168 | tf_op jit(solution)/shard_map/gather_sequence/ppermute | solution.py:32
  133.5 3.3 %collective-permute-start.16 = (bf16[2048,320]{0,1:T(8,128)(2,1)}, bf16[2048,320]{0,1:T(8,128)(2,1)}, u32[]{:S(2)}, u32[]{:S(2)}) collective-permute-start(bf16[2048,320]{0,1:T(8,128)(2,1)} %copy-done.11), channel_id=1, source_target_pairs={{0,24},{8,0},{16,8},{24,16},{1,25},{9,1},{17,9},{25,17},{2,26},{10... | collective-permute-start | bytes 3932168 | tf_op jit(solution)/shard_map/gather_sequence/ppermute | solution.py:32
  136.9 3.0 %fusion.68 = (bf16[8192,160]{0,1:T(8,128)(2,1)S(1)}, bf16[8192,160]{0,1:T(8,128)(2,1)S(1)}) fusion(bf16[8192,320]{0,1:T(8,128)(2,1)} %all-gather.2.cloned.1.call-done), kind=kLoop, calls=%fused_computation.159 | loop fusion | bytes 10485760 | tf_op jit(solution)/shard_map/gather_sequence/slice | solution.py:115
  139.8 1.8 select_reduce_fusion.1
  141.7 2.5 %select_reduce_fusion = f32[2,128]{1,0:T(2,128)S(1)} fusion(f32[2,128,8192]{2,1,0:T(8,128)S(1)} %get-tuple-element.58, f32[2,128]{1,0:T(2,128)S(1)} %get-tuple-element.57, pred[128,8192]{1,0:T(8,128)(4,1)S(1)} %broadcast_compare_fusion), kind=kLoop, calls=%fused_computation.10 | loop fusion | flops 8388352 | bytes 9439232 | tf_op jit(solution)/shard_map/query_pass/reduce_sum | solution.py:138
  144.2 3.5 %fusion.74 = (f32[2,128]{1,0:T(2,128)S(1)}, bf16[2,128,8192]{2,1,0:T(8,128)(2,1)S(1)}) fusion(bf16[128,2,80]{0,2,1:T(8,128)(2,1)S(1)} %bitcast.198, bf16[8192,2,80]{0,2,1:T(8,128)(2,1)S(1)} %bitcast.184, f32[2,128,8192]{2,1,0:T(8,128)S(1)} %get-tuple-element.58, f32[2,128]{1,0:T(2,128)S(1)} %log_add_fusion, pred[128,8192]{1,0:T(8,128)(4,1)S(1)} %broadcast_compare_fusion), kind=kOutput, calls=%fused_computation.165 | convolution fusion | flops 346029824 | bytes 16295936 | tf_op jit(solution)/shard_map/query_pass/qhd,khd->hqk/dot_general | solution.py:141
  147.7 2.0 fusion.42
  149.7 1.5 fusion.35
  153.4 5.5 %collective-permute-done.15 = bf16[2048,320]{0,1:T(8,128)(2,1)S(1)} collective-permute-done((bf16[2048,320]{0,1:T(8,128)(2,1)}, bf16[2048,320]{0,1:T(8,128)(2,1)S(1)}, u32[]{:S(2)}, u32[]{:S(2)}) %collective-permute-start.15) | collective-permute-done | bytes 1310752 | tf_op jit(solution)/shard_map/gather_sequence/ppermute | solution.py:32
  158.9 3.4 %collective-permute-done.16 = bf16[2048,320]{0,1:T(8,128)(2,1)} collective-permute-done((bf16[2048,320]{0,1:T(8,128)(2,1)}, bf16[2048,320]{0,1:T(8,128)(2,1)}, u32[]{:S(2)}, u32[]{:S(2)}) %collective-permute-start.16) | collective-permute-done | bytes 1310752 | tf_op jit(solution)/shard_map/gather_sequence/ppermute | solution.py:32
  163.0 10.3 %all-to-all-start = ((f32[64,2,2,128]{3,2,1,0:T(2,128)}), f32[64,2,2,128]{3,2,1,0:T(2,128)S(1)}, u32[]{:S(2)}, u32[]{:S(2)}) async-start(f32[64,2,2,128]{3,2,1,0:T(2,128)} %broadcast_in_dim.95), calls=%async_computation | async-start | bytes 262144 | tf_op jit(solution)/shard_map/gather_row_stats/all_to_all | solution.py:164
  174.2 2.4 collective-permute-start.17
  176.6 2.0 slice.136
  178.5 3.7 %collective-permute-start.18 = (bf16[1024,320]{0,1:T(8,128)(2,1)}, bf16[1024,320]{0,1:T(8,128)(2,1)}, u32[]{:S(2)}, u32[]{:S(2)}) collective-permute-start(bf16[1024,320]{0,1:T(8,128)(2,1)} %slice.136), channel_id=1, source_target_pairs={{0,24},{8,0},{16,8},{24,16},{1,25},{9,1},{17,9},{25,17},{2,26},{10... | collective-permute-start | bytes 1966088 | tf_op jit(solution)/shard_map/gather_row_stats/ppermute | solution.py:32
  182.2 2.9 %fusion.71 = (bf16[2048,160]{0,1:T(8,128)(2,1)}, bf16[2048,160]{0,1:T(8,128)(2,1)}, bf16[2048,160]{0,1:T(8,128)(2,1)}, bf16[2048,160]{0,1:T(8,128)(2,1)}) fusion(bf16[2048,320]{0,1:T(8,128)(2,1)} %collective-permute-done.16, bf16[2048,320]{0,1:T(8,128)(2,1)S(1)} %collective-permute-done.15), kind=kLoop, calls=%fused_computation.162 | loop fusion | bytes 5242880 | tf_op jit(solution)/shard_map/key_pass/slice | solution.py:173
  185.1 2.6 %all-to-all-done = f32[64,2,2,128]{3,2,1,0:T(2,128)S(1)} async-done(((f32[64,2,2,128]{3,2,1,0:T(2,128)}), f32[64,2,2,128]{3,2,1,0:T(2,128)S(1)}, u32[]{:S(2)}, u32[]{:S(2)}) %all-to-all-start) | async-done | bytes 131104 | tf_op jit(solution)/shard_map/gather_row_stats/all_to_all | solution.py:164
  190.9 1.9 fusion.19
  197.1 3.4 %fusion.27 = f32[2,80,128]{2,1,0:T(8,128)} fusion(bf16[2048,2,80]{0,2,1:T(8,128)(2,1)} %bitcast.176, f32[2,128,2048]{2,1,0:T(8,128)} %copy-done.2, bf16[128,2,80]{0,2,1:T(8,128)(2,1)S(1)} %bitcast.187, bf16[2048,2,80]{0,2,1:T(8,128)(2,1)} %bitcast.174, f32[2,2048]{1,0:T(2,128)S(1)} %get-tuple-element.45), kind=kOutput, calls=%fused_computation.49 | convolution fusion | flops 169345024 | bytes 3547136 | tf_op jit(solution)/shard_map/key_pass/hkq,qhd->khd/dot_general | solution.py:193
  200.5 2.6 %fusion.29 = f32[2,80,128]{2,1,0:T(8,128)} fusion(f32[2,80,128]{2,1,0:T(8,128)} %fusion.27, bf16[2048,2,80]{0,2,1:T(8,128)(2,1)} %bitcast.169, f32[2,128,2048]{2,1,0:T(8,128)S(1)} %fusion.19, bf16[128,2,80]{0,2,1:T(8,128)(2,1)S(1)} %bitcast.188, bf16[2048,2,80]{0,2,1:T(8,128)(2,1)S(1)} %bitcast.167, f32[2,2048]{1,0:T(2,128)} %get-tuple-element.43), kind=kOutput, calls=%fused_computation.52 | convolution fusion | flops 169365504 | bytes 3629056 | tf_op jit(solution)/shard_map/key_pass/hkq,qhd->khd/dot_general | solution.py:193
  203.1 1.9 fusion.10
  205.0 2.5 %fusion.25 = f32[2,80,128]{2,1,0:T(8,128)} fusion(bf16[2048,2,80]{0,2,1:T(8,128)(2,1)} %bitcast.173, f32[2,128,2048]{2,1,0:T(8,128)S(1)} %fusion.10, bf16[128,2,80]{0,2,1:T(8,128)(2,1)S(1)} %bitcast.189, bf16[2048,2,80]{0,2,1:T(8,128)(2,1)S(1)} %bitcast.170, f32[2,2048]{1,0:T(2,128)S(1)} %get-tuple-element.47), kind=kOutput, calls=%fused_computation.47 | convolution fusion | flops 169345024 | bytes 3547136 | tf_op jit(solution)/shard_map/key_pass/hkq,qhd->khd/dot_general | solution.py:193
  208.6 1.6 gather_fusion.5
  214.3 2.0 fusion.47
  216.3 1.5 convolution_add_fusion.1
  219.7 14.3 %all_to_all.10 = f32[4,129,320]{2,1,0:T(8,128)S(1)} all-to-all(f32[4,129,320]{2,1,0:T(8,128)S(1)} %copy.31), channel_id=1, replica_groups=mesh['z'=16,'y'=4,'tp'=4,'dp'=2] {'tp'}, dimensions={0} | all-to-all | bytes 1320960 | tf_op jit(solution)/shard_map/back_projection/all_to_all | solution.py:215
  (164 shorter events, 36.2 us)
Async XLA Ops:
  6.5 15.9 %copy-start = (bf16[160,1280]{1,0:T(8,128)(2,1)S(1)}, bf16[160,1280]{1,0:T(8,128)(2,1)}, u32[]{:S(2)}) copy-start(bf16[160,1280]{1,0:T(8,128)(2,1)} %param.16) | copy-start | bytes 1228804
  6.5 124.2 %all-gather.2.cloned.1.call-start = ((), (), s32[]{:S(2)}) async-start(), calls=%async_computation.2 | async-start | bytes 5570560 | tf_op jit(solution)/shard_map/gather_sequence/all_gather | solution.py:110
  7.5 14.8 %copy-start.24 = (f32[1280]{0:T(1024)S(1)}, f32[1280]{0:T(1024)}, u32[]{:S(2)}) copy-start(f32[1280]{0:T(1024)} %param.13) | copy-start | bytes 15364
  21.0 1.8 copy-start.9
  21.2 16.5 %copy-start.30 = (f32[80]{0:T(128)S(1)}, f32[80]{0:T(128)}, u32[]{:S(2)}) copy-start(f32[80]{0:T(128)} %param.18) | copy-start | bytes 964
  22.3 16.8 %copy-start.10 = (bf16[160,1280]{1,0:T(8,128)(2,1)S(1)}, bf16[160,1280]{1,0:T(8,128)(2,1)}, u32[]{:S(2)}) copy-start(bf16[160,1280]{1,0:T(8,128)(2,1)} %param.14) | copy-start | bytes 1228804
  22.4 28.4 %copy-start.1 = (s32[64]{0:T(128)S(1)}, s32[64]{0:T(128)}, u32[]{:S(2)}) copy-start(s32[64]{0:T(128)} %param.19) | copy-start | bytes 772
  39.1 16.2 %copy-start.21 = (bf16[128,160]{0,1:T(8,128)(2,1)}, bf16[128,160]{0,1:T(8,128)(2,1)S(1)}, u32[]{:S(2)}) copy-start(bf16[128,160]{0,1:T(8,128)(2,1)S(1)} %convolution_convert_fusion) | copy-start | bytes 122884
  39.4 15.9 %copy-start.15 = (bf16[128,160]{0,1:T(8,128)(2,1)}, bf16[128,160]{0,1:T(8,128)(2,1)S(1)}, u32[]{:S(2)}) copy-start(bf16[128,160]{0,1:T(8,128)(2,1)S(1)} %fusion.45) | copy-start | bytes 122884
  40.0 17.5 %collective-permute-start = (bf16[128,320]{0,1:T(8,128)(2,1)}, bf16[128,320]{0,1:T(8,128)(2,1)}, u32[]{:S(2)}, u32[]{:S(2)}) collective-permute-start(bf16[128,320]{0,1:T(8,128)(2,1)} %get-tuple-element.39), channel_id=1, source_target_pairs={{0,480},{32,0},{64,32},{96,64},{128,96},{160,128},{192,160},{224,1... | collective-permute-start | bytes 245768 | tf_op jit(solution)/shard_map/gather_sequence/ppermute | solution.py:32
  48.9 13.7 %collective-permute-start.7 = (bf16[128,320]{0,1:T(8,128)(2,1)}, bf16[128,320]{0,1:T(8,128)(2,1)}, u32[]{:S(2)}, u32[]{:S(2)}) collective-permute-start(bf16[128,320]{0,1:T(8,128)(2,1)} %get-tuple-element.39), channel_id=1, source_target_pairs={{0,32},{32,64},{64,96},{96,128},{128,160},{160,192},{192,224},{224... | collective-permute-start | bytes 245768 | tf_op jit(solution)/shard_map/gather_sequence/ppermute | solution.py:32
  51.6 3.7 %copy-start.26 = (s32[1024]{0:T(1024)}, s32[1024]{0:T(1024)S(1)}, u32[]{:S(2)}) copy-start(s32[1024]{0:T(1024)S(1)} %get-tuple-element.66) | copy-start | bytes 12292
  52.3 3.0 %copy-start.27 = (s32[1024]{0:T(1024)}, s32[1024]{0:T(1024)S(1)}, u32[]{:S(2)}) copy-start(s32[1024]{0:T(1024)S(1)} %get-tuple-element.68) | copy-start | bytes 12292
  57.5 8.8 %collective-permute-start.1 = (bf16[128,320]{0,1:T(8,128)(2,1)}, bf16[128,320]{0,1:T(8,128)(2,1)S(1)}, u32[]{:S(2)}, u32[]{:S(2)}) collective-permute-start(bf16[128,320]{0,1:T(8,128)(2,1)} %collective-permute-done), channel_id=1, source_target_pairs={{0,480},{32,0},{64,32},{96,64},{128,96},{160,128},{192,160},{224,1... | collective-permute-start | bytes 245768 | tf_op jit(solution)/shard_map/gather_sequence/ppermute | solution.py:32
  62.7 9.2 %collective-permute-start.8 = (bf16[128,320]{0,1:T(8,128)(2,1)}, bf16[128,320]{0,1:T(8,128)(2,1)S(1)}, u32[]{:S(2)}, u32[]{:S(2)}) collective-permute-start(bf16[128,320]{0,1:T(8,128)(2,1)} %collective-permute-done.7), channel_id=1, source_target_pairs={{0,32},{32,64},{64,96},{96,128},{128,160},{160,192},{192,224},{224... | collective-permute-start | bytes 245768 | tf_op jit(solution)/shard_map/gather_sequence/ppermute | solution.py:32
  66.4 9.0 %collective-permute-start.2 = (bf16[128,320]{0,1:T(8,128)(2,1)S(1)}, bf16[128,320]{0,1:T(8,128)(2,1)S(1)}, u32[]{:S(2)}, u32[]{:S(2)}) collective-permute-start(bf16[128,320]{0,1:T(8,128)(2,1)S(1)} %collective-permute-done.1), channel_id=1, source_target_pairs={{0,480},{32,0},{64,32},{96,64},{128,96},{160,128},{192,160},{224,1... | collective-permute-start | bytes 245768 | tf_op jit(solution)/shard_map/gather_sequence/ppermute | solution.py:32
  71.9 9.1 %collective-permute-start.9 = (bf16[128,320]{0,1:T(8,128)(2,1)S(1)}, bf16[128,320]{0,1:T(8,128)(2,1)S(1)}, u32[]{:S(2)}, u32[]{:S(2)}) collective-permute-start(bf16[128,320]{0,1:T(8,128)(2,1)S(1)} %collective-permute-done.8), channel_id=1, source_target_pairs={{0,32},{32,64},{64,96},{96,128},{128,160},{160,192},{192,224},{224... | collective-permute-start | bytes 245768 | tf_op jit(solution)/shard_map/gather_sequence/ppermute | solution.py:32
  75.3 9.4 %collective-permute-start.3 = (bf16[128,320]{0,1:T(8,128)(2,1)S(1)}, bf16[128,320]{0,1:T(8,128)(2,1)S(1)}, u32[]{:S(2)}, u32[]{:S(2)}) collective-permute-start(bf16[128,320]{0,1:T(8,128)(2,1)S(1)} %collective-permute-done.2), channel_id=1, source_target_pairs={{0,480},{32,0},{64,32},{96,64},{128,96},{160,128},{192,160},{224,1... | collective-permute-start | bytes 245768 | tf_op jit(solution)/shard_map/gather_sequence/ppermute | solution.py:32
  81.0 9.4 %collective-permute-start.10 = (bf16[128,320]{0,1:T(8,128)(2,1)S(1)}, bf16[128,320]{0,1:T(8,128)(2,1)S(1)}, u32[]{:S(2)}, u32[]{:S(2)}) collective-permute-start(bf16[128,320]{0,1:T(8,128)(2,1)S(1)} %collective-permute-done.9), channel_id=1, source_target_pairs={{0,32},{32,64},{64,96},{96,128},{128,160},{160,192},{192,224},{224... | collective-permute-start | bytes 245768 | tf_op jit(solution)/shard_map/gather_sequence/ppermute | solution.py:32
  84.7 9.3 %collective-permute-start.4 = (bf16[128,320]{0,1:T(8,128)(2,1)S(1)}, bf16[128,320]{0,1:T(8,128)(2,1)S(1)}, u32[]{:S(2)}, u32[]{:S(2)}) collective-permute-start(bf16[128,320]{0,1:T(8,128)(2,1)S(1)} %collective-permute-done.3), channel_id=1, source_target_pairs={{0,480},{32,0},{64,32},{96,64},{128,96},{160,128},{192,160},{224,1... | collective-permute-start | bytes 245768 | tf_op jit(solution)/shard_map/gather_sequence/ppermute | solution.py:32
  90.4 9.7 %collective-permute-start.11 = (bf16[128,320]{0,1:T(8,128)(2,1)S(1)}, bf16[128,320]{0,1:T(8,128)(2,1)S(1)}, u32[]{:S(2)}, u32[]{:S(2)}) collective-permute-start(bf16[128,320]{0,1:T(8,128)(2,1)S(1)} %collective-permute-done.10), channel_id=1, source_target_pairs={{0,32},{32,64},{64,96},{96,128},{128,160},{160,192},{192,224},{224... | collective-permute-start | bytes 245768 | tf_op jit(solution)/shard_map/gather_sequence/ppermute | solution.py:32
  94.0 9.7 %collective-permute-start.5 = (bf16[128,320]{0,1:T(8,128)(2,1)S(1)}, bf16[128,320]{0,1:T(8,128)(2,1)S(1)}, u32[]{:S(2)}, u32[]{:S(2)}) collective-permute-start(bf16[128,320]{0,1:T(8,128)(2,1)S(1)} %collective-permute-done.4), channel_id=1, source_target_pairs={{0,480},{32,0},{64,32},{96,64},{128,96},{160,128},{192,160},{224,1... | collective-permute-start | bytes 245768 | tf_op jit(solution)/shard_map/gather_sequence/ppermute | solution.py:32
  100.0 9.3 %collective-permute-start.12 = (bf16[128,320]{0,1:T(8,128)(2,1)S(1)}, bf16[128,320]{0,1:T(8,128)(2,1)S(1)}, u32[]{:S(2)}, u32[]{:S(2)}) collective-permute-start(bf16[128,320]{0,1:T(8,128)(2,1)S(1)} %collective-permute-done.11), channel_id=1, source_target_pairs={{0,32},{32,64},{64,96},{96,128},{128,160},{160,192},{192,224},{224... | collective-permute-start | bytes 245768 | tf_op jit(solution)/shard_map/gather_sequence/ppermute | solution.py:32
  103.7 16.8 %collective-permute-start.6 = (bf16[128,320]{0,1:T(8,128)(2,1)S(1)}, bf16[128,320]{0,1:T(8,128)(2,1)S(1)}, u32[]{:S(2)}, u32[]{:S(2)}) collective-permute-start(bf16[128,320]{0,1:T(8,128)(2,1)S(1)} %collective-permute-done.5), channel_id=1, source_target_pairs={{0,480},{32,0},{64,32},{96,64},{128,96},{160,128},{192,160},{224,1... | collective-permute-start | bytes 245768 | tf_op jit(solution)/shard_map/gather_sequence/ppermute | solution.py:32
  109.4 9.2 %collective-permute-start.13 = (bf16[128,320]{0,1:T(8,128)(2,1)S(1)}, bf16[128,320]{0,1:T(8,128)(2,1)S(1)}, u32[]{:S(2)}, u32[]{:S(2)}) collective-permute-start(bf16[128,320]{0,1:T(8,128)(2,1)S(1)} %collective-permute-done.12), channel_id=1, source_target_pairs={{0,32},{32,64},{64,96},{96,128},{128,160},{160,192},{192,224},{224... | collective-permute-start | bytes 245768 | tf_op jit(solution)/shard_map/gather_sequence/ppermute | solution.py:32
  118.6 7.6 %collective-permute-start.14 = (bf16[128,320]{0,1:T(8,128)(2,1)S(1)}, bf16[128,320]{0,1:T(8,128)(2,1)S(1)}, u32[]{:S(2)}, u32[]{:S(2)}) collective-permute-start(bf16[128,320]{0,1:T(8,128)(2,1)S(1)} %collective-permute-done.13), channel_id=1, source_target_pairs={{0,32},{32,64},{64,96},{96,128},{128,160},{160,192},{192,224},{224... | collective-permute-start | bytes 245768 | tf_op jit(solution)/shard_map/gather_sequence/ppermute | solution.py:32
  130.7 9.1 %copy-start.16 = (bf16[128,160]{0,1:T(8,128)(2,1)S(1)}, bf16[128,160]{0,1:T(8,128)(2,1)}, u32[]{:S(2)}) copy-start(bf16[128,160]{0,1:T(8,128)(2,1)} %copy-done.15) | copy-start | bytes 122884
  130.7 28.1 %collective-permute-start.15 = (bf16[2048,320]{0,1:T(8,128)(2,1)}, bf16[2048,320]{0,1:T(8,128)(2,1)S(1)}, u32[]{:S(2)}, u32[]{:S(2)}) collective-permute-start(bf16[2048,320]{0,1:T(8,128)(2,1)} %copy-done.11), channel_id=1, source_target_pairs={{0,8},{8,16},{16,24},{24,0},{1,9},{9,17},{17,25},{25,1},{2,10},{10... | collective-permute-start | bytes 3932168 | tf_op jit(solution)/shard_map/gather_sequence/ppermute | solution.py:32
  133.5 28.7 %collective-permute-start.16 = (bf16[2048,320]{0,1:T(8,128)(2,1)}, bf16[2048,320]{0,1:T(8,128)(2,1)}, u32[]{:S(2)}, u32[]{:S(2)}) collective-permute-start(bf16[2048,320]{0,1:T(8,128)(2,1)} %copy-done.11), channel_id=1, source_target_pairs={{0,24},{8,0},{16,8},{24,16},{1,25},{9,1},{17,9},{25,17},{2,26},{10... | collective-permute-start | bytes 3932168 | tf_op jit(solution)/shard_map/gather_sequence/ppermute | solution.py:32
  141.7 2.5 %copy-start.22 = (bf16[128,160]{0,1:T(8,128)(2,1)S(1)}, bf16[128,160]{0,1:T(8,128)(2,1)}, u32[]{:S(2)}) copy-start(bf16[128,160]{0,1:T(8,128)(2,1)} %copy-done.21) | copy-start | bytes 122884
  149.6 2.8 %copy-start.12 = (bf16[2048,320]{0,1:T(8,128)(2,1)S(1)}, bf16[2048,320]{0,1:T(8,128)(2,1)}, u32[]{:S(2)}) copy-start(bf16[2048,320]{0,1:T(8,128)(2,1)} %copy-done.11) | copy-start | bytes 3932164
  163.0 24.8 %all-to-all-start = ((f32[64,2,2,128]{3,2,1,0:T(2,128)}), f32[64,2,2,128]{3,2,1,0:T(2,128)S(1)}, u32[]{:S(2)}, u32[]{:S(2)}) async-start(f32[64,2,2,128]{3,2,1,0:T(2,128)} %broadcast_in_dim.95), calls=%async_computation | async-start | bytes 262144 | tf_op jit(solution)/shard_map/gather_row_stats/all_to_all | solution.py:164
  174.2 36.1 %collective-permute-start.17 = (bf16[1024,320]{0,1:T(8,128)(2,1)}, bf16[1024,320]{0,1:T(8,128)(2,1)}, u32[]{:S(2)}, u32[]{:S(2)}) collective-permute-start(bf16[1024,320]{0,1:T(8,128)(2,1)} %slice.135), channel_id=1, source_target_pairs={{0,8},{8,16},{16,24},{24,0},{1,9},{9,17},{17,25},{25,1},{2,10},{10... | collective-permute-start | bytes 1966088 | tf_op jit(solution)/shard_map/gather_row_stats/ppermute | solution.py:32
  178.5 32.9 %collective-permute-start.18 = (bf16[1024,320]{0,1:T(8,128)(2,1)}, bf16[1024,320]{0,1:T(8,128)(2,1)}, u32[]{:S(2)}, u32[]{:S(2)}) collective-permute-start(bf16[1024,320]{0,1:T(8,128)(2,1)} %slice.136), channel_id=1, source_target_pairs={{0,24},{8,0},{16,8},{24,16},{1,25},{9,1},{17,9},{25,17},{2,26},{10... | collective-permute-start | bytes 1966088 | tf_op jit(solution)/shard_map/gather_row_stats/ppermute | solution.py:32
  187.7 3.2 %copy-start.14 = (f32[64,2,2,128]{3,2,1,0:T(2,128)}, f32[64,2,2,128]{3,2,1,0:T(2,128)S(1)}, u32[]{:S(2)}) copy-start(f32[64,2,2,128]{3,2,1,0:T(2,128)S(1)} %all-to-all-done) | copy-start | bytes 393220
  192.7 1.1 copy-start.5
  192.8 1.1 copy-start.13
  192.8 1.1 copy-start.23
  193.3 2.7 %copy-start.4 = (bf16[2048,160]{0,1:T(8,128)(2,1)S(1)}, bf16[2048,160]{0,1:T(8,128)(2,1)}, u32[]{:S(2)}) copy-start(bf16[2048,160]{0,1:T(8,128)(2,1)} %get-tuple-element.33) | copy-start | bytes 1966084
  194.6 1.4 copy-start.2
  203.1 1.9 copy-start.3
  214.3 3.6 %copy-start.17 = (f32[2,80,128]{2,1,0:T(8,128)S(1)}, f32[2,80,128]{2,1,0:T(8,128)}, u32[]{:S(2)}) copy-start(f32[2,80,128]{2,1,0:T(8,128)} %convolution_add_fusion.3) | copy-start | bytes 245764
  214.3 3.6 %copy-start.18 = (f32[2,80,128]{2,1,0:T(8,128)S(1)}, f32[2,80,128]{2,1,0:T(8,128)}, u32[]{:S(2)}) copy-start(f32[2,80,128]{2,1,0:T(8,128)} %fusion.48) | copy-start | bytes 245764
  216.3 2.1 copy-start.8
  216.3 2.1 copy-start.25
  219.6 14.5 %copy-start.19 = (bf16[128,320]{0,1:T(8,128)(2,1)S(1)}, bf16[128,320]{0,1:T(8,128)(2,1)}, u32[]{:S(2)}) copy-start(bf16[128,320]{0,1:T(8,128)(2,1)} %param.11) | copy-start | bytes 245764
  219.7 14.5 %copy-start.20 = (bf16[128,320]{0,1:T(8,128)(2,1)S(1)}, bf16[128,320]{0,1:T(8,128)(2,1)}, u32[]{:S(2)}) copy-start(bf16[128,320]{0,1:T(8,128)(2,1)} %param.12) | copy-start | bytes 245764
  219.7 14.5 %copy-start.29 = (f32[128]{0:T(128)S(1)}, f32[128]{0:T(128)}, u32[]{:S(2)}) copy-start(f32[128]{0:T(128)} %copy-done.28) | copy-start | bytes 1540
  (4 other events, 3.3 us)
Sparse Core Ops, SparseCore 0:
  37.8 92.8 all-gather.1

commit v7 on v6

--- a/solution.py
+++ b/solution.py
@@ -109,7 +109,6 @@
         kv_all = lax.all_gather(kv, "y", axis=0, tiled=True)
         kv_all = lax.all_gather(kv_all, "z", axis=0, tiled=True)
         qg_z = jnp.concatenate(ring_gather(qg, "z", z_size), axis=0)
-        qg_z, kv_all = lax.optimization_barrier((qg_z, kv_all))
         qg_ahead, qg_behind = ring4_first(qg_z, "y")
         key_all = kv_all[:, :cols].reshape(all_rows, heads_here, head_width)
         value_all = kv_all[:, cols:].reshape(all_rows, heads_here, head_width)

time: 244 us -> 242 us (level)
  waiting for transfers between devices: 34.9 us -> 26.5 us
  local copies, waits for them, and re-layouts: 29 us -> 36.3 us
  matrix products: 32.8 us -> 36.1 us
  starting transfers between devices: 79.7 us -> 77.2 us
    ppermute x19, waiting for transfers between devices: 30 us -> 23.9 us  [shift(): lax.ppermute(data, axis, [(i, (i + step) % size) for i in range(size)])]
    unnamed x78 -> x90, local copies, waits for them, and re-layouts: 7.37 us -> 12.9 us
  transfers between devices with their start and end apart: 21 -> 21, of which waited for: 12 -> 13; matrix products, arithmetic and copies ran while one was open for 22% -> 26% of each run, Pallas kernels for 0% -> 0%
where the time goes in v7:
time: 242 us; the launch traced here: 240 us
  starting transfers between devices  77.2 us (32%)
  blocking collectives  40.2 us (17%)
  local copies, waits for them, and re-layouts  36.3 us (15%)
  matrix products  36.1 us (15%)
  waiting for transfers between devices  26.5 us (11%)
  between operations  15 us (6%)
  other arithmetic  8.26 us (3%)
    ppermute x19, starting transfers between devices, shift(): lax.ppermute(data, axis, [(i, (i + step) % size) for i in range(size)])  68.4 us
    ppermute x19, waiting for transfers between devices, shift(): lax.ppermute(data, axis, [(i, (i + step) % size) for i in range(size)])  23.9 us
    all_gather x1, blocking collectives, per_device(): kv_all = lax.all_gather(kv, 'y', axis=0, tiled=True)  14.6 us
    all_gather x1, blocking collectives, per_device(): gathered = lax.all_gather(both, 'tp', axis=1, tiled=True)  13.4 us
    unnamed x90, local copies, waits for them, and re-layouts  12.9 us
    all_to_all x1, blocking collectives, per_device(): received = lax.all_to_all(payload, 'tp', 0, 0, tiled=False)  12.3 us
    dot_general x4, matrix products, per_device(): jnp.einsum('hkq,qhd->khd', score_grad, query_part, preferred_element_type...  12.2 us
    all_to_all x1, starting transfers between devices, per_device(): stats_all = lax.all_to_all(sent, ('z', 'y'), 0, 0, tiled=False)  8.8 us
  transfers between devices with their start and end apart: 21, of which 13 were waited for; matrix products, arithmetic and copies ran while one was open for 26% of the time, Pallas kernels for 0%

profile of v7, /device:TPU:24, one launch (start us, length us, event | category | flops | bytes accessed | tf_op | source)
XLA Modules:
  0.0 239.6 jit_solution(12565881831422655984)
XLA Ops:
  7.5 13.4 %all_gather.9 = bf16[128,2560]{0,1:T(8,128)(2,1)S(1)} all-gather(bf16[128,640]{0,1:T(8,128)(2,1)S(1)} %pad_maximum_fusion.1), channel_id=1, replica_groups=mesh['z'=16,'y'=4,'tp'=4,'dp'=2] {'tp'}, dimensions={1}, use_global_device_ids=true | all-gather | bytes 819200 | tf_op jit(solution)/shard_map/gather_features/all_gather | solution.py:77
  23.1 14.6 %all_gather.10 = bf16[512,320]{0,1:T(8,128)(2,1)} all-gather(bf16[128,320]{0,1:T(8,128)(2,1)S(1)} %pad_maximum_fusion.2), channel_id=1, replica_groups=mesh['z'=16,'y'=4,'tp'=4,'dp'=2] {'y'}, dimensions={0}, use_global_device_ids=true | all-gather | bytes 409600 | tf_op jit(solution)/shard_map/gather_sequence/all_gather | solution.py:109
  39.1 8.9 %collective-permute-start = (bf16[128,320]{0,1:T(8,128)(2,1)S(1)}, bf16[128,320]{0,1:T(8,128)(2,1)S(1)}, u32[]{:S(2)}, u32[]{:S(2)}) collective-permute-start(bf16[128,320]{0,1:T(8,128)(2,1)S(1)} %get-tuple-element.35), channel_id=1, source_target_pairs={{0,480},{32,0},{64,32},{96,64},{128,96},{160,128},{192,160},{224,1... | collective-permute-start | bytes 245768 | tf_op jit(solution)/shard_map/gather_sequence/ppermute | solution.py:32
  48.0 1.9 collective-permute-start.7
  55.1 1.6 broadcast_compare_fusion.4
  56.7 5.1 %collective-permute-start.1 = (bf16[128,320]{0,1:T(8,128)(2,1)S(1)}, bf16[128,320]{0,1:T(8,128)(2,1)S(1)}, u32[]{:S(2)}, u32[]{:S(2)}) collective-permute-start(bf16[128,320]{0,1:T(8,128)(2,1)S(1)} %collective-permute-done), channel_id=1, source_target_pairs={{0,480},{32,0},{64,32},{96,64},{128,96},{160,128},{192,160},{224,1... | collective-permute-start | bytes 245768 | tf_op jit(solution)/shard_map/gather_sequence/ppermute | solution.py:32
  61.8 1.9 collective-permute-start.8
  64.8 5.6 %collective-permute-start.2 = (bf16[128,320]{0,1:T(8,128)(2,1)S(1)}, bf16[128,320]{0,1:T(8,128)(2,1)S(1)}, u32[]{:S(2)}, u32[]{:S(2)}) collective-permute-start(bf16[128,320]{0,1:T(8,128)(2,1)S(1)} %collective-permute-done.1), channel_id=1, source_target_pairs={{0,480},{32,0},{64,32},{96,64},{128,96},{160,128},{192,160},{224,1... | collective-permute-start | bytes 245768 | tf_op jit(solution)/shard_map/gather_sequence/ppermute | solution.py:32
  70.8 1.9 collective-permute-start.9
  73.8 5.6 %collective-permute-start.3 = (bf16[128,320]{0,1:T(8,128)(2,1)S(1)}, bf16[128,320]{0,1:T(8,128)(2,1)S(1)}, u32[]{:S(2)}, u32[]{:S(2)}) collective-permute-start(bf16[128,320]{0,1:T(8,128)(2,1)S(1)} %collective-permute-done.2), channel_id=1, source_target_pairs={{0,480},{32,0},{64,32},{96,64},{128,96},{160,128},{192,160},{224,1... | collective-permute-start | bytes 245768 | tf_op jit(solution)/shard_map/gather_sequence/ppermute | solution.py:32
  79.9 1.9 collective-permute-start.10
  82.9 5.6 %collective-permute-start.4 = (bf16[128,320]{0,1:T(8,128)(2,1)S(1)}, bf16[128,320]{0,1:T(8,128)(2,1)S(1)}, u32[]{:S(2)}, u32[]{:S(2)}) collective-permute-start(bf16[128,320]{0,1:T(8,128)(2,1)S(1)} %collective-permute-done.3), channel_id=1, source_target_pairs={{0,480},{32,0},{64,32},{96,64},{128,96},{160,128},{192,160},{224,1... | collective-permute-start | bytes 245768 | tf_op jit(solution)/shard_map/gather_sequence/ppermute | solution.py:32
  89.2 1.9 collective-permute-start.11
  91.8 5.1 %collective-permute-start.5 = (bf16[128,320]{0,1:T(8,128)(2,1)S(1)}, bf16[128,320]{0,1:T(8,128)(2,1)S(1)}, u32[]{:S(2)}, u32[]{:S(2)}) collective-permute-start(bf16[128,320]{0,1:T(8,128)(2,1)S(1)} %collective-permute-done.4), channel_id=1, source_target_pairs={{0,480},{32,0},{64,32},{96,64},{128,96},{160,128},{192,160},{224,1... | collective-permute-start | bytes 245768 | tf_op jit(solution)/shard_map/gather_sequence/ppermute | solution.py:32
  96.9 1.8 collective-permute-done.11
  98.8 1.9 collective-permute-start.12
  101.3 5.1 %collective-permute-start.6 = (bf16[128,320]{0,1:T(8,128)(2,1)S(1)}, bf16[128,320]{0,1:T(8,128)(2,1)S(1)}, u32[]{:S(2)}, u32[]{:S(2)}) collective-permute-start(bf16[128,320]{0,1:T(8,128)(2,1)S(1)} %collective-permute-done.5), channel_id=1, source_target_pairs={{0,480},{32,0},{64,32},{96,64},{128,96},{160,128},{192,160},{224,1... | collective-permute-start | bytes 245768 | tf_op jit(solution)/shard_map/gather_sequence/ppermute | solution.py:32
  106.5 1.7 collective-permute-done.12
  108.1 1.9 collective-permute-start.13
  110.7 6.7 %collective-permute-done.13 = bf16[128,320]{0,1:T(8,128)(2,1)S(1)} collective-permute-done((bf16[128,320]{0,1:T(8,128)(2,1)S(1)}, bf16[128,320]{0,1:T(8,128)(2,1)S(1)}, u32[]{:S(2)}, u32[]{:S(2)}) %collective-permute-start.13) | collective-permute-done | bytes 81952 | tf_op jit(solution)/shard_map/gather_sequence/ppermute | solution.py:32
  117.4 1.9 collective-permute-start.14
  120.0 6.2 %collective-permute-done.14 = bf16[128,320]{0,1:T(8,128)(2,1)S(1)} collective-permute-done((bf16[128,320]{0,1:T(8,128)(2,1)S(1)}, bf16[128,320]{0,1:T(8,128)(2,1)S(1)}, u32[]{:S(2)}, u32[]{:S(2)}) %collective-permute-start.14) | collective-permute-done | bytes 81952 | tf_op jit(solution)/shard_map/gather_sequence/ppermute | solution.py:32
  131.5 4.0 %collective-permute-start.15 = (bf16[2048,320]{0,1:T(8,128)(2,1)}, bf16[2048,320]{0,1:T(8,128)(2,1)S(1)}, u32[]{:S(2)}, u32[]{:S(2)}) collective-permute-start(bf16[2048,320]{0,1:T(8,128)(2,1)} %constant_dynamic-update-slice_fusion), channel_id=1, source_target_pairs={{0,8},{8,16},{16,24},{24,0},{1,9},{9,17},{17,25},{25,1},{2,10},{10... | collective-permute-start | bytes 3932168 | tf_op jit(solution)/shard_map/gather_sequence/ppermute | solution.py:32
  135.5 2.1 collective-permute-start.16
  137.6 2.3 fusion.71
  139.8 3.0 %fusion.70 = (bf16[8192,160]{0,1:T(8,128)(2,1)S(1)}, bf16[8192,160]{0,1:T(8,128)(2,1)S(1)}) fusion(bf16[8192,320]{0,1:T(8,128)(2,1)} %all-gather.2.cloned.1.call-done), kind=kLoop, calls=%fused_computation.160 | loop fusion | bytes 10485760 | tf_op jit(solution)/shard_map/gather_sequence/slice | solution.py:114
  142.8 1.8 select_reduce_fusion.1
  144.6 2.5 %select_reduce_fusion = f32[2,128]{1,0:T(2,128)S(1)} fusion(f32[2,128,8192]{2,1,0:T(8,128)S(1)} %get-tuple-element.54, f32[2,128]{1,0:T(2,128)S(1)} %get-tuple-element.53, pred[128,8192]{1,0:T(8,128)(4,1)S(1)} %broadcast_compare_fusion), kind=kLoop, calls=%fused_computation.10 | loop fusion | flops 8388352 | bytes 9439232 | tf_op jit(solution)/shard_map/query_pass/reduce_sum | solution.py:137
  147.1 3.5 %fusion.76 = (f32[2,128]{1,0:T(2,128)S(1)}, bf16[2,128,8192]{2,1,0:T(8,128)(2,1)S(1)}) fusion(bf16[128,2,80]{0,2,1:T(8,128)(2,1)S(1)} %bitcast.198, bf16[8192,2,80]{0,2,1:T(8,128)(2,1)S(1)} %bitcast.184, f32[2,128,8192]{2,1,0:T(8,128)S(1)} %get-tuple-element.54, f32[2,128]{1,0:T(2,128)S(1)} %log_add_fusion, pred[128,8192]{1,0:T(8,128)(4,1)S(1)} %broadcast_compare_fusion), kind=kOutput, calls=%fused_computation.166 | convolution fusion | flops 346029824 | bytes 16295936 | tf_op jit(solution)/shard_map/query_pass/qhd,khd->hqk/dot_general | solution.py:140
  150.6 2.0 fusion.43
  152.6 1.5 fusion.35
  155.5 4.4 %collective-permute-done.16 = bf16[2048,320]{0,1:T(8,128)(2,1)} collective-permute-done((bf16[2048,320]{0,1:T(8,128)(2,1)}, bf16[2048,320]{0,1:T(8,128)(2,1)}, u32[]{:S(2)}, u32[]{:S(2)}) %collective-permute-start.16) | collective-permute-done | bytes 1310752 | tf_op jit(solution)/shard_map/gather_sequence/ppermute | solution.py:32
  160.6 8.8 %all-to-all-start = ((f32[64,2,2,128]{3,2,1,0:T(2,128)}), f32[64,2,2,128]{3,2,1,0:T(2,128)S(1)}, u32[]{:S(2)}, u32[]{:S(2)}) async-start(f32[64,2,2,128]{3,2,1,0:T(2,128)} %broadcast_in_dim.95), calls=%async_computation | async-start | bytes 262144 | tf_op jit(solution)/shard_map/gather_row_stats/all_to_all | solution.py:163
  170.3 2.4 collective-permute-start.17
  172.7 2.0 slice.136
  174.7 3.7 %collective-permute-start.18 = (bf16[1024,320]{0,1:T(8,128)(2,1)}, bf16[1024,320]{0,1:T(8,128)(2,1)}, u32[]{:S(2)}, u32[]{:S(2)}) collective-permute-start(bf16[1024,320]{0,1:T(8,128)(2,1)} %slice.136), channel_id=1, source_target_pairs={{0,24},{8,0},{16,8},{24,16},{1,25},{9,1},{17,9},{25,17},{2,26},{10... | collective-permute-start | bytes 1966088 | tf_op jit(solution)/shard_map/gather_row_stats/ppermute | solution.py:32
  178.4 2.8 %fusion.72 = (bf16[2048,160]{0,1:T(8,128)(2,1)}, bf16[2048,160]{0,1:T(8,128)(2,1)}, bf16[2048,160]{0,1:T(8,128)(2,1)}, bf16[2048,160]{0,1:T(8,128)(2,1)}) fusion(bf16[2048,320]{0,1:T(8,128)(2,1)} %collective-permute-done.16, bf16[2048,320]{0,1:T(8,128)(2,1)S(1)} %collective-permute-done.15), kind=kLoop, calls=%fused_computation.162 | loop fusion | bytes 5242880 | tf_op jit(solution)/shard_map/key_pass/slice | solution.py:172
  181.2 2.6 %all-to-all-done = f32[64,2,2,128]{3,2,1,0:T(2,128)S(1)} async-done(((f32[64,2,2,128]{3,2,1,0:T(2,128)}), f32[64,2,2,128]{3,2,1,0:T(2,128)S(1)}, u32[]{:S(2)}, u32[]{:S(2)}) %all-to-all-start) | async-done | bytes 131104 | tf_op jit(solution)/shard_map/gather_row_stats/all_to_all | solution.py:163
  187.1 1.9 fusion.10
  190.1 2.7 %fusion.25 = f32[2,80,128]{2,1,0:T(8,128)} fusion(bf16[2048,2,80]{0,2,1:T(8,128)(2,1)} %bitcast.175, f32[2,128,2048]{2,1,0:T(8,128)S(1)} %fusion.10, bf16[128,2,80]{0,2,1:T(8,128)(2,1)S(1)} %bitcast.187, bf16[2048,2,80]{0,2,1:T(8,128)(2,1)} %bitcast.176, f32[2,2048]{1,0:T(2,128)S(1)} %get-tuple-element.43), kind=kOutput, calls=%fused_computation.47 | convolution fusion | flops 169345024 | bytes 3547136 | tf_op jit(solution)/shard_map/key_pass/hkq,qhd->khd/dot_general | solution.py:192
  192.8 1.8 fusion.16
  194.6 3.4 %fusion.27 = f32[2,80,128]{2,1,0:T(8,128)} fusion(bf16[2048,2,80]{0,2,1:T(8,128)(2,1)} %bitcast.173, f32[2,128,2048]{2,1,0:T(8,128)S(1)} %fusion.16, bf16[128,2,80]{0,2,1:T(8,128)(2,1)S(1)} %bitcast.188, bf16[2048,2,80]{0,2,1:T(8,128)(2,1)} %bitcast.170, f32[2,2048]{1,0:T(2,128)S(1)} %get-tuple-element.39), kind=kOutput, calls=%fused_computation.49 | convolution fusion | flops 169345024 | bytes 3547136 | tf_op jit(solution)/shard_map/key_pass/hkq,qhd->khd/dot_general | solution.py:192
  198.1 1.9 fusion.19
  201.2 1.6 gather_fusion.5
  209.2 3.4 %fusion.26 = f32[2,80,128]{2,1,0:T(8,128)} fusion(bf16[2048,2,80]{0,2,1:T(8,128)(2,1)} %bitcast.181, f32[2,128,2048]{2,1,0:T(8,128)} %copy-done.4, bf16[128,2,80]{0,2,1:T(8,128)(2,1)S(1)} %bitcast.189, bf16[2048,2,80]{0,2,1:T(8,128)(2,1)} %bitcast.179, f32[2,2048]{1,0:T(2,128)S(1)} %copy-done.28), kind=kOutput, calls=%fused_computation.48 | convolution fusion | flops 169345024 | bytes 3547136 | tf_op jit(solution)/shard_map/key_pass/hkq,qhd->khd/dot_general | solution.py:192
  212.7 2.6 %fusion.48 = bf16[2,80,128]{2,1,0:T(8,128)(2,1)} fusion(f32[2,80,128]{2,1,0:T(8,128)S(1)} %copy-done.20, f32[2,80,128]{2,1,0:T(8,128)} %fusion.26, f32[2,80,128]{2,1,0:T(8,128)S(1)} %copy-done.22, bf16[2048,2,80]{0,2,1:T(8,128)(2,1)} %bitcast.169, f32[2,128,2048]{2,1,0:T(8,128)S(1)} %fusion.19, bf16[128,2,80]{0,2,1:T(8,128)(2,1)S(1)} %bitcast.190, ...), kind=kOutput, calls=%fused_computation.65 | convolution fusion | flops 169426944 | bytes 3751936 | tf_op jit(solution)/shard_map/key_pass/hkq,qhd->khd/dot_general | solution.py:192
  215.2 1.6 convolution_add_fusion.1
  219.5 12.3 %all_to_all.10 = f32[4,129,320]{2,1,0:T(8,128)S(1)} all-to-all(f32[4,129,320]{2,1,0:T(8,128)S(1)} %copy.31), channel_id=1, replica_groups=mesh['z'=16,'y'=4,'tp'=4,'dp'=2] {'tp'}, dimensions={0} | all-to-all | bytes 1320960 | tf_op jit(solution)/shard_map/back_projection/all_to_all | solution.py:214
  (176 shorter events, 39.9 us)
Async XLA Ops:
  6.5 16.0 %copy-start = (bf16[160,1280]{1,0:T(8,128)(2,1)S(1)}, bf16[160,1280]{1,0:T(8,128)(2,1)}, u32[]{:S(2)}) copy-start(bf16[160,1280]{1,0:T(8,128)(2,1)} %param.16) | copy-start | bytes 1228804
  6.5 133.3 %all-gather.2.cloned.1.call-start = ((), (), s32[]{:S(2)}) async-start(), calls=%async_computation.2 | async-start | bytes 5570560 | tf_op jit(solution)/shard_map/gather_sequence/all_gather | solution.py:110
  7.5 14.9 %copy-start.29 = (f32[1280]{0:T(1024)S(1)}, f32[1280]{0:T(1024)}, u32[]{:S(2)}) copy-start(f32[1280]{0:T(1024)} %param.13) | copy-start | bytes 15364
  21.2 16.5 %copy-start.36 = (f32[80]{0:T(128)S(1)}, f32[80]{0:T(128)}, u32[]{:S(2)}) copy-start(f32[80]{0:T(128)} %param.18) | copy-start | bytes 964
  21.2 16.6 %copy-start.18 = (bf16[160,1280]{1,0:T(8,128)(2,1)S(1)}, bf16[160,1280]{1,0:T(8,128)(2,1)}, u32[]{:S(2)}) copy-start(bf16[160,1280]{1,0:T(8,128)(2,1)} %param.17) | copy-start | bytes 1228804
  22.4 15.7 %copy-start.34 = (f32[128]{0:T(128)}, f32[128]{0:T(128)S(1)}, u32[]{:S(2)}) copy-start(f32[128]{0:T(128)S(1)} %add_rsqrt_fusion) | copy-start | bytes 1540
  22.4 15.7 %copy-start.12 = (bf16[160,1280]{1,0:T(8,128)(2,1)S(1)}, bf16[160,1280]{1,0:T(8,128)(2,1)}, u32[]{:S(2)}) copy-start(bf16[160,1280]{1,0:T(8,128)(2,1)} %param.14) | copy-start | bytes 1228804
  22.5 27.4 %copy-start.1 = (s32[64]{0:T(128)S(1)}, s32[64]{0:T(128)}, u32[]{:S(2)}) copy-start(s32[64]{0:T(128)} %param.19) | copy-start | bytes 772
  38.1 16.9 %copy-start.25 = (bf16[128,160]{0,1:T(8,128)(2,1)}, bf16[128,160]{0,1:T(8,128)(2,1)S(1)}, u32[]{:S(2)}) copy-start(bf16[128,160]{0,1:T(8,128)(2,1)S(1)} %convolution_convert_fusion) | copy-start | bytes 122884
  39.1 17.6 %collective-permute-start = (bf16[128,320]{0,1:T(8,128)(2,1)S(1)}, bf16[128,320]{0,1:T(8,128)(2,1)S(1)}, u32[]{:S(2)}, u32[]{:S(2)}) collective-permute-start(bf16[128,320]{0,1:T(8,128)(2,1)S(1)} %get-tuple-element.35), channel_id=1, source_target_pairs={{0,480},{32,0},{64,32},{96,64},{128,96},{160,128},{192,160},{224,1... | collective-permute-start | bytes 245768 | tf_op jit(solution)/shard_map/gather_sequence/ppermute | solution.py:32
  48.0 13.9 %collective-permute-start.7 = (bf16[128,320]{0,1:T(8,128)(2,1)S(1)}, bf16[128,320]{0,1:T(8,128)(2,1)S(1)}, u32[]{:S(2)}, u32[]{:S(2)}) collective-permute-start(bf16[128,320]{0,1:T(8,128)(2,1)S(1)} %get-tuple-element.35), channel_id=1, source_target_pairs={{0,32},{32,64},{64,96},{96,128},{128,160},{160,192},{192,224},{224... | collective-permute-start | bytes 245768 | tf_op jit(solution)/shard_map/gather_sequence/ppermute | solution.py:32
  50.6 3.6 %copy-start.33 = (s32[1024]{0:T(1024)}, s32[1024]{0:T(1024)S(1)}, u32[]{:S(2)}) copy-start(s32[1024]{0:T(1024)S(1)} %get-tuple-element.63) | copy-start | bytes 12292
  56.7 8.1 %collective-permute-start.1 = (bf16[128,320]{0,1:T(8,128)(2,1)S(1)}, bf16[128,320]{0,1:T(8,128)(2,1)S(1)}, u32[]{:S(2)}, u32[]{:S(2)}) collective-permute-start(bf16[128,320]{0,1:T(8,128)(2,1)S(1)} %collective-permute-done), channel_id=1, source_target_pairs={{0,480},{32,0},{64,32},{96,64},{128,96},{160,128},{192,160},{224,1... | collective-permute-start | bytes 245768 | tf_op jit(solution)/shard_map/gather_sequence/ppermute | solution.py:32
  61.8 9.0 %collective-permute-start.8 = (bf16[128,320]{0,1:T(8,128)(2,1)S(1)}, bf16[128,320]{0,1:T(8,128)(2,1)S(1)}, u32[]{:S(2)}, u32[]{:S(2)}) collective-permute-start(bf16[128,320]{0,1:T(8,128)(2,1)S(1)} %collective-permute-done.7), channel_id=1, source_target_pairs={{0,32},{32,64},{64,96},{96,128},{128,160},{160,192},{192,224},{224... | collective-permute-start | bytes 245768 | tf_op jit(solution)/shard_map/gather_sequence/ppermute | solution.py:32
  64.8 9.1 %collective-permute-start.2 = (bf16[128,320]{0,1:T(8,128)(2,1)S(1)}, bf16[128,320]{0,1:T(8,128)(2,1)S(1)}, u32[]{:S(2)}, u32[]{:S(2)}) collective-permute-start(bf16[128,320]{0,1:T(8,128)(2,1)S(1)} %collective-permute-done.1), channel_id=1, source_target_pairs={{0,480},{32,0},{64,32},{96,64},{128,96},{160,128},{192,160},{224,1... | collective-permute-start | bytes 245768 | tf_op jit(solution)/shard_map/gather_sequence/ppermute | solution.py:32
  70.8 9.1 %collective-permute-start.9 = (bf16[128,320]{0,1:T(8,128)(2,1)S(1)}, bf16[128,320]{0,1:T(8,128)(2,1)S(1)}, u32[]{:S(2)}, u32[]{:S(2)}) collective-permute-start(bf16[128,320]{0,1:T(8,128)(2,1)S(1)} %collective-permute-done.8), channel_id=1, source_target_pairs={{0,32},{32,64},{64,96},{96,128},{128,160},{160,192},{192,224},{224... | collective-permute-start | bytes 245768 | tf_op jit(solution)/shard_map/gather_sequence/ppermute | solution.py:32
  73.8 9.0 %collective-permute-start.3 = (bf16[128,320]{0,1:T(8,128)(2,1)S(1)}, bf16[128,320]{0,1:T(8,128)(2,1)S(1)}, u32[]{:S(2)}, u32[]{:S(2)}) collective-permute-start(bf16[128,320]{0,1:T(8,128)(2,1)S(1)} %collective-permute-done.2), channel_id=1, source_target_pairs={{0,480},{32,0},{64,32},{96,64},{128,96},{160,128},{192,160},{224,1... | collective-permute-start | bytes 245768 | tf_op jit(solution)/shard_map/gather_sequence/ppermute | solution.py:32
  79.9 9.3 %collective-permute-start.10 = (bf16[128,320]{0,1:T(8,128)(2,1)S(1)}, bf16[128,320]{0,1:T(8,128)(2,1)S(1)}, u32[]{:S(2)}, u32[]{:S(2)}) collective-permute-start(bf16[128,320]{0,1:T(8,128)(2,1)S(1)} %collective-permute-done.9), channel_id=1, source_target_pairs={{0,32},{32,64},{64,96},{96,128},{128,160},{160,192},{192,224},{224... | collective-permute-start | bytes 245768 | tf_op jit(solution)/shard_map/gather_sequence/ppermute | solution.py:32
  82.9 8.9 %collective-permute-start.4 = (bf16[128,320]{0,1:T(8,128)(2,1)S(1)}, bf16[128,320]{0,1:T(8,128)(2,1)S(1)}, u32[]{:S(2)}, u32[]{:S(2)}) collective-permute-start(bf16[128,320]{0,1:T(8,128)(2,1)S(1)} %collective-permute-done.3), channel_id=1, source_target_pairs={{0,480},{32,0},{64,32},{96,64},{128,96},{160,128},{192,160},{224,1... | collective-permute-start | bytes 245768 | tf_op jit(solution)/shard_map/gather_sequence/ppermute | solution.py:32
  89.2 9.6 %collective-permute-start.11 = (bf16[128,320]{0,1:T(8,128)(2,1)S(1)}, bf16[128,320]{0,1:T(8,128)(2,1)S(1)}, u32[]{:S(2)}, u32[]{:S(2)}) collective-permute-start(bf16[128,320]{0,1:T(8,128)(2,1)S(1)} %collective-permute-done.10), channel_id=1, source_target_pairs={{0,32},{32,64},{64,96},{96,128},{128,160},{160,192},{192,224},{224... | collective-permute-start | bytes 245768 | tf_op jit(solution)/shard_map/gather_sequence/ppermute | solution.py:32
  91.8 9.6 %collective-permute-start.5 = (bf16[128,320]{0,1:T(8,128)(2,1)S(1)}, bf16[128,320]{0,1:T(8,128)(2,1)S(1)}, u32[]{:S(2)}, u32[]{:S(2)}) collective-permute-start(bf16[128,320]{0,1:T(8,128)(2,1)S(1)} %collective-permute-done.4), channel_id=1, source_target_pairs={{0,480},{32,0},{64,32},{96,64},{128,96},{160,128},{192,160},{224,1... | collective-permute-start | bytes 245768 | tf_op jit(solution)/shard_map/gather_sequence/ppermute | solution.py:32
  98.8 9.4 %collective-permute-start.12 = (bf16[128,320]{0,1:T(8,128)(2,1)S(1)}, bf16[128,320]{0,1:T(8,128)(2,1)S(1)}, u32[]{:S(2)}, u32[]{:S(2)}) collective-permute-start(bf16[128,320]{0,1:T(8,128)(2,1)S(1)} %collective-permute-done.11), channel_id=1, source_target_pairs={{0,32},{32,64},{64,96},{96,128},{128,160},{160,192},{192,224},{224... | collective-permute-start | bytes 245768 | tf_op jit(solution)/shard_map/gather_sequence/ppermute | solution.py:32
  101.3 18.0 %collective-permute-start.6 = (bf16[128,320]{0,1:T(8,128)(2,1)S(1)}, bf16[128,320]{0,1:T(8,128)(2,1)S(1)}, u32[]{:S(2)}, u32[]{:S(2)}) collective-permute-start(bf16[128,320]{0,1:T(8,128)(2,1)S(1)} %collective-permute-done.5), channel_id=1, source_target_pairs={{0,480},{32,0},{64,32},{96,64},{128,96},{160,128},{192,160},{224,1... | collective-permute-start | bytes 245768 | tf_op jit(solution)/shard_map/gather_sequence/ppermute | solution.py:32
  108.1 9.3 %collective-permute-start.13 = (bf16[128,320]{0,1:T(8,128)(2,1)S(1)}, bf16[128,320]{0,1:T(8,128)(2,1)S(1)}, u32[]{:S(2)}, u32[]{:S(2)}) collective-permute-start(bf16[128,320]{0,1:T(8,128)(2,1)S(1)} %collective-permute-done.12), channel_id=1, source_target_pairs={{0,32},{32,64},{64,96},{96,128},{128,160},{160,192},{192,224},{224... | collective-permute-start | bytes 245768 | tf_op jit(solution)/shard_map/gather_sequence/ppermute | solution.py:32
  117.4 8.8 %collective-permute-start.14 = (bf16[128,320]{0,1:T(8,128)(2,1)S(1)}, bf16[128,320]{0,1:T(8,128)(2,1)S(1)}, u32[]{:S(2)}, u32[]{:S(2)}) collective-permute-start(bf16[128,320]{0,1:T(8,128)(2,1)S(1)} %collective-permute-done.13), channel_id=1, source_target_pairs={{0,32},{32,64},{64,96},{96,128},{128,160},{160,192},{192,224},{224... | collective-permute-start | bytes 245768 | tf_op jit(solution)/shard_map/gather_sequence/ppermute | solution.py:32
  131.5 24.0 %collective-permute-start.15 = (bf16[2048,320]{0,1:T(8,128)(2,1)}, bf16[2048,320]{0,1:T(8,128)(2,1)S(1)}, u32[]{:S(2)}, u32[]{:S(2)}) collective-permute-start(bf16[2048,320]{0,1:T(8,128)(2,1)} %constant_dynamic-update-slice_fusion), channel_id=1, source_target_pairs={{0,8},{8,16},{16,24},{24,0},{1,9},{9,17},{17,25},{25,1},{2,10},{10... | collective-permute-start | bytes 3932168 | tf_op jit(solution)/shard_map/gather_sequence/ppermute | solution.py:32
  135.5 24.5 %collective-permute-start.16 = (bf16[2048,320]{0,1:T(8,128)(2,1)}, bf16[2048,320]{0,1:T(8,128)(2,1)}, u32[]{:S(2)}, u32[]{:S(2)}) collective-permute-start(bf16[2048,320]{0,1:T(8,128)(2,1)} %constant_dynamic-update-slice_fusion), channel_id=1, source_target_pairs={{0,24},{8,0},{16,8},{24,16},{1,25},{9,1},{17,9},{25,17},{2,26},{10... | collective-permute-start | bytes 3932168 | tf_op jit(solution)/shard_map/gather_sequence/ppermute | solution.py:32
  144.6 2.5 %copy-start.26 = (bf16[128,160]{0,1:T(8,128)(2,1)S(1)}, bf16[128,160]{0,1:T(8,128)(2,1)}, u32[]{:S(2)}) copy-start(bf16[128,160]{0,1:T(8,128)(2,1)} %copy-done.25) | copy-start | bytes 122884
  160.6 23.2 %all-to-all-start = ((f32[64,2,2,128]{3,2,1,0:T(2,128)}), f32[64,2,2,128]{3,2,1,0:T(2,128)S(1)}, u32[]{:S(2)}, u32[]{:S(2)}) async-start(f32[64,2,2,128]{3,2,1,0:T(2,128)} %broadcast_in_dim.95), calls=%async_computation | async-start | bytes 262144 | tf_op jit(solution)/shard_map/gather_row_stats/all_to_all | solution.py:163
  170.3 33.1 %collective-permute-start.17 = (bf16[1024,320]{0,1:T(8,128)(2,1)}, bf16[1024,320]{0,1:T(8,128)(2,1)}, u32[]{:S(2)}, u32[]{:S(2)}) collective-permute-start(bf16[1024,320]{0,1:T(8,128)(2,1)} %slice.135), channel_id=1, source_target_pairs={{0,8},{8,16},{16,24},{24,0},{1,9},{9,17},{17,25},{25,1},{2,10},{10... | collective-permute-start | bytes 1966088 | tf_op jit(solution)/shard_map/gather_row_stats/ppermute | solution.py:32
  174.7 29.9 %collective-permute-start.18 = (bf16[1024,320]{0,1:T(8,128)(2,1)}, bf16[1024,320]{0,1:T(8,128)(2,1)}, u32[]{:S(2)}, u32[]{:S(2)}) collective-permute-start(bf16[1024,320]{0,1:T(8,128)(2,1)} %slice.136), channel_id=1, source_target_pairs={{0,24},{8,0},{16,8},{24,16},{1,25},{9,1},{17,9},{25,17},{2,26},{10... | collective-permute-start | bytes 1966088 | tf_op jit(solution)/shard_map/gather_row_stats/ppermute | solution.py:32
  183.8 3.3 %copy-start.17 = (f32[64,2,2,128]{3,2,1,0:T(2,128)}, f32[64,2,2,128]{3,2,1,0:T(2,128)S(1)}, u32[]{:S(2)}) copy-start(f32[64,2,2,128]{3,2,1,0:T(2,128)S(1)} %all-to-all-done) | copy-start | bytes 393220
  186.5 2.5 %copy-start.6 = (bf16[2048,160]{0,1:T(8,128)(2,1)S(1)}, bf16[2048,160]{0,1:T(8,128)(2,1)}, u32[]{:S(2)}) copy-start(bf16[2048,160]{0,1:T(8,128)(2,1)} %get-tuple-element.60) | copy-start | bytes 1966084
  190.1 2.7 %copy-start.16 = (pred[128,2048]{1,0:T(8,128)(4,1)S(1)}, pred[128,2048]{1,0:T(8,128)(4,1)}, u32[]{:S(2)}) copy-start(pred[128,2048]{1,0:T(8,128)(4,1)} %get-tuple-element.50) | copy-start | bytes 786436
  194.6 3.5 %copy-start.2 = (f32[2,128,2048]{2,1,0:T(8,128)}, f32[2,128,2048]{2,1,0:T(8,128)S(1)}, u32[]{:S(2)}) copy-start(f32[2,128,2048]{2,1,0:T(8,128)S(1)} %fusion.16) | copy-start | bytes 6291460
  194.6 3.5 %copy-start.15 = (pred[128,2048]{1,0:T(8,128)(4,1)S(1)}, pred[128,2048]{1,0:T(8,128)(4,1)}, u32[]{:S(2)}) copy-start(pred[128,2048]{1,0:T(8,128)(4,1)} %get-tuple-element.49) | copy-start | bytes 786436
  205.9 3.2 %copy-start.7 = (bf16[2048,160]{0,1:T(8,128)(2,1)}, bf16[2048,160]{0,1:T(8,128)(2,1)S(1)}, u32[]{:S(2)}) copy-start(bf16[2048,160]{0,1:T(8,128)(2,1)S(1)} %get-tuple-element.29) | copy-start | bytes 1966084
  205.9 3.2 %copy-start.8 = (bf16[2048,160]{0,1:T(8,128)(2,1)}, bf16[2048,160]{0,1:T(8,128)(2,1)S(1)}, u32[]{:S(2)}) copy-start(bf16[2048,160]{0,1:T(8,128)(2,1)S(1)} %get-tuple-element.30) | copy-start | bytes 1966084
  209.2 3.5 %copy-start.20 = (f32[2,80,128]{2,1,0:T(8,128)S(1)}, f32[2,80,128]{2,1,0:T(8,128)}, u32[]{:S(2)}) copy-start(f32[2,80,128]{2,1,0:T(8,128)} %fusion.25) | copy-start | bytes 245764
  209.2 3.5 %copy-start.22 = (f32[2,80,128]{2,1,0:T(8,128)S(1)}, f32[2,80,128]{2,1,0:T(8,128)}, u32[]{:S(2)}) copy-start(f32[2,80,128]{2,1,0:T(8,128)} %fusion.27) | copy-start | bytes 245764
  209.2 3.5 %copy-start.27 = (f32[2,2048]{1,0:T(2,128)S(1)}, f32[2,2048]{1,0:T(2,128)}, u32[]{:S(2)}) copy-start(f32[2,2048]{1,0:T(2,128)} %get-tuple-element.37) | copy-start | bytes 49156
  212.6 4.2 %copy-start.19 = (f32[2,80,128]{2,1,0:T(8,128)S(1)}, f32[2,80,128]{2,1,0:T(8,128)}, u32[]{:S(2)}) copy-start(f32[2,80,128]{2,1,0:T(8,128)} %fusion.49) | copy-start | bytes 245764
  212.6 4.2 %copy-start.21 = (f32[2,80,128]{2,1,0:T(8,128)S(1)}, f32[2,80,128]{2,1,0:T(8,128)}, u32[]{:S(2)}) copy-start(f32[2,80,128]{2,1,0:T(8,128)} %fusion.53) | copy-start | bytes 245764
  215.2 3.0 %copy-start.10 = (f32[128,1280]{1,0:T(8,128)S(1)}, f32[128,1280]{1,0:T(8,128)}, u32[]{:S(2)}) copy-start(f32[128,1280]{1,0:T(8,128)} %copy-done.9) | copy-start | bytes 1966084
  215.2 3.0 %copy-start.30 = (f32[1280]{0:T(1024)S(1)}, f32[1280]{0:T(1024)}, u32[]{:S(2)}) copy-start(f32[1280]{0:T(1024)} %param.13) | copy-start | bytes 15364
  219.5 12.5 %copy-start.23 = (bf16[128,320]{0,1:T(8,128)(2,1)S(1)}, bf16[128,320]{0,1:T(8,128)(2,1)}, u32[]{:S(2)}) copy-start(bf16[128,320]{0,1:T(8,128)(2,1)} %param.11) | copy-start | bytes 245764
  219.5 12.5 %copy-start.24 = (bf16[128,320]{0,1:T(8,128)(2,1)S(1)}, bf16[128,320]{0,1:T(8,128)(2,1)}, u32[]{:S(2)}) copy-start(bf16[128,320]{0,1:T(8,128)(2,1)} %param.12) | copy-start | bytes 245764
  219.5 12.5 %copy-start.35 = (f32[128]{0:T(128)S(1)}, f32[128]{0:T(128)}, u32[]{:S(2)}) copy-start(f32[128]{0:T(128)} %copy-done.34) | copy-start | bytes 1540
  (10 other events, 17.2 us)
Sparse Core Ops, SparseCore 0:
  37.8 92.8 all-gather.1

commit v8 on v7

--- a/solution.py
+++ b/solution.py
@@ -1,9 +1,11 @@
+import functools
 import math
 
 import jax
 import jax.numpy as jnp
 import numpy as np
 from jax import lax
+from jax.experimental import pallas as pl
 from jax.sharding import Mesh
 from jax.sharding import PartitionSpec as P
 
@@ -59,6 +61,75 @@
     return [data, behind, far, ahead]
 
 
+def key_pass_kernel(own_ref, key_ref, value_ref, qg_ref, place_ref, stats_ref, dk_ref, dv_ref, *, heads, head_width):
+    step = pl.program_id(0)
+
+    @pl.when(step == 0)
+    def _():
+        dk_ref[...] = jnp.zeros_like(dk_ref)
+        dv_ref[...] = jnp.zeros_like(dv_ref)
+
+    cols = heads * head_width
+    query = qg_ref[:, :cols]
+    grad = qg_ref[:, cols:]
+    keys = key_ref[...]
+    values = value_ref[...]
+    visible = own_ref[...] <= place_ref[...]
+    column = lax.broadcasted_iota(jnp.int32, (1, cols), 1) // head_width
+    nt = (((1,), (1,)), ((), ()))
+    dk = dk_ref[...]
+    dv = dv_ref[...]
+    for h in range(heads):
+        mine = column == h
+        key_h = jnp.where(mine, keys, jnp.zeros_like(keys))
+        value_h = jnp.where(mine, values, jnp.zeros_like(values))
+        scores = lax.dot_general(key_h, query, nt, preferred_element_type=jnp.float32)
+        grad_probs = lax.dot_general(value_h, grad, nt, preferred_element_type=jnp.float32)
+        log_h = stats_ref[h : h + 1, :]
+        delta_h = stats_ref[heads + h : heads + h + 1, :]
+        attend = jnp.exp(jnp.where(visible, scores - log_h, masked_score))
+        score_grad = (attend * (grad_probs - delta_h)).astype(jnp.bfloat16)
+        part_k = jnp.dot(score_grad, query, preferred_element_type=jnp.float32)
+        part_v = jnp.dot(attend.astype(jnp.bfloat16), grad, preferred_element_type=jnp.float32)
+        dk = dk + jnp.where(mine, part_k, 0.0)
+        dv = dv + jnp.where(mine, part_v, 0.0)
+    dk_ref[...] = dk
+    dv_ref[...] = dv
+
+
+def key_pass(own_positions, keys, values, qg, place, stats, heads, head_width, block=512):
+    rows = keys.shape[0]
+    cols = keys.shape[1]
+    total = qg.shape[0]
+    steps = total // block
+    kernel = functools.partial(key_pass_kernel, heads=heads, head_width=head_width)
+    flops = steps * heads * 4 * 2 * rows * block * cols
+    return pl.pallas_call(
+        kernel,
+        grid=(steps,),
+        in_specs=[
+            pl.BlockSpec((rows, 1), lambda i: (0, 0)),
+            pl.BlockSpec((rows, cols), lambda i: (0, 0)),
+            pl.BlockSpec((rows, cols), lambda i: (0, 0)),
+            pl.BlockSpec((block, 2 * cols), lambda i: (i, 0)),
+            pl.BlockSpec((1, block), lambda i: (0, i)),
+            pl.BlockSpec((2 * heads, block), lambda i: (0, i)),
+        ],
+        out_specs=[
+            pl.BlockSpec((rows, cols), lambda i: (0, 0)),
+            pl.BlockSpec((rows, cols), lambda i: (0, 0)),
+        ],
+        out_shape=[
+            jax.ShapeDtypeStruct((rows, cols), jnp.float32),
+            jax.ShapeDtypeStruct((rows, cols), jnp.float32),
+        ],
+        cost_estimate=pl.CostEstimate(
+            flops=flops, transcendentals=steps * heads * rows * block,
+            bytes_accessed=total * 2 * cols * 2 + total * 4 * (2 * heads + 1) + rows * cols * 12,
+        ),
+    )(own_positions.reshape(rows, 1), keys, values, qg, place.reshape(1, total), stats)
+
+
 def per_device(
     inputs, out_grads, norm_gain, w_query, w_key, w_value, w_output, query_scale, offsets
 ):
@@ -164,40 +235,20 @@
 
     with jax.named_scope("key_pass"):
         piece_rows = qg_pieces[0].shape[0]
-        key_grad = jnp.zeros((row_count, heads_here, head_width), jnp.float32)
-        value_grad = jnp.zeros((row_count, heads_here, head_width), jnp.float32)
+        key_grad = jnp.zeros((row_count, cols), jnp.float32)
+        value_grad = jnp.zeros((row_count, cols), jnp.float32)
         for ry, piece in enumerate(qg_pieces):
             source = qg_source[ry * z_size : (ry + 1) * z_size]
-            query_part = piece[:, :cols].reshape(piece_rows, heads_here, head_width)
-            grad_part = piece[:, cols:].reshape(piece_rows, heads_here, head_width)
             place = block_positions(offsets[source], piece_rows)
             part_stats = stats_all[source]
-            log_part = jnp.transpose(part_stats[:, 0], (1, 0, 2)).reshape(heads_here, piece_rows)
-            delta_part = jnp.transpose(part_stats[:, 1], (1, 0, 2)).reshape(
-                heads_here, piece_rows
+            part_stats = jnp.transpose(part_stats, (1, 2, 0, 3)).reshape(
+                2 * heads_here, piece_rows
             )
-            scores_t = jnp.einsum(
-                "khd,qhd->hkq", key_heads, query_part, preferred_element_type=jnp.float32
+            part_k, part_v = key_pass(
+                own_positions, keys, values, piece, place, part_stats, heads_here, head_width
             )
-            visible_t = own_positions[None, :, None] <= place[None, None, :]
-            attend_t = jnp.exp(
-                jnp.where(visible_t, scores_t - log_part[:, None, :], masked_score)
-            )
-            grad_probs_t = jnp.einsum(
-                "khd,qhd->hkq", value_heads, grad_part, preferred_element_type=jnp.float32
-            )
-            score_grad = (attend_t * (grad_probs_t - delta_part[:, None, :])).astype(
-                jnp.bfloat16
-            )
-            key_grad = key_grad + jnp.einsum(
-                "hkq,qhd->khd", score_grad, query_part, preferred_element_type=jnp.float32
-            )
-            value_grad = value_grad + jnp.einsum(
-                "hkq,qhd->khd",
-                attend_t.astype(jnp.bfloat16),
-                grad_part,
-                preferred_element_type=jnp.float32,
-            )
+            key_grad = key_grad + part_k
+            value_grad = value_grad + part_v
         key_done = key_grad.reshape(row_count, cols).astype(jnp.bfloat16)
         value_done = value_grad.reshape(row_count, cols).astype(jnp.bfloat16)
 

time: 242 us -> 277 us (1.14)
  Pallas kernels: 0 us -> 20.8 us
  matrix products: 36.1 us -> 24.7 us
  local copies, waits for them, and re-layouts: 36.3 us -> 46.5 us
  waiting for transfers between devices: 26.5 us -> 32.9 us
  starting transfers between devices: 77.2 us -> 81.8 us
  other arithmetic: 8.26 us -> 11.5 us
    dot_general x12 -> x0, matrix products: 23.2 us -> none  [the longest x4 12.2 us: per_device(): jnp.einsum('hkq,qhd->khd', score_grad, query_part, preferred_element_type...]
    pallas_call x0 -> x4, Pallas kernels: none -> 20.8 us  [key_pass(): pl.pallas_call(kernel, grid=(steps,), in_specs=[pl.BlockSpec((rows, 1), l...]
    unnamed x90 -> x83, local copies, waits for them, and re-layouts: 12.9 us -> 1.97 us
    slice x1 -> x2, local copies, waits for them, and re-layouts: 2.95 us -> 12.4 us  [per_device(): value_all = kv_all[:, cols:].reshape(all_rows, heads_here, head_width)]
    ppermute x19, waiting for transfers between devices: 23.9 us -> 29.9 us  [shift(): lax.ppermute(data, axis, [(i, (i + step) % size) for i in range(size)])]
    dot_general x1, matrix products: 3.49 us -> 9.5 us  [per_device(): jnp.einsum('qhd,khd->hqk', grad_heads, value_all, preferred_element_type=...]
    gather x4, local copies, waits for them, and re-layouts: 3.64 us -> 8.85 us  [per_device(): part_stats = stats_all[source]]
    optimization_barrier x0 -> x2, local copies, waits for them, and re-layouts: none -> 5.11 us  [per_device(): lax.optimization_barrier((stats, qg_ahead, qg_behind))]
  transfers between devices with their start and end apart: 21 -> 21, of which waited for: 13 -> 9; matrix products, arithmetic and copies ran while one was open for 26% -> 21% of each run, Pallas kernels for 0% -> 6%
where the time goes in v8:
time: 277 us; the launch traced here: 275 us
  starting transfers between devices  81.8 us (30%)
  local copies, waits for them, and re-layouts  46.5 us (17%)
  blocking collectives  41.5 us (15%)
  waiting for transfers between devices  32.9 us (12%)
  matrix products  24.7 us (9%)
  Pallas kernels  20.8 us (8%)
  between operations  15.1 us (5%)
  other arithmetic  11.5 us (4%)
    ppermute x19, starting transfers between devices, shift(): lax.ppermute(data, axis, [(i, (i + step) % size) for i in range(size)])  71.1 us
    ppermute x19, waiting for transfers between devices, shift(): lax.ppermute(data, axis, [(i, (i + step) % size) for i in range(size)])  29.9 us
    pallas_call x4, Pallas kernels, key_pass(): pl.pallas_call(kernel, grid=(steps,), in_specs=[pl.BlockSpec((rows, 1), l...  20.8 us
    all_gather x1, blocking collectives, per_device(): kv_all = lax.all_gather(kv, 'y', axis=0, tiled=True)  15.3 us
    all_gather x1, blocking collectives, per_device(): gathered = lax.all_gather(both, 'tp', axis=1, tiled=True)  13.4 us
    all_to_all x1, blocking collectives, per_device(): received = lax.all_to_all(payload, 'tp', 0, 0, tiled=False)  12.8 us
    slice x2, local copies, waits for them, and re-layouts, per_device(): value_all = kv_all[:, cols:].reshape(all_rows, heads_here, head_width)  12.4 us
    all_to_all x1, starting transfers between devices, per_device(): stats_all = lax.all_to_all(sent, ('z', 'y'), 0, 0, tiled=False)  10.8 us
  transfers between devices with their start and end apart: 21, of which 9 were waited for; matrix products, arithmetic and copies ran while one was open for 21% of the time, Pallas kernels for 6%

profile of v8, /device:TPU:24, one launch (start us, length us, event | category | flops | bytes accessed | tf_op | source)
XLA Modules:
  0.0 274.7 jit_solution(16841785110909275384)
XLA Ops:
  7.5 13.4 %all_gather.9 = bf16[128,2560]{0,1:T(8,128)(2,1)S(1)} all-gather(bf16[128,640]{0,1:T(8,128)(2,1)S(1)} %pad_maximum_fusion.2), channel_id=1, replica_groups=mesh['z'=16,'y'=4,'tp'=4,'dp'=2] {'tp'}, dimensions={1}, use_global_device_ids=true | all-gather | bytes 819200 | tf_op jit(solution)/shard_map/gather_features/all_gather | solution.py:148
  23.0 15.3 %all_gather.10 = bf16[512,320]{1,0:T(8,128)(2,1)} all-gather(bf16[128,320]{1,0:T(8,128)(2,1)S(1)} %pad_maximum_fusion.3), channel_id=1, replica_groups=mesh['z'=16,'y'=4,'tp'=4,'dp'=2] {'y'}, dimensions={0}, use_global_device_ids=true | all-gather | bytes 409600 | tf_op jit(solution)/shard_map/gather_sequence/all_gather | solution.py:180
  39.2 9.4 %collective-permute-start = (bf16[128,320]{1,0:T(8,128)(2,1)S(1)}, bf16[128,320]{1,0:T(8,128)(2,1)S(1)}, u32[]{:S(2)}, u32[]{:S(2)}) collective-permute-start(bf16[128,320]{1,0:T(8,128)(2,1)S(1)} %get-tuple-element.40), channel_id=1, source_target_pairs={{0,480},{32,0},{64,32},{96,64},{128,96},{160,128},{192,160},{224,1... | collective-permute-start | bytes 245768 | tf_op jit(solution)/shard_map/gather_sequence/ppermute | solution.py:34
  48.6 1.9 collective-permute-start.7
  59.8 5.1 %collective-permute-start.1 = (bf16[128,320]{1,0:T(8,128)(2,1)S(1)}, bf16[128,320]{1,0:T(8,128)(2,1)S(1)}, u32[]{:S(2)}, u32[]{:S(2)}) collective-permute-start(bf16[128,320]{1,0:T(8,128)(2,1)S(1)} %collective-permute-done), channel_id=1, source_target_pairs={{0,480},{32,0},{64,32},{96,64},{128,96},{160,128},{192,160},{224,1... | collective-permute-start | bytes 245768 | tf_op jit(solution)/shard_map/gather_sequence/ppermute | solution.py:34
  64.9 1.9 collective-permute-start.8
  66.9 2.5 collective-permute-done.1
  69.4 5.6 %collective-permute-start.2 = (bf16[128,320]{1,0:T(8,128)(2,1)S(1)}, bf16[128,320]{1,0:T(8,128)(2,1)S(1)}, u32[]{:S(2)}, u32[]{:S(2)}) collective-permute-start(bf16[128,320]{1,0:T(8,128)(2,1)S(1)} %collective-permute-done.1), channel_id=1, source_target_pairs={{0,480},{32,0},{64,32},{96,64},{128,96},{160,128},{192,160},{224,1... | collective-permute-start | bytes 245768 | tf_op jit(solution)/shard_map/gather_sequence/ppermute | solution.py:34
  75.0 1.9 collective-permute-start.9
  76.9 2.9 %collective-permute-done.2 = bf16[128,320]{1,0:T(8,128)(2,1)S(1)} collective-permute-done((bf16[128,320]{1,0:T(8,128)(2,1)S(1)}, bf16[128,320]{1,0:T(8,128)(2,1)S(1)}, u32[]{:S(2)}, u32[]{:S(2)}) %collective-permute-start.2) | collective-permute-done | bytes 81952 | tf_op jit(solution)/shard_map/gather_sequence/ppermute | solution.py:34
  79.8 5.6 %collective-permute-start.3 = (bf16[128,320]{1,0:T(8,128)(2,1)S(1)}, bf16[128,320]{1,0:T(8,128)(2,1)S(1)}, u32[]{:S(2)}, u32[]{:S(2)}) collective-permute-start(bf16[128,320]{1,0:T(8,128)(2,1)S(1)} %collective-permute-done.2), channel_id=1, source_target_pairs={{0,480},{32,0},{64,32},{96,64},{128,96},{160,128},{192,160},{224,1... | collective-permute-start | bytes 245768 | tf_op jit(solution)/shard_map/gather_sequence/ppermute | solution.py:34
  85.4 1.9 collective-permute-start.10
  87.4 2.7 collective-permute-done.3
  90.1 5.6 %collective-permute-start.4 = (bf16[128,320]{1,0:T(8,128)(2,1)S(1)}, bf16[128,320]{1,0:T(8,128)(2,1)S(1)}, u32[]{:S(2)}, u32[]{:S(2)}) collective-permute-start(bf16[128,320]{1,0:T(8,128)(2,1)S(1)} %collective-permute-done.3), channel_id=1, source_target_pairs={{0,480},{32,0},{64,32},{96,64},{128,96},{160,128},{192,160},{224,1... | collective-permute-start | bytes 245768 | tf_op jit(solution)/shard_map/gather_sequence/ppermute | solution.py:34
  95.7 1.9 collective-permute-start.11
  97.6 3.0 %collective-permute-done.4 = bf16[128,320]{1,0:T(8,128)(2,1)S(1)} collective-permute-done((bf16[128,320]{1,0:T(8,128)(2,1)S(1)}, bf16[128,320]{1,0:T(8,128)(2,1)S(1)}, u32[]{:S(2)}, u32[]{:S(2)}) %collective-permute-start.4) | collective-permute-done | bytes 81952 | tf_op jit(solution)/shard_map/gather_sequence/ppermute | solution.py:34
  100.7 5.6 %collective-permute-start.5 = (bf16[128,320]{1,0:T(8,128)(2,1)S(1)}, bf16[128,320]{1,0:T(8,128)(2,1)S(1)}, u32[]{:S(2)}, u32[]{:S(2)}) collective-permute-start(bf16[128,320]{1,0:T(8,128)(2,1)S(1)} %collective-permute-done.4), channel_id=1, source_target_pairs={{0,480},{32,0},{64,32},{96,64},{128,96},{160,128},{192,160},{224,1... | collective-permute-start | bytes 245768 | tf_op jit(solution)/shard_map/gather_sequence/ppermute | solution.py:34
  108.2 2.6 collective-permute-done.5
  110.8 5.6 %collective-permute-start.6 = (bf16[128,320]{1,0:T(8,128)(2,1)S(1)}, bf16[128,320]{1,0:T(8,128)(2,1)S(1)}, u32[]{:S(2)}, u32[]{:S(2)}) collective-permute-start(bf16[128,320]{1,0:T(8,128)(2,1)S(1)} %collective-permute-done.5), channel_id=1, source_target_pairs={{0,480},{32,0},{64,32},{96,64},{128,96},{160,128},{192,160},{224,1... | collective-permute-start | bytes 245768 | tf_op jit(solution)/shard_map/gather_sequence/ppermute | solution.py:34
  118.7 8.2 %collective-permute-done.13 = bf16[128,320]{1,0:T(8,128)(2,1)S(1)} collective-permute-done((bf16[128,320]{1,0:T(8,128)(2,1)S(1)}, bf16[128,320]{1,0:T(8,128)(2,1)S(1)}, u32[]{:S(2)}, u32[]{:S(2)}) %collective-permute-start.13) | collective-permute-done | bytes 81952 | tf_op jit(solution)/shard_map/gather_sequence/ppermute | solution.py:34
  128.9 7.7 %collective-permute-done.14 = bf16[128,320]{1,0:T(8,128)(2,1)S(1)} collective-permute-done((bf16[128,320]{1,0:T(8,128)(2,1)S(1)}, bf16[128,320]{1,0:T(8,128)(2,1)S(1)}, u32[]{:S(2)}, u32[]{:S(2)}) %collective-permute-start.14) | collective-permute-done | bytes 81952 | tf_op jit(solution)/shard_map/gather_sequence/ppermute | solution.py:34
  138.4 2.6 collective-permute-start.15
  141.0 3.4 %collective-permute-start.16 = (bf16[2048,320]{0,1:T(8,128)(2,1)}, bf16[2048,320]{0,1:T(8,128)(2,1)}, u32[]{:S(2)}, u32[]{:S(2)}) collective-permute-start(bf16[2048,320]{0,1:T(8,128)(2,1)} %copy.112), channel_id=1, source_target_pairs={{0,24},{8,0},{16,8},{24,16},{1,25},{9,1},{17,9},{25,17},{2,26},{10... | collective-permute-start | bytes 3932168 | tf_op jit(solution)/shard_map/gather_sequence/ppermute | solution.py:34
  144.4 6.6 %fusion.32 = (bf16[8192,160]{1,0:T(8,128)(2,1)}, bf16[8192,160]{1,0:T(8,128)(2,1)}) fusion(bf16[8192,320]{1,0:T(8,128)(2,1)} %all-gather.2.cloned.1.call-done), kind=kLoop, calls=%fused_computation.103 | loop fusion | bytes 10485760 | tf_op jit(solution)/shard_map/gather_sequence/slice | solution.py:185
  151.1 4.5 %copy.109 = bf16[8192,160]{0,1:T(8,128)(2,1)S(1)} copy(bf16[8192,160]{1,0:T(8,128)(2,1)} %get-tuple-element.42) | data formatting | bytes 5242880 | tf_op jit(solution)/shard_map/gather_sequence/slice | solution.py:184
  155.6 3.1 %select_reduce_fusion.1 = (f32[2,128]{1,0:T(2,128)S(1)}, f32[2,128,8192]{2,1,0:T(8,128)S(1)}) fusion(pred[128,8192]{1,0:T(8,128)(4,1)} %broadcast_compare_fusion, bf16[128,2,80]{0,2,1:T(8,128)(2,1)S(1)} %bitcast.90, bf16[8192,2,80]{0,2,1:T(8,128)(2,1)S(1)} %bitcast.81), kind=kOutput, calls=%fused_computation.11 | convolution fusion | flops 339738368 | bytes 12100608 | tf_op jit(solution)/shard_map/query_pass/qhd,khd->hqk/dot_general | solution.py:202
  158.7 2.5 select_reduce_fusion
  161.9 5.8 %copy.110 = bf16[8192,160]{0,1:T(8,128)(2,1)} copy(bf16[8192,160]{1,0:T(8,128)(2,1)} %get-tuple-element.41) | data formatting | bytes 5242880 | tf_op jit(solution)/shard_map/gather_sequence/slice | solution.py:185
  167.7 9.5 %fusion.34 = (f32[2,128]{1,0:T(2,128)S(1)}, bf16[2,128,8192]{2,1,0:T(8,128)(2,1)}) fusion(bf16[128,2,80]{0,2,1:T(8,128)(2,1)S(1)} %bitcast.91, bf16[8192,2,80]{0,2,1:T(8,128)(2,1)} %bitcast.88, f32[2,128,8192]{2,1,0:T(8,128)} %copy-done.2, f32[2,128]{1,0:T(2,128)S(1)} %log_add_fusion, pred[128,8192]{1,0:T(8,128)(4,1)} %broadcast_compare_fusion), kind=kOutput, calls=%fused_computation.105 | convolution fusion | flops 346029824 | bytes 16295936 | tf_op jit(solution)/shard_map/query_pass/qhd,khd->hqk/dot_general | solution.py:211
  177.2 2.6 copy.121.qg_ref
  179.8 2.0 slice.79
  181.8 2.0 slice.80
  183.7 2.6 copy.116.qg_ref
  186.3 5.5 %fusion.19 = f32[128,2,80]{0,2,1:T(8,128)S(1)} fusion(bf16[8192,2,80]{0,2,1:T(8,128)(2,1)S(1)} %bitcast.82, f32[2,128,8192]{2,1,0:T(8,128)} %copy-done.2, f32[2,128]{1,0:T(2,128)S(1)} %log_add_fusion, pred[128,8192]{1,0:T(8,128)(4,1)} %broadcast_compare_fusion, f32[128,2]{0,1:T(2,128)S(1)} %bitcast.102), kind=kOutput, calls=%fused_computation.32 | convolution fusion | flops 341856256 | bytes 12142592 | tf_op jit(solution)/shard_map/query_pass/hqk,khd->hqd/dot_general | solution.py:222
  192.5 10.8 %all-to-all-start = ((f32[64,2,2,128]{3,2,1,0:T(2,128)}), f32[64,2,2,128]{3,2,1,0:T(2,128)}, u32[]{:S(2)}, u32[]{:S(2)}) async-start(f32[64,2,2,128]{3,2,1,0:T(2,128)} %broadcast_in_dim.27), calls=%async_computation | async-start | bytes 262144 | tf_op jit(solution)/shard_map/gather_row_stats/all_to_all | solution.py:234
  203.3 2.8 %collective-permute-start.18 = (bf16[1024,320]{0,1:T(8,128)(2,1)}, bf16[1024,320]{0,1:T(8,128)(2,1)}, u32[]{:S(2)}, u32[]{:S(2)}) collective-permute-start(bf16[1024,320]{0,1:T(8,128)(2,1)} %slice.80), channel_id=1, source_target_pairs={{0,24},{8,0},{16,8},{24,16},{1,25},{9,1},{17,9},{25,17},{2,26},{10... | collective-permute-start | bytes 1966088 | tf_op jit(solution)/shard_map/gather_row_stats/ppermute | solution.py:34
  206.1 4.5 %collective-permute-start.17 = (bf16[1024,320]{0,1:T(8,128)(2,1)}, bf16[1024,320]{0,1:T(8,128)(2,1)}, u32[]{:S(2)}, u32[]{:S(2)}) collective-permute-start(bf16[1024,320]{0,1:T(8,128)(2,1)} %slice.79), channel_id=1, source_target_pairs={{0,8},{8,16},{16,24},{24,0},{1,9},{9,17},{17,25},{25,1},{2,10},{10... | collective-permute-start | bytes 1966088 | tf_op jit(solution)/shard_map/gather_row_stats/ppermute | solution.py:34
  210.6 3.7 %fusion.13 = f32[128,2,80]{0,2,1:T(8,128)S(1)} fusion(f32[128,2,80]{0,2,1:T(8,128)S(1)} %fusion.19, bf16[8192,2,80]{0,2,1:T(8,128)(2,1)S(1)} %bitcast.83, bf16[2,128,8192]{2,1,0:T(8,128)(2,1)} %get-tuple-element.52), kind=kOutput, calls=%fused_computation.30 | convolution fusion | flops 335564800 | bytes 6979584 | tf_op jit(solution)/shard_map/query_pass/hqk,khd->hqd/dot_general | solution.py:216
  214.7 3.0 %all-to-all-done = f32[64,2,2,128]{3,2,1,0:T(2,128)} async-done(((f32[64,2,2,128]{3,2,1,0:T(2,128)}), f32[64,2,2,128]{3,2,1,0:T(2,128)}, u32[]{:S(2)}, u32[]{:S(2)}) %all-to-all-start) | async-done | bytes 131104 | tf_op jit(solution)/shard_map/gather_row_stats/all_to_all | solution.py:234
  217.6 2.2 gather_fusion.7
  219.9 2.2 gather_fusion.5
  222.1 2.2 gather_fusion.1
  224.3 2.2 gather_fusion.3
  226.5 5.2 %key_pass.4 = (f32[128,160]{1,0:T(8,128)}, f32[128,160]{1,0:T(8,128)}) custom-call(s32[128,1]{1,0:T(8,128)} %iota_add_fusion.own_ref, bf16[128,160]{1,0:T(8,128)(2,1)} %copy-done.14, bf16[128,160]{1,0:T(8,128)(2,1)} %copy-done.13, bf16[2048,320]{1,0:T(8,128)(2,1)} %copy-done.6, s32[1,2048]{1,0:T(1,128)} %bitcast.99, f32[4,2048]{1,0:T(4,128)} %bitcast.95), custom_call_target="tpu_custom_call" | custom-call | flops 671088640 | bytes 1597440 | tf_op jit(solution)/shard_map/key_pass/pallas_call | solution.py:107
  231.6 5.2 %key_pass.7 = (f32[128,160]{1,0:T(8,128)}, f32[128,160]{1,0:T(8,128)}) custom-call(s32[128,1]{1,0:T(8,128)} %iota_add_fusion.own_ref, bf16[128,160]{1,0:T(8,128)(2,1)} %copy-done.14, bf16[128,160]{1,0:T(8,128)(2,1)} %copy-done.13, bf16[2048,320]{1,0:T(8,128)(2,1)} %copy.121.qg_ref, s32[1,2048]{1,0:T(1,128)} %bitcast.97, f32[4,2048]{1,0:T(4,128)} %bitcast.93), custom_call_target="tpu_custom_call" | custom-call | flops 671088640 | bytes 1597440 | tf_op jit(solution)/shard_map/key_pass/pallas_call | solution.py:107
  236.8 5.2 %key_pass.5 = (f32[128,160]{1,0:T(8,128)}, f32[128,160]{1,0:T(8,128)}) custom-call(s32[128,1]{1,0:T(8,128)} %iota_add_fusion.own_ref, bf16[128,160]{1,0:T(8,128)(2,1)} %copy-done.14, bf16[128,160]{1,0:T(8,128)(2,1)} %copy-done.13, bf16[2048,320]{1,0:T(8,128)(2,1)} %copy.116.qg_ref, s32[1,2048]{1,0:T(1,128)} %bitcast.98, f32[4,2048]{1,0:T(4,128)} %bitcast.94), custom_call_target="tpu_custom_call" | custom-call | flops 671088640 | bytes 1597440 | tf_op jit(solution)/shard_map/key_pass/pallas_call | solution.py:107
  246.3 5.3 %key_pass.6 = (f32[128,160]{1,0:T(8,128)}, f32[128,160]{1,0:T(8,128)}) custom-call(s32[128,1]{1,0:T(8,128)} %iota_add_fusion.own_ref, bf16[128,160]{1,0:T(8,128)(2,1)} %copy-done.14, bf16[128,160]{1,0:T(8,128)(2,1)} %copy-done.13, bf16[2048,320]{1,0:T(8,128)(2,1)} %pad_maximum_fusion.qg_ref, s32[1,2048]{1,0:T(1,128)} %bitcast.96, f32[4,2048]{1,0:T(4,128)} %bitcast.92), custom_call_target="tpu_custom_call" | custom-call | flops 671088640 | bytes 1597440 | tf_op jit(solution)/shard_map/key_pass/pallas_call | solution.py:107
  254.1 12.8 %all_to_all.10 = f32[4,129,320]{2,1,0:T(8,128)S(1)} all-to-all(f32[4,129,320]{2,1,0:T(8,128)S(1)} %copy.124), channel_id=1, replica_groups=mesh['z'=16,'y'=4,'tp'=4,'dp'=2] {'tp'}, dimensions={0} | all-to-all | bytes 1320960 | tf_op jit(solution)/shard_map/back_projection/all_to_all | solution.py:265
  (163 shorter events, 29.7 us)
Async XLA Ops:
  6.5 15.7 %copy-start = (bf16[160,1280]{1,0:T(8,128)(2,1)S(1)}, bf16[160,1280]{1,0:T(8,128)(2,1)}, u32[]{:S(2)}) copy-start(bf16[160,1280]{1,0:T(8,128)(2,1)} %param.16) | copy-start | bytes 1228804
  6.5 137.9 %all-gather.2.cloned.1.call-start = ((), (), s32[]{:S(2)}) async-start(), calls=%async_computation.2 | async-start | bytes 6684672 | tf_op jit(solution)/shard_map/gather_sequence/all_gather | solution.py:181
  7.5 14.5 %copy-start.24 = (f32[1280]{0:T(1024)S(1)}, f32[1280]{0:T(1024)}, u32[]{:S(2)}) copy-start(f32[1280]{0:T(1024)} %param.13) | copy-start | bytes 15364
  21.5 16.8 %copy-start.33 = (f32[80]{0:T(128)S(1)}, f32[80]{0:T(128)}, u32[]{:S(2)}) copy-start(f32[80]{0:T(128)} %param.18) | copy-start | bytes 964
  21.5 16.9 %copy-start.10 = (bf16[160,1280]{1,0:T(8,128)(2,1)S(1)}, bf16[160,1280]{1,0:T(8,128)(2,1)}, u32[]{:S(2)}) copy-start(bf16[160,1280]{1,0:T(8,128)(2,1)} %param.17) | copy-start | bytes 1228804
  22.0 16.8 %copy-start.7 = (bf16[160,1280]{1,0:T(8,128)(2,1)S(1)}, bf16[160,1280]{1,0:T(8,128)(2,1)}, u32[]{:S(2)}) copy-start(bf16[160,1280]{1,0:T(8,128)(2,1)} %param.14) | copy-start | bytes 1228804
  22.6 29.5 %copy-start.13 = (bf16[128,160]{1,0:T(8,128)(2,1)}, bf16[128,160]{1,0:T(8,128)(2,1)S(1)}, u32[]{:S(2)}) copy-start(bf16[128,160]{1,0:T(8,128)(2,1)S(1)} %convolution_convert_fusion.value_ref) | copy-start | bytes 122884
  22.6 28.1 %copy-start.1 = (s32[64]{0:T(128)S(1)}, s32[64]{0:T(128)}, u32[]{:S(2)}) copy-start(s32[64]{0:T(128)} %param.19) | copy-start | bytes 772
  22.9 29.8 %copy-start.14 = (bf16[128,160]{1,0:T(8,128)(2,1)}, bf16[128,160]{1,0:T(8,128)(2,1)S(1)}, u32[]{:S(2)}) copy-start(bf16[128,160]{1,0:T(8,128)(2,1)S(1)} %convolution_convert_fusion.1.key_ref) | copy-start | bytes 122884
  38.7 20.5 %copy-start.15 = (bf16[128,160]{0,1:T(8,128)(2,1)}, bf16[128,160]{0,1:T(8,128)(2,1)S(1)}, u32[]{:S(2)}) copy-start(bf16[128,160]{0,1:T(8,128)(2,1)S(1)} %convolution_convert_fusion.2) | copy-start | bytes 122884
  39.2 20.6 %collective-permute-start = (bf16[128,320]{1,0:T(8,128)(2,1)S(1)}, bf16[128,320]{1,0:T(8,128)(2,1)S(1)}, u32[]{:S(2)}, u32[]{:S(2)}) collective-permute-start(bf16[128,320]{1,0:T(8,128)(2,1)S(1)} %get-tuple-element.40), channel_id=1, source_target_pairs={{0,480},{32,0},{64,32},{96,64},{128,96},{160,128},{192,160},{224,1... | collective-permute-start | bytes 245768 | tf_op jit(solution)/shard_map/gather_sequence/ppermute | solution.py:34
  48.6 16.4 %collective-permute-start.7 = (bf16[128,320]{1,0:T(8,128)(2,1)S(1)}, bf16[128,320]{1,0:T(8,128)(2,1)S(1)}, u32[]{:S(2)}, u32[]{:S(2)}) collective-permute-start(bf16[128,320]{1,0:T(8,128)(2,1)S(1)} %get-tuple-element.40), channel_id=1, source_target_pairs={{0,32},{32,64},{64,96},{96,128},{128,160},{160,192},{192,224},{224... | collective-permute-start | bytes 245768 | tf_op jit(solution)/shard_map/gather_sequence/ppermute | solution.py:34
  51.3 56.9 %copy-start.27 = (s32[1024]{0:T(1024)}, s32[1024]{0:T(1024)S(1)}, u32[]{:S(2)}) copy-start(s32[1024]{0:T(1024)S(1)} %get-tuple-element.56) | copy-start | bytes 12292
  51.4 56.9 %copy-start.28 = (s32[1024]{0:T(1024)}, s32[1024]{0:T(1024)S(1)}, u32[]{:S(2)}) copy-start(s32[1024]{0:T(1024)S(1)} %get-tuple-element.55) | copy-start | bytes 12292
  52.7 83.9 %copy-start.29 = (s32[1024]{0:T(1024)}, s32[1024]{0:T(1024)S(1)}, u32[]{:S(2)}) copy-start(s32[1024]{0:T(1024)S(1)} %get-tuple-element.57) | copy-start | bytes 12292
  52.7 83.9 %copy-start.30 = (s32[1024]{0:T(1024)}, s32[1024]{0:T(1024)S(1)}, u32[]{:S(2)}) copy-start(s32[1024]{0:T(1024)S(1)} %get-tuple-element.58) | copy-start | bytes 12292
  59.8 9.5 %collective-permute-start.1 = (bf16[128,320]{1,0:T(8,128)(2,1)S(1)}, bf16[128,320]{1,0:T(8,128)(2,1)S(1)}, u32[]{:S(2)}, u32[]{:S(2)}) collective-permute-start(bf16[128,320]{1,0:T(8,128)(2,1)S(1)} %collective-permute-done), channel_id=1, source_target_pairs={{0,480},{32,0},{64,32},{96,64},{128,96},{160,128},{192,160},{224,1... | collective-permute-start | bytes 245768 | tf_op jit(solution)/shard_map/gather_sequence/ppermute | solution.py:34
  64.9 10.0 %collective-permute-start.8 = (bf16[128,320]{1,0:T(8,128)(2,1)S(1)}, bf16[128,320]{1,0:T(8,128)(2,1)S(1)}, u32[]{:S(2)}, u32[]{:S(2)}) collective-permute-start(bf16[128,320]{1,0:T(8,128)(2,1)S(1)} %collective-permute-done.7), channel_id=1, source_target_pairs={{0,32},{32,64},{64,96},{96,128},{128,160},{160,192},{192,224},{224... | collective-permute-start | bytes 245768 | tf_op jit(solution)/shard_map/gather_sequence/ppermute | solution.py:34
  69.4 10.5 %collective-permute-start.2 = (bf16[128,320]{1,0:T(8,128)(2,1)S(1)}, bf16[128,320]{1,0:T(8,128)(2,1)S(1)}, u32[]{:S(2)}, u32[]{:S(2)}) collective-permute-start(bf16[128,320]{1,0:T(8,128)(2,1)S(1)} %collective-permute-done.1), channel_id=1, source_target_pairs={{0,480},{32,0},{64,32},{96,64},{128,96},{160,128},{192,160},{224,1... | collective-permute-start | bytes 245768 | tf_op jit(solution)/shard_map/gather_sequence/ppermute | solution.py:34
  75.0 10.4 %collective-permute-start.9 = (bf16[128,320]{1,0:T(8,128)(2,1)S(1)}, bf16[128,320]{1,0:T(8,128)(2,1)S(1)}, u32[]{:S(2)}, u32[]{:S(2)}) collective-permute-start(bf16[128,320]{1,0:T(8,128)(2,1)S(1)} %collective-permute-done.8), channel_id=1, source_target_pairs={{0,32},{32,64},{64,96},{96,128},{128,160},{160,192},{192,224},{224... | collective-permute-start | bytes 245768 | tf_op jit(solution)/shard_map/gather_sequence/ppermute | solution.py:34
  79.8 10.3 %collective-permute-start.3 = (bf16[128,320]{1,0:T(8,128)(2,1)S(1)}, bf16[128,320]{1,0:T(8,128)(2,1)S(1)}, u32[]{:S(2)}, u32[]{:S(2)}) collective-permute-start(bf16[128,320]{1,0:T(8,128)(2,1)S(1)} %collective-permute-done.2), channel_id=1, source_target_pairs={{0,480},{32,0},{64,32},{96,64},{128,96},{160,128},{192,160},{224,1... | collective-permute-start | bytes 245768 | tf_op jit(solution)/shard_map/gather_sequence/ppermute | solution.py:34
  85.4 10.3 %collective-permute-start.10 = (bf16[128,320]{1,0:T(8,128)(2,1)S(1)}, bf16[128,320]{1,0:T(8,128)(2,1)S(1)}, u32[]{:S(2)}, u32[]{:S(2)}) collective-permute-start(bf16[128,320]{1,0:T(8,128)(2,1)S(1)} %collective-permute-done.9), channel_id=1, source_target_pairs={{0,32},{32,64},{64,96},{96,128},{128,160},{160,192},{192,224},{224... | collective-permute-start | bytes 245768 | tf_op jit(solution)/shard_map/gather_sequence/ppermute | solution.py:34
  90.1 10.6 %collective-permute-start.4 = (bf16[128,320]{1,0:T(8,128)(2,1)S(1)}, bf16[128,320]{1,0:T(8,128)(2,1)S(1)}, u32[]{:S(2)}, u32[]{:S(2)}) collective-permute-start(bf16[128,320]{1,0:T(8,128)(2,1)S(1)} %collective-permute-done.3), channel_id=1, source_target_pairs={{0,480},{32,0},{64,32},{96,64},{128,96},{160,128},{192,160},{224,1... | collective-permute-start | bytes 245768 | tf_op jit(solution)/shard_map/gather_sequence/ppermute | solution.py:34
  95.7 10.6 %collective-permute-start.11 = (bf16[128,320]{1,0:T(8,128)(2,1)S(1)}, bf16[128,320]{1,0:T(8,128)(2,1)S(1)}, u32[]{:S(2)}, u32[]{:S(2)}) collective-permute-start(bf16[128,320]{1,0:T(8,128)(2,1)S(1)} %collective-permute-done.10), channel_id=1, source_target_pairs={{0,32},{32,64},{64,96},{96,128},{128,160},{160,192},{192,224},{224... | collective-permute-start | bytes 245768 | tf_op jit(solution)/shard_map/gather_sequence/ppermute | solution.py:34
  100.7 10.2 %collective-permute-start.5 = (bf16[128,320]{1,0:T(8,128)(2,1)S(1)}, bf16[128,320]{1,0:T(8,128)(2,1)S(1)}, u32[]{:S(2)}, u32[]{:S(2)}) collective-permute-start(bf16[128,320]{1,0:T(8,128)(2,1)S(1)} %collective-permute-done.4), channel_id=1, source_target_pairs={{0,480},{32,0},{64,32},{96,64},{128,96},{160,128},{192,160},{224,1... | collective-permute-start | bytes 245768 | tf_op jit(solution)/shard_map/gather_sequence/ppermute | solution.py:34
  106.3 10.5 %collective-permute-start.12 = (bf16[128,320]{1,0:T(8,128)(2,1)S(1)}, bf16[128,320]{1,0:T(8,128)(2,1)S(1)}, u32[]{:S(2)}, u32[]{:S(2)}) collective-permute-start(bf16[128,320]{1,0:T(8,128)(2,1)S(1)} %collective-permute-done.11), channel_id=1, source_target_pairs={{0,32},{32,64},{64,96},{96,128},{128,160},{160,192},{192,224},{224... | collective-permute-start | bytes 245768 | tf_op jit(solution)/shard_map/gather_sequence/ppermute | solution.py:34
  110.8 18.0 %collective-permute-start.6 = (bf16[128,320]{1,0:T(8,128)(2,1)S(1)}, bf16[128,320]{1,0:T(8,128)(2,1)S(1)}, u32[]{:S(2)}, u32[]{:S(2)}) collective-permute-start(bf16[128,320]{1,0:T(8,128)(2,1)S(1)} %collective-permute-done.5), channel_id=1, source_target_pairs={{0,480},{32,0},{64,32},{96,64},{128,96},{160,128},{192,160},{224,1... | collective-permute-start | bytes 245768 | tf_op jit(solution)/shard_map/gather_sequence/ppermute | solution.py:34
  116.8 10.1 %collective-permute-start.13 = (bf16[128,320]{1,0:T(8,128)(2,1)S(1)}, bf16[128,320]{1,0:T(8,128)(2,1)S(1)}, u32[]{:S(2)}, u32[]{:S(2)}) collective-permute-start(bf16[128,320]{1,0:T(8,128)(2,1)S(1)} %collective-permute-done.12), channel_id=1, source_target_pairs={{0,32},{32,64},{64,96},{96,128},{128,160},{160,192},{192,224},{224... | collective-permute-start | bytes 245768 | tf_op jit(solution)/shard_map/gather_sequence/ppermute | solution.py:34
  126.9 9.6 %collective-permute-start.14 = (bf16[128,320]{1,0:T(8,128)(2,1)S(1)}, bf16[128,320]{1,0:T(8,128)(2,1)S(1)}, u32[]{:S(2)}, u32[]{:S(2)}) collective-permute-start(bf16[128,320]{1,0:T(8,128)(2,1)S(1)} %collective-permute-done.13), channel_id=1, source_target_pairs={{0,32},{32,64},{64,96},{96,128},{128,160},{160,192},{192,224},{224... | collective-permute-start | bytes 245768 | tf_op jit(solution)/shard_map/gather_sequence/ppermute | solution.py:34
  136.8 14.3 %copy-start.6 = (bf16[2048,320]{1,0:T(8,128)(2,1)}, bf16[2048,320]{1,0:T(8,128)(2,1)S(1)}, u32[]{:S(2)}) copy-start(bf16[2048,320]{1,0:T(8,128)(2,1)S(1)} %constant_dynamic-update-slice_fusion.qg_ref) | copy-start | bytes 3932164
  138.4 38.8 %collective-permute-start.15 = (bf16[2048,320]{0,1:T(8,128)(2,1)}, bf16[2048,320]{0,1:T(8,128)(2,1)}, u32[]{:S(2)}, u32[]{:S(2)}) collective-permute-start(bf16[2048,320]{0,1:T(8,128)(2,1)} %copy.112), channel_id=1, source_target_pairs={{0,8},{8,16},{16,24},{24,0},{1,9},{9,17},{17,25},{25,1},{2,10},{10... | collective-permute-start | bytes 3932168 | tf_op jit(solution)/shard_map/gather_sequence/ppermute | solution.py:34
  141.0 36.3 %collective-permute-start.16 = (bf16[2048,320]{0,1:T(8,128)(2,1)}, bf16[2048,320]{0,1:T(8,128)(2,1)}, u32[]{:S(2)}, u32[]{:S(2)}) collective-permute-start(bf16[2048,320]{0,1:T(8,128)(2,1)} %copy.112), channel_id=1, source_target_pairs={{0,24},{8,0},{16,8},{24,16},{1,25},{9,1},{17,9},{25,17},{2,26},{10... | collective-permute-start | bytes 3932168 | tf_op jit(solution)/shard_map/gather_sequence/ppermute | solution.py:34
  161.9 5.8 %copy-start.16 = (bf16[128,160]{0,1:T(8,128)(2,1)S(1)}, bf16[128,160]{0,1:T(8,128)(2,1)}, u32[]{:S(2)}) copy-start(bf16[128,160]{0,1:T(8,128)(2,1)} %copy-done.15) | copy-start | bytes 122884
  192.5 25.1 %all-to-all-start = ((f32[64,2,2,128]{3,2,1,0:T(2,128)}), f32[64,2,2,128]{3,2,1,0:T(2,128)}, u32[]{:S(2)}, u32[]{:S(2)}) async-start(f32[64,2,2,128]{3,2,1,0:T(2,128)} %broadcast_in_dim.27), calls=%async_computation | async-start | bytes 262144 | tf_op jit(solution)/shard_map/gather_row_stats/all_to_all | solution.py:234
  203.3 38.7 %collective-permute-start.18 = (bf16[1024,320]{0,1:T(8,128)(2,1)}, bf16[1024,320]{0,1:T(8,128)(2,1)}, u32[]{:S(2)}, u32[]{:S(2)}) collective-permute-start(bf16[1024,320]{0,1:T(8,128)(2,1)} %slice.80), channel_id=1, source_target_pairs={{0,24},{8,0},{16,8},{24,16},{1,25},{9,1},{17,9},{25,17},{2,26},{10... | collective-permute-start | bytes 1966088 | tf_op jit(solution)/shard_map/gather_row_stats/ppermute | solution.py:34
  206.1 37.4 %collective-permute-start.17 = (bf16[1024,320]{0,1:T(8,128)(2,1)}, bf16[1024,320]{0,1:T(8,128)(2,1)}, u32[]{:S(2)}, u32[]{:S(2)}) collective-permute-start(bf16[1024,320]{0,1:T(8,128)(2,1)} %slice.79), channel_id=1, source_target_pairs={{0,8},{8,16},{16,24},{24,0},{1,9},{9,17},{17,25},{25,1},{2,10},{10... | collective-permute-start | bytes 1966088 | tf_op jit(solution)/shard_map/gather_row_stats/ppermute | solution.py:34
  210.6 3.7 %copy-start.26 = (f32[160]{0:T(256)S(1)}, f32[160]{0:T(256)}, u32[]{:S(2)}) copy-start(f32[160]{0:T(256)} %copy-done.25) | copy-start | bytes 1924
  244.9 6.7 %copy-start.9 = (bf16[160,1280]{1,0:T(8,128)(2,1)S(1)}, bf16[160,1280]{1,0:T(8,128)(2,1)}, u32[]{:S(2)}) copy-start(bf16[160,1280]{1,0:T(8,128)(2,1)} %param.15) | copy-start | bytes 1228804
  244.9 6.7 %copy-start.19 = (f32[128,160]{1,0:T(8,128)S(1)}, f32[128,160]{1,0:T(8,128)}, u32[]{:S(2)}) copy-start(f32[128,160]{1,0:T(8,128)} %get-tuple-element.29) | copy-start | bytes 245764
  244.9 6.7 %copy-start.21 = (f32[128,160]{1,0:T(8,128)S(1)}, f32[128,160]{1,0:T(8,128)}, u32[]{:S(2)}) copy-start(f32[128,160]{1,0:T(8,128)} %get-tuple-element.34) | copy-start | bytes 245764
  246.3 5.3 %copy-start.22 = (f32[128,160]{1,0:T(8,128)S(1)}, f32[128,160]{1,0:T(8,128)}, u32[]{:S(2)}) copy-start(f32[128,160]{1,0:T(8,128)} %get-tuple-element.31) | copy-start | bytes 245764
  246.3 6.5 %copy-start.5 = (f32[128,1280]{1,0:T(8,128)S(1)}, f32[128,1280]{1,0:T(8,128)}, u32[]{:S(2)}) copy-start(f32[128,1280]{1,0:T(8,128)} %copy-done.4) | copy-start | bytes 1966084
  246.3 6.5 %copy-start.17 = (f32[128,160]{1,0:T(8,128)S(1)}, f32[128,160]{1,0:T(8,128)}, u32[]{:S(2)}) copy-start(f32[128,160]{1,0:T(8,128)} %get-tuple-element.35) | copy-start | bytes 245764
  246.3 6.5 %copy-start.18 = (f32[128,160]{1,0:T(8,128)S(1)}, f32[128,160]{1,0:T(8,128)}, u32[]{:S(2)}) copy-start(f32[128,160]{1,0:T(8,128)} %get-tuple-element.38) | copy-start | bytes 245764
  246.3 6.5 %copy-start.20 = (f32[128,160]{1,0:T(8,128)S(1)}, f32[128,160]{1,0:T(8,128)}, u32[]{:S(2)}) copy-start(f32[128,160]{1,0:T(8,128)} %get-tuple-element.36) | copy-start | bytes 245764
  254.1 13.1 %copy-start.11 = (bf16[128,320]{0,1:T(8,128)(2,1)S(1)}, bf16[128,320]{0,1:T(8,128)(2,1)}, u32[]{:S(2)}) copy-start(bf16[128,320]{0,1:T(8,128)(2,1)} %param.11) | copy-start | bytes 245764
  254.1 13.1 %copy-start.12 = (bf16[128,320]{0,1:T(8,128)(2,1)S(1)}, bf16[128,320]{0,1:T(8,128)(2,1)}, u32[]{:S(2)}) copy-start(bf16[128,320]{0,1:T(8,128)(2,1)} %param.12) | copy-start | bytes 245764
  254.1 13.1 %copy-start.32 = (f32[128]{0:T(128)S(1)}, f32[128]{0:T(128)}, u32[]{:S(2)}) copy-start(f32[128]{0:T(128)} %copy-done.31) | copy-start | bytes 1540
  (7 other events, 11.4 us)
Sparse Core Ops, SparseCore 0:
  38.4 102.4 all-gather.1

commit v9 on v7

--- a/solution.py
+++ b/solution.py
@@ -106,7 +106,8 @@
     with jax.named_scope("gather_sequence"):
         kv = jnp.concatenate([keys, values], axis=1)
         qg = jnp.concatenate([queries, head_grads], axis=1)
-        kv_all = lax.all_gather(kv, "y", axis=0, tiled=True)
+        kv_ahead, kv_behind = ring4_first(kv, "y")
+        kv_all = jnp.concatenate(ring4_last(kv, kv_ahead, kv_behind, "y"), axis=0)
         kv_all = lax.all_gather(kv_all, "z", axis=0, tiled=True)
         qg_z = jnp.concatenate(ring_gather(qg, "z", z_size), axis=0)
         qg_ahead, qg_behind = ring4_first(qg_z, "y")
@@ -118,7 +119,8 @@
     abs_z = (z_index + rel_z) % z_size
     abs_y = (y_index + rel_y) % y_size
     qg_source = (abs_z[None, :] * y_size + abs_y[:, None]).reshape(shards)
-    key_positions = block_positions(offsets, all_rows)
+    kv_source = (lax.iota(jnp.int32, z_size)[:, None] * y_size + abs_y[None, :]).reshape(shards)
+    key_positions = block_positions(offsets[kv_source], all_rows)
     seq_index = z_index * y_size + y_index
     own_positions = offsets[seq_index] * PIECE + lax.iota(jnp.int32, row_count)
 

time: 242 us -> 248 us (1.025)
  starting transfers between devices: 77.2 us -> 92.7 us
  blocking collectives: 40.2 us -> 26 us
  waiting for transfers between devices: 26.5 us -> 29.2 us
    ppermute x19 -> x23, starting transfers between devices: 68.4 us -> 83.3 us  [shift(): lax.ppermute(data, axis, [(i, (i + step) % size) for i in range(size)])]
    all_gather x1 -> x0, blocking collectives: 14.6 us -> none  [per_device(): kv_all = lax.all_gather(kv, 'y', axis=0, tiled=True)]
    ppermute x19 -> x23, waiting for transfers between devices: 23.9 us -> 26.6 us  [shift(): lax.ppermute(data, axis, [(i, (i + step) % size) for i in range(size)])]
  transfers between devices with their start and end apart: 21 -> 25, of which waited for: 13 -> 15; matrix products, arithmetic and copies ran while one was open for 26% -> 25% of each run, Pallas kernels for 0% -> 0%
where the time goes in v9:
time: 248 us; the launch traced here: 245 us
  starting transfers between devices  92.7 us (37%)
  local copies, waits for them, and re-layouts  37.9 us (15%)
  matrix products  36.1 us (15%)
  waiting for transfers between devices  29.2 us (12%)
  blocking collectives  26 us (10%)
  between operations  15.1 us (6%)
  other arithmetic  8.35 us (3%)
    ppermute x23, starting transfers between devices, shift(): lax.ppermute(data, axis, [(i, (i + step) % size) for i in range(size)])  83.3 us
    ppermute x23, waiting for transfers between devices, shift(): lax.ppermute(data, axis, [(i, (i + step) % size) for i in range(size)])  26.6 us
    all_gather x1, blocking collectives, per_device(): gathered = lax.all_gather(both, 'tp', axis=1, tiled=True)  13.4 us
    unnamed x90, local copies, waits for them, and re-layouts  12.7 us
    all_to_all x1, blocking collectives, per_device(): received = lax.all_to_all(payload, 'tp', 0, 0, tiled=False)  12.6 us
    dot_general x4, matrix products, per_device(): jnp.einsum('hkq,qhd->khd', score_grad, query_part, preferred_element_type...  12.2 us
    all_to_all x1, starting transfers between devices, per_device(): stats_all = lax.all_to_all(sent, ('z', 'y'), 0, 0, tiled=False)  9.39 us
    dot_general x4, matrix products, per_device(): jnp.einsum('khd,qhd->hkq', key_heads, query_part, preferred_element_type=...  6.32 us
  transfers between devices with their start and end apart: 25, of which 15 were waited for; matrix products, arithmetic and copies ran while one was open for 25% of the time, Pallas kernels for 0%

profile of v9, /device:TPU:24, one launch (start us, length us, event | category | flops | bytes accessed | tf_op | source)
XLA Modules:
  0.0 245.3 jit_solution(5334590305703461804)
XLA Ops:
  7.5 13.4 %all_gather.6 = bf16[128,2560]{0,1:T(8,128)(2,1)S(1)} all-gather(bf16[128,640]{0,1:T(8,128)(2,1)S(1)} %pad_maximum_fusion.1), channel_id=1, replica_groups=mesh['z'=16,'y'=4,'tp'=4,'dp'=2] {'tp'}, dimensions={1}, use_global_device_ids=true | all-gather | bytes 819200 | tf_op jit(solution)/shard_map/gather_features/all_gather | solution.py:77
  22.9 7.2 %collective-permute-start.1 = (bf16[128,320]{0,1:T(8,128)(2,1)S(1)}, bf16[128,320]{0,1:T(8,128)(2,1)S(1)}, u32[]{:S(2)}, u32[]{:S(2)}) collective-permute-start(bf16[128,320]{0,1:T(8,128)(2,1)S(1)} %pad_maximum_fusion.2), channel_id=1, source_target_pairs={{0,8},{8,16},{16,24},{24,0},{1,9},{9,17},{17,25},{25,1},{2,10},{10... | collective-permute-start | bytes 245768 | tf_op jit(solution)/shard_map/gather_sequence/ppermute | solution.py:32
  30.1 1.9 collective-permute-start
  32.2 5.5 %collective-permute-start.2 = (bf16[64,320]{0,1:T(8,128)(2,1)S(1)}, bf16[64,320]{0,1:T(8,128)(2,1)S(1)}, u32[]{:S(2)}, u32[]{:S(2)}) collective-permute-start(bf16[64,320]{0,1:T(8,128)(2,1)S(1)} %bitcast.203), channel_id=1, source_target_pairs={{0,8},{8,16},{16,24},{24,0},{1,9},{9,17},{17,25},{25,1},{2,10},{10... | collective-permute-start | bytes 122888 | tf_op jit(solution)/shard_map/gather_sequence/ppermute | solution.py:32
  37.8 1.9 collective-permute-start.3
  39.7 5.6 %collective-permute-done.3 = bf16[64,320]{0,1:T(8,128)(2,1)S(1)} collective-permute-done((bf16[64,320]{0,1:T(8,128)(2,1)S(1)}, bf16[64,320]{0,1:T(8,128)(2,1)S(1)}, u32[]{:S(2)}, u32[]{:S(2)}) %collective-permute-start.3) | collective-permute-done | bytes 40992 | tf_op jit(solution)/shard_map/gather_sequence/ppermute | solution.py:32
  47.5 6.4 %collective-permute-start.4 = (bf16[128,320]{0,1:T(8,128)(2,1)S(1)}, bf16[128,320]{0,1:T(8,128)(2,1)S(1)}, u32[]{:S(2)}, u32[]{:S(2)}) collective-permute-start(bf16[128,320]{0,1:T(8,128)(2,1)S(1)} %get-tuple-element.35), channel_id=1, source_target_pairs={{0,480},{32,0},{64,32},{96,64},{128,96},{160,128},{192,160},{224,1... | collective-permute-start | bytes 245768 | tf_op jit(solution)/shard_map/gather_sequence/ppermute | solution.py:32
  53.9 1.9 collective-permute-start.11
  62.0 1.6 broadcast_compare_fusion.4
  63.6 5.1 %collective-permute-start.5 = (bf16[128,320]{0,1:T(8,128)(2,1)S(1)}, bf16[128,320]{0,1:T(8,128)(2,1)S(1)}, u32[]{:S(2)}, u32[]{:S(2)}) collective-permute-start(bf16[128,320]{0,1:T(8,128)(2,1)S(1)} %collective-permute-done.4), channel_id=1, source_target_pairs={{0,480},{32,0},{64,32},{96,64},{128,96},{160,128},{192,160},{224,1... | collective-permute-start | bytes 245768 | tf_op jit(solution)/shard_map/gather_sequence/ppermute | solution.py:32
  68.8 1.9 collective-permute-start.12
  72.3 5.6 %collective-permute-start.6 = (bf16[128,320]{0,1:T(8,128)(2,1)S(1)}, bf16[128,320]{0,1:T(8,128)(2,1)S(1)}, u32[]{:S(2)}, u32[]{:S(2)}) collective-permute-start(bf16[128,320]{0,1:T(8,128)(2,1)S(1)} %collective-permute-done.5), channel_id=1, source_target_pairs={{0,480},{32,0},{64,32},{96,64},{128,96},{160,128},{192,160},{224,1... | collective-permute-start | bytes 245768 | tf_op jit(solution)/shard_map/gather_sequence/ppermute | solution.py:32
  77.9 1.9 collective-permute-start.13
  81.6 5.6 %collective-permute-start.7 = (bf16[128,320]{0,1:T(8,128)(2,1)S(1)}, bf16[128,320]{0,1:T(8,128)(2,1)S(1)}, u32[]{:S(2)}, u32[]{:S(2)}) collective-permute-start(bf16[128,320]{0,1:T(8,128)(2,1)S(1)} %collective-permute-done.6), channel_id=1, source_target_pairs={{0,480},{32,0},{64,32},{96,64},{128,96},{160,128},{192,160},{224,1... | collective-permute-start | bytes 245768 | tf_op jit(solution)/shard_map/gather_sequence/ppermute | solution.py:32
  87.4 1.9 collective-permute-start.14
  90.2 5.6 %collective-permute-start.8 = (bf16[128,320]{0,1:T(8,128)(2,1)S(1)}, bf16[128,320]{0,1:T(8,128)(2,1)S(1)}, u32[]{:S(2)}, u32[]{:S(2)}) collective-permute-start(bf16[128,320]{0,1:T(8,128)(2,1)S(1)} %collective-permute-done.7), channel_id=1, source_target_pairs={{0,480},{32,0},{64,32},{96,64},{128,96},{160,128},{192,160},{224,1... | collective-permute-start | bytes 245768 | tf_op jit(solution)/shard_map/gather_sequence/ppermute | solution.py:32
  96.9 1.9 collective-permute-start.15
  100.0 5.6 %collective-permute-start.9 = (bf16[128,320]{0,1:T(8,128)(2,1)S(1)}, bf16[128,320]{0,1:T(8,128)(2,1)S(1)}, u32[]{:S(2)}, u32[]{:S(2)}) collective-permute-start(bf16[128,320]{0,1:T(8,128)(2,1)S(1)} %collective-permute-done.8), channel_id=1, source_target_pairs={{0,480},{32,0},{64,32},{96,64},{128,96},{160,128},{192,160},{224,1... | collective-permute-start | bytes 245768 | tf_op jit(solution)/shard_map/gather_sequence/ppermute | solution.py:32
  106.4 1.9 collective-permute-start.16
  109.5 5.6 %collective-permute-start.10 = (bf16[128,320]{0,1:T(8,128)(2,1)S(1)}, bf16[128,320]{0,1:T(8,128)(2,1)S(1)}, u32[]{:S(2)}, u32[]{:S(2)}) collective-permute-start(bf16[128,320]{0,1:T(8,128)(2,1)S(1)} %collective-permute-done.9), channel_id=1, source_target_pairs={{0,480},{32,0},{64,32},{96,64},{128,96},{160,128},{192,160},{224,1... | collective-permute-start | bytes 245768 | tf_op jit(solution)/shard_map/gather_sequence/ppermute | solution.py:32
  115.6 1.9 collective-permute-start.17
  118.2 6.6 %collective-permute-done.17 = bf16[128,320]{0,1:T(8,128)(2,1)S(1)} collective-permute-done((bf16[128,320]{0,1:T(8,128)(2,1)S(1)}, bf16[128,320]{0,1:T(8,128)(2,1)S(1)}, u32[]{:S(2)}, u32[]{:S(2)}) %collective-permute-start.17) | collective-permute-done | bytes 81952 | tf_op jit(solution)/shard_map/gather_sequence/ppermute | solution.py:32
  124.8 1.9 collective-permute-start.18
  127.5 5.4 %collective-permute-done.18 = bf16[128,320]{0,1:T(8,128)(2,1)S(1)} collective-permute-done((bf16[128,320]{0,1:T(8,128)(2,1)S(1)}, bf16[128,320]{0,1:T(8,128)(2,1)S(1)}, u32[]{:S(2)}, u32[]{:S(2)}) %collective-permute-start.18) | collective-permute-done | bytes 81952 | tf_op jit(solution)/shard_map/gather_sequence/ppermute | solution.py:32
  138.0 1.9 collective-permute-start.19
  140.0 4.1 %collective-permute-start.20 = (bf16[2048,320]{0,1:T(8,128)(2,1)}, bf16[2048,320]{0,1:T(8,128)(2,1)}, u32[]{:S(2)}, u32[]{:S(2)}) collective-permute-start(bf16[2048,320]{0,1:T(8,128)(2,1)} %constant_dynamic-update-slice_fusion), channel_id=1, source_target_pairs={{0,24},{8,0},{16,8},{24,16},{1,25},{9,1},{17,9},{25,17},{2,26},{10... | collective-permute-start | bytes 3932168 | tf_op jit(solution)/shard_map/gather_sequence/ppermute | solution.py:32
  144.1 2.3 fusion.72
  146.3 3.0 %fusion.71 = (bf16[8192,160]{0,1:T(8,128)(2,1)S(1)}, bf16[8192,160]{0,1:T(8,128)(2,1)S(1)}) fusion(bf16[8192,320]{0,1:T(8,128)(2,1)} %all-gather.2.cloned.1.call-done), kind=kLoop, calls=%fused_computation.166 | loop fusion | bytes 10485760 | tf_op jit(solution)/shard_map/gather_sequence/slice | solution.py:115
  149.3 1.8 select_reduce_fusion.1
  151.1 2.5 %select_reduce_fusion = f32[2,128]{1,0:T(2,128)S(1)} fusion(f32[2,128,8192]{2,1,0:T(8,128)S(1)} %get-tuple-element.54, f32[2,128]{1,0:T(2,128)S(1)} %get-tuple-element.53, pred[128,8192]{1,0:T(8,128)(4,1)S(1)} %broadcast_compare_fusion), kind=kLoop, calls=%fused_computation.11 | loop fusion | flops 8388352 | bytes 9439232 | tf_op jit(solution)/shard_map/query_pass/reduce_sum | solution.py:139
  153.6 3.5 %fusion.77 = (f32[2,128]{1,0:T(2,128)S(1)}, bf16[2,128,8192]{2,1,0:T(8,128)(2,1)S(1)}) fusion(bf16[128,2,80]{0,2,1:T(8,128)(2,1)S(1)} %bitcast.201, bf16[8192,2,80]{0,2,1:T(8,128)(2,1)S(1)} %bitcast.187, f32[2,128,8192]{2,1,0:T(8,128)S(1)} %get-tuple-element.54, f32[2,128]{1,0:T(2,128)S(1)} %log_add_fusion, pred[128,8192]{1,0:T(8,128)(4,1)S(1)} %broadcast_compare_fusion), kind=kOutput, calls=%fused_computation.172 | convolution fusion | flops 346029824 | bytes 16295936 | tf_op jit(solution)/shard_map/query_pass/qhd,khd->hqk/dot_general | solution.py:142
  157.1 2.0 fusion.43
  161.9 2.9 %collective-permute-done.20 = bf16[2048,320]{0,1:T(8,128)(2,1)} collective-permute-done((bf16[2048,320]{0,1:T(8,128)(2,1)}, bf16[2048,320]{0,1:T(8,128)(2,1)}, u32[]{:S(2)}, u32[]{:S(2)}) %collective-permute-start.20) | collective-permute-done | bytes 1310752 | tf_op jit(solution)/shard_map/gather_sequence/ppermute | solution.py:32
  165.5 9.4 %all-to-all-start = ((f32[64,2,2,128]{3,2,1,0:T(2,128)}), f32[64,2,2,128]{3,2,1,0:T(2,128)S(1)}, u32[]{:S(2)}, u32[]{:S(2)}) async-start(f32[64,2,2,128]{3,2,1,0:T(2,128)} %broadcast_in_dim.98), calls=%async_computation | async-start | bytes 262144 | tf_op jit(solution)/shard_map/gather_row_stats/all_to_all | solution.py:165
  175.8 2.4 collective-permute-start.21
  178.1 2.0 slice.144
  180.1 3.7 %collective-permute-start.22 = (bf16[1024,320]{0,1:T(8,128)(2,1)}, bf16[1024,320]{0,1:T(8,128)(2,1)}, u32[]{:S(2)}, u32[]{:S(2)}) collective-permute-start(bf16[1024,320]{0,1:T(8,128)(2,1)} %slice.144), channel_id=1, source_target_pairs={{0,24},{8,0},{16,8},{24,16},{1,25},{9,1},{17,9},{25,17},{2,26},{10... | collective-permute-start | bytes 1966088 | tf_op jit(solution)/shard_map/gather_row_stats/ppermute | solution.py:32
  183.8 2.8 %fusion.73 = (bf16[2048,160]{0,1:T(8,128)(2,1)}, bf16[2048,160]{0,1:T(8,128)(2,1)}, bf16[2048,160]{0,1:T(8,128)(2,1)}, bf16[2048,160]{0,1:T(8,128)(2,1)}) fusion(bf16[2048,320]{0,1:T(8,128)(2,1)} %collective-permute-done.20, bf16[2048,320]{0,1:T(8,128)(2,1)S(1)} %collective-permute-done.19), kind=kLoop, calls=%fused_computation.168 | loop fusion | bytes 5242880 | tf_op jit(solution)/shard_map/key_pass/slice | solution.py:174
  186.7 2.6 %all-to-all-done = f32[64,2,2,128]{3,2,1,0:T(2,128)S(1)} async-done(((f32[64,2,2,128]{3,2,1,0:T(2,128)}), f32[64,2,2,128]{3,2,1,0:T(2,128)S(1)}, u32[]{:S(2)}, u32[]{:S(2)}) %all-to-all-start) | async-done | bytes 131104 | tf_op jit(solution)/shard_map/gather_row_stats/all_to_all | solution.py:165
  192.5 1.9 fusion.10
  195.5 2.7 %fusion.25 = f32[2,80,128]{2,1,0:T(8,128)} fusion(bf16[2048,2,80]{0,2,1:T(8,128)(2,1)} %bitcast.178, f32[2,128,2048]{2,1,0:T(8,128)S(1)} %fusion.10, bf16[128,2,80]{0,2,1:T(8,128)(2,1)S(1)} %bitcast.190, bf16[2048,2,80]{0,2,1:T(8,128)(2,1)} %bitcast.179, f32[2,2048]{1,0:T(2,128)S(1)} %get-tuple-element.43), kind=kOutput, calls=%fused_computation.48 | convolution fusion | flops 169345024 | bytes 3547136 | tf_op jit(solution)/shard_map/key_pass/hkq,qhd->khd/dot_general | solution.py:194
  198.3 1.8 fusion.16
  200.1 3.4 %fusion.27 = f32[2,80,128]{2,1,0:T(8,128)} fusion(bf16[2048,2,80]{0,2,1:T(8,128)(2,1)} %bitcast.176, f32[2,128,2048]{2,1,0:T(8,128)S(1)} %fusion.16, bf16[128,2,80]{0,2,1:T(8,128)(2,1)S(1)} %bitcast.191, bf16[2048,2,80]{0,2,1:T(8,128)(2,1)} %bitcast.173, f32[2,2048]{1,0:T(2,128)S(1)} %get-tuple-element.39), kind=kOutput, calls=%fused_computation.50 | convolution fusion | flops 169345024 | bytes 3547136 | tf_op jit(solution)/shard_map/key_pass/hkq,qhd->khd/dot_general | solution.py:194
  203.5 1.9 fusion.19
  206.7 1.6 gather_fusion.6
  214.6 3.4 %fusion.26 = f32[2,80,128]{2,1,0:T(8,128)} fusion(bf16[2048,2,80]{0,2,1:T(8,128)(2,1)} %bitcast.184, f32[2,128,2048]{2,1,0:T(8,128)} %copy-done.4, bf16[128,2,80]{0,2,1:T(8,128)(2,1)S(1)} %bitcast.192, bf16[2048,2,80]{0,2,1:T(8,128)(2,1)} %bitcast.182, f32[2,2048]{1,0:T(2,128)S(1)} %copy-done.28), kind=kOutput, calls=%fused_computation.49 | convolution fusion | flops 169345024 | bytes 3547136 | tf_op jit(solution)/shard_map/key_pass/hkq,qhd->khd/dot_general | solution.py:194
  218.1 2.6 %fusion.48 = bf16[2,80,128]{2,1,0:T(8,128)(2,1)} fusion(f32[2,80,128]{2,1,0:T(8,128)S(1)} %copy-done.20, f32[2,80,128]{2,1,0:T(8,128)} %fusion.26, f32[2,80,128]{2,1,0:T(8,128)S(1)} %copy-done.22, bf16[2048,2,80]{0,2,1:T(8,128)(2,1)} %bitcast.172, f32[2,128,2048]{2,1,0:T(8,128)S(1)} %fusion.19, bf16[128,2,80]{0,2,1:T(8,128)(2,1)S(1)} %bitcast.193, ...), kind=kOutput, calls=%fused_computation.66 | convolution fusion | flops 169426944 | bytes 3751936 | tf_op jit(solution)/shard_map/key_pass/hkq,qhd->khd/dot_general | solution.py:194
  225.0 12.6 %all_to_all.10 = f32[4,129,320]{2,1,0:T(8,128)S(1)} all-to-all(f32[4,129,320]{2,1,0:T(8,128)S(1)} %copy.31), channel_id=1, replica_groups=mesh['z'=16,'y'=4,'tp'=4,'dp'=2] {'tp'}, dimensions={0} | all-to-all | bytes 1320960 | tf_op jit(solution)/shard_map/back_projection/all_to_all | solution.py:216
  (191 shorter events, 47.7 us)
Async XLA Ops:
  6.5 15.8 %copy-start = (bf16[160,1280]{1,0:T(8,128)(2,1)S(1)}, bf16[160,1280]{1,0:T(8,128)(2,1)}, u32[]{:S(2)}) copy-start(bf16[160,1280]{1,0:T(8,128)(2,1)} %param.16) | copy-start | bytes 1228804
  6.5 139.8 %all-gather.2.cloned.1.call-start = ((), (), s32[]{:S(2)}) async-start(), calls=%async_computation.2 | async-start | bytes 5570560 | tf_op jit(solution)/shard_map/gather_sequence/all_gather | solution.py:111
  7.5 14.0 %copy-start.29 = (f32[1280]{0:T(1024)S(1)}, f32[1280]{0:T(1024)}, u32[]{:S(2)}) copy-start(f32[1280]{0:T(1024)} %param.13) | copy-start | bytes 15364
  21.5 24.7 %copy-start.36 = (f32[80]{0:T(128)S(1)}, f32[80]{0:T(128)}, u32[]{:S(2)}) copy-start(f32[80]{0:T(128)} %param.18) | copy-start | bytes 964
  21.5 24.8 %copy-start.18 = (bf16[160,1280]{1,0:T(8,128)(2,1)S(1)}, bf16[160,1280]{1,0:T(8,128)(2,1)}, u32[]{:S(2)}) copy-start(bf16[160,1280]{1,0:T(8,128)(2,1)} %param.17) | copy-start | bytes 1228804
  21.5 25.0 %copy-start.34 = (f32[128]{0:T(128)}, f32[128]{0:T(128)S(1)}, u32[]{:S(2)}) copy-start(f32[128]{0:T(128)S(1)} %add_rsqrt_fusion) | copy-start | bytes 1540
  22.4 24.2 %copy-start.12 = (bf16[160,1280]{1,0:T(8,128)(2,1)S(1)}, bf16[160,1280]{1,0:T(8,128)(2,1)}, u32[]{:S(2)}) copy-start(bf16[160,1280]{1,0:T(8,128)(2,1)} %param.14) | copy-start | bytes 1228804
  22.6 33.4 %copy-start.1 = (s32[64]{0:T(128)S(1)}, s32[64]{0:T(128)}, u32[]{:S(2)}) copy-start(s32[64]{0:T(128)} %param.19) | copy-start | bytes 772
  22.9 9.2 %collective-permute-start.1 = (bf16[128,320]{0,1:T(8,128)(2,1)S(1)}, bf16[128,320]{0,1:T(8,128)(2,1)S(1)}, u32[]{:S(2)}, u32[]{:S(2)}) collective-permute-start(bf16[128,320]{0,1:T(8,128)(2,1)S(1)} %pad_maximum_fusion.2), channel_id=1, source_target_pairs={{0,8},{8,16},{16,24},{24,0},{1,9},{9,17},{17,25},{25,1},{2,10},{10... | collective-permute-start | bytes 245768 | tf_op jit(solution)/shard_map/gather_sequence/ppermute | solution.py:32
  30.1 7.5 %collective-permute-start = (bf16[128,320]{0,1:T(8,128)(2,1)S(1)}, bf16[128,320]{0,1:T(8,128)(2,1)S(1)}, u32[]{:S(2)}, u32[]{:S(2)}) collective-permute-start(bf16[128,320]{0,1:T(8,128)(2,1)S(1)} %pad_maximum_fusion.2), channel_id=1, source_target_pairs={{0,24},{8,0},{16,8},{24,16},{1,25},{9,1},{17,9},{25,17},{2,26},{10... | collective-permute-start | bytes 245768 | tf_op jit(solution)/shard_map/gather_sequence/ppermute | solution.py:32
  32.2 7.5 %collective-permute-start.2 = (bf16[64,320]{0,1:T(8,128)(2,1)S(1)}, bf16[64,320]{0,1:T(8,128)(2,1)S(1)}, u32[]{:S(2)}, u32[]{:S(2)}) collective-permute-start(bf16[64,320]{0,1:T(8,128)(2,1)S(1)} %bitcast.203), channel_id=1, source_target_pairs={{0,8},{8,16},{16,24},{24,0},{1,9},{9,17},{17,25},{25,1},{2,10},{10... | collective-permute-start | bytes 122888 | tf_op jit(solution)/shard_map/gather_sequence/ppermute | solution.py:32
  37.8 7.5 %collective-permute-start.3 = (bf16[64,320]{0,1:T(8,128)(2,1)S(1)}, bf16[64,320]{0,1:T(8,128)(2,1)S(1)}, u32[]{:S(2)}, u32[]{:S(2)}) collective-permute-start(bf16[64,320]{0,1:T(8,128)(2,1)S(1)} %slice.179), channel_id=1, source_target_pairs={{0,24},{8,0},{16,8},{24,16},{1,25},{9,1},{17,9},{25,17},{2,26},{10... | collective-permute-start | bytes 122888 | tf_op jit(solution)/shard_map/gather_sequence/ppermute | solution.py:32
  46.6 15.5 %copy-start.25 = (bf16[128,160]{0,1:T(8,128)(2,1)}, bf16[128,160]{0,1:T(8,128)(2,1)S(1)}, u32[]{:S(2)}) copy-start(bf16[128,160]{0,1:T(8,128)(2,1)S(1)} %convolution_convert_fusion) | copy-start | bytes 122884
  47.5 16.1 %collective-permute-start.4 = (bf16[128,320]{0,1:T(8,128)(2,1)S(1)}, bf16[128,320]{0,1:T(8,128)(2,1)S(1)}, u32[]{:S(2)}, u32[]{:S(2)}) collective-permute-start(bf16[128,320]{0,1:T(8,128)(2,1)S(1)} %get-tuple-element.35), channel_id=1, source_target_pairs={{0,480},{32,0},{64,32},{96,64},{128,96},{160,128},{192,160},{224,1... | collective-permute-start | bytes 245768 | tf_op jit(solution)/shard_map/gather_sequence/ppermute | solution.py:32
  53.9 14.9 %collective-permute-start.11 = (bf16[128,320]{0,1:T(8,128)(2,1)S(1)}, bf16[128,320]{0,1:T(8,128)(2,1)S(1)}, u32[]{:S(2)}, u32[]{:S(2)}) collective-permute-start(bf16[128,320]{0,1:T(8,128)(2,1)S(1)} %get-tuple-element.35), channel_id=1, source_target_pairs={{0,32},{32,64},{64,96},{96,128},{128,160},{160,192},{192,224},{224... | collective-permute-start | bytes 245768 | tf_op jit(solution)/shard_map/gather_sequence/ppermute | solution.py:32
  57.6 3.6 %copy-start.33 = (s32[1024]{0:T(1024)}, s32[1024]{0:T(1024)S(1)}, u32[]{:S(2)}) copy-start(s32[1024]{0:T(1024)S(1)} %get-tuple-element.61) | copy-start | bytes 12292
  63.6 8.6 %collective-permute-start.5 = (bf16[128,320]{0,1:T(8,128)(2,1)S(1)}, bf16[128,320]{0,1:T(8,128)(2,1)S(1)}, u32[]{:S(2)}, u32[]{:S(2)}) collective-permute-start(bf16[128,320]{0,1:T(8,128)(2,1)S(1)} %collective-permute-done.4), channel_id=1, source_target_pairs={{0,480},{32,0},{64,32},{96,64},{128,96},{160,128},{192,160},{224,1... | collective-permute-start | bytes 245768 | tf_op jit(solution)/shard_map/gather_sequence/ppermute | solution.py:32
  68.8 9.1 %collective-permute-start.12 = (bf16[128,320]{0,1:T(8,128)(2,1)S(1)}, bf16[128,320]{0,1:T(8,128)(2,1)S(1)}, u32[]{:S(2)}, u32[]{:S(2)}) collective-permute-start(bf16[128,320]{0,1:T(8,128)(2,1)S(1)} %collective-permute-done.11), channel_id=1, source_target_pairs={{0,32},{32,64},{64,96},{96,128},{128,160},{160,192},{192,224},{224... | collective-permute-start | bytes 245768 | tf_op jit(solution)/shard_map/gather_sequence/ppermute | solution.py:32
  72.3 9.3 %collective-permute-start.6 = (bf16[128,320]{0,1:T(8,128)(2,1)S(1)}, bf16[128,320]{0,1:T(8,128)(2,1)S(1)}, u32[]{:S(2)}, u32[]{:S(2)}) collective-permute-start(bf16[128,320]{0,1:T(8,128)(2,1)S(1)} %collective-permute-done.5), channel_id=1, source_target_pairs={{0,480},{32,0},{64,32},{96,64},{128,96},{160,128},{192,160},{224,1... | collective-permute-start | bytes 245768 | tf_op jit(solution)/shard_map/gather_sequence/ppermute | solution.py:32
  77.9 9.5 %collective-permute-start.13 = (bf16[128,320]{0,1:T(8,128)(2,1)S(1)}, bf16[128,320]{0,1:T(8,128)(2,1)S(1)}, u32[]{:S(2)}, u32[]{:S(2)}) collective-permute-start(bf16[128,320]{0,1:T(8,128)(2,1)S(1)} %collective-permute-done.12), channel_id=1, source_target_pairs={{0,32},{32,64},{64,96},{96,128},{128,160},{160,192},{192,224},{224... | collective-permute-start | bytes 245768 | tf_op jit(solution)/shard_map/gather_sequence/ppermute | solution.py:32
  81.6 8.7 %collective-permute-start.7 = (bf16[128,320]{0,1:T(8,128)(2,1)S(1)}, bf16[128,320]{0,1:T(8,128)(2,1)S(1)}, u32[]{:S(2)}, u32[]{:S(2)}) collective-permute-start(bf16[128,320]{0,1:T(8,128)(2,1)S(1)} %collective-permute-done.6), channel_id=1, source_target_pairs={{0,480},{32,0},{64,32},{96,64},{128,96},{160,128},{192,160},{224,1... | collective-permute-start | bytes 245768 | tf_op jit(solution)/shard_map/gather_sequence/ppermute | solution.py:32
  87.4 9.5 %collective-permute-start.14 = (bf16[128,320]{0,1:T(8,128)(2,1)S(1)}, bf16[128,320]{0,1:T(8,128)(2,1)S(1)}, u32[]{:S(2)}, u32[]{:S(2)}) collective-permute-start(bf16[128,320]{0,1:T(8,128)(2,1)S(1)} %collective-permute-done.13), channel_id=1, source_target_pairs={{0,32},{32,64},{64,96},{96,128},{128,160},{160,192},{192,224},{224... | collective-permute-start | bytes 245768 | tf_op jit(solution)/shard_map/gather_sequence/ppermute | solution.py:32
  90.2 9.8 %collective-permute-start.8 = (bf16[128,320]{0,1:T(8,128)(2,1)S(1)}, bf16[128,320]{0,1:T(8,128)(2,1)S(1)}, u32[]{:S(2)}, u32[]{:S(2)}) collective-permute-start(bf16[128,320]{0,1:T(8,128)(2,1)S(1)} %collective-permute-done.7), channel_id=1, source_target_pairs={{0,480},{32,0},{64,32},{96,64},{128,96},{160,128},{192,160},{224,1... | collective-permute-start | bytes 245768 | tf_op jit(solution)/shard_map/gather_sequence/ppermute | solution.py:32
  96.9 9.4 %collective-permute-start.15 = (bf16[128,320]{0,1:T(8,128)(2,1)S(1)}, bf16[128,320]{0,1:T(8,128)(2,1)S(1)}, u32[]{:S(2)}, u32[]{:S(2)}) collective-permute-start(bf16[128,320]{0,1:T(8,128)(2,1)S(1)} %collective-permute-done.14), channel_id=1, source_target_pairs={{0,32},{32,64},{64,96},{96,128},{128,160},{160,192},{192,224},{224... | collective-permute-start | bytes 245768 | tf_op jit(solution)/shard_map/gather_sequence/ppermute | solution.py:32
  100.0 9.5 %collective-permute-start.9 = (bf16[128,320]{0,1:T(8,128)(2,1)S(1)}, bf16[128,320]{0,1:T(8,128)(2,1)S(1)}, u32[]{:S(2)}, u32[]{:S(2)}) collective-permute-start(bf16[128,320]{0,1:T(8,128)(2,1)S(1)} %collective-permute-done.8), channel_id=1, source_target_pairs={{0,480},{32,0},{64,32},{96,64},{128,96},{160,128},{192,160},{224,1... | collective-permute-start | bytes 245768 | tf_op jit(solution)/shard_map/gather_sequence/ppermute | solution.py:32
  106.4 9.3 %collective-permute-start.16 = (bf16[128,320]{0,1:T(8,128)(2,1)S(1)}, bf16[128,320]{0,1:T(8,128)(2,1)S(1)}, u32[]{:S(2)}, u32[]{:S(2)}) collective-permute-start(bf16[128,320]{0,1:T(8,128)(2,1)S(1)} %collective-permute-done.15), channel_id=1, source_target_pairs={{0,32},{32,64},{64,96},{96,128},{128,160},{160,192},{192,224},{224... | collective-permute-start | bytes 245768 | tf_op jit(solution)/shard_map/gather_sequence/ppermute | solution.py:32
  109.5 17.3 %collective-permute-start.10 = (bf16[128,320]{0,1:T(8,128)(2,1)S(1)}, bf16[128,320]{0,1:T(8,128)(2,1)S(1)}, u32[]{:S(2)}, u32[]{:S(2)}) collective-permute-start(bf16[128,320]{0,1:T(8,128)(2,1)S(1)} %collective-permute-done.9), channel_id=1, source_target_pairs={{0,480},{32,0},{64,32},{96,64},{128,96},{160,128},{192,160},{224,1... | collective-permute-start | bytes 245768 | tf_op jit(solution)/shard_map/gather_sequence/ppermute | solution.py:32
  115.6 9.2 %collective-permute-start.17 = (bf16[128,320]{0,1:T(8,128)(2,1)S(1)}, bf16[128,320]{0,1:T(8,128)(2,1)S(1)}, u32[]{:S(2)}, u32[]{:S(2)}) collective-permute-start(bf16[128,320]{0,1:T(8,128)(2,1)S(1)} %collective-permute-done.16), channel_id=1, source_target_pairs={{0,32},{32,64},{64,96},{96,128},{128,160},{160,192},{192,224},{224... | collective-permute-start | bytes 245768 | tf_op jit(solution)/shard_map/gather_sequence/ppermute | solution.py:32
  124.8 8.0 %collective-permute-start.18 = (bf16[128,320]{0,1:T(8,128)(2,1)S(1)}, bf16[128,320]{0,1:T(8,128)(2,1)S(1)}, u32[]{:S(2)}, u32[]{:S(2)}) collective-permute-start(bf16[128,320]{0,1:T(8,128)(2,1)S(1)} %collective-permute-done.17), channel_id=1, source_target_pairs={{0,32},{32,64},{64,96},{96,128},{128,160},{160,192},{192,224},{224... | collective-permute-start | bytes 245768 | tf_op jit(solution)/shard_map/gather_sequence/ppermute | solution.py:32
  138.0 23.8 %collective-permute-start.19 = (bf16[2048,320]{0,1:T(8,128)(2,1)}, bf16[2048,320]{0,1:T(8,128)(2,1)S(1)}, u32[]{:S(2)}, u32[]{:S(2)}) collective-permute-start(bf16[2048,320]{0,1:T(8,128)(2,1)} %constant_dynamic-update-slice_fusion), channel_id=1, source_target_pairs={{0,8},{8,16},{16,24},{24,0},{1,9},{9,17},{17,25},{25,1},{2,10},{10... | collective-permute-start | bytes 3932168 | tf_op jit(solution)/shard_map/gather_sequence/ppermute | solution.py:32
  140.0 24.8 %collective-permute-start.20 = (bf16[2048,320]{0,1:T(8,128)(2,1)}, bf16[2048,320]{0,1:T(8,128)(2,1)}, u32[]{:S(2)}, u32[]{:S(2)}) collective-permute-start(bf16[2048,320]{0,1:T(8,128)(2,1)} %constant_dynamic-update-slice_fusion), channel_id=1, source_target_pairs={{0,24},{8,0},{16,8},{24,16},{1,25},{9,1},{17,9},{25,17},{2,26},{10... | collective-permute-start | bytes 3932168 | tf_op jit(solution)/shard_map/gather_sequence/ppermute | solution.py:32
  165.5 23.8 %all-to-all-start = ((f32[64,2,2,128]{3,2,1,0:T(2,128)}), f32[64,2,2,128]{3,2,1,0:T(2,128)S(1)}, u32[]{:S(2)}, u32[]{:S(2)}) async-start(f32[64,2,2,128]{3,2,1,0:T(2,128)} %broadcast_in_dim.98), calls=%async_computation | async-start | bytes 262144 | tf_op jit(solution)/shard_map/gather_row_stats/all_to_all | solution.py:165
  175.8 33.1 %collective-permute-start.21 = (bf16[1024,320]{0,1:T(8,128)(2,1)}, bf16[1024,320]{0,1:T(8,128)(2,1)}, u32[]{:S(2)}, u32[]{:S(2)}) collective-permute-start(bf16[1024,320]{0,1:T(8,128)(2,1)} %slice.143), channel_id=1, source_target_pairs={{0,8},{8,16},{16,24},{24,0},{1,9},{9,17},{17,25},{25,1},{2,10},{10... | collective-permute-start | bytes 1966088 | tf_op jit(solution)/shard_map/gather_row_stats/ppermute | solution.py:32
  180.1 29.9 %collective-permute-start.22 = (bf16[1024,320]{0,1:T(8,128)(2,1)}, bf16[1024,320]{0,1:T(8,128)(2,1)}, u32[]{:S(2)}, u32[]{:S(2)}) collective-permute-start(bf16[1024,320]{0,1:T(8,128)(2,1)} %slice.144), channel_id=1, source_target_pairs={{0,24},{8,0},{16,8},{24,16},{1,25},{9,1},{17,9},{25,17},{2,26},{10... | collective-permute-start | bytes 1966088 | tf_op jit(solution)/shard_map/gather_row_stats/ppermute | solution.py:32
  189.2 3.3 %copy-start.17 = (f32[64,2,2,128]{3,2,1,0:T(2,128)}, f32[64,2,2,128]{3,2,1,0:T(2,128)S(1)}, u32[]{:S(2)}) copy-start(f32[64,2,2,128]{3,2,1,0:T(2,128)S(1)} %all-to-all-done) | copy-start | bytes 393220
  200.1 3.5 %copy-start.2 = (f32[2,128,2048]{2,1,0:T(8,128)}, f32[2,128,2048]{2,1,0:T(8,128)S(1)}, u32[]{:S(2)}) copy-start(f32[2,128,2048]{2,1,0:T(8,128)S(1)} %fusion.16) | copy-start | bytes 6291460
  200.1 3.5 %copy-start.15 = (pred[128,2048]{1,0:T(8,128)(4,1)S(1)}, pred[128,2048]{1,0:T(8,128)(4,1)}, u32[]{:S(2)}) copy-start(pred[128,2048]{1,0:T(8,128)(4,1)} %get-tuple-element.49) | copy-start | bytes 786436
  211.4 3.2 %copy-start.7 = (bf16[2048,160]{0,1:T(8,128)(2,1)}, bf16[2048,160]{0,1:T(8,128)(2,1)S(1)}, u32[]{:S(2)}) copy-start(bf16[2048,160]{0,1:T(8,128)(2,1)S(1)} %get-tuple-element.29) | copy-start | bytes 1966084
  211.4 3.2 %copy-start.8 = (bf16[2048,160]{0,1:T(8,128)(2,1)}, bf16[2048,160]{0,1:T(8,128)(2,1)S(1)}, u32[]{:S(2)}) copy-start(bf16[2048,160]{0,1:T(8,128)(2,1)S(1)} %get-tuple-element.30) | copy-start | bytes 1966084
  214.6 3.4 %copy-start.20 = (f32[2,80,128]{2,1,0:T(8,128)S(1)}, f32[2,80,128]{2,1,0:T(8,128)}, u32[]{:S(2)}) copy-start(f32[2,80,128]{2,1,0:T(8,128)} %fusion.25) | copy-start | bytes 245764
  214.6 3.4 %copy-start.22 = (f32[2,80,128]{2,1,0:T(8,128)S(1)}, f32[2,80,128]{2,1,0:T(8,128)}, u32[]{:S(2)}) copy-start(f32[2,80,128]{2,1,0:T(8,128)} %fusion.27) | copy-start | bytes 245764
  214.6 3.4 %copy-start.27 = (f32[2,2048]{1,0:T(2,128)S(1)}, f32[2,2048]{1,0:T(2,128)}, u32[]{:S(2)}) copy-start(f32[2,2048]{1,0:T(2,128)} %get-tuple-element.37) | copy-start | bytes 49156
  218.1 4.2 %copy-start.19 = (f32[2,80,128]{2,1,0:T(8,128)S(1)}, f32[2,80,128]{2,1,0:T(8,128)}, u32[]{:S(2)}) copy-start(f32[2,80,128]{2,1,0:T(8,128)} %fusion.49) | copy-start | bytes 245764
  218.1 4.2 %copy-start.21 = (f32[2,80,128]{2,1,0:T(8,128)S(1)}, f32[2,80,128]{2,1,0:T(8,128)}, u32[]{:S(2)}) copy-start(f32[2,80,128]{2,1,0:T(8,128)} %fusion.53) | copy-start | bytes 245764
  220.7 3.0 %copy-start.30 = (f32[1280]{0:T(1024)S(1)}, f32[1280]{0:T(1024)}, u32[]{:S(2)}) copy-start(f32[1280]{0:T(1024)} %param.13) | copy-start | bytes 15364
  224.9 12.8 %copy-start.23 = (bf16[128,320]{0,1:T(8,128)(2,1)S(1)}, bf16[128,320]{0,1:T(8,128)(2,1)}, u32[]{:S(2)}) copy-start(bf16[128,320]{0,1:T(8,128)(2,1)} %param.11) | copy-start | bytes 245764
  224.9 12.8 %copy-start.24 = (bf16[128,320]{0,1:T(8,128)(2,1)S(1)}, bf16[128,320]{0,1:T(8,128)(2,1)}, u32[]{:S(2)}) copy-start(bf16[128,320]{0,1:T(8,128)(2,1)} %param.12) | copy-start | bytes 245764
  224.9 12.8 %copy-start.35 = (f32[128]{0:T(128)S(1)}, f32[128]{0:T(128)}, u32[]{:S(2)}) copy-start(f32[128]{0:T(128)} %copy-done.34) | copy-start | bytes 1540
  (14 other events, 27.7 us)
Sparse Core Ops, SparseCore 0:
  46.3 89.5 all-gather.1

commit v10 on v7

--- a/solution.py
+++ b/solution.py
@@ -177,23 +177,23 @@
                 heads_here, piece_rows
             )
             scores_t = jnp.einsum(
-                "khd,qhd->hkq", key_heads, query_part, preferred_element_type=jnp.float32
-            )
-            visible_t = own_positions[None, :, None] <= place[None, None, :]
+                "qhd,khd->hqk", query_part, key_heads, preferred_element_type=jnp.float32
+            )
+            visible_t = own_positions[None, None, :] <= place[None, :, None]
             attend_t = jnp.exp(
-                jnp.where(visible_t, scores_t - log_part[:, None, :], masked_score)
+                jnp.where(visible_t, scores_t - log_part[:, :, None], masked_score)
             )
             grad_probs_t = jnp.einsum(
-                "khd,qhd->hkq", value_heads, grad_part, preferred_element_type=jnp.float32
-            )
-            score_grad = (attend_t * (grad_probs_t - delta_part[:, None, :])).astype(
+                "qhd,khd->hqk", grad_part, value_heads, preferred_element_type=jnp.float32
+            )
+            score_grad = (attend_t * (grad_probs_t - delta_part[:, :, None])).astype(
                 jnp.bfloat16
             )
             key_grad = key_grad + jnp.einsum(
-                "hkq,qhd->khd", score_grad, query_part, preferred_element_type=jnp.float32
+                "hqk,qhd->khd", score_grad, query_part, preferred_element_type=jnp.float32
             )
             value_grad = value_grad + jnp.einsum(
-                "hkq,qhd->khd",
+                "hqk,qhd->khd",
                 attend_t.astype(jnp.bfloat16),
                 grad_part,
                 preferred_element_type=jnp.float32,

time: 242 us -> 243 us (level)
  waiting for transfers between devices: 26.5 us -> 23.7 us
    ppermute x19, waiting for transfers between devices: 23.9 us -> 21 us  [shift(): lax.ppermute(data, axis, [(i, (i + step) % size) for i in range(size)])]
    unnamed x90 -> x86, local copies, waits for them, and re-layouts: 12.9 us -> 12.9 us
  transfers between devices with their start and end apart: 21 -> 21, of which waited for: 13 -> 10; matrix products, arithmetic and copies ran while one was open for 26% -> 26% of each run, Pallas kernels for 0% -> 0%
where the time goes in v10:
time: 243 us; the launch traced here: 241 us
  starting transfers between devices  79.6 us (33%)
  blocking collectives  40.5 us (17%)
  local copies, waits for them, and re-layouts  37.3 us (15%)
  matrix products  35.5 us (15%)
  waiting for transfers between devices  23.7 us (10%)
  between operations  15.1 us (6%)
  other arithmetic  9.24 us (4%)
    ppermute x19, starting transfers between devices, shift(): lax.ppermute(data, axis, [(i, (i + step) % size) for i in range(size)])  69.9 us
    ppermute x19, waiting for transfers between devices, shift(): lax.ppermute(data, axis, [(i, (i + step) % size) for i in range(size)])  21 us
    all_gather x1, blocking collectives, per_device(): kv_all = lax.all_gather(kv, 'y', axis=0, tiled=True)  14.6 us
    all_gather x1, blocking collectives, per_device(): gathered = lax.all_gather(both, 'tp', axis=1, tiled=True)  13.4 us
    unnamed x86, local copies, waits for them, and re-layouts  12.9 us
    all_to_all x1, blocking collectives, per_device(): received = lax.all_to_all(payload, 'tp', 0, 0, tiled=False)  12.5 us
    dot_general x4, matrix products, per_device(): jnp.einsum('hqk,qhd->khd', score_grad, query_part, preferred_element_type...  12.1 us
    all_to_all x1, starting transfers between devices, per_device(): stats_all = lax.all_to_all(sent, ('z', 'y'), 0, 0, tiled=False)  9.75 us
  transfers between devices with their start and end apart: 21, of which 10 were waited for; matrix products, arithmetic and copies ran while one was open for 26% of the time, Pallas kernels for 0%

profile of v10, /device:TPU:24, one launch (start us, length us, event | category | flops | bytes accessed | tf_op | source)
XLA Modules:
  0.0 240.8 jit_solution(6059852894968092904)
XLA Ops:
  7.5 13.4 %all_gather.9 = bf16[128,2560]{0,1:T(8,128)(2,1)S(1)} all-gather(bf16[128,640]{0,1:T(8,128)(2,1)S(1)} %pad_maximum_fusion.1), channel_id=1, replica_groups=mesh['z'=16,'y'=4,'tp'=4,'dp'=2] {'tp'}, dimensions={1}, use_global_device_ids=true | all-gather | bytes 819200 | tf_op jit(solution)/shard_map/gather_features/all_gather | solution.py:77
  23.2 14.6 %all_gather.10 = bf16[512,320]{0,1:T(8,128)(2,1)} all-gather(bf16[128,320]{0,1:T(8,128)(2,1)S(1)} %pad_maximum_fusion.2), channel_id=1, replica_groups=mesh['z'=16,'y'=4,'tp'=4,'dp'=2] {'y'}, dimensions={0}, use_global_device_ids=true | all-gather | bytes 409600 | tf_op jit(solution)/shard_map/gather_sequence/all_gather | solution.py:109
  39.2 8.9 %collective-permute-start = (bf16[128,320]{0,1:T(8,128)(2,1)S(1)}, bf16[128,320]{0,1:T(8,128)(2,1)S(1)}, u32[]{:S(2)}, u32[]{:S(2)}) collective-permute-start(bf16[128,320]{0,1:T(8,128)(2,1)S(1)} %get-tuple-element.35), channel_id=1, source_target_pairs={{0,480},{32,0},{64,32},{96,64},{128,96},{160,128},{192,160},{224,1... | collective-permute-start | bytes 245768 | tf_op jit(solution)/shard_map/gather_sequence/ppermute | solution.py:32
  48.1 1.9 collective-permute-start.7
  55.3 2.6 %broadcast_compare_fusion.4 = (pred[2048,128]{1,0:T(8,128)(4,1)}, pred[2048,128]{1,0:T(8,128)(4,1)}, pred[2048,128]{1,0:T(8,128)(4,1)}, pred[2048,128]{1,0:T(8,128)(4,1)}) fusion(s32[128]{0:T(128)S(1)} %iota_add_fusion, s32[2048]{0:T(1024)S(1)} %add_bitcast_fusion.4, s32[2048]{0:T(1024)S(1)} %add_bitcast_fusion.3, s32[2048]{0:T(1024)S(1)} %add_bitcast_fusion.2, ...), kind=kLoop, calls=%fused_computation.86 | loop fusion | flops 1048576 | bytes 1081856 | tf_op jit(solution)/shard_map/key_pass/le | solution.py:182
  57.9 5.1 %collective-permute-start.1 = (bf16[128,320]{0,1:T(8,128)(2,1)S(1)}, bf16[128,320]{0,1:T(8,128)(2,1)S(1)}, u32[]{:S(2)}, u32[]{:S(2)}) collective-permute-start(bf16[128,320]{0,1:T(8,128)(2,1)S(1)} %collective-permute-done), channel_id=1, source_target_pairs={{0,480},{32,0},{64,32},{96,64},{128,96},{160,128},{192,160},{224,1... | collective-permute-start | bytes 245768 | tf_op jit(solution)/shard_map/gather_sequence/ppermute | solution.py:32
  63.1 1.9 collective-permute-start.8
  66.4 5.6 %collective-permute-start.2 = (bf16[128,320]{0,1:T(8,128)(2,1)S(1)}, bf16[128,320]{0,1:T(8,128)(2,1)S(1)}, u32[]{:S(2)}, u32[]{:S(2)}) collective-permute-start(bf16[128,320]{0,1:T(8,128)(2,1)S(1)} %collective-permute-done.1), channel_id=1, source_target_pairs={{0,480},{32,0},{64,32},{96,64},{128,96},{160,128},{192,160},{224,1... | collective-permute-start | bytes 245768 | tf_op jit(solution)/shard_map/gather_sequence/ppermute | solution.py:32
  72.0 1.9 collective-permute-start.9
  75.4 5.6 %collective-permute-start.3 = (bf16[128,320]{0,1:T(8,128)(2,1)S(1)}, bf16[128,320]{0,1:T(8,128)(2,1)S(1)}, u32[]{:S(2)}, u32[]{:S(2)}) collective-permute-start(bf16[128,320]{0,1:T(8,128)(2,1)S(1)} %collective-permute-done.2), channel_id=1, source_target_pairs={{0,480},{32,0},{64,32},{96,64},{128,96},{160,128},{192,160},{224,1... | collective-permute-start | bytes 245768 | tf_op jit(solution)/shard_map/gather_sequence/ppermute | solution.py:32
  81.0 1.9 collective-permute-start.10
  84.6 5.6 %collective-permute-start.4 = (bf16[128,320]{0,1:T(8,128)(2,1)S(1)}, bf16[128,320]{0,1:T(8,128)(2,1)S(1)}, u32[]{:S(2)}, u32[]{:S(2)}) collective-permute-start(bf16[128,320]{0,1:T(8,128)(2,1)S(1)} %collective-permute-done.3), channel_id=1, source_target_pairs={{0,480},{32,0},{64,32},{96,64},{128,96},{160,128},{192,160},{224,1... | collective-permute-start | bytes 245768 | tf_op jit(solution)/shard_map/gather_sequence/ppermute | solution.py:32
  90.2 1.9 collective-permute-start.11
  93.7 5.6 %collective-permute-start.5 = (bf16[128,320]{0,1:T(8,128)(2,1)S(1)}, bf16[128,320]{0,1:T(8,128)(2,1)S(1)}, u32[]{:S(2)}, u32[]{:S(2)}) collective-permute-start(bf16[128,320]{0,1:T(8,128)(2,1)S(1)} %collective-permute-done.4), channel_id=1, source_target_pairs={{0,480},{32,0},{64,32},{96,64},{128,96},{160,128},{192,160},{224,1... | collective-permute-start | bytes 245768 | tf_op jit(solution)/shard_map/gather_sequence/ppermute | solution.py:32
  100.0 1.9 collective-permute-start.12
  102.6 5.6 %collective-permute-start.6 = (bf16[128,320]{0,1:T(8,128)(2,1)S(1)}, bf16[128,320]{0,1:T(8,128)(2,1)S(1)}, u32[]{:S(2)}, u32[]{:S(2)}) collective-permute-start(bf16[128,320]{0,1:T(8,128)(2,1)S(1)} %collective-permute-done.5), channel_id=1, source_target_pairs={{0,480},{32,0},{64,32},{96,64},{128,96},{160,128},{192,160},{224,1... | collective-permute-start | bytes 245768 | tf_op jit(solution)/shard_map/gather_sequence/ppermute | solution.py:32
  108.1 1.6 collective-permute-done.12
  109.8 1.9 collective-permute-start.13
  112.3 6.4 %collective-permute-done.13 = bf16[128,320]{0,1:T(8,128)(2,1)S(1)} collective-permute-done((bf16[128,320]{0,1:T(8,128)(2,1)S(1)}, bf16[128,320]{0,1:T(8,128)(2,1)S(1)}, u32[]{:S(2)}, u32[]{:S(2)}) %collective-permute-start.13) | collective-permute-done | bytes 81952 | tf_op jit(solution)/shard_map/gather_sequence/ppermute | solution.py:32
  118.7 1.9 collective-permute-start.14
  121.4 5.4 %collective-permute-done.14 = bf16[128,320]{0,1:T(8,128)(2,1)S(1)} collective-permute-done((bf16[128,320]{0,1:T(8,128)(2,1)S(1)}, bf16[128,320]{0,1:T(8,128)(2,1)S(1)}, u32[]{:S(2)}, u32[]{:S(2)}) %collective-permute-start.14) | collective-permute-done | bytes 81952 | tf_op jit(solution)/shard_map/gather_sequence/ppermute | solution.py:32
  132.0 4.4 %collective-permute-start.15 = (bf16[2048,320]{0,1:T(8,128)(2,1)}, bf16[2048,320]{0,1:T(8,128)(2,1)S(1)}, u32[]{:S(2)}, u32[]{:S(2)}) collective-permute-start(bf16[2048,320]{0,1:T(8,128)(2,1)} %constant_dynamic-update-slice_fusion), channel_id=1, source_target_pairs={{0,8},{8,16},{16,24},{24,0},{1,9},{9,17},{17,25},{25,1},{2,10},{10... | collective-permute-start | bytes 3932168 | tf_op jit(solution)/shard_map/gather_sequence/ppermute | solution.py:32
  136.4 2.1 collective-permute-start.16
  138.5 2.2 fusion.71
  140.8 3.0 %fusion.70 = (bf16[8192,160]{0,1:T(8,128)(2,1)S(1)}, bf16[8192,160]{0,1:T(8,128)(2,1)S(1)}) fusion(bf16[8192,320]{0,1:T(8,128)(2,1)} %all-gather.2.cloned.1.call-done), kind=kLoop, calls=%fused_computation.160 | loop fusion | bytes 10485760 | tf_op jit(solution)/shard_map/gather_sequence/slice | solution.py:114
  143.7 1.8 select_reduce_fusion.1
  145.5 2.5 %select_reduce_fusion = f32[2,128]{1,0:T(2,128)S(1)} fusion(f32[2,128,8192]{2,1,0:T(8,128)S(1)} %get-tuple-element.54, f32[2,128]{1,0:T(2,128)S(1)} %get-tuple-element.53, pred[128,8192]{1,0:T(8,128)(4,1)S(1)} %broadcast_compare_fusion), kind=kLoop, calls=%fused_computation.10 | loop fusion | flops 8388352 | bytes 9439232 | tf_op jit(solution)/shard_map/query_pass/reduce_sum | solution.py:137
  148.0 3.5 %fusion.76 = (f32[2,128]{1,0:T(2,128)S(1)}, bf16[2,128,8192]{2,1,0:T(8,128)(2,1)S(1)}) fusion(bf16[128,2,80]{0,2,1:T(8,128)(2,1)S(1)} %bitcast.198, bf16[8192,2,80]{0,2,1:T(8,128)(2,1)S(1)} %bitcast.176, f32[2,128,8192]{2,1,0:T(8,128)S(1)} %get-tuple-element.54, f32[2,128]{1,0:T(2,128)S(1)} %log_add_fusion, pred[128,8192]{1,0:T(8,128)(4,1)S(1)} %broadcast_compare_fusion), kind=kOutput, calls=%fused_computation.166 | convolution fusion | flops 346029824 | bytes 16295936 | tf_op jit(solution)/shard_map/query_pass/qhd,khd->hqk/dot_general | solution.py:140
  151.6 2.0 fusion.43
  153.6 1.5 fusion.35
  156.3 3.5 %collective-permute-done.16 = bf16[2048,320]{0,1:T(8,128)(2,1)} collective-permute-done((bf16[2048,320]{0,1:T(8,128)(2,1)}, bf16[2048,320]{0,1:T(8,128)(2,1)}, u32[]{:S(2)}, u32[]{:S(2)}) %collective-permute-start.16) | collective-permute-done | bytes 1310752 | tf_op jit(solution)/shard_map/gather_sequence/ppermute | solution.py:32
  160.5 9.8 %all-to-all-start = ((f32[64,2,2,128]{3,2,1,0:T(2,128)}), f32[64,2,2,128]{3,2,1,0:T(2,128)S(1)}, u32[]{:S(2)}, u32[]{:S(2)}) async-start(f32[64,2,2,128]{3,2,1,0:T(2,128)} %broadcast_in_dim.95), calls=%async_computation | async-start | bytes 262144 | tf_op jit(solution)/shard_map/gather_row_stats/all_to_all | solution.py:163
  171.2 2.4 collective-permute-start.17
  173.5 2.0 slice.136
  175.5 3.7 %collective-permute-start.18 = (bf16[1024,320]{0,1:T(8,128)(2,1)}, bf16[1024,320]{0,1:T(8,128)(2,1)}, u32[]{:S(2)}, u32[]{:S(2)}) collective-permute-start(bf16[1024,320]{0,1:T(8,128)(2,1)} %slice.136), channel_id=1, source_target_pairs={{0,24},{8,0},{16,8},{24,16},{1,25},{9,1},{17,9},{25,17},{2,26},{10... | collective-permute-start | bytes 1966088 | tf_op jit(solution)/shard_map/gather_row_stats/ppermute | solution.py:32
  179.2 2.8 %fusion.72 = (bf16[2048,160]{0,1:T(8,128)(2,1)}, bf16[2048,160]{0,1:T(8,128)(2,1)}, bf16[2048,160]{0,1:T(8,128)(2,1)}, bf16[2048,160]{0,1:T(8,128)(2,1)}) fusion(bf16[2048,320]{0,1:T(8,128)(2,1)} %collective-permute-done.16, bf16[2048,320]{0,1:T(8,128)(2,1)S(1)} %collective-permute-done.15), kind=kLoop, calls=%fused_computation.162 | loop fusion | bytes 5242880 | tf_op jit(solution)/shard_map/key_pass/slice | solution.py:172
  182.0 2.6 %all-to-all-done = f32[64,2,2,128]{3,2,1,0:T(2,128)S(1)} async-done(((f32[64,2,2,128]{3,2,1,0:T(2,128)}), f32[64,2,2,128]{3,2,1,0:T(2,128)S(1)}, u32[]{:S(2)}, u32[]{:S(2)}) %all-to-all-start) | async-done | bytes 131104 | tf_op jit(solution)/shard_map/gather_row_stats/all_to_all | solution.py:163
  187.4 2.1 fusion.10
  189.9 2.4 fusion.25
  192.3 2.1 fusion.16
  194.4 3.1 %fusion.27 = f32[2,80,128]{2,1,0:T(8,128)S(1)} fusion(bf16[2048,2,80]{0,2,1:T(8,128)(2,1)} %bitcast.180, f32[2,2048,128]{2,1,0:T(8,128)S(1)} %fusion.16, bf16[2048,2,80]{0,2,1:T(8,128)(2,1)} %bitcast.168, bf16[128,2,80]{0,2,1:T(8,128)(2,1)S(1)} %bitcast.188, f32[2,2048]{1,0:T(2,128)S(1)} %get-tuple-element.39), kind=kOutput, calls=%fused_computation.49 | convolution fusion | flops 169345024 | bytes 3547136 | tf_op jit(solution)/shard_map/key_pass/hqk,qhd->khd/dot_general | solution.py:192
  197.6 2.2 fusion.19
  200.2 2.2 gather_fusion.5
  202.4 1.3 slice_bitcast_fusion.2
  209.9 3.7 %fusion.26 = f32[2,80,128]{2,1,0:T(8,128)} fusion(bf16[2048,2,80]{0,2,1:T(8,128)(2,1)} %bitcast.184, f32[2,2048,128]{2,1,0:T(8,128)} %copy-done.4, bf16[2048,2,80]{0,2,1:T(8,128)(2,1)} %bitcast.173, bf16[128,2,80]{0,2,1:T(8,128)(2,1)S(1)} %bitcast.189, f32[2,2048]{1,0:T(2,128)} %get-tuple-element.41), kind=kOutput, calls=%fused_computation.48 | convolution fusion | flops 169345024 | bytes 3547136 | tf_op jit(solution)/shard_map/key_pass/hqk,qhd->khd/dot_general | solution.py:192
  213.6 2.8 %fusion.48 = bf16[2,80,128]{2,1,0:T(8,128)(2,1)} fusion(f32[2,80,128]{2,1,0:T(8,128)S(1)} %fusion.25, f32[2,80,128]{2,1,0:T(8,128)} %fusion.26, f32[2,80,128]{2,1,0:T(8,128)S(1)} %fusion.27, bf16[2048,2,80]{0,2,1:T(8,128)(2,1)} %bitcast.178, f32[2,2048,128]{2,1,0:T(8,128)S(1)} %fusion.19, bf16[2048,2,80]{0,2,1:T(8,128)(2,1)S(1)} %bitcast.166, ...), kind=kOutput, calls=%fused_computation.65 | convolution fusion | flops 169426944 | bytes 3751936 | tf_op jit(solution)/shard_map/key_pass/hqk,qhd->khd/dot_general | solution.py:192
  216.4 1.6 convolution_add_fusion.1
  220.5 12.5 %all_to_all.10 = f32[4,129,320]{2,1,0:T(8,128)S(1)} all-to-all(f32[4,129,320]{2,1,0:T(8,128)S(1)} %copy.31), channel_id=1, replica_groups=mesh['z'=16,'y'=4,'tp'=4,'dp'=2] {'tp'}, dimensions={0} | all-to-all | bytes 1320960 | tf_op jit(solution)/shard_map/back_projection/all_to_all | solution.py:214
  (172 shorter events, 38.8 us)
Async XLA Ops:
  6.5 16.0 %copy-start = (bf16[160,1280]{1,0:T(8,128)(2,1)S(1)}, bf16[160,1280]{1,0:T(8,128)(2,1)}, u32[]{:S(2)}) copy-start(bf16[160,1280]{1,0:T(8,128)(2,1)} %param.16) | copy-start | bytes 1228804
  6.5 134.2 %all-gather.2.cloned.1.call-start = ((), (), s32[]{:S(2)}) async-start(), calls=%async_computation.2 | async-start | bytes 5570560 | tf_op jit(solution)/shard_map/gather_sequence/all_gather | solution.py:110
  7.5 14.9 %copy-start.24 = (f32[1280]{0:T(1024)S(1)}, f32[1280]{0:T(1024)}, u32[]{:S(2)}) copy-start(f32[1280]{0:T(1024)} %param.13) | copy-start | bytes 15364
  21.0 1.9 copy-start.11
  21.2 16.6 %copy-start.34 = (f32[80]{0:T(128)S(1)}, f32[80]{0:T(128)}, u32[]{:S(2)}) copy-start(f32[80]{0:T(128)} %param.18) | copy-start | bytes 964
  21.2 16.7 %copy-start.15 = (bf16[160,1280]{1,0:T(8,128)(2,1)S(1)}, bf16[160,1280]{1,0:T(8,128)(2,1)}, u32[]{:S(2)}) copy-start(bf16[160,1280]{1,0:T(8,128)(2,1)} %param.17) | copy-start | bytes 1228804
  22.4 15.8 %copy-start.12 = (bf16[160,1280]{1,0:T(8,128)(2,1)S(1)}, bf16[160,1280]{1,0:T(8,128)(2,1)}, u32[]{:S(2)}) copy-start(bf16[160,1280]{1,0:T(8,128)(2,1)} %param.14) | copy-start | bytes 1228804
  22.5 27.5 %copy-start.1 = (s32[64]{0:T(128)S(1)}, s32[64]{0:T(128)}, u32[]{:S(2)}) copy-start(s32[64]{0:T(128)} %param.19) | copy-start | bytes 772
  23.2 169.1 %copy-start.19 = (bf16[128,160]{0,1:T(8,128)(2,1)}, bf16[128,160]{0,1:T(8,128)(2,1)S(1)}, u32[]{:S(2)}) copy-start(bf16[128,160]{0,1:T(8,128)(2,1)S(1)} %convolution_convert_fusion.2) | copy-start | bytes 122884
  37.9 16.5 %copy-start.26 = (f32[160]{0:T(256)}, f32[160]{0:T(256)S(1)}, u32[]{:S(2)}) copy-start(f32[160]{0:T(256)S(1)} %mul.182) | copy-start | bytes 1924
  38.2 17.1 %copy-start.22 = (bf16[128,160]{0,1:T(8,128)(2,1)}, bf16[128,160]{0,1:T(8,128)(2,1)S(1)}, u32[]{:S(2)}) copy-start(bf16[128,160]{0,1:T(8,128)(2,1)S(1)} %convolution_convert_fusion) | copy-start | bytes 122884
  39.2 18.7 %collective-permute-start = (bf16[128,320]{0,1:T(8,128)(2,1)S(1)}, bf16[128,320]{0,1:T(8,128)(2,1)S(1)}, u32[]{:S(2)}, u32[]{:S(2)}) collective-permute-start(bf16[128,320]{0,1:T(8,128)(2,1)S(1)} %get-tuple-element.35), channel_id=1, source_target_pairs={{0,480},{32,0},{64,32},{96,64},{128,96},{160,128},{192,160},{224,1... | collective-permute-start | bytes 245768 | tf_op jit(solution)/shard_map/gather_sequence/ppermute | solution.py:32
  48.1 15.0 %collective-permute-start.7 = (bf16[128,320]{0,1:T(8,128)(2,1)S(1)}, bf16[128,320]{0,1:T(8,128)(2,1)S(1)}, u32[]{:S(2)}, u32[]{:S(2)}) collective-permute-start(bf16[128,320]{0,1:T(8,128)(2,1)S(1)} %get-tuple-element.35), channel_id=1, source_target_pairs={{0,32},{32,64},{64,96},{96,128},{128,160},{160,192},{192,224},{224... | collective-permute-start | bytes 245768 | tf_op jit(solution)/shard_map/gather_sequence/ppermute | solution.py:32
  50.8 3.7 %copy-start.30 = (s32[1024]{0:T(1024)}, s32[1024]{0:T(1024)S(1)}, u32[]{:S(2)}) copy-start(s32[1024]{0:T(1024)S(1)} %get-tuple-element.63) | copy-start | bytes 12292
  52.2 2.3 copy-start.28
  52.2 2.3 copy-start.31
  57.9 8.5 %collective-permute-start.1 = (bf16[128,320]{0,1:T(8,128)(2,1)S(1)}, bf16[128,320]{0,1:T(8,128)(2,1)S(1)}, u32[]{:S(2)}, u32[]{:S(2)}) collective-permute-start(bf16[128,320]{0,1:T(8,128)(2,1)S(1)} %collective-permute-done), channel_id=1, source_target_pairs={{0,480},{32,0},{64,32},{96,64},{128,96},{160,128},{192,160},{224,1... | collective-permute-start | bytes 245768 | tf_op jit(solution)/shard_map/gather_sequence/ppermute | solution.py:32
  63.1 9.0 %collective-permute-start.8 = (bf16[128,320]{0,1:T(8,128)(2,1)S(1)}, bf16[128,320]{0,1:T(8,128)(2,1)S(1)}, u32[]{:S(2)}, u32[]{:S(2)}) collective-permute-start(bf16[128,320]{0,1:T(8,128)(2,1)S(1)} %collective-permute-done.7), channel_id=1, source_target_pairs={{0,32},{32,64},{64,96},{96,128},{128,160},{160,192},{192,224},{224... | collective-permute-start | bytes 245768 | tf_op jit(solution)/shard_map/gather_sequence/ppermute | solution.py:32
  66.4 9.0 %collective-permute-start.2 = (bf16[128,320]{0,1:T(8,128)(2,1)S(1)}, bf16[128,320]{0,1:T(8,128)(2,1)S(1)}, u32[]{:S(2)}, u32[]{:S(2)}) collective-permute-start(bf16[128,320]{0,1:T(8,128)(2,1)S(1)} %collective-permute-done.1), channel_id=1, source_target_pairs={{0,480},{32,0},{64,32},{96,64},{128,96},{160,128},{192,160},{224,1... | collective-permute-start | bytes 245768 | tf_op jit(solution)/shard_map/gather_sequence/ppermute | solution.py:32
  72.0 9.0 %collective-permute-start.9 = (bf16[128,320]{0,1:T(8,128)(2,1)S(1)}, bf16[128,320]{0,1:T(8,128)(2,1)S(1)}, u32[]{:S(2)}, u32[]{:S(2)}) collective-permute-start(bf16[128,320]{0,1:T(8,128)(2,1)S(1)} %collective-permute-done.8), channel_id=1, source_target_pairs={{0,32},{32,64},{64,96},{96,128},{128,160},{160,192},{192,224},{224... | collective-permute-start | bytes 245768 | tf_op jit(solution)/shard_map/gather_sequence/ppermute | solution.py:32
  75.4 9.2 %collective-permute-start.3 = (bf16[128,320]{0,1:T(8,128)(2,1)S(1)}, bf16[128,320]{0,1:T(8,128)(2,1)S(1)}, u32[]{:S(2)}, u32[]{:S(2)}) collective-permute-start(bf16[128,320]{0,1:T(8,128)(2,1)S(1)} %collective-permute-done.2), channel_id=1, source_target_pairs={{0,480},{32,0},{64,32},{96,64},{128,96},{160,128},{192,160},{224,1... | collective-permute-start | bytes 245768 | tf_op jit(solution)/shard_map/gather_sequence/ppermute | solution.py:32
  81.0 9.2 %collective-permute-start.10 = (bf16[128,320]{0,1:T(8,128)(2,1)S(1)}, bf16[128,320]{0,1:T(8,128)(2,1)S(1)}, u32[]{:S(2)}, u32[]{:S(2)}) collective-permute-start(bf16[128,320]{0,1:T(8,128)(2,1)S(1)} %collective-permute-done.9), channel_id=1, source_target_pairs={{0,32},{32,64},{64,96},{96,128},{128,160},{160,192},{192,224},{224... | collective-permute-start | bytes 245768 | tf_op jit(solution)/shard_map/gather_sequence/ppermute | solution.py:32
  84.6 9.0 %collective-permute-start.4 = (bf16[128,320]{0,1:T(8,128)(2,1)S(1)}, bf16[128,320]{0,1:T(8,128)(2,1)S(1)}, u32[]{:S(2)}, u32[]{:S(2)}) collective-permute-start(bf16[128,320]{0,1:T(8,128)(2,1)S(1)} %collective-permute-done.3), channel_id=1, source_target_pairs={{0,480},{32,0},{64,32},{96,64},{128,96},{160,128},{192,160},{224,1... | collective-permute-start | bytes 245768 | tf_op jit(solution)/shard_map/gather_sequence/ppermute | solution.py:32
  90.2 9.7 %collective-permute-start.11 = (bf16[128,320]{0,1:T(8,128)(2,1)S(1)}, bf16[128,320]{0,1:T(8,128)(2,1)S(1)}, u32[]{:S(2)}, u32[]{:S(2)}) collective-permute-start(bf16[128,320]{0,1:T(8,128)(2,1)S(1)} %collective-permute-done.10), channel_id=1, source_target_pairs={{0,32},{32,64},{64,96},{96,128},{128,160},{160,192},{192,224},{224... | collective-permute-start | bytes 245768 | tf_op jit(solution)/shard_map/gather_sequence/ppermute | solution.py:32
  93.7 8.9 %collective-permute-start.5 = (bf16[128,320]{0,1:T(8,128)(2,1)S(1)}, bf16[128,320]{0,1:T(8,128)(2,1)S(1)}, u32[]{:S(2)}, u32[]{:S(2)}) collective-permute-start(bf16[128,320]{0,1:T(8,128)(2,1)S(1)} %collective-permute-done.4), channel_id=1, source_target_pairs={{0,480},{32,0},{64,32},{96,64},{128,96},{160,128},{192,160},{224,1... | collective-permute-start | bytes 245768 | tf_op jit(solution)/shard_map/gather_sequence/ppermute | solution.py:32
  100.0 9.8 %collective-permute-start.12 = (bf16[128,320]{0,1:T(8,128)(2,1)S(1)}, bf16[128,320]{0,1:T(8,128)(2,1)S(1)}, u32[]{:S(2)}, u32[]{:S(2)}) collective-permute-start(bf16[128,320]{0,1:T(8,128)(2,1)S(1)} %collective-permute-done.11), channel_id=1, source_target_pairs={{0,32},{32,64},{64,96},{96,128},{128,160},{160,192},{192,224},{224... | collective-permute-start | bytes 245768 | tf_op jit(solution)/shard_map/gather_sequence/ppermute | solution.py:32
  102.6 18.1 %collective-permute-start.6 = (bf16[128,320]{0,1:T(8,128)(2,1)S(1)}, bf16[128,320]{0,1:T(8,128)(2,1)S(1)}, u32[]{:S(2)}, u32[]{:S(2)}) collective-permute-start(bf16[128,320]{0,1:T(8,128)(2,1)S(1)} %collective-permute-done.5), channel_id=1, source_target_pairs={{0,480},{32,0},{64,32},{96,64},{128,96},{160,128},{192,160},{224,1... | collective-permute-start | bytes 245768 | tf_op jit(solution)/shard_map/gather_sequence/ppermute | solution.py:32
  109.8 9.0 %collective-permute-start.13 = (bf16[128,320]{0,1:T(8,128)(2,1)S(1)}, bf16[128,320]{0,1:T(8,128)(2,1)S(1)}, u32[]{:S(2)}, u32[]{:S(2)}) collective-permute-start(bf16[128,320]{0,1:T(8,128)(2,1)S(1)} %collective-permute-done.12), channel_id=1, source_target_pairs={{0,32},{32,64},{64,96},{96,128},{128,160},{160,192},{192,224},{224... | collective-permute-start | bytes 245768 | tf_op jit(solution)/shard_map/gather_sequence/ppermute | solution.py:32
  118.7 8.0 %collective-permute-start.14 = (bf16[128,320]{0,1:T(8,128)(2,1)S(1)}, bf16[128,320]{0,1:T(8,128)(2,1)S(1)}, u32[]{:S(2)}, u32[]{:S(2)}) collective-permute-start(bf16[128,320]{0,1:T(8,128)(2,1)S(1)} %collective-permute-done.13), channel_id=1, source_target_pairs={{0,32},{32,64},{64,96},{96,128},{128,160},{160,192},{192,224},{224... | collective-permute-start | bytes 245768 | tf_op jit(solution)/shard_map/gather_sequence/ppermute | solution.py:32
  132.0 24.4 %collective-permute-start.15 = (bf16[2048,320]{0,1:T(8,128)(2,1)}, bf16[2048,320]{0,1:T(8,128)(2,1)S(1)}, u32[]{:S(2)}, u32[]{:S(2)}) collective-permute-start(bf16[2048,320]{0,1:T(8,128)(2,1)} %constant_dynamic-update-slice_fusion), channel_id=1, source_target_pairs={{0,8},{8,16},{16,24},{24,0},{1,9},{9,17},{17,25},{25,1},{2,10},{10... | collective-permute-start | bytes 3932168 | tf_op jit(solution)/shard_map/gather_sequence/ppermute | solution.py:32
  136.4 23.4 %collective-permute-start.16 = (bf16[2048,320]{0,1:T(8,128)(2,1)}, bf16[2048,320]{0,1:T(8,128)(2,1)}, u32[]{:S(2)}, u32[]{:S(2)}) collective-permute-start(bf16[2048,320]{0,1:T(8,128)(2,1)} %constant_dynamic-update-slice_fusion), channel_id=1, source_target_pairs={{0,24},{8,0},{16,8},{24,16},{1,25},{9,1},{17,9},{25,17},{2,26},{10... | collective-permute-start | bytes 3932168 | tf_op jit(solution)/shard_map/gather_sequence/ppermute | solution.py:32
  145.5 2.5 %copy-start.23 = (bf16[128,160]{0,1:T(8,128)(2,1)S(1)}, bf16[128,160]{0,1:T(8,128)(2,1)}, u32[]{:S(2)}) copy-start(bf16[128,160]{0,1:T(8,128)(2,1)} %copy-done.22) | copy-start | bytes 122884
  160.5 24.1 %all-to-all-start = ((f32[64,2,2,128]{3,2,1,0:T(2,128)}), f32[64,2,2,128]{3,2,1,0:T(2,128)S(1)}, u32[]{:S(2)}, u32[]{:S(2)}) async-start(f32[64,2,2,128]{3,2,1,0:T(2,128)} %broadcast_in_dim.95), calls=%async_computation | async-start | bytes 262144 | tf_op jit(solution)/shard_map/gather_row_stats/all_to_all | solution.py:163
  171.2 32.6 %collective-permute-start.17 = (bf16[1024,320]{0,1:T(8,128)(2,1)}, bf16[1024,320]{0,1:T(8,128)(2,1)}, u32[]{:S(2)}, u32[]{:S(2)}) collective-permute-start(bf16[1024,320]{0,1:T(8,128)(2,1)} %slice.135), channel_id=1, source_target_pairs={{0,8},{8,16},{16,24},{24,0},{1,9},{9,17},{17,25},{25,1},{2,10},{10... | collective-permute-start | bytes 1966088 | tf_op jit(solution)/shard_map/gather_row_stats/ppermute | solution.py:32
  175.5 29.4 %collective-permute-start.18 = (bf16[1024,320]{0,1:T(8,128)(2,1)}, bf16[1024,320]{0,1:T(8,128)(2,1)}, u32[]{:S(2)}, u32[]{:S(2)}) collective-permute-start(bf16[1024,320]{0,1:T(8,128)(2,1)} %slice.136), channel_id=1, source_target_pairs={{0,24},{8,0},{16,8},{24,16},{1,25},{9,1},{17,9},{25,17},{2,26},{10... | collective-permute-start | bytes 1966088 | tf_op jit(solution)/shard_map/gather_row_stats/ppermute | solution.py:32
  184.6 2.8 %copy-start.14 = (f32[64,2,2,128]{3,2,1,0:T(2,128)}, f32[64,2,2,128]{3,2,1,0:T(2,128)S(1)}, u32[]{:S(2)}) copy-start(f32[64,2,2,128]{3,2,1,0:T(2,128)S(1)} %all-to-all-done) | copy-start | bytes 393220
  186.8 2.7 %copy-start.6 = (bf16[2048,160]{0,1:T(8,128)(2,1)S(1)}, bf16[2048,160]{0,1:T(8,128)(2,1)}, u32[]{:S(2)}) copy-start(bf16[2048,160]{0,1:T(8,128)(2,1)} %get-tuple-element.60) | copy-start | bytes 1966084
  194.4 3.2 %copy-start.2 = (f32[2,2048,128]{2,1,0:T(8,128)}, f32[2,2048,128]{2,1,0:T(8,128)S(1)}, u32[]{:S(2)}) copy-start(f32[2,2048,128]{2,1,0:T(8,128)S(1)} %fusion.16) | copy-start | bytes 6291460
  194.4 3.2 %copy-start.20 = (bf16[128,160]{0,1:T(8,128)(2,1)S(1)}, bf16[128,160]{0,1:T(8,128)(2,1)}, u32[]{:S(2)}) copy-start(bf16[128,160]{0,1:T(8,128)(2,1)} %copy-done.19) | copy-start | bytes 122884
  194.4 3.2 %copy-start.25 = (f32[2,2048]{1,0:T(2,128)S(1)}, f32[2,2048]{1,0:T(2,128)}, u32[]{:S(2)}) copy-start(f32[2,2048]{1,0:T(2,128)} %get-tuple-element.38) | copy-start | bytes 49156
  197.5 2.3 copy-start.5
  197.6 2.2 copy-start.3
  206.2 3.7 %copy-start.7 = (bf16[2048,160]{0,1:T(8,128)(2,1)}, bf16[2048,160]{0,1:T(8,128)(2,1)S(1)}, u32[]{:S(2)}) copy-start(bf16[2048,160]{0,1:T(8,128)(2,1)S(1)} %get-tuple-element.29) | copy-start | bytes 1966084
  206.2 3.7 %copy-start.10 = (bf16[2048,160]{0,1:T(8,128)(2,1)}, bf16[2048,160]{0,1:T(8,128)(2,1)S(1)}, u32[]{:S(2)}) copy-start(bf16[2048,160]{0,1:T(8,128)(2,1)S(1)} %get-tuple-element.30) | copy-start | bytes 1966084
  216.4 2.8 %copy-start.9 = (f32[128,1280]{1,0:T(8,128)S(1)}, f32[128,1280]{1,0:T(8,128)}, u32[]{:S(2)}) copy-start(f32[128,1280]{1,0:T(8,128)} %copy-done.8) | copy-start | bytes 1966084
  220.5 12.8 %copy-start.16 = (bf16[128,320]{0,1:T(8,128)(2,1)S(1)}, bf16[128,320]{0,1:T(8,128)(2,1)}, u32[]{:S(2)}) copy-start(bf16[128,320]{0,1:T(8,128)(2,1)} %param.11) | copy-start | bytes 245764
  220.5 12.7 %copy-start.17 = (bf16[128,320]{0,1:T(8,128)(2,1)S(1)}, bf16[128,320]{0,1:T(8,128)(2,1)}, u32[]{:S(2)}) copy-start(bf16[128,320]{0,1:T(8,128)(2,1)} %param.12) | copy-start | bytes 245764
  220.5 12.7 %copy-start.33 = (f32[128]{0:T(128)S(1)}, f32[128]{0:T(128)}, u32[]{:S(2)}) copy-start(f32[128]{0:T(128)} %copy-done.32) | copy-start | bytes 1540
  (8 other events, 10.0 us)
Sparse Core Ops, SparseCore 0:
  37.9 92.6 all-gather.1

commit v11 on v7

--- a/solution.py
+++ b/solution.py
@@ -157,7 +157,6 @@
 
     with jax.named_scope("gather_row_stats"):
         stats = jnp.stack([log_total, row_delta], axis=0)
-        stats, qg_ahead, qg_behind = lax.optimization_barrier((stats, qg_ahead, qg_behind))
         qg_pieces = ring4_last(qg_z, qg_ahead, qg_behind, "y")
         sent = jnp.broadcast_to(stats[None], (shards,) + stats.shape)
         stats_all = lax.all_to_all(sent, ("z", "y"), 0, 0, tiled=False)

time: 242 us -> 265 us (1.095)
  waiting for transfers between devices: 26.5 us -> 61.9 us
  local copies, waits for them, and re-layouts: 36.3 us -> 21.2 us
    ppermute x19, waiting for transfers between devices: 23.9 us -> 52.5 us  [shift(): lax.ppermute(data, axis, [(i, (i + step) % size) for i in range(size)])]
    unnamed x90 -> x78, local copies, waits for them, and re-layouts: 12.9 us -> 1.59 us
    all_to_all x1, waiting for transfers between devices: 2.59 us -> 9.32 us  [per_device(): stats_all = lax.all_to_all(sent, ('z', 'y'), 0, 0, tiled=False)]
    gather x4, local copies, waits for them, and re-layouts: 3.64 us -> 6.35 us  [per_device(): part_stats = stats_all[source]]
  transfers between devices with their start and end apart: 21 -> 21, of which waited for: 13 -> 12; matrix products, arithmetic and copies ran while one was open for 26% -> 7% of each run, Pallas kernels for 0% -> 0%
where the time goes in v11:
time: 265 us; the launch traced here: 263 us
  starting transfers between devices  78.1 us (29%)
  waiting for transfers between devices  61.9 us (23%)
  blocking collectives  40.5 us (15%)
  matrix products  37.7 us (14%)
  local copies, waits for them, and re-layouts  21.2 us (8%)
  between operations  15 us (6%)
  other arithmetic  8.57 us (3%)
    ppermute x19, starting transfers between devices, shift(): lax.ppermute(data, axis, [(i, (i + step) % size) for i in range(size)])  67.6 us
    ppermute x19, waiting for transfers between devices, shift(): lax.ppermute(data, axis, [(i, (i + step) % size) for i in range(size)])  52.5 us
    all_gather x1, blocking collectives, per_device(): kv_all = lax.all_gather(kv, 'y', axis=0, tiled=True)  14.6 us
    all_gather x1, blocking collectives, per_device(): gathered = lax.all_gather(both, 'tp', axis=1, tiled=True)  13.4 us
    all_to_all x1, blocking collectives, per_device(): received = lax.all_to_all(payload, 'tp', 0, 0, tiled=False)  12.5 us
    all_to_all x1, starting transfers between devices, per_device(): stats_all = lax.all_to_all(sent, ('z', 'y'), 0, 0, tiled=False)  10.6 us
    dot_general x4, matrix products, per_device(): jnp.einsum('hkq,qhd->khd', score_grad, query_part, preferred_element_type...  9.58 us
    all_to_all x1, waiting for transfers between devices, per_device(): stats_all = lax.all_to_all(sent, ('z', 'y'), 0, 0, tiled=False)  9.32 us
  transfers between devices with their start and end apart: 21, of which 12 were waited for; matrix products, arithmetic and copies ran while one was open for 7% of the time, Pallas kernels for 0%

profile of v11, /device:TPU:24, one launch (start us, length us, event | category | flops | bytes accessed | tf_op | source)
XLA Modules:
  0.0 263.0 jit_solution(3491487884475349032)
XLA Ops:
  7.5 13.4 %all_gather.9 = bf16[128,2560]{0,1:T(8,128)(2,1)S(1)} all-gather(bf16[128,640]{0,1:T(8,128)(2,1)S(1)} %pad_maximum_fusion.1), channel_id=1, replica_groups=mesh['z'=16,'y'=4,'tp'=4,'dp'=2] {'tp'}, dimensions={1}, use_global_device_ids=true | all-gather | bytes 819200 | tf_op jit(solution)/shard_map/gather_features/all_gather | solution.py:77
  23.2 14.6 %all_gather.10 = bf16[512,320]{0,1:T(8,128)(2,1)} all-gather(bf16[128,320]{0,1:T(8,128)(2,1)S(1)} %pad_maximum_fusion.2), channel_id=1, replica_groups=mesh['z'=16,'y'=4,'tp'=4,'dp'=2] {'y'}, dimensions={0}, use_global_device_ids=true | all-gather | bytes 409600 | tf_op jit(solution)/shard_map/gather_sequence/all_gather | solution.py:109
  38.5 8.9 %collective-permute-start = (bf16[128,320]{0,1:T(8,128)(2,1)S(1)}, bf16[128,320]{0,1:T(8,128)(2,1)S(1)}, u32[]{:S(2)}, u32[]{:S(2)}) collective-permute-start(bf16[128,320]{0,1:T(8,128)(2,1)S(1)} %get-tuple-element.29), channel_id=1, source_target_pairs={{0,480},{32,0},{64,32},{96,64},{128,96},{160,128},{192,160},{224,1... | collective-permute-start | bytes 245768 | tf_op jit(solution)/shard_map/gather_sequence/ppermute | solution.py:32
  47.4 1.9 collective-permute-start.7
  55.3 5.1 %collective-permute-start.1 = (bf16[128,320]{0,1:T(8,128)(2,1)S(1)}, bf16[128,320]{0,1:T(8,128)(2,1)S(1)}, u32[]{:S(2)}, u32[]{:S(2)}) collective-permute-start(bf16[128,320]{0,1:T(8,128)(2,1)S(1)} %collective-permute-done), channel_id=1, source_target_pairs={{0,480},{32,0},{64,32},{96,64},{128,96},{160,128},{192,160},{224,1... | collective-permute-start | bytes 245768 | tf_op jit(solution)/shard_map/gather_sequence/ppermute | solution.py:32
  60.5 1.9 collective-permute-start.8
  63.3 4.6 %collective-permute-start.2 = (bf16[128,320]{0,1:T(8,128)(2,1)S(1)}, bf16[128,320]{0,1:T(8,128)(2,1)S(1)}, u32[]{:S(2)}, u32[]{:S(2)}) collective-permute-start(bf16[128,320]{0,1:T(8,128)(2,1)S(1)} %collective-permute-done.1), channel_id=1, source_target_pairs={{0,480},{32,0},{64,32},{96,64},{128,96},{160,128},{192,160},{224,1... | collective-permute-start | bytes 245768 | tf_op jit(solution)/shard_map/gather_sequence/ppermute | solution.py:32
  68.0 1.7 collective-permute-done.8
  69.7 1.9 collective-permute-start.9
  71.7 5.5 %collective-permute-start.3 = (bf16[128,320]{0,1:T(8,128)(2,1)S(1)}, bf16[128,320]{0,1:T(8,128)(2,1)S(1)}, u32[]{:S(2)}, u32[]{:S(2)}) collective-permute-start(bf16[128,320]{0,1:T(8,128)(2,1)S(1)} %collective-permute-done.2), channel_id=1, source_target_pairs={{0,480},{32,0},{64,32},{96,64},{128,96},{160,128},{192,160},{224,1... | collective-permute-start | bytes 245768 | tf_op jit(solution)/shard_map/gather_sequence/ppermute | solution.py:32
  77.2 1.7 collective-permute-done.9
  79.0 1.9 collective-permute-start.10
  80.9 5.6 %collective-permute-start.4 = (bf16[128,320]{0,1:T(8,128)(2,1)S(1)}, bf16[128,320]{0,1:T(8,128)(2,1)S(1)}, u32[]{:S(2)}, u32[]{:S(2)}) collective-permute-start(bf16[128,320]{0,1:T(8,128)(2,1)S(1)} %collective-permute-done.3), channel_id=1, source_target_pairs={{0,480},{32,0},{64,32},{96,64},{128,96},{160,128},{192,160},{224,1... | collective-permute-start | bytes 245768 | tf_op jit(solution)/shard_map/gather_sequence/ppermute | solution.py:32
  87.7 1.9 collective-permute-start.11
  89.7 5.5 %collective-permute-start.5 = (bf16[128,320]{0,1:T(8,128)(2,1)S(1)}, bf16[128,320]{0,1:T(8,128)(2,1)S(1)}, u32[]{:S(2)}, u32[]{:S(2)}) collective-permute-start(bf16[128,320]{0,1:T(8,128)(2,1)S(1)} %collective-permute-done.4), channel_id=1, source_target_pairs={{0,480},{32,0},{64,32},{96,64},{128,96},{160,128},{192,160},{224,1... | collective-permute-start | bytes 245768 | tf_op jit(solution)/shard_map/gather_sequence/ppermute | solution.py:32
  95.2 2.4 collective-permute-done.11
  97.6 1.9 collective-permute-start.12
  99.5 5.1 %collective-permute-start.6 = (bf16[128,320]{0,1:T(8,128)(2,1)S(1)}, bf16[128,320]{0,1:T(8,128)(2,1)S(1)}, u32[]{:S(2)}, u32[]{:S(2)}) collective-permute-start(bf16[128,320]{0,1:T(8,128)(2,1)S(1)} %collective-permute-done.5), channel_id=1, source_target_pairs={{0,480},{32,0},{64,32},{96,64},{128,96},{160,128},{192,160},{224,1... | collective-permute-start | bytes 245768 | tf_op jit(solution)/shard_map/gather_sequence/ppermute | solution.py:32
  104.6 2.4 collective-permute-done.12
  107.1 1.9 collective-permute-start.13
  109.0 7.7 %collective-permute-done.13 = bf16[128,320]{0,1:T(8,128)(2,1)S(1)} collective-permute-done((bf16[128,320]{0,1:T(8,128)(2,1)S(1)}, bf16[128,320]{0,1:T(8,128)(2,1)S(1)}, u32[]{:S(2)}, u32[]{:S(2)}) %collective-permute-start.13) | collective-permute-done | bytes 81952 | tf_op jit(solution)/shard_map/gather_sequence/ppermute | solution.py:32
  116.7 1.9 collective-permute-start.14
  118.6 7.0 %collective-permute-done.14 = bf16[128,320]{0,1:T(8,128)(2,1)S(1)} collective-permute-done((bf16[128,320]{0,1:T(8,128)(2,1)S(1)}, bf16[128,320]{0,1:T(8,128)(2,1)S(1)}, u32[]{:S(2)}, u32[]{:S(2)}) %collective-permute-start.14) | collective-permute-done | bytes 81952 | tf_op jit(solution)/shard_map/gather_sequence/ppermute | solution.py:32
  125.8 2.2 collective-permute-start.16
  128.1 3.6 %collective-permute-start.15 = (bf16[2048,320]{0,1:T(8,128)(2,1)S(1)}, bf16[2048,320]{0,1:T(8,128)(2,1)S(1)}, u32[]{:S(2)}, u32[]{:S(2)}) collective-permute-start(bf16[2048,320]{0,1:T(8,128)(2,1)S(1)} %constant_dynamic-update-slice_fusion), channel_id=1, source_target_pairs={{0,24},{8,0},{16,8},{24,16},{1,25},{9,1},{17,9},{25,17},{2,26},{10... | collective-permute-start | bytes 3932168 | tf_op jit(solution)/shard_map/gather_sequence/ppermute | solution.py:32
  134.6 20.1 %collective-permute-done.16 = bf16[2048,320]{0,1:T(8,128)(2,1)S(1)} collective-permute-done((bf16[2048,320]{0,1:T(8,128)(2,1)S(1)}, bf16[2048,320]{0,1:T(8,128)(2,1)S(1)}, u32[]{:S(2)}, u32[]{:S(2)}) %collective-permute-start.16) | collective-permute-done | bytes 1310752 | tf_op jit(solution)/shard_map/gather_sequence/ppermute | solution.py:32
  154.8 2.2 collective-permute-start.17
  157.1 3.8 %collective-permute-start.18 = (bf16[1024,320]{0,1:T(8,128)(2,1)S(1)}, bf16[1024,320]{0,1:T(8,128)(2,1)S(1)}, u32[]{:S(2)}, u32[]{:S(2)}) collective-permute-start(bf16[1024,320]{0,1:T(8,128)(2,1)S(1)} %slice.180), channel_id=1, source_target_pairs={{0,24},{8,0},{16,8},{24,16},{1,25},{9,1},{17,9},{25,17},{2,26},{10... | collective-permute-start | bytes 1966088 | tf_op jit(solution)/shard_map/gather_row_stats/ppermute | solution.py:32
  163.3 3.9 %collective-permute-done.17 = bf16[1024,320]{0,1:T(8,128)(2,1)S(1)} collective-permute-done((bf16[1024,320]{0,1:T(8,128)(2,1)S(1)}, bf16[1024,320]{0,1:T(8,128)(2,1)S(1)}, u32[]{:S(2)}, u32[]{:S(2)}) %collective-permute-start.17) | collective-permute-done | bytes 655392 | tf_op jit(solution)/shard_map/gather_row_stats/ppermute | solution.py:32
  167.3 3.5 %collective-permute-done.18 = bf16[1024,320]{0,1:T(8,128)(2,1)S(1)} collective-permute-done((bf16[1024,320]{0,1:T(8,128)(2,1)S(1)}, bf16[1024,320]{0,1:T(8,128)(2,1)S(1)}, u32[]{:S(2)}, u32[]{:S(2)}) %collective-permute-start.18) | collective-permute-done | bytes 655392 | tf_op jit(solution)/shard_map/gather_row_stats/ppermute | solution.py:32
  172.1 3.1 %fusion.70 = (bf16[8192,160]{0,1:T(8,128)(2,1)S(1)}, bf16[8192,160]{0,1:T(8,128)(2,1)S(1)}) fusion(bf16[8192,320]{0,1:T(8,128)(2,1)} %all-gather.2.cloned.1.call-done), kind=kLoop, calls=%fused_computation.160 | loop fusion | bytes 10485760 | tf_op jit(solution)/shard_map/gather_sequence/slice | solution.py:114
  175.2 1.8 select_reduce_fusion.1
  176.9 2.5 select_reduce_fusion
  179.4 4.8 %fusion.76 = (f32[2,128]{1,0:T(2,128)S(1)}, bf16[2,128,8192]{2,1,0:T(8,128)(2,1)}) fusion(bf16[128,2,80]{0,2,1:T(8,128)(2,1)S(1)} %bitcast.198, bf16[8192,2,80]{0,2,1:T(8,128)(2,1)S(1)} %bitcast.184, f32[2,128,8192]{2,1,0:T(8,128)S(1)} %get-tuple-element.48, f32[2,128]{1,0:T(2,128)S(1)} %log_add_fusion, pred[128,8192]{1,0:T(8,128)(4,1)S(1)} %copy-done.2), kind=kOutput, calls=%fused_computation.166 | convolution fusion | flops 346029824 | bytes 16295936 | tf_op jit(solution)/shard_map/query_pass/qhd,khd->hqk/dot_general | solution.py:140
  184.3 2.6 fusion.43
  187.6 10.6 %all-to-all-start = ((f32[64,2,2,128]{3,2,1,0:T(2,128)}), f32[64,2,2,128]{3,2,1,0:T(2,128)}, u32[]{:S(2)}, u32[]{:S(2)}) async-start(f32[64,2,2,128]{3,2,1,0:T(2,128)} %broadcast_in_dim.95), calls=%async_computation | async-start | bytes 262144 | tf_op jit(solution)/shard_map/gather_row_stats/all_to_all | solution.py:162
  198.1 3.7 %fusion.35 = f32[128,2,80]{0,2,1:T(8,128)S(1)} fusion(f32[128,2,80]{0,2,1:T(8,128)} %fusion.43, bf16[8192,2,80]{0,2,1:T(8,128)(2,1)S(1)} %bitcast.165, bf16[2,128,8192]{2,1,0:T(8,128)(2,1)} %get-tuple-element.50), kind=kOutput, calls=%fused_computation.56 | convolution fusion | flops 335564800 | bytes 6979584 | tf_op jit(solution)/shard_map/query_pass/hqk,khd->hqd/dot_general | solution.py:145
  203.1 9.3 %all-to-all-done = f32[64,2,2,128]{3,2,1,0:T(2,128)} async-done(((f32[64,2,2,128]{3,2,1,0:T(2,128)}), f32[64,2,2,128]{3,2,1,0:T(2,128)}, u32[]{:S(2)}, u32[]{:S(2)}) %all-to-all-start) | async-done | bytes 131104 | tf_op jit(solution)/shard_map/gather_row_stats/all_to_all | solution.py:162
  215.5 1.9 fusion.10
  218.4 2.5 fusion.25
  221.0 1.9 fusion.13
  224.0 2.5 fusion.26
  226.5 1.7 gather_fusion.3
  228.2 1.8 fusion.16
  231.1 2.5 fusion.27
  235.4 1.8 fusion.19
  237.2 2.0 fusion.48
  242.7 12.5 %all_to_all.10 = f32[4,129,320]{2,1,0:T(8,128)S(1)} all-to-all(f32[4,129,320]{2,1,0:T(8,128)S(1)} %copy.31), channel_id=1, replica_groups=mesh['z'=16,'y'=4,'tp'=4,'dp'=2] {'tp'}, dimensions={0} | all-to-all | bytes 1320960 | tf_op jit(solution)/shard_map/back_projection/all_to_all | solution.py:213
  (165 shorter events, 32.6 us)
Async XLA Ops:
  6.5 15.9 %copy-start = (bf16[160,1280]{1,0:T(8,128)(2,1)S(1)}, bf16[160,1280]{1,0:T(8,128)(2,1)}, u32[]{:S(2)}) copy-start(bf16[160,1280]{1,0:T(8,128)(2,1)} %param.16) | copy-start | bytes 1228804
  6.5 165.5 %all-gather.2.cloned.1.call-start = ((), (), s32[]{:S(2)}) async-start(), calls=%async_computation.2 | async-start | bytes 5570560 | tf_op jit(solution)/shard_map/gather_sequence/all_gather | solution.py:110
  7.5 14.8 %copy-start.24 = (f32[1280]{0:T(1024)S(1)}, f32[1280]{0:T(1024)}, u32[]{:S(2)}) copy-start(f32[1280]{0:T(1024)} %param.13) | copy-start | bytes 15364
  21.2 16.6 %copy-start.30 = (f32[80]{0:T(128)S(1)}, f32[80]{0:T(128)}, u32[]{:S(2)}) copy-start(f32[80]{0:T(128)} %param.18) | copy-start | bytes 964
  21.2 16.7 %copy-start.10 = (bf16[160,1280]{1,0:T(8,128)(2,1)S(1)}, bf16[160,1280]{1,0:T(8,128)(2,1)}, u32[]{:S(2)}) copy-start(bf16[160,1280]{1,0:T(8,128)(2,1)} %param.14) | copy-start | bytes 1228804
  22.3 15.9 %copy-start.14 = (bf16[160,1280]{1,0:T(8,128)(2,1)S(1)}, bf16[160,1280]{1,0:T(8,128)(2,1)}, u32[]{:S(2)}) copy-start(bf16[160,1280]{1,0:T(8,128)(2,1)} %param.17) | copy-start | bytes 1228804
  22.4 26.9 %copy-start.1 = (s32[64]{0:T(128)S(1)}, s32[64]{0:T(128)}, u32[]{:S(2)}) copy-start(s32[64]{0:T(128)} %param.19) | copy-start | bytes 772
  38.2 17.1 %copy-start.15 = (bf16[128,160]{0,1:T(8,128)(2,1)}, bf16[128,160]{0,1:T(8,128)(2,1)S(1)}, u32[]{:S(2)}) copy-start(bf16[128,160]{0,1:T(8,128)(2,1)S(1)} %fusion.46) | copy-start | bytes 122884
  38.4 51.2 %copy-start.22 = (bf16[128,160]{0,1:T(8,128)(2,1)}, bf16[128,160]{0,1:T(8,128)(2,1)S(1)}, u32[]{:S(2)}) copy-start(bf16[128,160]{0,1:T(8,128)(2,1)S(1)} %convolution_convert_fusion) | copy-start | bytes 122884
  38.5 16.8 %collective-permute-start = (bf16[128,320]{0,1:T(8,128)(2,1)S(1)}, bf16[128,320]{0,1:T(8,128)(2,1)S(1)}, u32[]{:S(2)}, u32[]{:S(2)}) collective-permute-start(bf16[128,320]{0,1:T(8,128)(2,1)S(1)} %get-tuple-element.29), channel_id=1, source_target_pairs={{0,480},{32,0},{64,32},{96,64},{128,96},{160,128},{192,160},{224,1... | collective-permute-start | bytes 245768 | tf_op jit(solution)/shard_map/gather_sequence/ppermute | solution.py:32
  47.4 13.1 %collective-permute-start.7 = (bf16[128,320]{0,1:T(8,128)(2,1)S(1)}, bf16[128,320]{0,1:T(8,128)(2,1)S(1)}, u32[]{:S(2)}, u32[]{:S(2)}) collective-permute-start(bf16[128,320]{0,1:T(8,128)(2,1)S(1)} %get-tuple-element.29), channel_id=1, source_target_pairs={{0,32},{32,64},{64,96},{96,128},{128,160},{160,192},{192,224},{224... | collective-permute-start | bytes 245768 | tf_op jit(solution)/shard_map/gather_sequence/ppermute | solution.py:32
  50.0 5.2 %copy-start.26 = (s32[1024]{0:T(1024)}, s32[1024]{0:T(1024)S(1)}, u32[]{:S(2)}) copy-start(s32[1024]{0:T(1024)S(1)} %get-tuple-element.56) | copy-start | bytes 12292
  50.1 5.2 %copy-start.27 = (s32[1024]{0:T(1024)}, s32[1024]{0:T(1024)S(1)}, u32[]{:S(2)}) copy-start(s32[1024]{0:T(1024)S(1)} %get-tuple-element.55) | copy-start | bytes 12292
  55.3 8.0 %collective-permute-start.1 = (bf16[128,320]{0,1:T(8,128)(2,1)S(1)}, bf16[128,320]{0,1:T(8,128)(2,1)S(1)}, u32[]{:S(2)}, u32[]{:S(2)}) collective-permute-start(bf16[128,320]{0,1:T(8,128)(2,1)S(1)} %collective-permute-done), channel_id=1, source_target_pairs={{0,480},{32,0},{64,32},{96,64},{128,96},{160,128},{192,160},{224,1... | collective-permute-start | bytes 245768 | tf_op jit(solution)/shard_map/gather_sequence/ppermute | solution.py:32
  60.5 9.3 %collective-permute-start.8 = (bf16[128,320]{0,1:T(8,128)(2,1)S(1)}, bf16[128,320]{0,1:T(8,128)(2,1)S(1)}, u32[]{:S(2)}, u32[]{:S(2)}) collective-permute-start(bf16[128,320]{0,1:T(8,128)(2,1)S(1)} %collective-permute-done.7), channel_id=1, source_target_pairs={{0,32},{32,64},{64,96},{96,128},{128,160},{160,192},{192,224},{224... | collective-permute-start | bytes 245768 | tf_op jit(solution)/shard_map/gather_sequence/ppermute | solution.py:32
  63.3 8.3 %collective-permute-start.2 = (bf16[128,320]{0,1:T(8,128)(2,1)S(1)}, bf16[128,320]{0,1:T(8,128)(2,1)S(1)}, u32[]{:S(2)}, u32[]{:S(2)}) collective-permute-start(bf16[128,320]{0,1:T(8,128)(2,1)S(1)} %collective-permute-done.1), channel_id=1, source_target_pairs={{0,480},{32,0},{64,32},{96,64},{128,96},{160,128},{192,160},{224,1... | collective-permute-start | bytes 245768 | tf_op jit(solution)/shard_map/gather_sequence/ppermute | solution.py:32
  69.7 9.2 %collective-permute-start.9 = (bf16[128,320]{0,1:T(8,128)(2,1)S(1)}, bf16[128,320]{0,1:T(8,128)(2,1)S(1)}, u32[]{:S(2)}, u32[]{:S(2)}) collective-permute-start(bf16[128,320]{0,1:T(8,128)(2,1)S(1)} %collective-permute-done.8), channel_id=1, source_target_pairs={{0,32},{32,64},{64,96},{96,128},{128,160},{160,192},{192,224},{224... | collective-permute-start | bytes 245768 | tf_op jit(solution)/shard_map/gather_sequence/ppermute | solution.py:32
  71.7 9.2 %collective-permute-start.3 = (bf16[128,320]{0,1:T(8,128)(2,1)S(1)}, bf16[128,320]{0,1:T(8,128)(2,1)S(1)}, u32[]{:S(2)}, u32[]{:S(2)}) collective-permute-start(bf16[128,320]{0,1:T(8,128)(2,1)S(1)} %collective-permute-done.2), channel_id=1, source_target_pairs={{0,480},{32,0},{64,32},{96,64},{128,96},{160,128},{192,160},{224,1... | collective-permute-start | bytes 245768 | tf_op jit(solution)/shard_map/gather_sequence/ppermute | solution.py:32
  79.0 8.7 %collective-permute-start.10 = (bf16[128,320]{0,1:T(8,128)(2,1)S(1)}, bf16[128,320]{0,1:T(8,128)(2,1)S(1)}, u32[]{:S(2)}, u32[]{:S(2)}) collective-permute-start(bf16[128,320]{0,1:T(8,128)(2,1)S(1)} %collective-permute-done.9), channel_id=1, source_target_pairs={{0,32},{32,64},{64,96},{96,128},{128,160},{160,192},{192,224},{224... | collective-permute-start | bytes 245768 | tf_op jit(solution)/shard_map/gather_sequence/ppermute | solution.py:32
  80.9 8.7 %collective-permute-start.4 = (bf16[128,320]{0,1:T(8,128)(2,1)S(1)}, bf16[128,320]{0,1:T(8,128)(2,1)S(1)}, u32[]{:S(2)}, u32[]{:S(2)}) collective-permute-start(bf16[128,320]{0,1:T(8,128)(2,1)S(1)} %collective-permute-done.3), channel_id=1, source_target_pairs={{0,480},{32,0},{64,32},{96,64},{128,96},{160,128},{192,160},{224,1... | collective-permute-start | bytes 245768 | tf_op jit(solution)/shard_map/gather_sequence/ppermute | solution.py:32
  87.7 9.8 %collective-permute-start.11 = (bf16[128,320]{0,1:T(8,128)(2,1)S(1)}, bf16[128,320]{0,1:T(8,128)(2,1)S(1)}, u32[]{:S(2)}, u32[]{:S(2)}) collective-permute-start(bf16[128,320]{0,1:T(8,128)(2,1)S(1)} %collective-permute-done.10), channel_id=1, source_target_pairs={{0,32},{32,64},{64,96},{96,128},{128,160},{160,192},{192,224},{224... | collective-permute-start | bytes 245768 | tf_op jit(solution)/shard_map/gather_sequence/ppermute | solution.py:32
  89.7 9.8 %collective-permute-start.5 = (bf16[128,320]{0,1:T(8,128)(2,1)S(1)}, bf16[128,320]{0,1:T(8,128)(2,1)S(1)}, u32[]{:S(2)}, u32[]{:S(2)}) collective-permute-start(bf16[128,320]{0,1:T(8,128)(2,1)S(1)} %collective-permute-done.4), channel_id=1, source_target_pairs={{0,480},{32,0},{64,32},{96,64},{128,96},{160,128},{192,160},{224,1... | collective-permute-start | bytes 245768 | tf_op jit(solution)/shard_map/gather_sequence/ppermute | solution.py:32
  97.6 9.5 %collective-permute-start.12 = (bf16[128,320]{0,1:T(8,128)(2,1)S(1)}, bf16[128,320]{0,1:T(8,128)(2,1)S(1)}, u32[]{:S(2)}, u32[]{:S(2)}) collective-permute-start(bf16[128,320]{0,1:T(8,128)(2,1)S(1)} %collective-permute-done.11), channel_id=1, source_target_pairs={{0,32},{32,64},{64,96},{96,128},{128,160},{160,192},{192,224},{224... | collective-permute-start | bytes 245768 | tf_op jit(solution)/shard_map/gather_sequence/ppermute | solution.py:32
  99.5 19.1 %collective-permute-start.6 = (bf16[128,320]{0,1:T(8,128)(2,1)S(1)}, bf16[128,320]{0,1:T(8,128)(2,1)S(1)}, u32[]{:S(2)}, u32[]{:S(2)}) collective-permute-start(bf16[128,320]{0,1:T(8,128)(2,1)S(1)} %collective-permute-done.5), channel_id=1, source_target_pairs={{0,480},{32,0},{64,32},{96,64},{128,96},{160,128},{192,160},{224,1... | collective-permute-start | bytes 245768 | tf_op jit(solution)/shard_map/gather_sequence/ppermute | solution.py:32
  107.1 9.6 %collective-permute-start.13 = (bf16[128,320]{0,1:T(8,128)(2,1)S(1)}, bf16[128,320]{0,1:T(8,128)(2,1)S(1)}, u32[]{:S(2)}, u32[]{:S(2)}) collective-permute-start(bf16[128,320]{0,1:T(8,128)(2,1)S(1)} %collective-permute-done.12), channel_id=1, source_target_pairs={{0,32},{32,64},{64,96},{96,128},{128,160},{160,192},{192,224},{224... | collective-permute-start | bytes 245768 | tf_op jit(solution)/shard_map/gather_sequence/ppermute | solution.py:32
  116.7 8.9 %collective-permute-start.14 = (bf16[128,320]{0,1:T(8,128)(2,1)S(1)}, bf16[128,320]{0,1:T(8,128)(2,1)S(1)}, u32[]{:S(2)}, u32[]{:S(2)}) collective-permute-start(bf16[128,320]{0,1:T(8,128)(2,1)S(1)} %collective-permute-done.13), channel_id=1, source_target_pairs={{0,32},{32,64},{64,96},{96,128},{128,160},{160,192},{192,224},{224... | collective-permute-start | bytes 245768 | tf_op jit(solution)/shard_map/gather_sequence/ppermute | solution.py:32
  125.8 28.9 %collective-permute-start.16 = (bf16[2048,320]{0,1:T(8,128)(2,1)S(1)}, bf16[2048,320]{0,1:T(8,128)(2,1)S(1)}, u32[]{:S(2)}, u32[]{:S(2)}) collective-permute-start(bf16[2048,320]{0,1:T(8,128)(2,1)S(1)} %constant_dynamic-update-slice_fusion), channel_id=1, source_target_pairs={{0,8},{8,16},{16,24},{24,0},{1,9},{9,17},{17,25},{25,1},{2,10},{10... | collective-permute-start | bytes 3932168 | tf_op jit(solution)/shard_map/gather_sequence/ppermute | solution.py:32
  128.1 28.9 %collective-permute-start.15 = (bf16[2048,320]{0,1:T(8,128)(2,1)S(1)}, bf16[2048,320]{0,1:T(8,128)(2,1)S(1)}, u32[]{:S(2)}, u32[]{:S(2)}) collective-permute-start(bf16[2048,320]{0,1:T(8,128)(2,1)S(1)} %constant_dynamic-update-slice_fusion), channel_id=1, source_target_pairs={{0,24},{8,0},{16,8},{24,16},{1,25},{9,1},{17,9},{25,17},{2,26},{10... | collective-permute-start | bytes 3932168 | tf_op jit(solution)/shard_map/gather_sequence/ppermute | solution.py:32
  154.8 12.5 %collective-permute-start.17 = (bf16[1024,320]{0,1:T(8,128)(2,1)S(1)}, bf16[1024,320]{0,1:T(8,128)(2,1)S(1)}, u32[]{:S(2)}, u32[]{:S(2)}) collective-permute-start(bf16[1024,320]{0,1:T(8,128)(2,1)S(1)} %slice.179), channel_id=1, source_target_pairs={{0,8},{8,16},{16,24},{24,0},{1,9},{9,17},{17,25},{25,1},{2,10},{10... | collective-permute-start | bytes 1966088 | tf_op jit(solution)/shard_map/gather_row_stats/ppermute | solution.py:32
  157.1 13.7 %collective-permute-start.18 = (bf16[1024,320]{0,1:T(8,128)(2,1)S(1)}, bf16[1024,320]{0,1:T(8,128)(2,1)S(1)}, u32[]{:S(2)}, u32[]{:S(2)}) collective-permute-start(bf16[1024,320]{0,1:T(8,128)(2,1)S(1)} %slice.180), channel_id=1, source_target_pairs={{0,24},{8,0},{16,8},{24,16},{1,25},{9,1},{17,9},{25,17},{2,26},{10... | collective-permute-start | bytes 1966088 | tf_op jit(solution)/shard_map/gather_row_stats/ppermute | solution.py:32
  172.1 3.1 %copy-start.2 = (pred[128,8192]{1,0:T(8,128)(4,1)S(1)}, pred[128,8192]{1,0:T(8,128)(4,1)}, u32[]{:S(2)}) copy-start(pred[128,8192]{1,0:T(8,128)(4,1)} %broadcast_compare_fusion) | copy-start | bytes 3145732
  172.1 3.1 %copy-start.16 = (bf16[128,160]{0,1:T(8,128)(2,1)S(1)}, bf16[128,160]{0,1:T(8,128)(2,1)}, u32[]{:S(2)}) copy-start(bf16[128,160]{0,1:T(8,128)(2,1)} %copy-done.15) | copy-start | bytes 122884
  176.9 2.5 copy-start.23
  187.6 24.9 %all-to-all-start = ((f32[64,2,2,128]{3,2,1,0:T(2,128)}), f32[64,2,2,128]{3,2,1,0:T(2,128)}, u32[]{:S(2)}, u32[]{:S(2)}) async-start(f32[64,2,2,128]{3,2,1,0:T(2,128)} %broadcast_in_dim.95), calls=%async_computation | async-start | bytes 262144 | tf_op jit(solution)/shard_map/gather_row_stats/all_to_all | solution.py:162
  201.9 15.4 %copy-start.5 = (bf16[2048,160]{0,1:T(8,128)(2,1)S(1)}, bf16[2048,160]{0,1:T(8,128)(2,1)}, u32[]{:S(2)}) copy-start(bf16[2048,160]{0,1:T(8,128)(2,1)} %get-tuple-element.25) | copy-start | bytes 1966084
  218.4 2.5 copy-start.13
  224.0 4.2 %copy-start.12 = (pred[128,2048]{1,0:T(8,128)(4,1)S(1)}, pred[128,2048]{1,0:T(8,128)(4,1)}, u32[]{:S(2)}) copy-start(pred[128,2048]{1,0:T(8,128)(4,1)} %get-tuple-element.44) | copy-start | bytes 786436
  226.5 3.5 %copy-start.4 = (bf16[2048,160]{0,1:T(8,128)(2,1)S(1)}, bf16[2048,160]{0,1:T(8,128)(2,1)}, u32[]{:S(2)}) copy-start(bf16[2048,160]{0,1:T(8,128)(2,1)} %get-tuple-element.21) | copy-start | bytes 1966084
  231.1 4.2 %copy-start.11 = (pred[128,2048]{1,0:T(8,128)(4,1)S(1)}, pred[128,2048]{1,0:T(8,128)(4,1)}, u32[]{:S(2)}) copy-start(pred[128,2048]{1,0:T(8,128)(4,1)} %get-tuple-element.43) | copy-start | bytes 786436
  233.7 3.5 %copy-start.3 = (bf16[2048,160]{0,1:T(8,128)(2,1)S(1)}, bf16[2048,160]{0,1:T(8,128)(2,1)}, u32[]{:S(2)}) copy-start(bf16[2048,160]{0,1:T(8,128)(2,1)} %get-tuple-element.19) | copy-start | bytes 1966084
  237.2 3.6 %copy-start.17 = (f32[2,80,128]{2,1,0:T(8,128)S(1)}, f32[2,80,128]{2,1,0:T(8,128)}, u32[]{:S(2)}) copy-start(f32[2,80,128]{2,1,0:T(8,128)} %fusion.49) | copy-start | bytes 245764
  237.2 3.6 %copy-start.18 = (f32[2,80,128]{2,1,0:T(8,128)S(1)}, f32[2,80,128]{2,1,0:T(8,128)}, u32[]{:S(2)}) copy-start(f32[2,80,128]{2,1,0:T(8,128)} %fusion.51) | copy-start | bytes 245764
  237.2 3.6 %copy-start.19 = (f32[2,80,128]{2,1,0:T(8,128)S(1)}, f32[2,80,128]{2,1,0:T(8,128)}, u32[]{:S(2)}) copy-start(f32[2,80,128]{2,1,0:T(8,128)} %fusion.53) | copy-start | bytes 245764
  239.2 2.1 copy-start.8
  239.2 2.1 copy-start.25
  242.6 12.8 %copy-start.20 = (bf16[128,320]{0,1:T(8,128)(2,1)S(1)}, bf16[128,320]{0,1:T(8,128)(2,1)}, u32[]{:S(2)}) copy-start(bf16[128,320]{0,1:T(8,128)(2,1)} %param.11) | copy-start | bytes 245764
  242.6 12.8 %copy-start.21 = (bf16[128,320]{0,1:T(8,128)(2,1)S(1)}, bf16[128,320]{0,1:T(8,128)(2,1)}, u32[]{:S(2)}) copy-start(bf16[128,320]{0,1:T(8,128)(2,1)} %param.12) | copy-start | bytes 245764
  242.6 12.8 %copy-start.29 = (f32[128]{0:T(128)S(1)}, f32[128]{0:T(128)}, u32[]{:S(2)}) copy-start(f32[128]{0:T(128)} %copy-done.28) | copy-start | bytes 1540
  (4 other events, 5.2 us)
Sparse Core Ops, SparseCore 0:
  37.9 92.8 all-gather.1

commit v12 on v7

--- a/solution.py
+++ b/solution.py
@@ -189,12 +189,14 @@
             score_grad = (attend_t * (grad_probs_t - delta_part[:, None, :])).astype(
                 jnp.bfloat16
             )
+            plain_t = attend_t.astype(jnp.bfloat16)
+            score_grad, plain_t = lax.optimization_barrier((score_grad, plain_t))
             key_grad = key_grad + jnp.einsum(
                 "hkq,qhd->khd", score_grad, query_part, preferred_element_type=jnp.float32
             )
             value_grad = value_grad + jnp.einsum(
                 "hkq,qhd->khd",
-                attend_t.astype(jnp.bfloat16),
+                plain_t,
                 grad_part,
                 preferred_element_type=jnp.float32,
             )

time: 242 us -> 237 us (0.979)
  matrix products: 36.1 us -> 31.5 us
  waiting for transfers between devices: 26.5 us -> 23.7 us
    dot_general x4, matrix products: 12.2 us -> 3.3 us  [per_device(): jnp.einsum('hkq,qhd->khd', score_grad, query_part, preferred_element_type...]
    dot_general x4 -> x8, matrix products: 4.74 us -> 7.6 us  [the longest x4 4.66 us: per_device(): jnp.einsum('hkq,qhd->khd', plain_t, grad_part, preferred_element_type=jnp...]
    gather x4, local copies, waits for them, and re-layouts: 3.64 us -> 6.46 us  [per_device(): part_stats = stats_all[source]]
    dot_general x4, matrix products: 6.32 us -> 9.01 us  [per_device(): jnp.einsum('khd,qhd->hkq', key_heads, query_part, preferred_element_type=...]
    unnamed x90 -> x74, local copies, waits for them, and re-layouts: 12.9 us -> 11.3 us
  transfers between devices with their start and end apart: 21 -> 21, of which waited for: 13 -> 13; matrix products, arithmetic and copies ran while one was open for 26% -> 28% of each run, Pallas kernels for 0% -> 0%
where the time goes in v12:
time: 237 us; the launch traced here: 234 us
  starting transfers between devices  78.7 us (33%)
  blocking collectives  40.2 us (17%)
  local copies, waits for them, and re-layouts  37.1 us (16%)
  matrix products  31.5 us (13%)
  waiting for transfers between devices  23.7 us (10%)
  between operations  14.9 us (6%)
  other arithmetic  8.24 us (3%)
    ppermute x19, starting transfers between devices, shift(): lax.ppermute(data, axis, [(i, (i + step) % size) for i in range(size)])  68.8 us
    ppermute x19, waiting for transfers between devices, shift(): lax.ppermute(data, axis, [(i, (i + step) % size) for i in range(size)])  22.5 us
    all_gather x1, blocking collectives, per_device(): kv_all = lax.all_gather(kv, 'y', axis=0, tiled=True)  14.6 us
    all_gather x1, blocking collectives, per_device(): gathered = lax.all_gather(both, 'tp', axis=1, tiled=True)  13.4 us
    all_to_all x1, blocking collectives, per_device(): received = lax.all_to_all(payload, 'tp', 0, 0, tiled=False)  12.3 us
    unnamed x74, local copies, waits for them, and re-layouts  11.3 us
    all_to_all x1, starting transfers between devices, per_device(): stats_all = lax.all_to_all(sent, ('z', 'y'), 0, 0, tiled=False)  9.95 us
    dot_general x4, matrix products, per_device(): jnp.einsum('khd,qhd->hkq', key_heads, query_part, preferred_element_type=...  9.01 us
  transfers between devices with their start and end apart: 21, of which 13 were waited for; matrix products, arithmetic and copies ran while one was open for 28% of the time, Pallas kernels for 0%

profile of v12, /device:TPU:24, one launch (start us, length us, event | category | flops | bytes accessed | tf_op | source)
XLA Modules:
  0.0 234.4 jit_solution(15772210486136860648)
XLA Ops:
  7.5 13.4 %all_gather.9 = bf16[128,2560]{0,1:T(8,128)(2,1)S(1)} all-gather(bf16[128,640]{0,1:T(8,128)(2,1)S(1)} %pad_maximum_fusion.1), channel_id=1, replica_groups=mesh['z'=16,'y'=4,'tp'=4,'dp'=2] {'tp'}, dimensions={1}, use_global_device_ids=true | all-gather | bytes 819200 | tf_op jit(solution)/shard_map/gather_features/all_gather | solution.py:77
  22.3 14.6 %all_gather.10 = bf16[512,320]{0,1:T(8,128)(2,1)} all-gather(bf16[128,320]{0,1:T(8,128)(2,1)S(1)} %pad_maximum_fusion.2), channel_id=1, replica_groups=mesh['z'=16,'y'=4,'tp'=4,'dp'=2] {'y'}, dimensions={0}, use_global_device_ids=true | all-gather | bytes 409600 | tf_op jit(solution)/shard_map/gather_sequence/all_gather | solution.py:109
  38.2 8.9 %collective-permute-start = (bf16[128,320]{0,1:T(8,128)(2,1)S(1)}, bf16[128,320]{0,1:T(8,128)(2,1)S(1)}, u32[]{:S(2)}, u32[]{:S(2)}) collective-permute-start(bf16[128,320]{0,1:T(8,128)(2,1)S(1)} %get-tuple-element.51), channel_id=1, source_target_pairs={{0,480},{32,0},{64,32},{96,64},{128,96},{160,128},{192,160},{224,1... | collective-permute-start | bytes 245768 | tf_op jit(solution)/shard_map/gather_sequence/ppermute | solution.py:32
  47.1 1.9 collective-permute-start.7
  54.2 1.6 broadcast_compare_fusion.4
  55.8 5.1 %collective-permute-start.1 = (bf16[128,320]{0,1:T(8,128)(2,1)S(1)}, bf16[128,320]{0,1:T(8,128)(2,1)S(1)}, u32[]{:S(2)}, u32[]{:S(2)}) collective-permute-start(bf16[128,320]{0,1:T(8,128)(2,1)S(1)} %collective-permute-done), channel_id=1, source_target_pairs={{0,480},{32,0},{64,32},{96,64},{128,96},{160,128},{192,160},{224,1... | collective-permute-start | bytes 245768 | tf_op jit(solution)/shard_map/gather_sequence/ppermute | solution.py:32
  61.0 1.9 collective-permute-start.8
  63.8 5.6 %collective-permute-start.2 = (bf16[128,320]{0,1:T(8,128)(2,1)S(1)}, bf16[128,320]{0,1:T(8,128)(2,1)S(1)}, u32[]{:S(2)}, u32[]{:S(2)}) collective-permute-start(bf16[128,320]{0,1:T(8,128)(2,1)S(1)} %collective-permute-done.1), channel_id=1, source_target_pairs={{0,480},{32,0},{64,32},{96,64},{128,96},{160,128},{192,160},{224,1... | collective-permute-start | bytes 245768 | tf_op jit(solution)/shard_map/gather_sequence/ppermute | solution.py:32
  70.0 1.9 collective-permute-start.9
  72.8 5.6 %collective-permute-start.3 = (bf16[128,320]{0,1:T(8,128)(2,1)S(1)}, bf16[128,320]{0,1:T(8,128)(2,1)S(1)}, u32[]{:S(2)}, u32[]{:S(2)}) collective-permute-start(bf16[128,320]{0,1:T(8,128)(2,1)S(1)} %collective-permute-done.2), channel_id=1, source_target_pairs={{0,480},{32,0},{64,32},{96,64},{128,96},{160,128},{192,160},{224,1... | collective-permute-start | bytes 245768 | tf_op jit(solution)/shard_map/gather_sequence/ppermute | solution.py:32
  79.0 1.9 collective-permute-start.10
  81.8 5.6 %collective-permute-start.4 = (bf16[128,320]{0,1:T(8,128)(2,1)S(1)}, bf16[128,320]{0,1:T(8,128)(2,1)S(1)}, u32[]{:S(2)}, u32[]{:S(2)}) collective-permute-start(bf16[128,320]{0,1:T(8,128)(2,1)S(1)} %collective-permute-done.3), channel_id=1, source_target_pairs={{0,480},{32,0},{64,32},{96,64},{128,96},{160,128},{192,160},{224,1... | collective-permute-start | bytes 245768 | tf_op jit(solution)/shard_map/gather_sequence/ppermute | solution.py:32
  88.1 1.9 collective-permute-start.11
  90.7 5.5 %collective-permute-start.5 = (bf16[128,320]{0,1:T(8,128)(2,1)S(1)}, bf16[128,320]{0,1:T(8,128)(2,1)S(1)}, u32[]{:S(2)}, u32[]{:S(2)}) collective-permute-start(bf16[128,320]{0,1:T(8,128)(2,1)S(1)} %collective-permute-done.4), channel_id=1, source_target_pairs={{0,480},{32,0},{64,32},{96,64},{128,96},{160,128},{192,160},{224,1... | collective-permute-start | bytes 245768 | tf_op jit(solution)/shard_map/gather_sequence/ppermute | solution.py:32
  96.2 1.7 collective-permute-done.11
  97.9 1.9 collective-permute-start.12
  100.4 5.1 %collective-permute-start.6 = (bf16[128,320]{0,1:T(8,128)(2,1)S(1)}, bf16[128,320]{0,1:T(8,128)(2,1)S(1)}, u32[]{:S(2)}, u32[]{:S(2)}) collective-permute-start(bf16[128,320]{0,1:T(8,128)(2,1)S(1)} %collective-permute-done.5), channel_id=1, source_target_pairs={{0,480},{32,0},{64,32},{96,64},{128,96},{160,128},{192,160},{224,1... | collective-permute-start | bytes 245768 | tf_op jit(solution)/shard_map/gather_sequence/ppermute | solution.py:32
  105.6 1.9 collective-permute-done.12
  107.4 1.9 collective-permute-start.13
  110.0 6.8 %collective-permute-done.13 = bf16[128,320]{0,1:T(8,128)(2,1)S(1)} collective-permute-done((bf16[128,320]{0,1:T(8,128)(2,1)S(1)}, bf16[128,320]{0,1:T(8,128)(2,1)S(1)}, u32[]{:S(2)}, u32[]{:S(2)}) %collective-permute-start.13) | collective-permute-done | bytes 81952 | tf_op jit(solution)/shard_map/gather_sequence/ppermute | solution.py:32
  116.8 1.9 collective-permute-start.14
  119.4 6.0 %collective-permute-done.14 = bf16[128,320]{0,1:T(8,128)(2,1)S(1)} collective-permute-done((bf16[128,320]{0,1:T(8,128)(2,1)S(1)}, bf16[128,320]{0,1:T(8,128)(2,1)S(1)}, u32[]{:S(2)}, u32[]{:S(2)}) %collective-permute-start.14) | collective-permute-done | bytes 81952 | tf_op jit(solution)/shard_map/gather_sequence/ppermute | solution.py:32
  130.6 3.9 %collective-permute-start.15 = (bf16[2048,320]{0,1:T(8,128)(2,1)}, bf16[2048,320]{0,1:T(8,128)(2,1)}, u32[]{:S(2)}, u32[]{:S(2)}) collective-permute-start(bf16[2048,320]{0,1:T(8,128)(2,1)} %constant_dynamic-update-slice_fusion), channel_id=1, source_target_pairs={{0,8},{8,16},{16,24},{24,0},{1,9},{9,17},{17,25},{25,1},{2,10},{10... | collective-permute-start | bytes 3932168 | tf_op jit(solution)/shard_map/gather_sequence/ppermute | solution.py:32
  134.6 2.1 collective-permute-start.16
  136.7 2.3 fusion.55
  138.9 3.0 %fusion.54 = (bf16[8192,160]{0,1:T(8,128)(2,1)S(1)}, bf16[8192,160]{0,1:T(8,128)(2,1)S(1)}) fusion(bf16[8192,320]{0,1:T(8,128)(2,1)} %all-gather.2.cloned.1.call-done), kind=kLoop, calls=%fused_computation.145 | loop fusion | bytes 10485760 | tf_op jit(solution)/shard_map/gather_sequence/slice | solution.py:114
  141.9 1.8 select_reduce_fusion.1
  143.7 2.5 %select_reduce_fusion = f32[2,128]{1,0:T(2,128)S(1)} fusion(f32[2,128,8192]{2,1,0:T(8,128)S(1)} %get-tuple-element.70, f32[2,128]{1,0:T(2,128)S(1)} %get-tuple-element.69, pred[128,8192]{1,0:T(8,128)(4,1)S(1)} %broadcast_compare_fusion), kind=kLoop, calls=%fused_computation.10 | loop fusion | flops 8388352 | bytes 9439232 | tf_op jit(solution)/shard_map/query_pass/reduce_sum | solution.py:137
  146.2 3.5 %fusion.60 = (f32[2,128]{1,0:T(2,128)S(1)}, bf16[2,128,8192]{2,1,0:T(8,128)(2,1)S(1)}) fusion(bf16[128,2,80]{0,2,1:T(8,128)(2,1)S(1)} %bitcast.206, bf16[8192,2,80]{0,2,1:T(8,128)(2,1)S(1)} %bitcast.192, f32[2,128,8192]{2,1,0:T(8,128)S(1)} %get-tuple-element.70, f32[2,128]{1,0:T(2,128)S(1)} %log_add_fusion, pred[128,8192]{1,0:T(8,128)(4,1)S(1)} %broadcast_compare_fusion), kind=kOutput, calls=%fused_computation.151 | convolution fusion | flops 346029824 | bytes 16295936 | tf_op jit(solution)/shard_map/query_pass/qhd,khd->hqk/dot_general | solution.py:140
  149.7 2.0 fusion.38
  151.7 1.5 fusion.28
  154.8 3.1 %collective-permute-done.16 = bf16[2048,320]{0,1:T(8,128)(2,1)} collective-permute-done((bf16[2048,320]{0,1:T(8,128)(2,1)}, bf16[2048,320]{0,1:T(8,128)(2,1)}, u32[]{:S(2)}, u32[]{:S(2)}) %collective-permute-start.16) | collective-permute-done | bytes 1310752 | tf_op jit(solution)/shard_map/gather_sequence/ppermute | solution.py:32
  158.6 10.0 %all-to-all-start = ((f32[64,2,2,128]{3,2,1,0:T(2,128)}), f32[64,2,2,128]{3,2,1,0:T(2,128)}, u32[]{:S(2)}, u32[]{:S(2)}) async-start(f32[64,2,2,128]{3,2,1,0:T(2,128)} %broadcast_in_dim.95), calls=%async_computation | async-start | bytes 262144 | tf_op jit(solution)/shard_map/gather_row_stats/all_to_all | solution.py:163
  168.6 2.1 slice.135
  170.7 2.4 %collective-permute-start.17 = (bf16[1024,320]{0,1:T(8,128)(2,1)}, bf16[1024,320]{0,1:T(8,128)(2,1)}, u32[]{:S(2)}, u32[]{:S(2)}) collective-permute-start(bf16[1024,320]{0,1:T(8,128)(2,1)} %slice.135), channel_id=1, source_target_pairs={{0,8},{8,16},{16,24},{24,0},{1,9},{9,17},{17,25},{25,1},{2,10},{10... | collective-permute-start | bytes 1966088 | tf_op jit(solution)/shard_map/gather_row_stats/ppermute | solution.py:32
  173.1 2.0 slice.136
  175.1 3.6 %collective-permute-start.18 = (bf16[1024,320]{0,1:T(8,128)(2,1)}, bf16[1024,320]{0,1:T(8,128)(2,1)}, u32[]{:S(2)}, u32[]{:S(2)}) collective-permute-start(bf16[1024,320]{0,1:T(8,128)(2,1)} %slice.136), channel_id=1, source_target_pairs={{0,24},{8,0},{16,8},{24,16},{1,25},{9,1},{17,9},{25,17},{2,26},{10... | collective-permute-start | bytes 1966088 | tf_op jit(solution)/shard_map/gather_row_stats/ppermute | solution.py:32
  178.7 3.0 %fusion.56 = (bf16[2048,160]{0,1:T(8,128)(2,1)}, bf16[2048,160]{0,1:T(8,128)(2,1)S(1)}, bf16[2048,160]{0,1:T(8,128)(2,1)S(1)}, bf16[2048,160]{0,1:T(8,128)(2,1)}) fusion(bf16[2048,320]{0,1:T(8,128)(2,1)} %collective-permute-done.16, bf16[2048,320]{0,1:T(8,128)(2,1)} %collective-permute-done.15), kind=kLoop, calls=%fused_computation.147 | loop fusion | bytes 5242880 | tf_op jit(solution)/shard_map/key_pass/slice | solution.py:172
  182.9 1.6 gather_fusion.7
  184.5 2.8 %fusion.61 = (bf16[2,128,2048]{2,1,0:T(8,128)(2,1)}, f32[2,128,2048]{2,1,0:T(8,128)S(1)}) fusion(f32[2,2048]{1,0:T(2,128)S(1)} %get-tuple-element.60, bf16[128,2,80]{0,2,1:T(8,128)(2,1)S(1)} %bitcast.199, bf16[2048,2,80]{0,2,1:T(8,128)(2,1)S(1)} %bitcast.176, pred[128,2048]{1,0:T(8,128)(4,1)} %get-tuple-element.68), kind=kOutput, calls=%fused_computation.152 | convolution fusion | flops 85458944 | bytes 4120576 | tf_op jit(solution)/shard_map/key_pass/khd,qhd->hkq/dot_general | solution.py:179
  189.0 1.6 gather_fusion.3
  190.6 2.7 %fusion.63 = (bf16[2,128,2048]{2,1,0:T(8,128)(2,1)}, f32[2,128,2048]{2,1,0:T(8,128)S(1)}) fusion(f32[2,2048]{1,0:T(2,128)S(1)} %get-tuple-element.56, bf16[128,2,80]{0,2,1:T(8,128)(2,1)S(1)} %bitcast.200, bf16[2048,2,80]{0,2,1:T(8,128)(2,1)S(1)} %bitcast.174, pred[128,2048]{1,0:T(8,128)(4,1)} %get-tuple-element.66), kind=kOutput, calls=%fused_computation.154 | convolution fusion | flops 85458944 | bytes 4120576 | tf_op jit(solution)/shard_map/key_pass/khd,qhd->hkq/dot_general | solution.py:179
  195.0 1.6 gather_fusion.1
  196.6 2.5 %fusion.71 = f32[2,80,128]{2,1,0:T(8,128)} fusion(bf16[2048,2,80]{0,2,1:T(8,128)(2,1)} %bitcast.184, bf16[2,128,2048]{2,1,0:T(8,128)(2,1)} %get-tuple-element.38), kind=kOutput, calls=%fused_computation.162 | convolution fusion | flops 83886080 | bytes 1785856 | tf_op jit(solution)/shard_map/key_pass/hkq,qhd->khd/dot_general | solution.py:197
  199.2 2.8 %fusion.64 = (bf16[2,128,2048]{2,1,0:T(8,128)(2,1)}, f32[2,128,2048]{2,1,0:T(8,128)S(1)}) fusion(f32[2,2048]{1,0:T(2,128)S(1)} %get-tuple-element.54, bf16[128,2,80]{0,2,1:T(8,128)(2,1)S(1)} %bitcast.201, bf16[2048,2,80]{0,2,1:T(8,128)(2,1)S(1)} %bitcast.180, pred[128,2048]{1,0:T(8,128)(4,1)} %get-tuple-element.65), kind=kOutput, calls=%fused_computation.155 | convolution fusion | flops 85458944 | bytes 4120576 | tf_op jit(solution)/shard_map/key_pass/khd,qhd->hkq/dot_general | solution.py:179
  201.9 1.5 fusion.20
  204.6 1.6 gather_fusion.5
  214.3 12.3 %all_to_all.10 = f32[4,129,320]{2,1,0:T(8,128)S(1)} all-to-all(f32[4,129,320]{2,1,0:T(8,128)S(1)} %copy.31), channel_id=1, replica_groups=mesh['z'=16,'y'=4,'tp'=4,'dp'=2] {'tp'}, dimensions={0} | all-to-all | bytes 1320960 | tf_op jit(solution)/shard_map/back_projection/all_to_all | solution.py:216
  (164 shorter events, 37.1 us)
Async XLA Ops:
  6.5 15.1 %copy-start = (bf16[160,1280]{1,0:T(8,128)(2,1)S(1)}, bf16[160,1280]{1,0:T(8,128)(2,1)}, u32[]{:S(2)}) copy-start(bf16[160,1280]{1,0:T(8,128)(2,1)} %param.16) | copy-start | bytes 1228804
  6.5 132.4 %all-gather.2.cloned.1.call-start = ((), (), s32[]{:S(2)}) async-start(), calls=%async_computation.2 | async-start | bytes 5570560 | tf_op jit(solution)/shard_map/gather_sequence/all_gather | solution.py:110
  7.5 13.9 %copy-start.20 = (f32[1280]{0:T(1024)S(1)}, f32[1280]{0:T(1024)}, u32[]{:S(2)}) copy-start(f32[1280]{0:T(1024)} %param.13) | copy-start | bytes 15364
  21.2 15.7 %copy-start.28 = (f32[80]{0:T(128)S(1)}, f32[80]{0:T(128)}, u32[]{:S(2)}) copy-start(f32[80]{0:T(128)} %param.18) | copy-start | bytes 964
  21.2 15.8 %copy-start.13 = (bf16[160,1280]{1,0:T(8,128)(2,1)S(1)}, bf16[160,1280]{1,0:T(8,128)(2,1)}, u32[]{:S(2)}) copy-start(bf16[160,1280]{1,0:T(8,128)(2,1)} %param.17) | copy-start | bytes 1228804
  21.5 15.8 %copy-start.10 = (bf16[160,1280]{1,0:T(8,128)(2,1)S(1)}, bf16[160,1280]{1,0:T(8,128)(2,1)}, u32[]{:S(2)}) copy-start(bf16[160,1280]{1,0:T(8,128)(2,1)} %param.14) | copy-start | bytes 1228804
  21.6 27.4 %copy-start.1 = (s32[64]{0:T(128)S(1)}, s32[64]{0:T(128)}, u32[]{:S(2)}) copy-start(s32[64]{0:T(128)} %param.19) | copy-start | bytes 772
  38.2 17.6 %collective-permute-start = (bf16[128,320]{0,1:T(8,128)(2,1)S(1)}, bf16[128,320]{0,1:T(8,128)(2,1)S(1)}, u32[]{:S(2)}, u32[]{:S(2)}) collective-permute-start(bf16[128,320]{0,1:T(8,128)(2,1)S(1)} %get-tuple-element.51), channel_id=1, source_target_pairs={{0,480},{32,0},{64,32},{96,64},{128,96},{160,128},{192,160},{224,1... | collective-permute-start | bytes 245768 | tf_op jit(solution)/shard_map/gather_sequence/ppermute | solution.py:32
  47.1 13.8 %collective-permute-start.7 = (bf16[128,320]{0,1:T(8,128)(2,1)S(1)}, bf16[128,320]{0,1:T(8,128)(2,1)S(1)}, u32[]{:S(2)}, u32[]{:S(2)}) collective-permute-start(bf16[128,320]{0,1:T(8,128)(2,1)S(1)} %get-tuple-element.51), channel_id=1, source_target_pairs={{0,32},{32,64},{64,96},{96,128},{128,160},{160,192},{192,224},{224... | collective-permute-start | bytes 245768 | tf_op jit(solution)/shard_map/gather_sequence/ppermute | solution.py:32
  49.8 1.3 copy-start.23
  49.8 6.0 %copy-start.24 = (s32[1024]{0:T(1024)}, s32[1024]{0:T(1024)S(1)}, u32[]{:S(2)}) copy-start(s32[1024]{0:T(1024)S(1)} %get-tuple-element.87) | copy-start | bytes 12292
  51.2 58.8 %copy-start.22 = (s32[1024]{0:T(1024)}, s32[1024]{0:T(1024)S(1)}, u32[]{:S(2)}) copy-start(s32[1024]{0:T(1024)S(1)} %get-tuple-element.86) | copy-start | bytes 12292
  51.2 58.8 %copy-start.25 = (s32[1024]{0:T(1024)}, s32[1024]{0:T(1024)S(1)}, u32[]{:S(2)}) copy-start(s32[1024]{0:T(1024)S(1)} %get-tuple-element.85) | copy-start | bytes 12292
  55.8 8.0 %collective-permute-start.1 = (bf16[128,320]{0,1:T(8,128)(2,1)S(1)}, bf16[128,320]{0,1:T(8,128)(2,1)S(1)}, u32[]{:S(2)}, u32[]{:S(2)}) collective-permute-start(bf16[128,320]{0,1:T(8,128)(2,1)S(1)} %collective-permute-done), channel_id=1, source_target_pairs={{0,480},{32,0},{64,32},{96,64},{128,96},{160,128},{192,160},{224,1... | collective-permute-start | bytes 245768 | tf_op jit(solution)/shard_map/gather_sequence/ppermute | solution.py:32
  61.0 9.0 %collective-permute-start.8 = (bf16[128,320]{0,1:T(8,128)(2,1)S(1)}, bf16[128,320]{0,1:T(8,128)(2,1)S(1)}, u32[]{:S(2)}, u32[]{:S(2)}) collective-permute-start(bf16[128,320]{0,1:T(8,128)(2,1)S(1)} %collective-permute-done.7), channel_id=1, source_target_pairs={{0,32},{32,64},{64,96},{96,128},{128,160},{160,192},{192,224},{224... | collective-permute-start | bytes 245768 | tf_op jit(solution)/shard_map/gather_sequence/ppermute | solution.py:32
  63.8 9.0 %collective-permute-start.2 = (bf16[128,320]{0,1:T(8,128)(2,1)S(1)}, bf16[128,320]{0,1:T(8,128)(2,1)S(1)}, u32[]{:S(2)}, u32[]{:S(2)}) collective-permute-start(bf16[128,320]{0,1:T(8,128)(2,1)S(1)} %collective-permute-done.1), channel_id=1, source_target_pairs={{0,480},{32,0},{64,32},{96,64},{128,96},{160,128},{192,160},{224,1... | collective-permute-start | bytes 245768 | tf_op jit(solution)/shard_map/gather_sequence/ppermute | solution.py:32
  70.0 9.0 %collective-permute-start.9 = (bf16[128,320]{0,1:T(8,128)(2,1)S(1)}, bf16[128,320]{0,1:T(8,128)(2,1)S(1)}, u32[]{:S(2)}, u32[]{:S(2)}) collective-permute-start(bf16[128,320]{0,1:T(8,128)(2,1)S(1)} %collective-permute-done.8), channel_id=1, source_target_pairs={{0,32},{32,64},{64,96},{96,128},{128,160},{160,192},{192,224},{224... | collective-permute-start | bytes 245768 | tf_op jit(solution)/shard_map/gather_sequence/ppermute | solution.py:32
  72.8 8.9 %collective-permute-start.3 = (bf16[128,320]{0,1:T(8,128)(2,1)S(1)}, bf16[128,320]{0,1:T(8,128)(2,1)S(1)}, u32[]{:S(2)}, u32[]{:S(2)}) collective-permute-start(bf16[128,320]{0,1:T(8,128)(2,1)S(1)} %collective-permute-done.2), channel_id=1, source_target_pairs={{0,480},{32,0},{64,32},{96,64},{128,96},{160,128},{192,160},{224,1... | collective-permute-start | bytes 245768 | tf_op jit(solution)/shard_map/gather_sequence/ppermute | solution.py:32
  79.0 9.1 %collective-permute-start.10 = (bf16[128,320]{0,1:T(8,128)(2,1)S(1)}, bf16[128,320]{0,1:T(8,128)(2,1)S(1)}, u32[]{:S(2)}, u32[]{:S(2)}) collective-permute-start(bf16[128,320]{0,1:T(8,128)(2,1)S(1)} %collective-permute-done.9), channel_id=1, source_target_pairs={{0,32},{32,64},{64,96},{96,128},{128,160},{160,192},{192,224},{224... | collective-permute-start | bytes 245768 | tf_op jit(solution)/shard_map/gather_sequence/ppermute | solution.py:32
  81.8 8.9 %collective-permute-start.4 = (bf16[128,320]{0,1:T(8,128)(2,1)S(1)}, bf16[128,320]{0,1:T(8,128)(2,1)S(1)}, u32[]{:S(2)}, u32[]{:S(2)}) collective-permute-start(bf16[128,320]{0,1:T(8,128)(2,1)S(1)} %collective-permute-done.3), channel_id=1, source_target_pairs={{0,480},{32,0},{64,32},{96,64},{128,96},{160,128},{192,160},{224,1... | collective-permute-start | bytes 245768 | tf_op jit(solution)/shard_map/gather_sequence/ppermute | solution.py:32
  88.1 9.8 %collective-permute-start.11 = (bf16[128,320]{0,1:T(8,128)(2,1)S(1)}, bf16[128,320]{0,1:T(8,128)(2,1)S(1)}, u32[]{:S(2)}, u32[]{:S(2)}) collective-permute-start(bf16[128,320]{0,1:T(8,128)(2,1)S(1)} %collective-permute-done.10), channel_id=1, source_target_pairs={{0,32},{32,64},{64,96},{96,128},{128,160},{160,192},{192,224},{224... | collective-permute-start | bytes 245768 | tf_op jit(solution)/shard_map/gather_sequence/ppermute | solution.py:32
  90.7 9.8 %collective-permute-start.5 = (bf16[128,320]{0,1:T(8,128)(2,1)S(1)}, bf16[128,320]{0,1:T(8,128)(2,1)S(1)}, u32[]{:S(2)}, u32[]{:S(2)}) collective-permute-start(bf16[128,320]{0,1:T(8,128)(2,1)S(1)} %collective-permute-done.4), channel_id=1, source_target_pairs={{0,480},{32,0},{64,32},{96,64},{128,96},{160,128},{192,160},{224,1... | collective-permute-start | bytes 245768 | tf_op jit(solution)/shard_map/gather_sequence/ppermute | solution.py:32
  97.9 9.6 %collective-permute-start.12 = (bf16[128,320]{0,1:T(8,128)(2,1)S(1)}, bf16[128,320]{0,1:T(8,128)(2,1)S(1)}, u32[]{:S(2)}, u32[]{:S(2)}) collective-permute-start(bf16[128,320]{0,1:T(8,128)(2,1)S(1)} %collective-permute-done.11), channel_id=1, source_target_pairs={{0,32},{32,64},{64,96},{96,128},{128,160},{160,192},{192,224},{224... | collective-permute-start | bytes 245768 | tf_op jit(solution)/shard_map/gather_sequence/ppermute | solution.py:32
  100.4 18.3 %collective-permute-start.6 = (bf16[128,320]{0,1:T(8,128)(2,1)S(1)}, bf16[128,320]{0,1:T(8,128)(2,1)S(1)}, u32[]{:S(2)}, u32[]{:S(2)}) collective-permute-start(bf16[128,320]{0,1:T(8,128)(2,1)S(1)} %collective-permute-done.5), channel_id=1, source_target_pairs={{0,480},{32,0},{64,32},{96,64},{128,96},{160,128},{192,160},{224,1... | collective-permute-start | bytes 245768 | tf_op jit(solution)/shard_map/gather_sequence/ppermute | solution.py:32
  107.4 9.4 %collective-permute-start.13 = (bf16[128,320]{0,1:T(8,128)(2,1)S(1)}, bf16[128,320]{0,1:T(8,128)(2,1)S(1)}, u32[]{:S(2)}, u32[]{:S(2)}) collective-permute-start(bf16[128,320]{0,1:T(8,128)(2,1)S(1)} %collective-permute-done.12), channel_id=1, source_target_pairs={{0,32},{32,64},{64,96},{96,128},{128,160},{160,192},{192,224},{224... | collective-permute-start | bytes 245768 | tf_op jit(solution)/shard_map/gather_sequence/ppermute | solution.py:32
  116.8 8.6 %collective-permute-start.14 = (bf16[128,320]{0,1:T(8,128)(2,1)S(1)}, bf16[128,320]{0,1:T(8,128)(2,1)S(1)}, u32[]{:S(2)}, u32[]{:S(2)}) collective-permute-start(bf16[128,320]{0,1:T(8,128)(2,1)S(1)} %collective-permute-done.13), channel_id=1, source_target_pairs={{0,32},{32,64},{64,96},{96,128},{128,160},{160,192},{192,224},{224... | collective-permute-start | bytes 245768 | tf_op jit(solution)/shard_map/gather_sequence/ppermute | solution.py:32
  130.6 24.2 %collective-permute-start.15 = (bf16[2048,320]{0,1:T(8,128)(2,1)}, bf16[2048,320]{0,1:T(8,128)(2,1)}, u32[]{:S(2)}, u32[]{:S(2)}) collective-permute-start(bf16[2048,320]{0,1:T(8,128)(2,1)} %constant_dynamic-update-slice_fusion), channel_id=1, source_target_pairs={{0,8},{8,16},{16,24},{24,0},{1,9},{9,17},{17,25},{25,1},{2,10},{10... | collective-permute-start | bytes 3932168 | tf_op jit(solution)/shard_map/gather_sequence/ppermute | solution.py:32
  134.6 23.4 %collective-permute-start.16 = (bf16[2048,320]{0,1:T(8,128)(2,1)}, bf16[2048,320]{0,1:T(8,128)(2,1)}, u32[]{:S(2)}, u32[]{:S(2)}) collective-permute-start(bf16[2048,320]{0,1:T(8,128)(2,1)} %constant_dynamic-update-slice_fusion), channel_id=1, source_target_pairs={{0,24},{8,0},{16,8},{24,16},{1,25},{9,1},{17,9},{25,17},{2,26},{10... | collective-permute-start | bytes 3932168 | tf_op jit(solution)/shard_map/gather_sequence/ppermute | solution.py:32
  151.7 1.7 copy-start.11
  158.6 24.2 %all-to-all-start = ((f32[64,2,2,128]{3,2,1,0:T(2,128)}), f32[64,2,2,128]{3,2,1,0:T(2,128)}, u32[]{:S(2)}, u32[]{:S(2)}) async-start(f32[64,2,2,128]{3,2,1,0:T(2,128)} %broadcast_in_dim.95), calls=%async_computation | async-start | bytes 262144 | tf_op jit(solution)/shard_map/gather_row_stats/all_to_all | solution.py:163
  170.7 35.6 %collective-permute-start.17 = (bf16[1024,320]{0,1:T(8,128)(2,1)}, bf16[1024,320]{0,1:T(8,128)(2,1)}, u32[]{:S(2)}, u32[]{:S(2)}) collective-permute-start(bf16[1024,320]{0,1:T(8,128)(2,1)} %slice.135), channel_id=1, source_target_pairs={{0,8},{8,16},{16,24},{24,0},{1,9},{9,17},{17,25},{25,1},{2,10},{10... | collective-permute-start | bytes 1966088 | tf_op jit(solution)/shard_map/gather_row_stats/ppermute | solution.py:32
  175.1 32.3 %collective-permute-start.18 = (bf16[1024,320]{0,1:T(8,128)(2,1)}, bf16[1024,320]{0,1:T(8,128)(2,1)}, u32[]{:S(2)}, u32[]{:S(2)}) collective-permute-start(bf16[1024,320]{0,1:T(8,128)(2,1)} %slice.136), channel_id=1, source_target_pairs={{0,24},{8,0},{16,8},{24,16},{1,25},{9,1},{17,9},{25,17},{2,26},{10... | collective-permute-start | bytes 1966088 | tf_op jit(solution)/shard_map/gather_row_stats/ppermute | solution.py:32
  184.5 2.8 %copy-start.3 = (bf16[2048,160]{0,1:T(8,128)(2,1)S(1)}, bf16[2048,160]{0,1:T(8,128)(2,1)}, u32[]{:S(2)}) copy-start(bf16[2048,160]{0,1:T(8,128)(2,1)} %get-tuple-element.84) | copy-start | bytes 1966084
  190.6 2.8 %copy-start.2 = (bf16[2048,160]{0,1:T(8,128)(2,1)S(1)}, bf16[2048,160]{0,1:T(8,128)(2,1)}, u32[]{:S(2)}) copy-start(bf16[2048,160]{0,1:T(8,128)(2,1)} %get-tuple-element.43) | copy-start | bytes 1966084
  199.2 2.8 %copy-start.4 = (bf16[2048,160]{0,1:T(8,128)(2,1)S(1)}, bf16[2048,160]{0,1:T(8,128)(2,1)}, u32[]{:S(2)}) copy-start(bf16[2048,160]{0,1:T(8,128)(2,1)} %get-tuple-element.41) | copy-start | bytes 1966084
  201.9 1.5 copy-start.5
  207.4 1.3 copy-start.12
  210.0 1.2 copy-start.7
  210.0 1.2 copy-start.14
  210.0 1.2 copy-start.15
  210.5 1.3 copy-start.8
  211.2 1.3 copy-start.6
  211.2 1.3 copy-start.16
  211.2 1.3 copy-start.17
  211.7 1.2 copy-start.21
  214.3 12.5 %copy-start.18 = (bf16[128,320]{0,1:T(8,128)(2,1)S(1)}, bf16[128,320]{0,1:T(8,128)(2,1)}, u32[]{:S(2)}) copy-start(bf16[128,320]{0,1:T(8,128)(2,1)} %param.11) | copy-start | bytes 245764
  214.3 12.5 %copy-start.19 = (bf16[128,320]{0,1:T(8,128)(2,1)S(1)}, bf16[128,320]{0,1:T(8,128)(2,1)}, u32[]{:S(2)}) copy-start(bf16[128,320]{0,1:T(8,128)(2,1)} %param.12) | copy-start | bytes 245764
  214.3 12.5 %copy-start.27 = (f32[128]{0:T(128)S(1)}, f32[128]{0:T(128)}, u32[]{:S(2)}) copy-start(f32[128]{0:T(128)} %copy-done.26) | copy-start | bytes 1540
  (2 other events, 1.5 us)
Sparse Core Ops, SparseCore 0:
  37.0 92.8 all-gather.1

commit v13 on v12

--- a/solution.py
+++ b/solution.py
@@ -142,14 +142,14 @@
         )
         weighted = attend * grad_probs
         row_delta = jnp.sum(weighted, axis=2)
+        weighted_bf = weighted.astype(jnp.bfloat16)
+        plain = attend.astype(jnp.bfloat16)
+        weighted_bf, plain, row_delta = lax.optimization_barrier((weighted_bf, plain, row_delta))
         first_sum = jnp.einsum(
-            "hqk,khd->hqd",
-            weighted.astype(jnp.bfloat16),
-            key_all,
-            preferred_element_type=jnp.float32,
+            "hqk,khd->hqd", weighted_bf, key_all, preferred_element_type=jnp.float32
         )
         second_sum = jnp.einsum(
-            "hqk,khd->hqd", attend.astype(jnp.bfloat16), key_all, preferred_element_type=jnp.float32
+            "hqk,khd->hqd", plain, key_all, preferred_element_type=jnp.float32
         )
         query_grad = first_sum - row_delta[:, :, None] * second_sum
         query_grad = jnp.transpose(query_grad, (1, 0, 2)).reshape(row_count, cols)

time: 237 us -> 237 us (level)
  transfers between devices with their start and end apart: 21 -> 21, of which waited for: 13 -> 12; matrix products, arithmetic and copies ran while one was open for 28% -> 29% of each run, Pallas kernels for 0% -> 0%
where the time goes in v13:
time: 237 us; the launch traced here: 234 us
  starting transfers between devices  78.7 us (33%)
  blocking collectives  40.2 us (17%)
  local copies, waits for them, and re-layouts  37.2 us (16%)
  matrix products  30.9 us (13%)
  waiting for transfers between devices  22.5 us (9%)
  between operations  14.9 us (6%)
  other arithmetic  9.9 us (4%)
    ppermute x19, starting transfers between devices, shift(): lax.ppermute(data, axis, [(i, (i + step) % size) for i in range(size)])  68.8 us
    ppermute x19, waiting for transfers between devices, shift(): lax.ppermute(data, axis, [(i, (i + step) % size) for i in range(size)])  21.3 us
    all_gather x1, blocking collectives, per_device(): kv_all = lax.all_gather(kv, 'y', axis=0, tiled=True)  14.6 us
    all_gather x1, blocking collectives, per_device(): gathered = lax.all_gather(both, 'tp', axis=1, tiled=True)  13.4 us
    all_to_all x1, blocking collectives, per_device(): received = lax.all_to_all(payload, 'tp', 0, 0, tiled=False)  12.3 us
    unnamed x74, local copies, waits for them, and re-layouts  11.3 us
    all_to_all x1, starting transfers between devices, per_device(): stats_all = lax.all_to_all(sent, ('z', 'y'), 0, 0, tiled=False)  9.95 us
    dot_general x4, matrix products, per_device(): jnp.einsum('khd,qhd->hkq', key_heads, query_part, preferred_element_type=...  9.01 us
  transfers between devices with their start and end apart: 21, of which 12 were waited for; matrix products, arithmetic and copies ran while one was open for 29% of the time, Pallas kernels for 0%

profile of v13, /device:TPU:24, one launch (start us, length us, event | category | flops | bytes accessed | tf_op | source)
XLA Modules:
  0.0 234.4 jit_solution(1700394373625116184)
XLA Ops:
  7.5 13.4 %all_gather.9 = bf16[128,2560]{0,1:T(8,128)(2,1)S(1)} all-gather(bf16[128,640]{0,1:T(8,128)(2,1)S(1)} %pad_maximum_fusion.1), channel_id=1, replica_groups=mesh['z'=16,'y'=4,'tp'=4,'dp'=2] {'tp'}, dimensions={1}, use_global_device_ids=true | all-gather | bytes 819200 | tf_op jit(solution)/shard_map/gather_features/all_gather | solution.py:77
  22.3 14.6 %all_gather.10 = bf16[512,320]{0,1:T(8,128)(2,1)} all-gather(bf16[128,320]{0,1:T(8,128)(2,1)S(1)} %pad_maximum_fusion.2), channel_id=1, replica_groups=mesh['z'=16,'y'=4,'tp'=4,'dp'=2] {'y'}, dimensions={0}, use_global_device_ids=true | all-gather | bytes 409600 | tf_op jit(solution)/shard_map/gather_sequence/all_gather | solution.py:109
  38.2 8.9 %collective-permute-start = (bf16[128,320]{0,1:T(8,128)(2,1)S(1)}, bf16[128,320]{0,1:T(8,128)(2,1)S(1)}, u32[]{:S(2)}, u32[]{:S(2)}) collective-permute-start(bf16[128,320]{0,1:T(8,128)(2,1)S(1)} %get-tuple-element.59), channel_id=1, source_target_pairs={{0,480},{32,0},{64,32},{96,64},{128,96},{160,128},{192,160},{224,1... | collective-permute-start | bytes 245768 | tf_op jit(solution)/shard_map/gather_sequence/ppermute | solution.py:32
  47.1 1.9 collective-permute-start.7
  54.2 1.6 broadcast_compare_fusion.4
  55.8 5.1 %collective-permute-start.1 = (bf16[128,320]{0,1:T(8,128)(2,1)S(1)}, bf16[128,320]{0,1:T(8,128)(2,1)S(1)}, u32[]{:S(2)}, u32[]{:S(2)}) collective-permute-start(bf16[128,320]{0,1:T(8,128)(2,1)S(1)} %collective-permute-done), channel_id=1, source_target_pairs={{0,480},{32,0},{64,32},{96,64},{128,96},{160,128},{192,160},{224,1... | collective-permute-start | bytes 245768 | tf_op jit(solution)/shard_map/gather_sequence/ppermute | solution.py:32
  61.0 1.9 collective-permute-start.8
  63.8 5.6 %collective-permute-start.2 = (bf16[128,320]{0,1:T(8,128)(2,1)S(1)}, bf16[128,320]{0,1:T(8,128)(2,1)S(1)}, u32[]{:S(2)}, u32[]{:S(2)}) collective-permute-start(bf16[128,320]{0,1:T(8,128)(2,1)S(1)} %collective-permute-done.1), channel_id=1, source_target_pairs={{0,480},{32,0},{64,32},{96,64},{128,96},{160,128},{192,160},{224,1... | collective-permute-start | bytes 245768 | tf_op jit(solution)/shard_map/gather_sequence/ppermute | solution.py:32
  70.0 1.9 collective-permute-start.9
  72.8 5.6 %collective-permute-start.3 = (bf16[128,320]{0,1:T(8,128)(2,1)S(1)}, bf16[128,320]{0,1:T(8,128)(2,1)S(1)}, u32[]{:S(2)}, u32[]{:S(2)}) collective-permute-start(bf16[128,320]{0,1:T(8,128)(2,1)S(1)} %collective-permute-done.2), channel_id=1, source_target_pairs={{0,480},{32,0},{64,32},{96,64},{128,96},{160,128},{192,160},{224,1... | collective-permute-start | bytes 245768 | tf_op jit(solution)/shard_map/gather_sequence/ppermute | solution.py:32
  79.0 1.9 collective-permute-start.10
  81.8 5.6 %collective-permute-start.4 = (bf16[128,320]{0,1:T(8,128)(2,1)S(1)}, bf16[128,320]{0,1:T(8,128)(2,1)S(1)}, u32[]{:S(2)}, u32[]{:S(2)}) collective-permute-start(bf16[128,320]{0,1:T(8,128)(2,1)S(1)} %collective-permute-done.3), channel_id=1, source_target_pairs={{0,480},{32,0},{64,32},{96,64},{128,96},{160,128},{192,160},{224,1... | collective-permute-start | bytes 245768 | tf_op jit(solution)/shard_map/gather_sequence/ppermute | solution.py:32
  88.1 1.9 collective-permute-start.11
  90.7 5.5 %collective-permute-start.5 = (bf16[128,320]{0,1:T(8,128)(2,1)S(1)}, bf16[128,320]{0,1:T(8,128)(2,1)S(1)}, u32[]{:S(2)}, u32[]{:S(2)}) collective-permute-start(bf16[128,320]{0,1:T(8,128)(2,1)S(1)} %collective-permute-done.4), channel_id=1, source_target_pairs={{0,480},{32,0},{64,32},{96,64},{128,96},{160,128},{192,160},{224,1... | collective-permute-start | bytes 245768 | tf_op jit(solution)/shard_map/gather_sequence/ppermute | solution.py:32
  96.2 1.7 collective-permute-done.11
  97.9 1.9 collective-permute-start.12
  100.4 5.1 %collective-permute-start.6 = (bf16[128,320]{0,1:T(8,128)(2,1)S(1)}, bf16[128,320]{0,1:T(8,128)(2,1)S(1)}, u32[]{:S(2)}, u32[]{:S(2)}) collective-permute-start(bf16[128,320]{0,1:T(8,128)(2,1)S(1)} %collective-permute-done.5), channel_id=1, source_target_pairs={{0,480},{32,0},{64,32},{96,64},{128,96},{160,128},{192,160},{224,1... | collective-permute-start | bytes 245768 | tf_op jit(solution)/shard_map/gather_sequence/ppermute | solution.py:32
  105.6 1.9 collective-permute-done.12
  107.4 1.9 collective-permute-start.13
  110.0 6.8 %collective-permute-done.13 = bf16[128,320]{0,1:T(8,128)(2,1)S(1)} collective-permute-done((bf16[128,320]{0,1:T(8,128)(2,1)S(1)}, bf16[128,320]{0,1:T(8,128)(2,1)S(1)}, u32[]{:S(2)}, u32[]{:S(2)}) %collective-permute-start.13) | collective-permute-done | bytes 81952 | tf_op jit(solution)/shard_map/gather_sequence/ppermute | solution.py:32
  116.8 1.9 collective-permute-start.14
  119.4 6.0 %collective-permute-done.14 = bf16[128,320]{0,1:T(8,128)(2,1)S(1)} collective-permute-done((bf16[128,320]{0,1:T(8,128)(2,1)S(1)}, bf16[128,320]{0,1:T(8,128)(2,1)S(1)}, u32[]{:S(2)}, u32[]{:S(2)}) %collective-permute-start.14) | collective-permute-done | bytes 81952 | tf_op jit(solution)/shard_map/gather_sequence/ppermute | solution.py:32
  130.6 3.9 %collective-permute-start.15 = (bf16[2048,320]{0,1:T(8,128)(2,1)}, bf16[2048,320]{0,1:T(8,128)(2,1)}, u32[]{:S(2)}, u32[]{:S(2)}) collective-permute-start(bf16[2048,320]{0,1:T(8,128)(2,1)} %constant_dynamic-update-slice_fusion), channel_id=1, source_target_pairs={{0,8},{8,16},{16,24},{24,0},{1,9},{9,17},{17,25},{25,1},{2,10},{10... | collective-permute-start | bytes 3932168 | tf_op jit(solution)/shard_map/gather_sequence/ppermute | solution.py:32
  134.6 2.1 collective-permute-start.16
  136.7 2.3 fusion.38
  138.9 3.1 %fusion.37 = (bf16[8192,160]{0,1:T(8,128)(2,1)S(1)}, bf16[8192,160]{0,1:T(8,128)(2,1)S(1)}) fusion(bf16[8192,320]{0,1:T(8,128)(2,1)} %all-gather.2.cloned.1.call-done), kind=kLoop, calls=%fused_computation.139 | loop fusion | bytes 10485760 | tf_op jit(solution)/shard_map/gather_sequence/slice | solution.py:113
  142.1 1.8 select_reduce_fusion.1
  143.8 2.5 %select_reduce_fusion = f32[2,128]{1,0:T(2,128)S(1)} fusion(f32[2,128,8192]{2,1,0:T(8,128)S(1)} %get-tuple-element.78, f32[2,128]{1,0:T(2,128)S(1)} %get-tuple-element.77, pred[128,8192]{1,0:T(8,128)(4,1)S(1)} %broadcast_compare_fusion), kind=kLoop, calls=%fused_computation.10 | loop fusion | flops 8388352 | bytes 9439232 | tf_op jit(solution)/shard_map/query_pass/reduce_sum | solution.py:137
  146.3 1.7 fusion
  148.0 3.3 %fusion.36 = (f32[2,128]{1,0:T(2,128)S(1)}, bf16[2,128,8192]{2,1,0:T(8,128)(2,1)S(1)}) fusion(bf16[128,2,80]{0,2,1:T(8,128)(2,1)S(1)} %bitcast.207, bf16[8192,2,80]{0,2,1:T(8,128)(2,1)S(1)} %bitcast.193, f32[2,128,8192]{2,1,0:T(8,128)S(1)} %get-tuple-element.78, f32[2,128]{1,0:T(2,128)S(1)} %log_add_fusion, pred[128,8192]{1,0:T(8,128)(4,1)S(1)} %broadcast_compare_fusion), kind=kOutput, calls=%fused_computation.138 | convolution fusion | flops 346029824 | bytes 16295936 | tf_op jit(solution)/shard_map/query_pass/qhd,khd->hqk/dot_general | solution.py:140
  151.3 1.5 convolution_bitcast_fusion.1
  152.9 1.5 fusion.23
  155.6 2.3 collective-permute-done.16
  158.6 10.0 %all-to-all-start = ((f32[64,2,2,128]{3,2,1,0:T(2,128)}), f32[64,2,2,128]{3,2,1,0:T(2,128)}, u32[]{:S(2)}, u32[]{:S(2)}) async-start(f32[64,2,2,128]{3,2,1,0:T(2,128)} %broadcast_in_dim.95), calls=%async_computation | async-start | bytes 262144 | tf_op jit(solution)/shard_map/gather_row_stats/all_to_all | solution.py:163
  168.6 2.1 slice.135
  170.7 2.4 %collective-permute-start.17 = (bf16[1024,320]{0,1:T(8,128)(2,1)}, bf16[1024,320]{0,1:T(8,128)(2,1)}, u32[]{:S(2)}, u32[]{:S(2)}) collective-permute-start(bf16[1024,320]{0,1:T(8,128)(2,1)} %slice.135), channel_id=1, source_target_pairs={{0,8},{8,16},{16,24},{24,0},{1,9},{9,17},{17,25},{25,1},{2,10},{10... | collective-permute-start | bytes 1966088 | tf_op jit(solution)/shard_map/gather_row_stats/ppermute | solution.py:32
  173.1 2.0 slice.136
  175.1 3.6 %collective-permute-start.18 = (bf16[1024,320]{0,1:T(8,128)(2,1)}, bf16[1024,320]{0,1:T(8,128)(2,1)}, u32[]{:S(2)}, u32[]{:S(2)}) collective-permute-start(bf16[1024,320]{0,1:T(8,128)(2,1)} %slice.136), channel_id=1, source_target_pairs={{0,24},{8,0},{16,8},{24,16},{1,25},{9,1},{17,9},{25,17},{2,26},{10... | collective-permute-start | bytes 1966088 | tf_op jit(solution)/shard_map/gather_row_stats/ppermute | solution.py:32
  178.7 3.0 %fusion.39 = (bf16[2048,160]{0,1:T(8,128)(2,1)}, bf16[2048,160]{0,1:T(8,128)(2,1)S(1)}, bf16[2048,160]{0,1:T(8,128)(2,1)S(1)}, bf16[2048,160]{0,1:T(8,128)(2,1)}) fusion(bf16[2048,320]{0,1:T(8,128)(2,1)} %collective-permute-done.16, bf16[2048,320]{0,1:T(8,128)(2,1)} %collective-permute-done.15), kind=kLoop, calls=%fused_computation.141 | loop fusion | bytes 5242880 | tf_op jit(solution)/shard_map/key_pass/slice | solution.py:172
  182.9 1.6 gather_fusion.7
  184.5 2.8 %fusion.43 = (bf16[2,128,2048]{2,1,0:T(8,128)(2,1)}, f32[2,128,2048]{2,1,0:T(8,128)S(1)}) fusion(f32[2,2048]{1,0:T(2,128)S(1)} %get-tuple-element.68, bf16[128,2,80]{0,2,1:T(8,128)(2,1)S(1)} %bitcast.200, bf16[2048,2,80]{0,2,1:T(8,128)(2,1)S(1)} %bitcast.177, pred[128,2048]{1,0:T(8,128)(4,1)} %get-tuple-element.76), kind=kOutput, calls=%fused_computation.145 | convolution fusion | flops 85458944 | bytes 4120576 | tf_op jit(solution)/shard_map/key_pass/khd,qhd->hkq/dot_general | solution.py:179
  189.0 1.6 gather_fusion.3
  190.6 2.7 %fusion.45 = (bf16[2,128,2048]{2,1,0:T(8,128)(2,1)}, f32[2,128,2048]{2,1,0:T(8,128)S(1)}) fusion(f32[2,2048]{1,0:T(2,128)S(1)} %get-tuple-element.64, bf16[128,2,80]{0,2,1:T(8,128)(2,1)S(1)} %bitcast.201, bf16[2048,2,80]{0,2,1:T(8,128)(2,1)S(1)} %bitcast.175, pred[128,2048]{1,0:T(8,128)(4,1)} %get-tuple-element.74), kind=kOutput, calls=%fused_computation.147 | convolution fusion | flops 85458944 | bytes 4120576 | tf_op jit(solution)/shard_map/key_pass/khd,qhd->hkq/dot_general | solution.py:179
  195.0 1.6 gather_fusion.1
  196.6 2.5 %fusion.53 = f32[2,80,128]{2,1,0:T(8,128)} fusion(bf16[2048,2,80]{0,2,1:T(8,128)(2,1)} %bitcast.185, bf16[2,128,2048]{2,1,0:T(8,128)(2,1)} %get-tuple-element.44), kind=kOutput, calls=%fused_computation.155 | convolution fusion | flops 83886080 | bytes 1785856 | tf_op jit(solution)/shard_map/key_pass/hkq,qhd->khd/dot_general | solution.py:197
  199.2 2.8 %fusion.46 = (bf16[2,128,2048]{2,1,0:T(8,128)(2,1)}, f32[2,128,2048]{2,1,0:T(8,128)S(1)}) fusion(f32[2,2048]{1,0:T(2,128)S(1)} %get-tuple-element.62, bf16[128,2,80]{0,2,1:T(8,128)(2,1)S(1)} %bitcast.202, bf16[2048,2,80]{0,2,1:T(8,128)(2,1)S(1)} %bitcast.181, pred[128,2048]{1,0:T(8,128)(4,1)} %get-tuple-element.73), kind=kOutput, calls=%fused_computation.148 | convolution fusion | flops 85458944 | bytes 4120576 | tf_op jit(solution)/shard_map/key_pass/khd,qhd->hkq/dot_general | solution.py:179
  204.6 1.6 gather_fusion.5
  214.3 12.3 %all_to_all.10 = f32[4,129,320]{2,1,0:T(8,128)S(1)} all-to-all(f32[4,129,320]{2,1,0:T(8,128)S(1)} %copy.31), channel_id=1, replica_groups=mesh['z'=16,'y'=4,'tp'=4,'dp'=2] {'tp'}, dimensions={0} | all-to-all | bytes 1320960 | tf_op jit(solution)/shard_map/back_projection/all_to_all | solution.py:216
  (165 shorter events, 38.2 us)
Async XLA Ops:
  6.5 15.1 %copy-start = (bf16[160,1280]{1,0:T(8,128)(2,1)S(1)}, bf16[160,1280]{1,0:T(8,128)(2,1)}, u32[]{:S(2)}) copy-start(bf16[160,1280]{1,0:T(8,128)(2,1)} %param.16) | copy-start | bytes 1228804
  6.5 132.4 %all-gather.2.cloned.1.call-start = ((), (), s32[]{:S(2)}) async-start(), calls=%async_computation.2 | async-start | bytes 5570560 | tf_op jit(solution)/shard_map/gather_sequence/all_gather | solution.py:110
  7.5 13.9 %copy-start.20 = (f32[1280]{0:T(1024)S(1)}, f32[1280]{0:T(1024)}, u32[]{:S(2)}) copy-start(f32[1280]{0:T(1024)} %param.13) | copy-start | bytes 15364
  21.2 15.7 %copy-start.28 = (f32[80]{0:T(128)S(1)}, f32[80]{0:T(128)}, u32[]{:S(2)}) copy-start(f32[80]{0:T(128)} %param.18) | copy-start | bytes 964
  21.2 15.8 %copy-start.13 = (bf16[160,1280]{1,0:T(8,128)(2,1)S(1)}, bf16[160,1280]{1,0:T(8,128)(2,1)}, u32[]{:S(2)}) copy-start(bf16[160,1280]{1,0:T(8,128)(2,1)} %param.17) | copy-start | bytes 1228804
  21.5 15.8 %copy-start.10 = (bf16[160,1280]{1,0:T(8,128)(2,1)S(1)}, bf16[160,1280]{1,0:T(8,128)(2,1)}, u32[]{:S(2)}) copy-start(bf16[160,1280]{1,0:T(8,128)(2,1)} %param.14) | copy-start | bytes 1228804
  21.6 27.4 %copy-start.1 = (s32[64]{0:T(128)S(1)}, s32[64]{0:T(128)}, u32[]{:S(2)}) copy-start(s32[64]{0:T(128)} %param.19) | copy-start | bytes 772
  38.2 17.6 %collective-permute-start = (bf16[128,320]{0,1:T(8,128)(2,1)S(1)}, bf16[128,320]{0,1:T(8,128)(2,1)S(1)}, u32[]{:S(2)}, u32[]{:S(2)}) collective-permute-start(bf16[128,320]{0,1:T(8,128)(2,1)S(1)} %get-tuple-element.59), channel_id=1, source_target_pairs={{0,480},{32,0},{64,32},{96,64},{128,96},{160,128},{192,160},{224,1... | collective-permute-start | bytes 245768 | tf_op jit(solution)/shard_map/gather_sequence/ppermute | solution.py:32
  47.1 13.8 %collective-permute-start.7 = (bf16[128,320]{0,1:T(8,128)(2,1)S(1)}, bf16[128,320]{0,1:T(8,128)(2,1)S(1)}, u32[]{:S(2)}, u32[]{:S(2)}) collective-permute-start(bf16[128,320]{0,1:T(8,128)(2,1)S(1)} %get-tuple-element.59), channel_id=1, source_target_pairs={{0,32},{32,64},{64,96},{96,128},{128,160},{160,192},{192,224},{224... | collective-permute-start | bytes 245768 | tf_op jit(solution)/shard_map/gather_sequence/ppermute | solution.py:32
  49.8 1.3 copy-start.23
  49.8 6.0 %copy-start.24 = (s32[1024]{0:T(1024)}, s32[1024]{0:T(1024)S(1)}, u32[]{:S(2)}) copy-start(s32[1024]{0:T(1024)S(1)} %get-tuple-element.94) | copy-start | bytes 12292
  51.2 58.8 %copy-start.22 = (s32[1024]{0:T(1024)}, s32[1024]{0:T(1024)S(1)}, u32[]{:S(2)}) copy-start(s32[1024]{0:T(1024)S(1)} %get-tuple-element.93) | copy-start | bytes 12292
  51.2 58.8 %copy-start.25 = (s32[1024]{0:T(1024)}, s32[1024]{0:T(1024)S(1)}, u32[]{:S(2)}) copy-start(s32[1024]{0:T(1024)S(1)} %get-tuple-element.92) | copy-start | bytes 12292
  55.8 8.0 %collective-permute-start.1 = (bf16[128,320]{0,1:T(8,128)(2,1)S(1)}, bf16[128,320]{0,1:T(8,128)(2,1)S(1)}, u32[]{:S(2)}, u32[]{:S(2)}) collective-permute-start(bf16[128,320]{0,1:T(8,128)(2,1)S(1)} %collective-permute-done), channel_id=1, source_target_pairs={{0,480},{32,0},{64,32},{96,64},{128,96},{160,128},{192,160},{224,1... | collective-permute-start | bytes 245768 | tf_op jit(solution)/shard_map/gather_sequence/ppermute | solution.py:32
  61.0 9.0 %collective-permute-start.8 = (bf16[128,320]{0,1:T(8,128)(2,1)S(1)}, bf16[128,320]{0,1:T(8,128)(2,1)S(1)}, u32[]{:S(2)}, u32[]{:S(2)}) collective-permute-start(bf16[128,320]{0,1:T(8,128)(2,1)S(1)} %collective-permute-done.7), channel_id=1, source_target_pairs={{0,32},{32,64},{64,96},{96,128},{128,160},{160,192},{192,224},{224... | collective-permute-start | bytes 245768 | tf_op jit(solution)/shard_map/gather_sequence/ppermute | solution.py:32
  63.8 9.0 %collective-permute-start.2 = (bf16[128,320]{0,1:T(8,128)(2,1)S(1)}, bf16[128,320]{0,1:T(8,128)(2,1)S(1)}, u32[]{:S(2)}, u32[]{:S(2)}) collective-permute-start(bf16[128,320]{0,1:T(8,128)(2,1)S(1)} %collective-permute-done.1), channel_id=1, source_target_pairs={{0,480},{32,0},{64,32},{96,64},{128,96},{160,128},{192,160},{224,1... | collective-permute-start | bytes 245768 | tf_op jit(solution)/shard_map/gather_sequence/ppermute | solution.py:32
  70.0 9.0 %collective-permute-start.9 = (bf16[128,320]{0,1:T(8,128)(2,1)S(1)}, bf16[128,320]{0,1:T(8,128)(2,1)S(1)}, u32[]{:S(2)}, u32[]{:S(2)}) collective-permute-start(bf16[128,320]{0,1:T(8,128)(2,1)S(1)} %collective-permute-done.8), channel_id=1, source_target_pairs={{0,32},{32,64},{64,96},{96,128},{128,160},{160,192},{192,224},{224... | collective-permute-start | bytes 245768 | tf_op jit(solution)/shard_map/gather_sequence/ppermute | solution.py:32
  72.8 8.9 %collective-permute-start.3 = (bf16[128,320]{0,1:T(8,128)(2,1)S(1)}, bf16[128,320]{0,1:T(8,128)(2,1)S(1)}, u32[]{:S(2)}, u32[]{:S(2)}) collective-permute-start(bf16[128,320]{0,1:T(8,128)(2,1)S(1)} %collective-permute-done.2), channel_id=1, source_target_pairs={{0,480},{32,0},{64,32},{96,64},{128,96},{160,128},{192,160},{224,1... | collective-permute-start | bytes 245768 | tf_op jit(solution)/shard_map/gather_sequence/ppermute | solution.py:32
  79.0 9.1 %collective-permute-start.10 = (bf16[128,320]{0,1:T(8,128)(2,1)S(1)}, bf16[128,320]{0,1:T(8,128)(2,1)S(1)}, u32[]{:S(2)}, u32[]{:S(2)}) collective-permute-start(bf16[128,320]{0,1:T(8,128)(2,1)S(1)} %collective-permute-done.9), channel_id=1, source_target_pairs={{0,32},{32,64},{64,96},{96,128},{128,160},{160,192},{192,224},{224... | collective-permute-start | bytes 245768 | tf_op jit(solution)/shard_map/gather_sequence/ppermute | solution.py:32
  81.8 8.9 %collective-permute-start.4 = (bf16[128,320]{0,1:T(8,128)(2,1)S(1)}, bf16[128,320]{0,1:T(8,128)(2,1)S(1)}, u32[]{:S(2)}, u32[]{:S(2)}) collective-permute-start(bf16[128,320]{0,1:T(8,128)(2,1)S(1)} %collective-permute-done.3), channel_id=1, source_target_pairs={{0,480},{32,0},{64,32},{96,64},{128,96},{160,128},{192,160},{224,1... | collective-permute-start | bytes 245768 | tf_op jit(solution)/shard_map/gather_sequence/ppermute | solution.py:32
  88.1 9.8 %collective-permute-start.11 = (bf16[128,320]{0,1:T(8,128)(2,1)S(1)}, bf16[128,320]{0,1:T(8,128)(2,1)S(1)}, u32[]{:S(2)}, u32[]{:S(2)}) collective-permute-start(bf16[128,320]{0,1:T(8,128)(2,1)S(1)} %collective-permute-done.10), channel_id=1, source_target_pairs={{0,32},{32,64},{64,96},{96,128},{128,160},{160,192},{192,224},{224... | collective-permute-start | bytes 245768 | tf_op jit(solution)/shard_map/gather_sequence/ppermute | solution.py:32
  90.7 9.8 %collective-permute-start.5 = (bf16[128,320]{0,1:T(8,128)(2,1)S(1)}, bf16[128,320]{0,1:T(8,128)(2,1)S(1)}, u32[]{:S(2)}, u32[]{:S(2)}) collective-permute-start(bf16[128,320]{0,1:T(8,128)(2,1)S(1)} %collective-permute-done.4), channel_id=1, source_target_pairs={{0,480},{32,0},{64,32},{96,64},{128,96},{160,128},{192,160},{224,1... | collective-permute-start | bytes 245768 | tf_op jit(solution)/shard_map/gather_sequence/ppermute | solution.py:32
  97.9 9.6 %collective-permute-start.12 = (bf16[128,320]{0,1:T(8,128)(2,1)S(1)}, bf16[128,320]{0,1:T(8,128)(2,1)S(1)}, u32[]{:S(2)}, u32[]{:S(2)}) collective-permute-start(bf16[128,320]{0,1:T(8,128)(2,1)S(1)} %collective-permute-done.11), channel_id=1, source_target_pairs={{0,32},{32,64},{64,96},{96,128},{128,160},{160,192},{192,224},{224... | collective-permute-start | bytes 245768 | tf_op jit(solution)/shard_map/gather_sequence/ppermute | solution.py:32
  100.4 18.3 %collective-permute-start.6 = (bf16[128,320]{0,1:T(8,128)(2,1)S(1)}, bf16[128,320]{0,1:T(8,128)(2,1)S(1)}, u32[]{:S(2)}, u32[]{:S(2)}) collective-permute-start(bf16[128,320]{0,1:T(8,128)(2,1)S(1)} %collective-permute-done.5), channel_id=1, source_target_pairs={{0,480},{32,0},{64,32},{96,64},{128,96},{160,128},{192,160},{224,1... | collective-permute-start | bytes 245768 | tf_op jit(solution)/shard_map/gather_sequence/ppermute | solution.py:32
  107.4 9.4 %collective-permute-start.13 = (bf16[128,320]{0,1:T(8,128)(2,1)S(1)}, bf16[128,320]{0,1:T(8,128)(2,1)S(1)}, u32[]{:S(2)}, u32[]{:S(2)}) collective-permute-start(bf16[128,320]{0,1:T(8,128)(2,1)S(1)} %collective-permute-done.12), channel_id=1, source_target_pairs={{0,32},{32,64},{64,96},{96,128},{128,160},{160,192},{192,224},{224... | collective-permute-start | bytes 245768 | tf_op jit(solution)/shard_map/gather_sequence/ppermute | solution.py:32
  116.8 8.6 %collective-permute-start.14 = (bf16[128,320]{0,1:T(8,128)(2,1)S(1)}, bf16[128,320]{0,1:T(8,128)(2,1)S(1)}, u32[]{:S(2)}, u32[]{:S(2)}) collective-permute-start(bf16[128,320]{0,1:T(8,128)(2,1)S(1)} %collective-permute-done.13), channel_id=1, source_target_pairs={{0,32},{32,64},{64,96},{96,128},{128,160},{160,192},{192,224},{224... | collective-permute-start | bytes 245768 | tf_op jit(solution)/shard_map/gather_sequence/ppermute | solution.py:32
  130.6 25.0 %collective-permute-start.15 = (bf16[2048,320]{0,1:T(8,128)(2,1)}, bf16[2048,320]{0,1:T(8,128)(2,1)}, u32[]{:S(2)}, u32[]{:S(2)}) collective-permute-start(bf16[2048,320]{0,1:T(8,128)(2,1)} %constant_dynamic-update-slice_fusion), channel_id=1, source_target_pairs={{0,8},{8,16},{16,24},{24,0},{1,9},{9,17},{17,25},{25,1},{2,10},{10... | collective-permute-start | bytes 3932168 | tf_op jit(solution)/shard_map/gather_sequence/ppermute | solution.py:32
  134.6 23.4 %collective-permute-start.16 = (bf16[2048,320]{0,1:T(8,128)(2,1)}, bf16[2048,320]{0,1:T(8,128)(2,1)}, u32[]{:S(2)}, u32[]{:S(2)}) collective-permute-start(bf16[2048,320]{0,1:T(8,128)(2,1)} %constant_dynamic-update-slice_fusion), channel_id=1, source_target_pairs={{0,24},{8,0},{16,8},{24,16},{1,25},{9,1},{17,9},{25,17},{2,26},{10... | collective-permute-start | bytes 3932168 | tf_op jit(solution)/shard_map/gather_sequence/ppermute | solution.py:32
  152.8 1.7 copy-start.11
  158.6 24.2 %all-to-all-start = ((f32[64,2,2,128]{3,2,1,0:T(2,128)}), f32[64,2,2,128]{3,2,1,0:T(2,128)}, u32[]{:S(2)}, u32[]{:S(2)}) async-start(f32[64,2,2,128]{3,2,1,0:T(2,128)} %broadcast_in_dim.95), calls=%async_computation | async-start | bytes 262144 | tf_op jit(solution)/shard_map/gather_row_stats/all_to_all | solution.py:163
  170.7 35.6 %collective-permute-start.17 = (bf16[1024,320]{0,1:T(8,128)(2,1)}, bf16[1024,320]{0,1:T(8,128)(2,1)}, u32[]{:S(2)}, u32[]{:S(2)}) collective-permute-start(bf16[1024,320]{0,1:T(8,128)(2,1)} %slice.135), channel_id=1, source_target_pairs={{0,8},{8,16},{16,24},{24,0},{1,9},{9,17},{17,25},{25,1},{2,10},{10... | collective-permute-start | bytes 1966088 | tf_op jit(solution)/shard_map/gather_row_stats/ppermute | solution.py:32
  175.1 32.3 %collective-permute-start.18 = (bf16[1024,320]{0,1:T(8,128)(2,1)}, bf16[1024,320]{0,1:T(8,128)(2,1)}, u32[]{:S(2)}, u32[]{:S(2)}) collective-permute-start(bf16[1024,320]{0,1:T(8,128)(2,1)} %slice.136), channel_id=1, source_target_pairs={{0,24},{8,0},{16,8},{24,16},{1,25},{9,1},{17,9},{25,17},{2,26},{10... | collective-permute-start | bytes 1966088 | tf_op jit(solution)/shard_map/gather_row_stats/ppermute | solution.py:32
  184.5 2.8 %copy-start.3 = (bf16[2048,160]{0,1:T(8,128)(2,1)S(1)}, bf16[2048,160]{0,1:T(8,128)(2,1)}, u32[]{:S(2)}) copy-start(bf16[2048,160]{0,1:T(8,128)(2,1)} %get-tuple-element.91) | copy-start | bytes 1966084
  190.6 2.8 %copy-start.2 = (bf16[2048,160]{0,1:T(8,128)(2,1)S(1)}, bf16[2048,160]{0,1:T(8,128)(2,1)}, u32[]{:S(2)}) copy-start(bf16[2048,160]{0,1:T(8,128)(2,1)} %get-tuple-element.51) | copy-start | bytes 1966084
  199.2 2.8 %copy-start.4 = (bf16[2048,160]{0,1:T(8,128)(2,1)S(1)}, bf16[2048,160]{0,1:T(8,128)(2,1)}, u32[]{:S(2)}) copy-start(bf16[2048,160]{0,1:T(8,128)(2,1)} %get-tuple-element.49) | copy-start | bytes 1966084
  201.9 1.5 copy-start.5
  207.4 1.3 copy-start.12
  210.0 1.2 copy-start.7
  210.0 1.2 copy-start.14
  210.0 1.2 copy-start.15
  210.5 1.3 copy-start.8
  211.2 1.3 copy-start.6
  211.2 1.3 copy-start.16
  211.2 1.3 copy-start.17
  211.7 1.2 copy-start.21
  214.3 12.5 %copy-start.18 = (bf16[128,320]{0,1:T(8,128)(2,1)S(1)}, bf16[128,320]{0,1:T(8,128)(2,1)}, u32[]{:S(2)}) copy-start(bf16[128,320]{0,1:T(8,128)(2,1)} %param.11) | copy-start | bytes 245764
  214.3 12.5 %copy-start.19 = (bf16[128,320]{0,1:T(8,128)(2,1)S(1)}, bf16[128,320]{0,1:T(8,128)(2,1)}, u32[]{:S(2)}) copy-start(bf16[128,320]{0,1:T(8,128)(2,1)} %param.12) | copy-start | bytes 245764
  214.3 12.5 %copy-start.27 = (f32[128]{0:T(128)S(1)}, f32[128]{0:T(128)}, u32[]{:S(2)}) copy-start(f32[128]{0:T(128)} %copy-done.26) | copy-start | bytes 1540
  (2 other events, 1.5 us)
Sparse Core Ops, SparseCore 0:
  37.0 92.8 all-gather.1

commit v14 on v12

--- a/solution.py
+++ b/solution.py
@@ -164,6 +164,7 @@
 
     with jax.named_scope("key_pass"):
         piece_rows = qg_pieces[0].shape[0]
+        stats_ordered = stats_all[qg_source]
         key_grad = jnp.zeros((row_count, heads_here, head_width), jnp.float32)
         value_grad = jnp.zeros((row_count, heads_here, head_width), jnp.float32)
         for ry, piece in enumerate(qg_pieces):
@@ -171,7 +172,7 @@
             query_part = piece[:, :cols].reshape(piece_rows, heads_here, head_width)
             grad_part = piece[:, cols:].reshape(piece_rows, heads_here, head_width)
             place = block_positions(offsets[source], piece_rows)
-            part_stats = stats_all[source]
+            part_stats = stats_ordered[ry * z_size : (ry + 1) * z_size]
             log_part = jnp.transpose(part_stats[:, 0], (1, 0, 2)).reshape(heads_here, piece_rows)
             delta_part = jnp.transpose(part_stats[:, 1], (1, 0, 2)).reshape(
                 heads_here, piece_rows

time: 237 us -> 223 us (0.941)
  matrix products: 31.5 us -> 21.5 us
  local copies, waits for them, and re-layouts: 37.1 us -> 33.8 us
    dot_general x4, matrix products: 9.01 us -> 3.99 us  [per_device(): jnp.einsum('khd,qhd->hkq', key_heads, query_part, preferred_element_type=...]
    gather x4 -> x1, local copies, waits for them, and re-layouts: 6.46 us -> 2.26 us  [per_device(): stats_ordered = stats_all[qg_source]]
    dot_general x4, matrix products: 4.66 us -> 1.95 us  [per_device(): jnp.einsum('hkq,qhd->khd', plain_t, grad_part, preferred_element_type=jnp...]
    unnamed x74 -> x50, local copies, waits for them, and re-layouts: 11.3 us -> 11.4 us
  transfers between devices with their start and end apart: 21 -> 21, of which waited for: 13 -> 13; matrix products, arithmetic and copies ran while one was open for 28% -> 24% of each run, Pallas kernels for 0% -> 0%
where the time goes in v14:
time: 223 us; the launch traced here: 221 us
  starting transfers between devices  78.5 us (35%)
  blocking collectives  40.2 us (18%)
  local copies, waits for them, and re-layouts  33.8 us (15%)
  waiting for transfers between devices  23.5 us (11%)
  matrix products  21.5 us (10%)
  between operations  14.9 us (7%)
  other arithmetic  8.23 us (4%)
    ppermute x19, starting transfers between devices, shift(): lax.ppermute(data, axis, [(i, (i + step) % size) for i in range(size)])  68.9 us
    ppermute x19, waiting for transfers between devices, shift(): lax.ppermute(data, axis, [(i, (i + step) % size) for i in range(size)])  22.3 us
    all_gather x1, blocking collectives, per_device(): kv_all = lax.all_gather(kv, 'y', axis=0, tiled=True)  14.6 us
    all_gather x1, blocking collectives, per_device(): gathered = lax.all_gather(both, 'tp', axis=1, tiled=True)  13.4 us
    all_to_all x1, blocking collectives, per_device(): received = lax.all_to_all(payload, 'tp', 0, 0, tiled=False)  12.3 us
    unnamed x50, local copies, waits for them, and re-layouts  11.4 us
    all_to_all x1, starting transfers between devices, per_device(): stats_all = lax.all_to_all(sent, ('z', 'y'), 0, 0, tiled=False)  9.59 us
    slice x3, local copies, waits for them, and re-layouts, per_device(): grad_part = piece[:, cols:].reshape(piece_rows, heads_here, head_width)  5.38 us
  transfers between devices with their start and end apart: 21, of which 13 were waited for; matrix products, arithmetic and copies ran while one was open for 24% of the time, Pallas kernels for 0%

profile of v14, /device:TPU:24, one launch (start us, length us, event | category | flops | bytes accessed | tf_op | source)
XLA Modules:
  0.0 220.6 jit_solution(20203477085637994)
XLA Ops:
  6.5 1.0 pad_maximum_fusion.1
  7.5 13.4 %all_gather.9 = bf16[128,2560]{0,1:T(8,128)(2,1)S(1)} all-gather(bf16[128,640]{0,1:T(8,128)(2,1)S(1)} %pad_maximum_fusion.1), channel_id=1, replica_groups=mesh['z'=16,'y'=4,'tp'=4,'dp'=2] {'tp'}, dimensions={1}, use_global_device_ids=true | all-gather | bytes 819200 | tf_op jit(solution)/shard_map/gather_features/all_gather | solution.py:77
  22.3 14.6 %all_gather.10 = bf16[512,320]{0,1:T(8,128)(2,1)} all-gather(bf16[128,320]{0,1:T(8,128)(2,1)S(1)} %pad_maximum_fusion.2), channel_id=1, replica_groups=mesh['z'=16,'y'=4,'tp'=4,'dp'=2] {'y'}, dimensions={0}, use_global_device_ids=true | all-gather | bytes 409600 | tf_op jit(solution)/shard_map/gather_sequence/all_gather | solution.py:109
  38.2 8.9 %collective-permute-start = (bf16[128,320]{0,1:T(8,128)(2,1)S(1)}, bf16[128,320]{0,1:T(8,128)(2,1)S(1)}, u32[]{:S(2)}, u32[]{:S(2)}) collective-permute-start(bf16[128,320]{0,1:T(8,128)(2,1)S(1)} %get-tuple-element.59), channel_id=1, source_target_pairs={{0,480},{32,0},{64,32},{96,64},{128,96},{160,128},{192,160},{224,1... | collective-permute-start | bytes 245768 | tf_op jit(solution)/shard_map/gather_sequence/ppermute | solution.py:32
  47.1 1.9 collective-permute-start.7
  53.6 1.6 broadcast_compare_fusion.4
  55.9 5.1 %collective-permute-start.1 = (bf16[128,320]{0,1:T(8,128)(2,1)S(1)}, bf16[128,320]{0,1:T(8,128)(2,1)S(1)}, u32[]{:S(2)}, u32[]{:S(2)}) collective-permute-start(bf16[128,320]{0,1:T(8,128)(2,1)S(1)} %collective-permute-done), channel_id=1, source_target_pairs={{0,480},{32,0},{64,32},{96,64},{128,96},{160,128},{192,160},{224,1... | collective-permute-start | bytes 245768 | tf_op jit(solution)/shard_map/gather_sequence/ppermute | solution.py:32
  61.0 1.9 collective-permute-start.8
  64.1 5.6 %collective-permute-start.2 = (bf16[128,320]{0,1:T(8,128)(2,1)S(1)}, bf16[128,320]{0,1:T(8,128)(2,1)S(1)}, u32[]{:S(2)}, u32[]{:S(2)}) collective-permute-start(bf16[128,320]{0,1:T(8,128)(2,1)S(1)} %collective-permute-done.1), channel_id=1, source_target_pairs={{0,480},{32,0},{64,32},{96,64},{128,96},{160,128},{192,160},{224,1... | collective-permute-start | bytes 245768 | tf_op jit(solution)/shard_map/gather_sequence/ppermute | solution.py:32
  70.0 1.9 collective-permute-start.9
  73.2 5.6 %collective-permute-start.3 = (bf16[128,320]{0,1:T(8,128)(2,1)S(1)}, bf16[128,320]{0,1:T(8,128)(2,1)S(1)}, u32[]{:S(2)}, u32[]{:S(2)}) collective-permute-start(bf16[128,320]{0,1:T(8,128)(2,1)S(1)} %collective-permute-done.2), channel_id=1, source_target_pairs={{0,480},{32,0},{64,32},{96,64},{128,96},{160,128},{192,160},{224,1... | collective-permute-start | bytes 245768 | tf_op jit(solution)/shard_map/gather_sequence/ppermute | solution.py:32
  79.1 1.9 collective-permute-start.10
  82.4 5.6 %collective-permute-start.4 = (bf16[128,320]{0,1:T(8,128)(2,1)S(1)}, bf16[128,320]{0,1:T(8,128)(2,1)S(1)}, u32[]{:S(2)}, u32[]{:S(2)}) collective-permute-start(bf16[128,320]{0,1:T(8,128)(2,1)S(1)} %collective-permute-done.3), channel_id=1, source_target_pairs={{0,480},{32,0},{64,32},{96,64},{128,96},{160,128},{192,160},{224,1... | collective-permute-start | bytes 245768 | tf_op jit(solution)/shard_map/gather_sequence/ppermute | solution.py:32
  88.0 1.9 collective-permute-start.11
  90.8 5.6 %collective-permute-start.5 = (bf16[128,320]{0,1:T(8,128)(2,1)S(1)}, bf16[128,320]{0,1:T(8,128)(2,1)S(1)}, u32[]{:S(2)}, u32[]{:S(2)}) collective-permute-start(bf16[128,320]{0,1:T(8,128)(2,1)S(1)} %collective-permute-done.4), channel_id=1, source_target_pairs={{0,480},{32,0},{64,32},{96,64},{128,96},{160,128},{192,160},{224,1... | collective-permute-start | bytes 245768 | tf_op jit(solution)/shard_map/gather_sequence/ppermute | solution.py:32
  96.4 1.3 collective-permute-done.11
  97.7 1.9 collective-permute-start.12
  100.3 5.1 %collective-permute-start.6 = (bf16[128,320]{0,1:T(8,128)(2,1)S(1)}, bf16[128,320]{0,1:T(8,128)(2,1)S(1)}, u32[]{:S(2)}, u32[]{:S(2)}) collective-permute-start(bf16[128,320]{0,1:T(8,128)(2,1)S(1)} %collective-permute-done.5), channel_id=1, source_target_pairs={{0,480},{32,0},{64,32},{96,64},{128,96},{160,128},{192,160},{224,1... | collective-permute-start | bytes 245768 | tf_op jit(solution)/shard_map/gather_sequence/ppermute | solution.py:32
  105.5 1.8 collective-permute-done.12
  107.3 1.9 collective-permute-start.13
  109.9 6.6 %collective-permute-done.13 = bf16[128,320]{0,1:T(8,128)(2,1)S(1)} collective-permute-done((bf16[128,320]{0,1:T(8,128)(2,1)S(1)}, bf16[128,320]{0,1:T(8,128)(2,1)S(1)}, u32[]{:S(2)}, u32[]{:S(2)}) %collective-permute-start.13) | collective-permute-done | bytes 81952 | tf_op jit(solution)/shard_map/gather_sequence/ppermute | solution.py:32
  116.5 1.9 collective-permute-start.14
  119.1 6.2 %collective-permute-done.14 = bf16[128,320]{0,1:T(8,128)(2,1)S(1)} collective-permute-done((bf16[128,320]{0,1:T(8,128)(2,1)S(1)}, bf16[128,320]{0,1:T(8,128)(2,1)S(1)}, u32[]{:S(2)}, u32[]{:S(2)}) %collective-permute-start.14) | collective-permute-done | bytes 81952 | tf_op jit(solution)/shard_map/gather_sequence/ppermute | solution.py:32
  130.4 3.8 %collective-permute-start.15 = (bf16[2048,320]{0,1:T(8,128)(2,1)}, bf16[2048,320]{0,1:T(8,128)(2,1)}, u32[]{:S(2)}, u32[]{:S(2)}) collective-permute-start(bf16[2048,320]{0,1:T(8,128)(2,1)} %constant_dynamic-update-slice_fusion), channel_id=1, source_target_pairs={{0,8},{8,16},{16,24},{24,0},{1,9},{9,17},{17,25},{25,1},{2,10},{10... | collective-permute-start | bytes 3932168 | tf_op jit(solution)/shard_map/gather_sequence/ppermute | solution.py:32
  134.2 2.3 %collective-permute-start.16 = (bf16[2048,320]{0,1:T(8,128)(2,1)}, bf16[2048,320]{0,1:T(8,128)(2,1)}, u32[]{:S(2)}, u32[]{:S(2)}) collective-permute-start(bf16[2048,320]{0,1:T(8,128)(2,1)} %constant_dynamic-update-slice_fusion), channel_id=1, source_target_pairs={{0,24},{8,0},{16,8},{24,16},{1,25},{9,1},{17,9},{25,17},{2,26},{10... | collective-permute-start | bytes 3932168 | tf_op jit(solution)/shard_map/gather_sequence/ppermute | solution.py:32
  136.5 2.2 %fusion.56 = (bf16[2048,160]{0,1:T(8,128)(2,1)}, bf16[2048,160]{0,1:T(8,128)(2,1)S(1)}) fusion(bf16[2048,320]{0,1:T(8,128)(2,1)} %constant_dynamic-update-slice_fusion), kind=kLoop, calls=%fused_computation.146 | loop fusion | bytes 2621440 | tf_op jit(solution)/shard_map/key_pass/slice | solution.py:173
  138.7 3.0 %fusion.55 = (bf16[8192,160]{0,1:T(8,128)(2,1)S(1)}, bf16[8192,160]{0,1:T(8,128)(2,1)S(1)}) fusion(bf16[8192,320]{0,1:T(8,128)(2,1)} %all-gather.2.cloned.1.call-done), kind=kLoop, calls=%fused_computation.145 | loop fusion | bytes 10485760 | tf_op jit(solution)/shard_map/gather_sequence/slice | solution.py:114
  141.7 1.8 select_reduce_fusion.1
  143.5 2.5 %select_reduce_fusion = f32[2,128]{1,0:T(2,128)S(1)} fusion(f32[2,128,8192]{2,1,0:T(8,128)S(1)} %get-tuple-element.70, f32[2,128]{1,0:T(2,128)S(1)} %get-tuple-element.69, pred[128,8192]{1,0:T(8,128)(4,1)S(1)} %broadcast_compare_fusion), kind=kLoop, calls=%fused_computation.7 | loop fusion | flops 8388352 | bytes 9439232 | tf_op jit(solution)/shard_map/query_pass/reduce_sum | solution.py:137
  146.0 3.5 %fusion.61 = (f32[2,128]{1,0:T(2,128)S(1)}, bf16[2,128,8192]{2,1,0:T(8,128)(2,1)S(1)}) fusion(bf16[128,2,80]{0,2,1:T(8,128)(2,1)S(1)} %bitcast.208, bf16[8192,2,80]{0,2,1:T(8,128)(2,1)S(1)} %bitcast.194, f32[2,128,8192]{2,1,0:T(8,128)S(1)} %get-tuple-element.70, f32[2,128]{1,0:T(2,128)S(1)} %log_add_fusion, pred[128,8192]{1,0:T(8,128)(4,1)S(1)} %broadcast_compare_fusion), kind=kOutput, calls=%fused_computation.151 | convolution fusion | flops 346029824 | bytes 16295936 | tf_op jit(solution)/shard_map/query_pass/qhd,khd->hqk/dot_general | solution.py:140
  149.5 2.0 fusion.38
  151.5 1.5 fusion.28
  153.1 1.1 fusion.66
  154.4 3.6 %collective-permute-done.16 = bf16[2048,320]{0,1:T(8,128)(2,1)} collective-permute-done((bf16[2048,320]{0,1:T(8,128)(2,1)}, bf16[2048,320]{0,1:T(8,128)(2,1)}, u32[]{:S(2)}, u32[]{:S(2)}) %collective-permute-start.16) | collective-permute-done | bytes 1310752 | tf_op jit(solution)/shard_map/gather_sequence/ppermute | solution.py:32
  158.7 9.6 %all-to-all-start = ((f32[64,2,2,128]{3,2,1,0:T(2,128)}), f32[64,2,2,128]{3,2,1,0:T(2,128)}, u32[]{:S(2)}, u32[]{:S(2)}) async-start(f32[64,2,2,128]{3,2,1,0:T(2,128)} %broadcast_in_dim.92), calls=%async_computation | async-start | bytes 262144 | tf_op jit(solution)/shard_map/gather_row_stats/all_to_all | solution.py:163
  168.3 2.0 slice.147
  170.3 2.4 %collective-permute-start.17 = (bf16[1024,320]{0,1:T(8,128)(2,1)}, bf16[1024,320]{0,1:T(8,128)(2,1)}, u32[]{:S(2)}, u32[]{:S(2)}) collective-permute-start(bf16[1024,320]{0,1:T(8,128)(2,1)} %slice.147), channel_id=1, source_target_pairs={{0,8},{8,16},{16,24},{24,0},{1,9},{9,17},{17,25},{25,1},{2,10},{10... | collective-permute-start | bytes 1966088 | tf_op jit(solution)/shard_map/gather_row_stats/ppermute | solution.py:32
  172.7 2.0 slice.148
  174.7 3.6 %collective-permute-start.18 = (bf16[1024,320]{0,1:T(8,128)(2,1)}, bf16[1024,320]{0,1:T(8,128)(2,1)}, u32[]{:S(2)}, u32[]{:S(2)}) collective-permute-start(bf16[1024,320]{0,1:T(8,128)(2,1)} %slice.148), channel_id=1, source_target_pairs={{0,24},{8,0},{16,8},{24,16},{1,25},{9,1},{17,9},{25,17},{2,26},{10... | collective-permute-start | bytes 1966088 | tf_op jit(solution)/shard_map/gather_row_stats/ppermute | solution.py:32
  178.3 3.0 %fusion.57 = (bf16[2048,160]{0,1:T(8,128)(2,1)}, bf16[2048,160]{0,1:T(8,128)(2,1)S(1)}, bf16[2048,160]{0,1:T(8,128)(2,1)S(1)}, bf16[2048,160]{0,1:T(8,128)(2,1)}) fusion(bf16[2048,320]{0,1:T(8,128)(2,1)} %collective-permute-done.16, bf16[2048,320]{0,1:T(8,128)(2,1)} %collective-permute-done.15), kind=kLoop, calls=%fused_computation.147 | loop fusion | bytes 5242880 | tf_op jit(solution)/shard_map/key_pass/slice | solution.py:173
  181.4 1.2 all-to-all-done
  182.5 2.3 %gather_fusion.1 = f32[64,2,2,128]{3,2,1,0:T(2,128)} fusion(f32[64,2,2,128]{3,2,1,0:T(2,128)} %all-to-all-done, s32[1024]{0:T(1024)S(1)} %pad_clamp_fusion.3), kind=kCustom, calls=%fused_computation.1 | custom fusion | bytes 262400 | tf_op jit(solution)/shard_map/key_pass/gather | solution.py:167
  184.8 0.8 slice_bitcast_fusion.6
  185.7 1.8 fusion.62
  193.1 1.1 constant_dynamic-update-slice_fusion.17
  194.3 1.2 constant_dynamic-update-slice_fusion.16
  195.6 0.7 fusion.63
  200.5 12.3 %all_to_all.10 = f32[4,129,320]{2,1,0:T(8,128)S(1)} all-to-all(f32[4,129,320]{2,1,0:T(8,128)S(1)} %copy.31), channel_id=1, replica_groups=mesh['z'=16,'y'=4,'tp'=4,'dp'=2] {'tp'}, dimensions={0} | all-to-all | bytes 1320960 | tf_op jit(solution)/shard_map/back_projection/all_to_all | solution.py:217
  (137 shorter events, 31.2 us)
Async XLA Ops:
  6.5 15.1 %copy-start = (bf16[160,1280]{1,0:T(8,128)(2,1)S(1)}, bf16[160,1280]{1,0:T(8,128)(2,1)}, u32[]{:S(2)}) copy-start(bf16[160,1280]{1,0:T(8,128)(2,1)} %param.16) | copy-start | bytes 1228804
  6.5 132.2 %all-gather.2.cloned.1.call-start = ((), (), s32[]{:S(2)}) async-start(), calls=%async_computation.2 | async-start | bytes 5570560 | tf_op jit(solution)/shard_map/gather_sequence/all_gather | solution.py:110
  7.5 13.9 %copy-start.15 = (f32[1280]{0:T(1024)S(1)}, f32[1280]{0:T(1024)}, u32[]{:S(2)}) copy-start(f32[1280]{0:T(1024)} %param.13) | copy-start | bytes 15364
  21.0 1.0 copy-start.6
  21.2 15.7 %copy-start.16 = (f32[80]{0:T(128)S(1)}, f32[80]{0:T(128)}, u32[]{:S(2)}) copy-start(f32[80]{0:T(128)} %param.18) | copy-start | bytes 964
  21.2 15.8 %copy-start.12 = (bf16[160,1280]{1,0:T(8,128)(2,1)S(1)}, bf16[160,1280]{1,0:T(8,128)(2,1)}, u32[]{:S(2)}) copy-start(bf16[160,1280]{1,0:T(8,128)(2,1)} %param.17) | copy-start | bytes 1228804
  21.5 15.8 %copy-start.7 = (bf16[160,1280]{1,0:T(8,128)(2,1)S(1)}, bf16[160,1280]{1,0:T(8,128)(2,1)}, u32[]{:S(2)}) copy-start(bf16[160,1280]{1,0:T(8,128)(2,1)} %param.14) | copy-start | bytes 1228804
  21.6 27.6 %copy-start.1 = (s32[64]{0:T(128)S(1)}, s32[64]{0:T(128)}, u32[]{:S(2)}) copy-start(s32[64]{0:T(128)} %param.19) | copy-start | bytes 772
  38.2 17.7 %collective-permute-start = (bf16[128,320]{0,1:T(8,128)(2,1)S(1)}, bf16[128,320]{0,1:T(8,128)(2,1)S(1)}, u32[]{:S(2)}, u32[]{:S(2)}) collective-permute-start(bf16[128,320]{0,1:T(8,128)(2,1)S(1)} %get-tuple-element.59), channel_id=1, source_target_pairs={{0,480},{32,0},{64,32},{96,64},{128,96},{160,128},{192,160},{224,1... | collective-permute-start | bytes 245768 | tf_op jit(solution)/shard_map/gather_sequence/ppermute | solution.py:32
  47.1 13.9 %collective-permute-start.7 = (bf16[128,320]{0,1:T(8,128)(2,1)S(1)}, bf16[128,320]{0,1:T(8,128)(2,1)S(1)}, u32[]{:S(2)}, u32[]{:S(2)}) collective-permute-start(bf16[128,320]{0,1:T(8,128)(2,1)S(1)} %get-tuple-element.59), channel_id=1, source_target_pairs={{0,32},{32,64},{64,96},{96,128},{128,160},{160,192},{192,224},{224... | collective-permute-start | bytes 245768 | tf_op jit(solution)/shard_map/gather_sequence/ppermute | solution.py:32
  55.9 8.2 %collective-permute-start.1 = (bf16[128,320]{0,1:T(8,128)(2,1)S(1)}, bf16[128,320]{0,1:T(8,128)(2,1)S(1)}, u32[]{:S(2)}, u32[]{:S(2)}) collective-permute-start(bf16[128,320]{0,1:T(8,128)(2,1)S(1)} %collective-permute-done), channel_id=1, source_target_pairs={{0,480},{32,0},{64,32},{96,64},{128,96},{160,128},{192,160},{224,1... | collective-permute-start | bytes 245768 | tf_op jit(solution)/shard_map/gather_sequence/ppermute | solution.py:32
  61.0 9.0 %collective-permute-start.8 = (bf16[128,320]{0,1:T(8,128)(2,1)S(1)}, bf16[128,320]{0,1:T(8,128)(2,1)S(1)}, u32[]{:S(2)}, u32[]{:S(2)}) collective-permute-start(bf16[128,320]{0,1:T(8,128)(2,1)S(1)} %collective-permute-done.7), channel_id=1, source_target_pairs={{0,32},{32,64},{64,96},{96,128},{128,160},{160,192},{192,224},{224... | collective-permute-start | bytes 245768 | tf_op jit(solution)/shard_map/gather_sequence/ppermute | solution.py:32
  64.1 9.1 %collective-permute-start.2 = (bf16[128,320]{0,1:T(8,128)(2,1)S(1)}, bf16[128,320]{0,1:T(8,128)(2,1)S(1)}, u32[]{:S(2)}, u32[]{:S(2)}) collective-permute-start(bf16[128,320]{0,1:T(8,128)(2,1)S(1)} %collective-permute-done.1), channel_id=1, source_target_pairs={{0,480},{32,0},{64,32},{96,64},{128,96},{160,128},{192,160},{224,1... | collective-permute-start | bytes 245768 | tf_op jit(solution)/shard_map/gather_sequence/ppermute | solution.py:32
  70.0 9.0 %collective-permute-start.9 = (bf16[128,320]{0,1:T(8,128)(2,1)S(1)}, bf16[128,320]{0,1:T(8,128)(2,1)S(1)}, u32[]{:S(2)}, u32[]{:S(2)}) collective-permute-start(bf16[128,320]{0,1:T(8,128)(2,1)S(1)} %collective-permute-done.8), channel_id=1, source_target_pairs={{0,32},{32,64},{64,96},{96,128},{128,160},{160,192},{192,224},{224... | collective-permute-start | bytes 245768 | tf_op jit(solution)/shard_map/gather_sequence/ppermute | solution.py:32
  73.2 9.2 %collective-permute-start.3 = (bf16[128,320]{0,1:T(8,128)(2,1)S(1)}, bf16[128,320]{0,1:T(8,128)(2,1)S(1)}, u32[]{:S(2)}, u32[]{:S(2)}) collective-permute-start(bf16[128,320]{0,1:T(8,128)(2,1)S(1)} %collective-permute-done.2), channel_id=1, source_target_pairs={{0,480},{32,0},{64,32},{96,64},{128,96},{160,128},{192,160},{224,1... | collective-permute-start | bytes 245768 | tf_op jit(solution)/shard_map/gather_sequence/ppermute | solution.py:32
  79.1 8.9 %collective-permute-start.10 = (bf16[128,320]{0,1:T(8,128)(2,1)S(1)}, bf16[128,320]{0,1:T(8,128)(2,1)S(1)}, u32[]{:S(2)}, u32[]{:S(2)}) collective-permute-start(bf16[128,320]{0,1:T(8,128)(2,1)S(1)} %collective-permute-done.9), channel_id=1, source_target_pairs={{0,32},{32,64},{64,96},{96,128},{128,160},{160,192},{192,224},{224... | collective-permute-start | bytes 245768 | tf_op jit(solution)/shard_map/gather_sequence/ppermute | solution.py:32
  82.4 8.5 %collective-permute-start.4 = (bf16[128,320]{0,1:T(8,128)(2,1)S(1)}, bf16[128,320]{0,1:T(8,128)(2,1)S(1)}, u32[]{:S(2)}, u32[]{:S(2)}) collective-permute-start(bf16[128,320]{0,1:T(8,128)(2,1)S(1)} %collective-permute-done.3), channel_id=1, source_target_pairs={{0,480},{32,0},{64,32},{96,64},{128,96},{160,128},{192,160},{224,1... | collective-permute-start | bytes 245768 | tf_op jit(solution)/shard_map/gather_sequence/ppermute | solution.py:32
  88.0 9.8 %collective-permute-start.11 = (bf16[128,320]{0,1:T(8,128)(2,1)S(1)}, bf16[128,320]{0,1:T(8,128)(2,1)S(1)}, u32[]{:S(2)}, u32[]{:S(2)}) collective-permute-start(bf16[128,320]{0,1:T(8,128)(2,1)S(1)} %collective-permute-done.10), channel_id=1, source_target_pairs={{0,32},{32,64},{64,96},{96,128},{128,160},{160,192},{192,224},{224... | collective-permute-start | bytes 245768 | tf_op jit(solution)/shard_map/gather_sequence/ppermute | solution.py:32
  90.8 9.5 %collective-permute-start.5 = (bf16[128,320]{0,1:T(8,128)(2,1)S(1)}, bf16[128,320]{0,1:T(8,128)(2,1)S(1)}, u32[]{:S(2)}, u32[]{:S(2)}) collective-permute-start(bf16[128,320]{0,1:T(8,128)(2,1)S(1)} %collective-permute-done.4), channel_id=1, source_target_pairs={{0,480},{32,0},{64,32},{96,64},{128,96},{160,128},{192,160},{224,1... | collective-permute-start | bytes 245768 | tf_op jit(solution)/shard_map/gather_sequence/ppermute | solution.py:32
  97.7 9.6 %collective-permute-start.12 = (bf16[128,320]{0,1:T(8,128)(2,1)S(1)}, bf16[128,320]{0,1:T(8,128)(2,1)S(1)}, u32[]{:S(2)}, u32[]{:S(2)}) collective-permute-start(bf16[128,320]{0,1:T(8,128)(2,1)S(1)} %collective-permute-done.11), channel_id=1, source_target_pairs={{0,32},{32,64},{64,96},{96,128},{128,160},{160,192},{192,224},{224... | collective-permute-start | bytes 245768 | tf_op jit(solution)/shard_map/gather_sequence/ppermute | solution.py:32
  100.3 18.1 %collective-permute-start.6 = (bf16[128,320]{0,1:T(8,128)(2,1)S(1)}, bf16[128,320]{0,1:T(8,128)(2,1)S(1)}, u32[]{:S(2)}, u32[]{:S(2)}) collective-permute-start(bf16[128,320]{0,1:T(8,128)(2,1)S(1)} %collective-permute-done.5), channel_id=1, source_target_pairs={{0,480},{32,0},{64,32},{96,64},{128,96},{160,128},{192,160},{224,1... | collective-permute-start | bytes 245768 | tf_op jit(solution)/shard_map/gather_sequence/ppermute | solution.py:32
  107.3 9.2 %collective-permute-start.13 = (bf16[128,320]{0,1:T(8,128)(2,1)S(1)}, bf16[128,320]{0,1:T(8,128)(2,1)S(1)}, u32[]{:S(2)}, u32[]{:S(2)}) collective-permute-start(bf16[128,320]{0,1:T(8,128)(2,1)S(1)} %collective-permute-done.12), channel_id=1, source_target_pairs={{0,32},{32,64},{64,96},{96,128},{128,160},{160,192},{192,224},{224... | collective-permute-start | bytes 245768 | tf_op jit(solution)/shard_map/gather_sequence/ppermute | solution.py:32
  116.5 8.8 %collective-permute-start.14 = (bf16[128,320]{0,1:T(8,128)(2,1)S(1)}, bf16[128,320]{0,1:T(8,128)(2,1)S(1)}, u32[]{:S(2)}, u32[]{:S(2)}) collective-permute-start(bf16[128,320]{0,1:T(8,128)(2,1)S(1)} %collective-permute-done.13), channel_id=1, source_target_pairs={{0,32},{32,64},{64,96},{96,128},{128,160},{160,192},{192,224},{224... | collective-permute-start | bytes 245768 | tf_op jit(solution)/shard_map/gather_sequence/ppermute | solution.py:32
  130.4 24.0 %collective-permute-start.15 = (bf16[2048,320]{0,1:T(8,128)(2,1)}, bf16[2048,320]{0,1:T(8,128)(2,1)}, u32[]{:S(2)}, u32[]{:S(2)}) collective-permute-start(bf16[2048,320]{0,1:T(8,128)(2,1)} %constant_dynamic-update-slice_fusion), channel_id=1, source_target_pairs={{0,8},{8,16},{16,24},{24,0},{1,9},{9,17},{17,25},{25,1},{2,10},{10... | collective-permute-start | bytes 3932168 | tf_op jit(solution)/shard_map/gather_sequence/ppermute | solution.py:32
  134.2 23.8 %collective-permute-start.16 = (bf16[2048,320]{0,1:T(8,128)(2,1)}, bf16[2048,320]{0,1:T(8,128)(2,1)}, u32[]{:S(2)}, u32[]{:S(2)}) collective-permute-start(bf16[2048,320]{0,1:T(8,128)(2,1)} %constant_dynamic-update-slice_fusion), channel_id=1, source_target_pairs={{0,24},{8,0},{16,8},{24,16},{1,25},{9,1},{17,9},{25,17},{2,26},{10... | collective-permute-start | bytes 3932168 | tf_op jit(solution)/shard_map/gather_sequence/ppermute | solution.py:32
  151.4 1.7 copy-start.8
  158.7 23.9 %all-to-all-start = ((f32[64,2,2,128]{3,2,1,0:T(2,128)}), f32[64,2,2,128]{3,2,1,0:T(2,128)}, u32[]{:S(2)}, u32[]{:S(2)}) async-start(f32[64,2,2,128]{3,2,1,0:T(2,128)} %broadcast_in_dim.92), calls=%async_computation | async-start | bytes 262144 | tf_op jit(solution)/shard_map/gather_row_stats/all_to_all | solution.py:163
  170.3 22.8 %collective-permute-start.17 = (bf16[1024,320]{0,1:T(8,128)(2,1)}, bf16[1024,320]{0,1:T(8,128)(2,1)}, u32[]{:S(2)}, u32[]{:S(2)}) collective-permute-start(bf16[1024,320]{0,1:T(8,128)(2,1)} %slice.147), channel_id=1, source_target_pairs={{0,8},{8,16},{16,24},{24,0},{1,9},{9,17},{17,25},{25,1},{2,10},{10... | collective-permute-start | bytes 1966088 | tf_op jit(solution)/shard_map/gather_row_stats/ppermute | solution.py:32
  174.7 19.6 %collective-permute-start.18 = (bf16[1024,320]{0,1:T(8,128)(2,1)}, bf16[1024,320]{0,1:T(8,128)(2,1)}, u32[]{:S(2)}, u32[]{:S(2)}) collective-permute-start(bf16[1024,320]{0,1:T(8,128)(2,1)} %slice.148), channel_id=1, source_target_pairs={{0,24},{8,0},{16,8},{24,16},{1,25},{9,1},{17,9},{25,17},{2,26},{10... | collective-permute-start | bytes 1966088 | tf_op jit(solution)/shard_map/gather_row_stats/ppermute | solution.py:32
  185.7 1.8 copy-start.3
  187.4 1.0 copy-start.11
  188.4 1.1 copy-start.2
  189.2 1.0 copy-start.10
  190.0 1.1 copy-start.4
  194.3 1.3 copy-start.9
  197.3 1.1 copy-start.5
  200.5 12.5 %copy-start.13 = (bf16[128,320]{0,1:T(8,128)(2,1)S(1)}, bf16[128,320]{0,1:T(8,128)(2,1)}, u32[]{:S(2)}) copy-start(bf16[128,320]{0,1:T(8,128)(2,1)} %param.11) | copy-start | bytes 245764
  200.5 12.5 %copy-start.14 = (bf16[128,320]{0,1:T(8,128)(2,1)S(1)}, bf16[128,320]{0,1:T(8,128)(2,1)}, u32[]{:S(2)}) copy-start(bf16[128,320]{0,1:T(8,128)(2,1)} %param.12) | copy-start | bytes 245764
Sparse Core Ops, SparseCore 0:
  37.0 92.6 all-gather.1

commit v15 on v14

--- a/solution.py
+++ b/solution.py
@@ -52,10 +52,7 @@
 
 
 def ring4_last(data, ahead, behind, axis):
-    half = data.shape[0] // 2
-    far = jnp.concatenate(
-        [shift(ahead[:half], axis, 4, 1), shift(behind[half:], axis, 4, -1)], axis=0
-    )
+    far = shift(ahead, axis, 4, 1)
     return [data, behind, far, ahead]
 
 

time: 223 us -> 222 us (level)
  waiting for transfers between devices: 23.5 us -> 31.1 us
  local copies, waits for them, and re-layouts: 33.8 us -> 29 us
  starting transfers between devices: 78.5 us -> 75.2 us
    all_to_all x1, waiting for transfers between devices: 1.19 us -> 8.46 us  [per_device(): stats_all = lax.all_to_all(sent, ('z', 'y'), 0, 0, tiled=False)]
    slice x2 -> x0, local copies, waits for them, and re-layouts: 4.02 us -> none  [the longest x1 2.02 us: ring4_last(): ahead[:half]]
    ppermute x19 -> x18, starting transfers between devices: 68.9 us -> 65.9 us  [shift(): lax.ppermute(data, axis, [(i, (i + step) % size) for i in range(size)])]
    unnamed x50 -> x49, local copies, waits for them, and re-layouts: 11.4 us -> 10.4 us
    ppermute x19 -> x18, waiting for transfers between devices: 22.3 us -> 22.7 us  [shift(): lax.ppermute(data, axis, [(i, (i + step) % size) for i in range(size)])]
  transfers between devices with their start and end apart: 21 -> 20, of which waited for: 13 -> 13; matrix products, arithmetic and copies ran while one was open for 24% -> 22% of each run, Pallas kernels for 0% -> 0%
where the time goes in v15:
time: 222 us; the launch traced here: 220 us
  starting transfers between devices  75.2 us (34%)
  blocking collectives  40.2 us (18%)
  waiting for transfers between devices  31.1 us (14%)
  local copies, waits for them, and re-layouts  29 us (13%)
  matrix products  21.5 us (10%)
  between operations  14.8 us (7%)
  other arithmetic  8.25 us (4%)
    ppermute x18, starting transfers between devices, shift(): lax.ppermute(data, axis, [(i, (i + step) % size) for i in range(size)])  65.9 us
    ppermute x18, waiting for transfers between devices, shift(): lax.ppermute(data, axis, [(i, (i + step) % size) for i in range(size)])  22.7 us
    all_gather x1, blocking collectives, per_device(): kv_all = lax.all_gather(kv, 'y', axis=0, tiled=True)  14.6 us
    all_gather x1, blocking collectives, per_device(): gathered = lax.all_gather(both, 'tp', axis=1, tiled=True)  13.4 us
    all_to_all x1, blocking collectives, per_device(): received = lax.all_to_all(payload, 'tp', 0, 0, tiled=False)  12.3 us
    unnamed x49, local copies, waits for them, and re-layouts  10.4 us
    all_to_all x1, starting transfers between devices, per_device(): stats_all = lax.all_to_all(sent, ('z', 'y'), 0, 0, tiled=False)  9.26 us
    all_to_all x1, waiting for transfers between devices, per_device(): stats_all = lax.all_to_all(sent, ('z', 'y'), 0, 0, tiled=False)  8.46 us
  transfers between devices with their start and end apart: 20, of which 13 were waited for; matrix products, arithmetic and copies ran while one was open for 22% of the time, Pallas kernels for 0%

profile of v15, /device:TPU:24, one launch (start us, length us, event | category | flops | bytes accessed | tf_op | source)
XLA Modules:
  0.0 220.1 jit_solution(9224660764763108338)
XLA Ops:
  6.5 1.0 pad_maximum_fusion.1
  7.5 13.4 %all_gather.9 = bf16[128,2560]{0,1:T(8,128)(2,1)S(1)} all-gather(bf16[128,640]{0,1:T(8,128)(2,1)S(1)} %pad_maximum_fusion.1), channel_id=1, replica_groups=mesh['z'=16,'y'=4,'tp'=4,'dp'=2] {'tp'}, dimensions={1}, use_global_device_ids=true | all-gather | bytes 819200 | tf_op jit(solution)/shard_map/gather_features/all_gather | solution.py:74
  22.3 14.6 %all_gather.10 = bf16[512,320]{0,1:T(8,128)(2,1)} all-gather(bf16[128,320]{0,1:T(8,128)(2,1)S(1)} %pad_maximum_fusion.2), channel_id=1, replica_groups=mesh['z'=16,'y'=4,'tp'=4,'dp'=2] {'y'}, dimensions={0}, use_global_device_ids=true | all-gather | bytes 409600 | tf_op jit(solution)/shard_map/gather_sequence/all_gather | solution.py:106
  38.2 8.9 %collective-permute-start = (bf16[128,320]{0,1:T(8,128)(2,1)S(1)}, bf16[128,320]{0,1:T(8,128)(2,1)S(1)}, u32[]{:S(2)}, u32[]{:S(2)}) collective-permute-start(bf16[128,320]{0,1:T(8,128)(2,1)S(1)} %get-tuple-element.59), channel_id=1, source_target_pairs={{0,480},{32,0},{64,32},{96,64},{128,96},{160,128},{192,160},{224,1... | collective-permute-start | bytes 245768 | tf_op jit(solution)/shard_map/gather_sequence/ppermute | solution.py:32
  47.1 1.9 collective-permute-start.7
  53.6 1.6 broadcast_compare_fusion.4
  55.9 5.1 %collective-permute-start.1 = (bf16[128,320]{0,1:T(8,128)(2,1)S(1)}, bf16[128,320]{0,1:T(8,128)(2,1)S(1)}, u32[]{:S(2)}, u32[]{:S(2)}) collective-permute-start(bf16[128,320]{0,1:T(8,128)(2,1)S(1)} %collective-permute-done), channel_id=1, source_target_pairs={{0,480},{32,0},{64,32},{96,64},{128,96},{160,128},{192,160},{224,1... | collective-permute-start | bytes 245768 | tf_op jit(solution)/shard_map/gather_sequence/ppermute | solution.py:32
  61.1 1.9 collective-permute-start.8
  64.2 5.6 %collective-permute-start.2 = (bf16[128,320]{0,1:T(8,128)(2,1)S(1)}, bf16[128,320]{0,1:T(8,128)(2,1)S(1)}, u32[]{:S(2)}, u32[]{:S(2)}) collective-permute-start(bf16[128,320]{0,1:T(8,128)(2,1)S(1)} %collective-permute-done.1), channel_id=1, source_target_pairs={{0,480},{32,0},{64,32},{96,64},{128,96},{160,128},{192,160},{224,1... | collective-permute-start | bytes 245768 | tf_op jit(solution)/shard_map/gather_sequence/ppermute | solution.py:32
  70.1 1.9 collective-permute-start.9
  73.2 5.6 %collective-permute-start.3 = (bf16[128,320]{0,1:T(8,128)(2,1)S(1)}, bf16[128,320]{0,1:T(8,128)(2,1)S(1)}, u32[]{:S(2)}, u32[]{:S(2)}) collective-permute-start(bf16[128,320]{0,1:T(8,128)(2,1)S(1)} %collective-permute-done.2), channel_id=1, source_target_pairs={{0,480},{32,0},{64,32},{96,64},{128,96},{160,128},{192,160},{224,1... | collective-permute-start | bytes 245768 | tf_op jit(solution)/shard_map/gather_sequence/ppermute | solution.py:32
  79.1 1.9 collective-permute-start.10
  82.2 5.6 %collective-permute-start.4 = (bf16[128,320]{0,1:T(8,128)(2,1)S(1)}, bf16[128,320]{0,1:T(8,128)(2,1)S(1)}, u32[]{:S(2)}, u32[]{:S(2)}) collective-permute-start(bf16[128,320]{0,1:T(8,128)(2,1)S(1)} %collective-permute-done.3), channel_id=1, source_target_pairs={{0,480},{32,0},{64,32},{96,64},{128,96},{160,128},{192,160},{224,1... | collective-permute-start | bytes 245768 | tf_op jit(solution)/shard_map/gather_sequence/ppermute | solution.py:32
  88.1 1.9 collective-permute-start.11
  90.8 5.6 %collective-permute-start.5 = (bf16[128,320]{0,1:T(8,128)(2,1)S(1)}, bf16[128,320]{0,1:T(8,128)(2,1)S(1)}, u32[]{:S(2)}, u32[]{:S(2)}) collective-permute-start(bf16[128,320]{0,1:T(8,128)(2,1)S(1)} %collective-permute-done.4), channel_id=1, source_target_pairs={{0,480},{32,0},{64,32},{96,64},{128,96},{160,128},{192,160},{224,1... | collective-permute-start | bytes 245768 | tf_op jit(solution)/shard_map/gather_sequence/ppermute | solution.py:32
  96.4 1.2 collective-permute-done.11
  97.6 1.9 collective-permute-start.12
  100.2 5.1 %collective-permute-start.6 = (bf16[128,320]{0,1:T(8,128)(2,1)S(1)}, bf16[128,320]{0,1:T(8,128)(2,1)S(1)}, u32[]{:S(2)}, u32[]{:S(2)}) collective-permute-start(bf16[128,320]{0,1:T(8,128)(2,1)S(1)} %collective-permute-done.5), channel_id=1, source_target_pairs={{0,480},{32,0},{64,32},{96,64},{128,96},{160,128},{192,160},{224,1... | collective-permute-start | bytes 245768 | tf_op jit(solution)/shard_map/gather_sequence/ppermute | solution.py:32
  105.3 2.0 collective-permute-done.12
  107.3 1.9 collective-permute-start.13
  109.9 6.9 %collective-permute-done.13 = bf16[128,320]{0,1:T(8,128)(2,1)S(1)} collective-permute-done((bf16[128,320]{0,1:T(8,128)(2,1)S(1)}, bf16[128,320]{0,1:T(8,128)(2,1)S(1)}, u32[]{:S(2)}, u32[]{:S(2)}) %collective-permute-start.13) | collective-permute-done | bytes 81952 | tf_op jit(solution)/shard_map/gather_sequence/ppermute | solution.py:32
  116.8 1.9 collective-permute-start.14
  119.3 6.2 %collective-permute-done.14 = bf16[128,320]{0,1:T(8,128)(2,1)S(1)} collective-permute-done((bf16[128,320]{0,1:T(8,128)(2,1)S(1)}, bf16[128,320]{0,1:T(8,128)(2,1)S(1)}, u32[]{:S(2)}, u32[]{:S(2)}) %collective-permute-start.14) | collective-permute-done | bytes 81952 | tf_op jit(solution)/shard_map/gather_sequence/ppermute | solution.py:32
  130.8 4.3 %collective-permute-start.15 = (bf16[2048,320]{0,1:T(8,128)(2,1)}, bf16[2048,320]{0,1:T(8,128)(2,1)}, u32[]{:S(2)}, u32[]{:S(2)}) collective-permute-start(bf16[2048,320]{0,1:T(8,128)(2,1)} %constant_dynamic-update-slice_fusion), channel_id=1, source_target_pairs={{0,8},{8,16},{16,24},{24,0},{1,9},{9,17},{17,25},{25,1},{2,10},{10... | collective-permute-start | bytes 3932168 | tf_op jit(solution)/shard_map/gather_sequence/ppermute | solution.py:32
  135.1 2.1 collective-permute-start.16
  137.2 2.2 %fusion.56 = (bf16[2048,160]{0,1:T(8,128)(2,1)}, bf16[2048,160]{0,1:T(8,128)(2,1)S(1)}) fusion(bf16[2048,320]{0,1:T(8,128)(2,1)} %constant_dynamic-update-slice_fusion), kind=kLoop, calls=%fused_computation.144 | loop fusion | bytes 2621440 | tf_op jit(solution)/shard_map/key_pass/slice | solution.py:170
  139.5 3.0 %fusion.55 = (bf16[8192,160]{0,1:T(8,128)(2,1)S(1)}, bf16[8192,160]{0,1:T(8,128)(2,1)S(1)}) fusion(bf16[8192,320]{0,1:T(8,128)(2,1)} %all-gather.2.cloned.1.call-done), kind=kLoop, calls=%fused_computation.143 | loop fusion | bytes 10485760 | tf_op jit(solution)/shard_map/gather_sequence/slice | solution.py:111
  142.4 1.8 select_reduce_fusion.1
  144.2 2.5 %select_reduce_fusion = f32[2,128]{1,0:T(2,128)S(1)} fusion(f32[2,128,8192]{2,1,0:T(8,128)S(1)} %get-tuple-element.70, f32[2,128]{1,0:T(2,128)S(1)} %get-tuple-element.69, pred[128,8192]{1,0:T(8,128)(4,1)S(1)} %broadcast_compare_fusion), kind=kLoop, calls=%fused_computation.7 | loop fusion | flops 8388352 | bytes 9439232 | tf_op jit(solution)/shard_map/query_pass/reduce_sum | solution.py:134
  146.7 3.5 %fusion.61 = (f32[2,128]{1,0:T(2,128)S(1)}, bf16[2,128,8192]{2,1,0:T(8,128)(2,1)S(1)}) fusion(bf16[128,2,80]{0,2,1:T(8,128)(2,1)S(1)} %bitcast.208, bf16[8192,2,80]{0,2,1:T(8,128)(2,1)S(1)} %bitcast.194, f32[2,128,8192]{2,1,0:T(8,128)S(1)} %get-tuple-element.70, f32[2,128]{1,0:T(2,128)S(1)} %log_add_fusion, pred[128,8192]{1,0:T(8,128)(4,1)S(1)} %broadcast_compare_fusion), kind=kOutput, calls=%fused_computation.149 | convolution fusion | flops 346029824 | bytes 16295936 | tf_op jit(solution)/shard_map/query_pass/qhd,khd->hqk/dot_general | solution.py:137
  150.2 2.0 fusion.38
  152.2 1.5 fusion.28
  153.9 1.1 fusion.66
  155.0 3.7 %collective-permute-done.16 = bf16[2048,320]{0,1:T(8,128)(2,1)} collective-permute-done((bf16[2048,320]{0,1:T(8,128)(2,1)}, bf16[2048,320]{0,1:T(8,128)(2,1)}, u32[]{:S(2)}, u32[]{:S(2)}) %collective-permute-start.16) | collective-permute-done | bytes 1310752 | tf_op jit(solution)/shard_map/gather_sequence/ppermute | solution.py:32
  158.7 0.7 broadcast_in_dim.92
  159.4 9.3 %all-to-all-start = ((f32[64,2,2,128]{3,2,1,0:T(2,128)}), f32[64,2,2,128]{3,2,1,0:T(2,128)}, u32[]{:S(2)}, u32[]{:S(2)}) async-start(f32[64,2,2,128]{3,2,1,0:T(2,128)} %broadcast_in_dim.92), calls=%async_computation | async-start | bytes 262144 | tf_op jit(solution)/shard_map/gather_row_stats/all_to_all | solution.py:160
  168.7 2.7 %collective-permute-start.17 = (bf16[2048,320]{0,1:T(8,128)(2,1)}, bf16[2048,320]{0,1:T(8,128)(2,1)}, u32[]{:S(2)}, u32[]{:S(2)}) collective-permute-start(bf16[2048,320]{0,1:T(8,128)(2,1)} %collective-permute-done.15), channel_id=1, source_target_pairs={{0,8},{8,16},{16,24},{24,0},{1,9},{9,17},{17,25},{25,1},{2,10},{10... | collective-permute-start | bytes 3932168 | tf_op jit(solution)/shard_map/gather_row_stats/ppermute | solution.py:32
  171.4 3.1 %fusion.57 = (bf16[2048,160]{0,1:T(8,128)(2,1)}, bf16[2048,160]{0,1:T(8,128)(2,1)S(1)}, bf16[2048,160]{0,1:T(8,128)(2,1)S(1)}, bf16[2048,160]{0,1:T(8,128)(2,1)}) fusion(bf16[2048,320]{0,1:T(8,128)(2,1)} %collective-permute-done.16, bf16[2048,320]{0,1:T(8,128)(2,1)} %collective-permute-done.15), kind=kLoop, calls=%fused_computation.145 | loop fusion | bytes 5242880 | tf_op jit(solution)/shard_map/key_pass/slice | solution.py:170
  174.4 8.5 %all-to-all-done = f32[64,2,2,128]{3,2,1,0:T(2,128)} async-done(((f32[64,2,2,128]{3,2,1,0:T(2,128)}), f32[64,2,2,128]{3,2,1,0:T(2,128)}, u32[]{:S(2)}, u32[]{:S(2)}) %all-to-all-start) | async-done | bytes 131104 | tf_op jit(solution)/shard_map/gather_row_stats/all_to_all | solution.py:160
  182.9 2.3 %gather_fusion.1 = f32[64,2,2,128]{3,2,1,0:T(2,128)} fusion(f32[64,2,2,128]{3,2,1,0:T(2,128)} %all-to-all-done, s32[1024]{0:T(1024)S(1)} %pad_clamp_fusion.3), kind=kCustom, calls=%fused_computation.1 | custom fusion | bytes 262400 | tf_op jit(solution)/shard_map/key_pass/gather | solution.py:164
  185.2 0.8 slice_bitcast_fusion.6
  186.0 1.8 fusion.62
  188.7 0.7 fusion.64
  190.4 0.7 fusion.65
  193.7 1.4 fusion.58
  195.2 0.7 fusion.63
  200.0 12.3 %all_to_all.10 = f32[4,129,320]{2,1,0:T(8,128)S(1)} all-to-all(f32[4,129,320]{2,1,0:T(8,128)S(1)} %copy.31), channel_id=1, replica_groups=mesh['z'=16,'y'=4,'tp'=4,'dp'=2] {'tp'}, dimensions={0} | all-to-all | bytes 1320960 | tf_op jit(solution)/shard_map/back_projection/all_to_all | solution.py:214
  212.5 0.7 add_convert_fusion
  (131 shorter events, 28.2 us)
Async XLA Ops:
  6.5 15.1 %copy-start = (bf16[160,1280]{1,0:T(8,128)(2,1)S(1)}, bf16[160,1280]{1,0:T(8,128)(2,1)}, u32[]{:S(2)}) copy-start(bf16[160,1280]{1,0:T(8,128)(2,1)} %param.16) | copy-start | bytes 1228804
  6.5 132.9 %all-gather.2.cloned.1.call-start = ((), (), s32[]{:S(2)}) async-start(), calls=%async_computation.2 | async-start | bytes 5570560 | tf_op jit(solution)/shard_map/gather_sequence/all_gather | solution.py:107
  7.5 13.9 %copy-start.15 = (f32[1280]{0:T(1024)S(1)}, f32[1280]{0:T(1024)}, u32[]{:S(2)}) copy-start(f32[1280]{0:T(1024)} %param.13) | copy-start | bytes 15364
  21.0 1.0 copy-start.6
  21.2 15.7 %copy-start.16 = (f32[80]{0:T(128)S(1)}, f32[80]{0:T(128)}, u32[]{:S(2)}) copy-start(f32[80]{0:T(128)} %param.18) | copy-start | bytes 964
  21.2 15.8 %copy-start.12 = (bf16[160,1280]{1,0:T(8,128)(2,1)S(1)}, bf16[160,1280]{1,0:T(8,128)(2,1)}, u32[]{:S(2)}) copy-start(bf16[160,1280]{1,0:T(8,128)(2,1)} %param.17) | copy-start | bytes 1228804
  21.5 15.8 %copy-start.7 = (bf16[160,1280]{1,0:T(8,128)(2,1)S(1)}, bf16[160,1280]{1,0:T(8,128)(2,1)}, u32[]{:S(2)}) copy-start(bf16[160,1280]{1,0:T(8,128)(2,1)} %param.14) | copy-start | bytes 1228804
  21.6 27.6 %copy-start.1 = (s32[64]{0:T(128)S(1)}, s32[64]{0:T(128)}, u32[]{:S(2)}) copy-start(s32[64]{0:T(128)} %param.19) | copy-start | bytes 772
  38.2 17.7 %collective-permute-start = (bf16[128,320]{0,1:T(8,128)(2,1)S(1)}, bf16[128,320]{0,1:T(8,128)(2,1)S(1)}, u32[]{:S(2)}, u32[]{:S(2)}) collective-permute-start(bf16[128,320]{0,1:T(8,128)(2,1)S(1)} %get-tuple-element.59), channel_id=1, source_target_pairs={{0,480},{32,0},{64,32},{96,64},{128,96},{160,128},{192,160},{224,1... | collective-permute-start | bytes 245768 | tf_op jit(solution)/shard_map/gather_sequence/ppermute | solution.py:32
  47.1 13.9 %collective-permute-start.7 = (bf16[128,320]{0,1:T(8,128)(2,1)S(1)}, bf16[128,320]{0,1:T(8,128)(2,1)S(1)}, u32[]{:S(2)}, u32[]{:S(2)}) collective-permute-start(bf16[128,320]{0,1:T(8,128)(2,1)S(1)} %get-tuple-element.59), channel_id=1, source_target_pairs={{0,32},{32,64},{64,96},{96,128},{128,160},{160,192},{192,224},{224... | collective-permute-start | bytes 245768 | tf_op jit(solution)/shard_map/gather_sequence/ppermute | solution.py:32
  55.9 8.2 %collective-permute-start.1 = (bf16[128,320]{0,1:T(8,128)(2,1)S(1)}, bf16[128,320]{0,1:T(8,128)(2,1)S(1)}, u32[]{:S(2)}, u32[]{:S(2)}) collective-permute-start(bf16[128,320]{0,1:T(8,128)(2,1)S(1)} %collective-permute-done), channel_id=1, source_target_pairs={{0,480},{32,0},{64,32},{96,64},{128,96},{160,128},{192,160},{224,1... | collective-permute-start | bytes 245768 | tf_op jit(solution)/shard_map/gather_sequence/ppermute | solution.py:32
  61.1 9.0 %collective-permute-start.8 = (bf16[128,320]{0,1:T(8,128)(2,1)S(1)}, bf16[128,320]{0,1:T(8,128)(2,1)S(1)}, u32[]{:S(2)}, u32[]{:S(2)}) collective-permute-start(bf16[128,320]{0,1:T(8,128)(2,1)S(1)} %collective-permute-done.7), channel_id=1, source_target_pairs={{0,32},{32,64},{64,96},{96,128},{128,160},{160,192},{192,224},{224... | collective-permute-start | bytes 245768 | tf_op jit(solution)/shard_map/gather_sequence/ppermute | solution.py:32
  64.2 9.1 %collective-permute-start.2 = (bf16[128,320]{0,1:T(8,128)(2,1)S(1)}, bf16[128,320]{0,1:T(8,128)(2,1)S(1)}, u32[]{:S(2)}, u32[]{:S(2)}) collective-permute-start(bf16[128,320]{0,1:T(8,128)(2,1)S(1)} %collective-permute-done.1), channel_id=1, source_target_pairs={{0,480},{32,0},{64,32},{96,64},{128,96},{160,128},{192,160},{224,1... | collective-permute-start | bytes 245768 | tf_op jit(solution)/shard_map/gather_sequence/ppermute | solution.py:32
  70.1 9.1 %collective-permute-start.9 = (bf16[128,320]{0,1:T(8,128)(2,1)S(1)}, bf16[128,320]{0,1:T(8,128)(2,1)S(1)}, u32[]{:S(2)}, u32[]{:S(2)}) collective-permute-start(bf16[128,320]{0,1:T(8,128)(2,1)S(1)} %collective-permute-done.8), channel_id=1, source_target_pairs={{0,32},{32,64},{64,96},{96,128},{128,160},{160,192},{192,224},{224... | collective-permute-start | bytes 245768 | tf_op jit(solution)/shard_map/gather_sequence/ppermute | solution.py:32
  73.2 9.0 %collective-permute-start.3 = (bf16[128,320]{0,1:T(8,128)(2,1)S(1)}, bf16[128,320]{0,1:T(8,128)(2,1)S(1)}, u32[]{:S(2)}, u32[]{:S(2)}) collective-permute-start(bf16[128,320]{0,1:T(8,128)(2,1)S(1)} %collective-permute-done.2), channel_id=1, source_target_pairs={{0,480},{32,0},{64,32},{96,64},{128,96},{160,128},{192,160},{224,1... | collective-permute-start | bytes 245768 | tf_op jit(solution)/shard_map/gather_sequence/ppermute | solution.py:32
  79.1 9.0 %collective-permute-start.10 = (bf16[128,320]{0,1:T(8,128)(2,1)S(1)}, bf16[128,320]{0,1:T(8,128)(2,1)S(1)}, u32[]{:S(2)}, u32[]{:S(2)}) collective-permute-start(bf16[128,320]{0,1:T(8,128)(2,1)S(1)} %collective-permute-done.9), channel_id=1, source_target_pairs={{0,32},{32,64},{64,96},{96,128},{128,160},{160,192},{192,224},{224... | collective-permute-start | bytes 245768 | tf_op jit(solution)/shard_map/gather_sequence/ppermute | solution.py:32
  82.2 8.6 %collective-permute-start.4 = (bf16[128,320]{0,1:T(8,128)(2,1)S(1)}, bf16[128,320]{0,1:T(8,128)(2,1)S(1)}, u32[]{:S(2)}, u32[]{:S(2)}) collective-permute-start(bf16[128,320]{0,1:T(8,128)(2,1)S(1)} %collective-permute-done.3), channel_id=1, source_target_pairs={{0,480},{32,0},{64,32},{96,64},{128,96},{160,128},{192,160},{224,1... | collective-permute-start | bytes 245768 | tf_op jit(solution)/shard_map/gather_sequence/ppermute | solution.py:32
  88.1 9.4 %collective-permute-start.11 = (bf16[128,320]{0,1:T(8,128)(2,1)S(1)}, bf16[128,320]{0,1:T(8,128)(2,1)S(1)}, u32[]{:S(2)}, u32[]{:S(2)}) collective-permute-start(bf16[128,320]{0,1:T(8,128)(2,1)S(1)} %collective-permute-done.10), channel_id=1, source_target_pairs={{0,32},{32,64},{64,96},{96,128},{128,160},{160,192},{192,224},{224... | collective-permute-start | bytes 245768 | tf_op jit(solution)/shard_map/gather_sequence/ppermute | solution.py:32
  90.8 9.4 %collective-permute-start.5 = (bf16[128,320]{0,1:T(8,128)(2,1)S(1)}, bf16[128,320]{0,1:T(8,128)(2,1)S(1)}, u32[]{:S(2)}, u32[]{:S(2)}) collective-permute-start(bf16[128,320]{0,1:T(8,128)(2,1)S(1)} %collective-permute-done.4), channel_id=1, source_target_pairs={{0,480},{32,0},{64,32},{96,64},{128,96},{160,128},{192,160},{224,1... | collective-permute-start | bytes 245768 | tf_op jit(solution)/shard_map/gather_sequence/ppermute | solution.py:32
  97.6 9.7 %collective-permute-start.12 = (bf16[128,320]{0,1:T(8,128)(2,1)S(1)}, bf16[128,320]{0,1:T(8,128)(2,1)S(1)}, u32[]{:S(2)}, u32[]{:S(2)}) collective-permute-start(bf16[128,320]{0,1:T(8,128)(2,1)S(1)} %collective-permute-done.11), channel_id=1, source_target_pairs={{0,32},{32,64},{64,96},{96,128},{128,160},{160,192},{192,224},{224... | collective-permute-start | bytes 245768 | tf_op jit(solution)/shard_map/gather_sequence/ppermute | solution.py:32
  100.2 18.5 %collective-permute-start.6 = (bf16[128,320]{0,1:T(8,128)(2,1)S(1)}, bf16[128,320]{0,1:T(8,128)(2,1)S(1)}, u32[]{:S(2)}, u32[]{:S(2)}) collective-permute-start(bf16[128,320]{0,1:T(8,128)(2,1)S(1)} %collective-permute-done.5), channel_id=1, source_target_pairs={{0,480},{32,0},{64,32},{96,64},{128,96},{160,128},{192,160},{224,1... | collective-permute-start | bytes 245768 | tf_op jit(solution)/shard_map/gather_sequence/ppermute | solution.py:32
  107.3 9.4 %collective-permute-start.13 = (bf16[128,320]{0,1:T(8,128)(2,1)S(1)}, bf16[128,320]{0,1:T(8,128)(2,1)S(1)}, u32[]{:S(2)}, u32[]{:S(2)}) collective-permute-start(bf16[128,320]{0,1:T(8,128)(2,1)S(1)} %collective-permute-done.12), channel_id=1, source_target_pairs={{0,32},{32,64},{64,96},{96,128},{128,160},{160,192},{192,224},{224... | collective-permute-start | bytes 245768 | tf_op jit(solution)/shard_map/gather_sequence/ppermute | solution.py:32
  116.8 8.8 %collective-permute-start.14 = (bf16[128,320]{0,1:T(8,128)(2,1)S(1)}, bf16[128,320]{0,1:T(8,128)(2,1)S(1)}, u32[]{:S(2)}, u32[]{:S(2)}) collective-permute-start(bf16[128,320]{0,1:T(8,128)(2,1)S(1)} %collective-permute-done.13), channel_id=1, source_target_pairs={{0,32},{32,64},{64,96},{96,128},{128,160},{160,192},{192,224},{224... | collective-permute-start | bytes 245768 | tf_op jit(solution)/shard_map/gather_sequence/ppermute | solution.py:32
  130.8 24.2 %collective-permute-start.15 = (bf16[2048,320]{0,1:T(8,128)(2,1)}, bf16[2048,320]{0,1:T(8,128)(2,1)}, u32[]{:S(2)}, u32[]{:S(2)}) collective-permute-start(bf16[2048,320]{0,1:T(8,128)(2,1)} %constant_dynamic-update-slice_fusion), channel_id=1, source_target_pairs={{0,8},{8,16},{16,24},{24,0},{1,9},{9,17},{17,25},{25,1},{2,10},{10... | collective-permute-start | bytes 3932168 | tf_op jit(solution)/shard_map/gather_sequence/ppermute | solution.py:32
  135.1 23.6 %collective-permute-start.16 = (bf16[2048,320]{0,1:T(8,128)(2,1)}, bf16[2048,320]{0,1:T(8,128)(2,1)}, u32[]{:S(2)}, u32[]{:S(2)}) collective-permute-start(bf16[2048,320]{0,1:T(8,128)(2,1)} %constant_dynamic-update-slice_fusion), channel_id=1, source_target_pairs={{0,24},{8,0},{16,8},{24,16},{1,25},{9,1},{17,9},{25,17},{2,26},{10... | collective-permute-start | bytes 3932168 | tf_op jit(solution)/shard_map/gather_sequence/ppermute | solution.py:32
  152.2 1.7 copy-start.8
  159.4 23.5 %all-to-all-start = ((f32[64,2,2,128]{3,2,1,0:T(2,128)}), f32[64,2,2,128]{3,2,1,0:T(2,128)}, u32[]{:S(2)}, u32[]{:S(2)}) async-start(f32[64,2,2,128]{3,2,1,0:T(2,128)} %broadcast_in_dim.92), calls=%async_computation | async-start | bytes 262144 | tf_op jit(solution)/shard_map/gather_row_stats/all_to_all | solution.py:160
  168.7 25.0 %collective-permute-start.17 = (bf16[2048,320]{0,1:T(8,128)(2,1)}, bf16[2048,320]{0,1:T(8,128)(2,1)}, u32[]{:S(2)}, u32[]{:S(2)}) collective-permute-start(bf16[2048,320]{0,1:T(8,128)(2,1)} %collective-permute-done.15), channel_id=1, source_target_pairs={{0,8},{8,16},{16,24},{24,0},{1,9},{9,17},{17,25},{25,1},{2,10},{10... | collective-permute-start | bytes 3932168 | tf_op jit(solution)/shard_map/gather_row_stats/ppermute | solution.py:32
  186.0 1.8 copy-start.3
  187.8 1.0 copy-start.11
  188.3 1.2 copy-start.2
  189.5 1.0 copy-start.10
  190.0 1.2 copy-start.4
  193.2 1.9 copy-start.9
  196.9 1.1 copy-start.5
  200.0 12.5 %copy-start.13 = (bf16[128,320]{0,1:T(8,128)(2,1)S(1)}, bf16[128,320]{0,1:T(8,128)(2,1)}, u32[]{:S(2)}) copy-start(bf16[128,320]{0,1:T(8,128)(2,1)} %param.11) | copy-start | bytes 245764
  200.0 12.5 %copy-start.14 = (bf16[128,320]{0,1:T(8,128)(2,1)S(1)}, bf16[128,320]{0,1:T(8,128)(2,1)}, u32[]{:S(2)}) copy-start(bf16[128,320]{0,1:T(8,128)(2,1)} %param.12) | copy-start | bytes 245764
Sparse Core Ops, SparseCore 0:
  37.0 92.7 all-gather.1

commit v16 on v14

--- a/solution.py
+++ b/solution.py
@@ -165,13 +165,14 @@
     with jax.named_scope("key_pass"):
         piece_rows = qg_pieces[0].shape[0]
         stats_ordered = stats_all[qg_source]
+        query_places = block_positions(offsets[qg_source], all_rows)
         key_grad = jnp.zeros((row_count, heads_here, head_width), jnp.float32)
         value_grad = jnp.zeros((row_count, heads_here, head_width), jnp.float32)
         for ry, piece in enumerate(qg_pieces):
             source = qg_source[ry * z_size : (ry + 1) * z_size]
             query_part = piece[:, :cols].reshape(piece_rows, heads_here, head_width)
             grad_part = piece[:, cols:].reshape(piece_rows, heads_here, head_width)
-            place = block_positions(offsets[source], piece_rows)
+            place = query_places[ry * piece_rows : (ry + 1) * piece_rows]
             part_stats = stats_ordered[ry * z_size : (ry + 1) * z_size]
             log_part = jnp.transpose(part_stats[:, 0], (1, 0, 2)).reshape(heads_here, piece_rows)
             delta_part = jnp.transpose(part_stats[:, 1], (1, 0, 2)).reshape(

time: 223 us -> 221 us (level)
  transfers between devices with their start and end apart: 21 -> 21, of which waited for: 13 -> 11; matrix products, arithmetic and copies ran while one was open for 24% -> 23% of each run, Pallas kernels for 0% -> 0%
where the time goes in v16:
time: 221 us; the launch traced here: 218 us
  starting transfers between devices  76.6 us (35%)
  blocking collectives  40.2 us (18%)
  local copies, waits for them, and re-layouts  31.9 us (14%)
  waiting for transfers between devices  25.3 us (11%)
  matrix products  21.5 us (10%)
  between operations  14.8 us (7%)
  other arithmetic  7.99 us (4%)
    ppermute x19, starting transfers between devices, shift(): lax.ppermute(data, axis, [(i, (i + step) % size) for i in range(size)])  67.3 us
    ppermute x19, waiting for transfers between devices, shift(): lax.ppermute(data, axis, [(i, (i + step) % size) for i in range(size)])  24.2 us
    all_gather x1, blocking collectives, per_device(): kv_all = lax.all_gather(kv, 'y', axis=0, tiled=True)  14.6 us
    all_gather x1, blocking collectives, per_device(): gathered = lax.all_gather(both, 'tp', axis=1, tiled=True)  13.4 us
    all_to_all x1, blocking collectives, per_device(): received = lax.all_to_all(payload, 'tp', 0, 0, tiled=False)  12.3 us
    unnamed x50, local copies, waits for them, and re-layouts  11.4 us
    all_to_all x1, starting transfers between devices, per_device(): stats_all = lax.all_to_all(sent, ('z', 'y'), 0, 0, tiled=False)  9.32 us
    slice x3, local copies, waits for them, and re-layouts, per_device(): grad_part = piece[:, cols:].reshape(piece_rows, heads_here, head_width)  5.4 us
  transfers between devices with their start and end apart: 21, of which 11 were waited for; matrix products, arithmetic and copies ran while one was open for 23% of the time, Pallas kernels for 0%

profile of v16, /device:TPU:24, one launch (start us, length us, event | category | flops | bytes accessed | tf_op | source)
XLA Modules:
  0.0 218.3 jit_solution(6411096085846394718)
XLA Ops:
  6.5 1.0 pad_maximum_fusion.1
  7.5 13.4 %all_gather.9 = bf16[128,2560]{0,1:T(8,128)(2,1)S(1)} all-gather(bf16[128,640]{0,1:T(8,128)(2,1)S(1)} %pad_maximum_fusion.1), channel_id=1, replica_groups=mesh['z'=16,'y'=4,'tp'=4,'dp'=2] {'tp'}, dimensions={1}, use_global_device_ids=true | all-gather | bytes 819200 | tf_op jit(solution)/shard_map/gather_features/all_gather | solution.py:77
  22.3 14.6 %all_gather.10 = bf16[512,320]{0,1:T(8,128)(2,1)} all-gather(bf16[128,320]{0,1:T(8,128)(2,1)S(1)} %pad_maximum_fusion.2), channel_id=1, replica_groups=mesh['z'=16,'y'=4,'tp'=4,'dp'=2] {'y'}, dimensions={0}, use_global_device_ids=true | all-gather | bytes 409600 | tf_op jit(solution)/shard_map/gather_sequence/all_gather | solution.py:109
  38.2 8.9 %collective-permute-start = (bf16[128,320]{0,1:T(8,128)(2,1)S(1)}, bf16[128,320]{0,1:T(8,128)(2,1)S(1)}, u32[]{:S(2)}, u32[]{:S(2)}) collective-permute-start(bf16[128,320]{0,1:T(8,128)(2,1)S(1)} %get-tuple-element.59), channel_id=1, source_target_pairs={{0,480},{32,0},{64,32},{96,64},{128,96},{160,128},{192,160},{224,1... | collective-permute-start | bytes 245768 | tf_op jit(solution)/shard_map/gather_sequence/ppermute | solution.py:32
  47.1 1.9 collective-permute-start.7
  52.1 1.6 broadcast_compare_fusion.4
  53.7 5.1 %collective-permute-start.1 = (bf16[128,320]{0,1:T(8,128)(2,1)S(1)}, bf16[128,320]{0,1:T(8,128)(2,1)S(1)}, u32[]{:S(2)}, u32[]{:S(2)}) collective-permute-start(bf16[128,320]{0,1:T(8,128)(2,1)S(1)} %collective-permute-done), channel_id=1, source_target_pairs={{0,480},{32,0},{64,32},{96,64},{128,96},{160,128},{192,160},{224,1... | collective-permute-start | bytes 245768 | tf_op jit(solution)/shard_map/gather_sequence/ppermute | solution.py:32
  58.9 1.9 collective-permute-start.8
  61.7 4.9 %collective-permute-start.2 = (bf16[128,320]{0,1:T(8,128)(2,1)S(1)}, bf16[128,320]{0,1:T(8,128)(2,1)S(1)}, u32[]{:S(2)}, u32[]{:S(2)}) collective-permute-start(bf16[128,320]{0,1:T(8,128)(2,1)S(1)} %collective-permute-done.1), channel_id=1, source_target_pairs={{0,480},{32,0},{64,32},{96,64},{128,96},{160,128},{192,160},{224,1... | collective-permute-start | bytes 245768 | tf_op jit(solution)/shard_map/gather_sequence/ppermute | solution.py:32
  66.6 1.6 collective-permute-done.8
  68.2 1.9 collective-permute-start.9
  70.7 5.1 %collective-permute-start.3 = (bf16[128,320]{0,1:T(8,128)(2,1)S(1)}, bf16[128,320]{0,1:T(8,128)(2,1)S(1)}, u32[]{:S(2)}, u32[]{:S(2)}) collective-permute-start(bf16[128,320]{0,1:T(8,128)(2,1)S(1)} %collective-permute-done.2), channel_id=1, source_target_pairs={{0,480},{32,0},{64,32},{96,64},{128,96},{160,128},{192,160},{224,1... | collective-permute-start | bytes 245768 | tf_op jit(solution)/shard_map/gather_sequence/ppermute | solution.py:32
  75.9 1.3 collective-permute-done.9
  77.2 1.9 collective-permute-start.10
  79.8 5.2 %collective-permute-start.4 = (bf16[128,320]{0,1:T(8,128)(2,1)S(1)}, bf16[128,320]{0,1:T(8,128)(2,1)S(1)}, u32[]{:S(2)}, u32[]{:S(2)}) collective-permute-start(bf16[128,320]{0,1:T(8,128)(2,1)S(1)} %collective-permute-done.3), channel_id=1, source_target_pairs={{0,480},{32,0},{64,32},{96,64},{128,96},{160,128},{192,160},{224,1... | collective-permute-start | bytes 245768 | tf_op jit(solution)/shard_map/gather_sequence/ppermute | solution.py:32
  85.9 1.9 collective-permute-start.11
  88.4 5.5 %collective-permute-start.5 = (bf16[128,320]{0,1:T(8,128)(2,1)S(1)}, bf16[128,320]{0,1:T(8,128)(2,1)S(1)}, u32[]{:S(2)}, u32[]{:S(2)}) collective-permute-start(bf16[128,320]{0,1:T(8,128)(2,1)S(1)} %collective-permute-done.4), channel_id=1, source_target_pairs={{0,480},{32,0},{64,32},{96,64},{128,96},{160,128},{192,160},{224,1... | collective-permute-start | bytes 245768 | tf_op jit(solution)/shard_map/gather_sequence/ppermute | solution.py:32
  94.0 1.0 collective-permute-done.11
  94.9 1.9 collective-permute-start.12
  97.5 5.1 %collective-permute-start.6 = (bf16[128,320]{0,1:T(8,128)(2,1)S(1)}, bf16[128,320]{0,1:T(8,128)(2,1)S(1)}, u32[]{:S(2)}, u32[]{:S(2)}) collective-permute-start(bf16[128,320]{0,1:T(8,128)(2,1)S(1)} %collective-permute-done.5), channel_id=1, source_target_pairs={{0,480},{32,0},{64,32},{96,64},{128,96},{160,128},{192,160},{224,1... | collective-permute-start | bytes 245768 | tf_op jit(solution)/shard_map/gather_sequence/ppermute | solution.py:32
  102.7 1.7 collective-permute-done.12
  104.4 1.9 collective-permute-start.13
  107.0 7.6 %collective-permute-done.13 = bf16[128,320]{0,1:T(8,128)(2,1)S(1)} collective-permute-done((bf16[128,320]{0,1:T(8,128)(2,1)S(1)}, bf16[128,320]{0,1:T(8,128)(2,1)S(1)}, u32[]{:S(2)}, u32[]{:S(2)}) %collective-permute-start.13) | collective-permute-done | bytes 81952 | tf_op jit(solution)/shard_map/gather_sequence/ppermute | solution.py:32
  114.6 1.9 collective-permute-start.14
  117.1 6.3 %collective-permute-done.14 = bf16[128,320]{0,1:T(8,128)(2,1)S(1)} collective-permute-done((bf16[128,320]{0,1:T(8,128)(2,1)S(1)}, bf16[128,320]{0,1:T(8,128)(2,1)S(1)}, u32[]{:S(2)}, u32[]{:S(2)}) %collective-permute-start.14) | collective-permute-done | bytes 81952 | tf_op jit(solution)/shard_map/gather_sequence/ppermute | solution.py:32
  128.7 3.7 %collective-permute-start.15 = (bf16[2048,320]{0,1:T(8,128)(2,1)}, bf16[2048,320]{0,1:T(8,128)(2,1)}, u32[]{:S(2)}, u32[]{:S(2)}) collective-permute-start(bf16[2048,320]{0,1:T(8,128)(2,1)} %constant_dynamic-update-slice_fusion), channel_id=1, source_target_pairs={{0,8},{8,16},{16,24},{24,0},{1,9},{9,17},{17,25},{25,1},{2,10},{10... | collective-permute-start | bytes 3932168 | tf_op jit(solution)/shard_map/gather_sequence/ppermute | solution.py:32
  132.4 2.3 %collective-permute-start.16 = (bf16[2048,320]{0,1:T(8,128)(2,1)}, bf16[2048,320]{0,1:T(8,128)(2,1)}, u32[]{:S(2)}, u32[]{:S(2)}) collective-permute-start(bf16[2048,320]{0,1:T(8,128)(2,1)} %constant_dynamic-update-slice_fusion), channel_id=1, source_target_pairs={{0,24},{8,0},{16,8},{24,16},{1,25},{9,1},{17,9},{25,17},{2,26},{10... | collective-permute-start | bytes 3932168 | tf_op jit(solution)/shard_map/gather_sequence/ppermute | solution.py:32
  134.7 2.2 %fusion.52 = (bf16[2048,160]{0,1:T(8,128)(2,1)}, bf16[2048,160]{0,1:T(8,128)(2,1)S(1)}) fusion(bf16[2048,320]{0,1:T(8,128)(2,1)} %constant_dynamic-update-slice_fusion), kind=kLoop, calls=%fused_computation.129 | loop fusion | bytes 2621440 | tf_op jit(solution)/shard_map/key_pass/slice | solution.py:174
  137.0 3.0 %fusion.51 = (bf16[8192,160]{0,1:T(8,128)(2,1)S(1)}, bf16[8192,160]{0,1:T(8,128)(2,1)S(1)}) fusion(bf16[8192,320]{0,1:T(8,128)(2,1)} %all-gather.2.cloned.1.call-done), kind=kLoop, calls=%fused_computation.128 | loop fusion | bytes 10485760 | tf_op jit(solution)/shard_map/gather_sequence/slice | solution.py:114
  139.9 1.8 select_reduce_fusion.1
  141.7 2.5 %select_reduce_fusion = f32[2,128]{1,0:T(2,128)S(1)} fusion(f32[2,128,8192]{2,1,0:T(8,128)S(1)} %get-tuple-element.70, f32[2,128]{1,0:T(2,128)S(1)} %get-tuple-element.69, pred[128,8192]{1,0:T(8,128)(4,1)S(1)} %broadcast_compare_fusion), kind=kLoop, calls=%fused_computation.4 | loop fusion | flops 8388352 | bytes 9439232 | tf_op jit(solution)/shard_map/query_pass/reduce_sum | solution.py:137
  144.2 3.5 %fusion.57 = (f32[2,128]{1,0:T(2,128)S(1)}, bf16[2,128,8192]{2,1,0:T(8,128)(2,1)S(1)}) fusion(bf16[128,2,80]{0,2,1:T(8,128)(2,1)S(1)} %bitcast.192, bf16[8192,2,80]{0,2,1:T(8,128)(2,1)S(1)} %bitcast.178, f32[2,128,8192]{2,1,0:T(8,128)S(1)} %get-tuple-element.70, f32[2,128]{1,0:T(2,128)S(1)} %log_add_fusion, pred[128,8192]{1,0:T(8,128)(4,1)S(1)} %broadcast_compare_fusion), kind=kOutput, calls=%fused_computation.134 | convolution fusion | flops 346029824 | bytes 16295936 | tf_op jit(solution)/shard_map/query_pass/qhd,khd->hqk/dot_general | solution.py:140
  147.7 2.0 fusion.38
  149.7 1.5 fusion.28
  151.4 1.1 fusion.62
  152.9 3.2 %collective-permute-done.16 = bf16[2048,320]{0,1:T(8,128)(2,1)} collective-permute-done((bf16[2048,320]{0,1:T(8,128)(2,1)}, bf16[2048,320]{0,1:T(8,128)(2,1)}, u32[]{:S(2)}, u32[]{:S(2)}) %collective-permute-start.16) | collective-permute-done | bytes 1310752 | tf_op jit(solution)/shard_map/gather_sequence/ppermute | solution.py:32
  156.8 9.3 %all-to-all-start = ((f32[64,2,2,128]{3,2,1,0:T(2,128)}), f32[64,2,2,128]{3,2,1,0:T(2,128)}, u32[]{:S(2)}, u32[]{:S(2)}) async-start(f32[64,2,2,128]{3,2,1,0:T(2,128)} %broadcast_in_dim.87), calls=%async_computation | async-start | bytes 262144 | tf_op jit(solution)/shard_map/gather_row_stats/all_to_all | solution.py:163
  166.1 2.0 slice.137
  168.1 2.4 %collective-permute-start.17 = (bf16[1024,320]{0,1:T(8,128)(2,1)}, bf16[1024,320]{0,1:T(8,128)(2,1)}, u32[]{:S(2)}, u32[]{:S(2)}) collective-permute-start(bf16[1024,320]{0,1:T(8,128)(2,1)} %slice.137), channel_id=1, source_target_pairs={{0,8},{8,16},{16,24},{24,0},{1,9},{9,17},{17,25},{25,1},{2,10},{10... | collective-permute-start | bytes 1966088 | tf_op jit(solution)/shard_map/gather_row_stats/ppermute | solution.py:32
  170.6 2.0 slice.138
  172.6 3.6 %collective-permute-start.18 = (bf16[1024,320]{0,1:T(8,128)(2,1)}, bf16[1024,320]{0,1:T(8,128)(2,1)}, u32[]{:S(2)}, u32[]{:S(2)}) collective-permute-start(bf16[1024,320]{0,1:T(8,128)(2,1)} %slice.138), channel_id=1, source_target_pairs={{0,24},{8,0},{16,8},{24,16},{1,25},{9,1},{17,9},{25,17},{2,26},{10... | collective-permute-start | bytes 1966088 | tf_op jit(solution)/shard_map/gather_row_stats/ppermute | solution.py:32
  176.2 3.0 %fusion.53 = (bf16[2048,160]{0,1:T(8,128)(2,1)}, bf16[2048,160]{0,1:T(8,128)(2,1)S(1)}, bf16[2048,160]{0,1:T(8,128)(2,1)S(1)}, bf16[2048,160]{0,1:T(8,128)(2,1)}) fusion(bf16[2048,320]{0,1:T(8,128)(2,1)} %collective-permute-done.16, bf16[2048,320]{0,1:T(8,128)(2,1)} %collective-permute-done.15), kind=kLoop, calls=%fused_computation.130 | loop fusion | bytes 5242880 | tf_op jit(solution)/shard_map/key_pass/slice | solution.py:174
  179.2 1.1 all-to-all-done
  180.3 2.3 %gather_fusion.1 = f32[64,2,2,128]{3,2,1,0:T(2,128)} fusion(f32[64,2,2,128]{3,2,1,0:T(2,128)} %all-to-all-done, s32[1024]{0:T(1024)S(1)} %pad_clamp_fusion), kind=kCustom, calls=%fused_computation.1 | custom fusion | bytes 262400 | tf_op jit(solution)/shard_map/key_pass/gather | solution.py:167
  183.4 1.8 fusion.58
  190.9 1.1 constant_dynamic-update-slice_fusion.17
  192.0 1.2 constant_dynamic-update-slice_fusion.16
  198.3 12.3 %all_to_all.10 = f32[4,129,320]{2,1,0:T(8,128)S(1)} all-to-all(f32[4,129,320]{2,1,0:T(8,128)S(1)} %copy.31), channel_id=1, replica_groups=mesh['z'=16,'y'=4,'tp'=4,'dp'=2] {'tp'}, dimensions={0} | all-to-all | bytes 1320960 | tf_op jit(solution)/shard_map/back_projection/all_to_all | solution.py:218
  (126 shorter events, 29.4 us)
Async XLA Ops:
  6.5 15.1 %copy-start = (bf16[160,1280]{1,0:T(8,128)(2,1)S(1)}, bf16[160,1280]{1,0:T(8,128)(2,1)}, u32[]{:S(2)}) copy-start(bf16[160,1280]{1,0:T(8,128)(2,1)} %param.16) | copy-start | bytes 1228804
  6.5 130.4 %all-gather.2.cloned.1.call-start = ((), (), s32[]{:S(2)}) async-start(), calls=%async_computation.2 | async-start | bytes 5570560 | tf_op jit(solution)/shard_map/gather_sequence/all_gather | solution.py:110
  7.5 13.9 %copy-start.15 = (f32[1280]{0:T(1024)S(1)}, f32[1280]{0:T(1024)}, u32[]{:S(2)}) copy-start(f32[1280]{0:T(1024)} %param.13) | copy-start | bytes 15364
  21.0 1.0 copy-start.6
  21.2 15.7 %copy-start.16 = (f32[80]{0:T(128)S(1)}, f32[80]{0:T(128)}, u32[]{:S(2)}) copy-start(f32[80]{0:T(128)} %param.18) | copy-start | bytes 964
  21.2 15.8 %copy-start.12 = (bf16[160,1280]{1,0:T(8,128)(2,1)S(1)}, bf16[160,1280]{1,0:T(8,128)(2,1)}, u32[]{:S(2)}) copy-start(bf16[160,1280]{1,0:T(8,128)(2,1)} %param.17) | copy-start | bytes 1228804
  21.5 15.8 %copy-start.7 = (bf16[160,1280]{1,0:T(8,128)(2,1)S(1)}, bf16[160,1280]{1,0:T(8,128)(2,1)}, u32[]{:S(2)}) copy-start(bf16[160,1280]{1,0:T(8,128)(2,1)} %param.14) | copy-start | bytes 1228804
  21.6 27.6 %copy-start.1 = (s32[64]{0:T(128)S(1)}, s32[64]{0:T(128)}, u32[]{:S(2)}) copy-start(s32[64]{0:T(128)} %param.19) | copy-start | bytes 772
  38.2 15.5 %collective-permute-start = (bf16[128,320]{0,1:T(8,128)(2,1)S(1)}, bf16[128,320]{0,1:T(8,128)(2,1)S(1)}, u32[]{:S(2)}, u32[]{:S(2)}) collective-permute-start(bf16[128,320]{0,1:T(8,128)(2,1)S(1)} %get-tuple-element.59), channel_id=1, source_target_pairs={{0,480},{32,0},{64,32},{96,64},{128,96},{160,128},{192,160},{224,1... | collective-permute-start | bytes 245768 | tf_op jit(solution)/shard_map/gather_sequence/ppermute | solution.py:32
  47.1 11.7 %collective-permute-start.7 = (bf16[128,320]{0,1:T(8,128)(2,1)S(1)}, bf16[128,320]{0,1:T(8,128)(2,1)S(1)}, u32[]{:S(2)}, u32[]{:S(2)}) collective-permute-start(bf16[128,320]{0,1:T(8,128)(2,1)S(1)} %get-tuple-element.59), channel_id=1, source_target_pairs={{0,32},{32,64},{64,96},{96,128},{128,160},{160,192},{192,224},{224... | collective-permute-start | bytes 245768 | tf_op jit(solution)/shard_map/gather_sequence/ppermute | solution.py:32
  53.7 7.9 %collective-permute-start.1 = (bf16[128,320]{0,1:T(8,128)(2,1)S(1)}, bf16[128,320]{0,1:T(8,128)(2,1)S(1)}, u32[]{:S(2)}, u32[]{:S(2)}) collective-permute-start(bf16[128,320]{0,1:T(8,128)(2,1)S(1)} %collective-permute-done), channel_id=1, source_target_pairs={{0,480},{32,0},{64,32},{96,64},{128,96},{160,128},{192,160},{224,1... | collective-permute-start | bytes 245768 | tf_op jit(solution)/shard_map/gather_sequence/ppermute | solution.py:32
  58.9 9.3 %collective-permute-start.8 = (bf16[128,320]{0,1:T(8,128)(2,1)S(1)}, bf16[128,320]{0,1:T(8,128)(2,1)S(1)}, u32[]{:S(2)}, u32[]{:S(2)}) collective-permute-start(bf16[128,320]{0,1:T(8,128)(2,1)S(1)} %collective-permute-done.7), channel_id=1, source_target_pairs={{0,32},{32,64},{64,96},{96,128},{128,160},{160,192},{192,224},{224... | collective-permute-start | bytes 245768 | tf_op jit(solution)/shard_map/gather_sequence/ppermute | solution.py:32
  61.7 9.1 %collective-permute-start.2 = (bf16[128,320]{0,1:T(8,128)(2,1)S(1)}, bf16[128,320]{0,1:T(8,128)(2,1)S(1)}, u32[]{:S(2)}, u32[]{:S(2)}) collective-permute-start(bf16[128,320]{0,1:T(8,128)(2,1)S(1)} %collective-permute-done.1), channel_id=1, source_target_pairs={{0,480},{32,0},{64,32},{96,64},{128,96},{160,128},{192,160},{224,1... | collective-permute-start | bytes 245768 | tf_op jit(solution)/shard_map/gather_sequence/ppermute | solution.py:32
  68.2 9.0 %collective-permute-start.9 = (bf16[128,320]{0,1:T(8,128)(2,1)S(1)}, bf16[128,320]{0,1:T(8,128)(2,1)S(1)}, u32[]{:S(2)}, u32[]{:S(2)}) collective-permute-start(bf16[128,320]{0,1:T(8,128)(2,1)S(1)} %collective-permute-done.8), channel_id=1, source_target_pairs={{0,32},{32,64},{64,96},{96,128},{128,160},{160,192},{192,224},{224... | collective-permute-start | bytes 245768 | tf_op jit(solution)/shard_map/gather_sequence/ppermute | solution.py:32
  70.7 9.0 %collective-permute-start.3 = (bf16[128,320]{0,1:T(8,128)(2,1)S(1)}, bf16[128,320]{0,1:T(8,128)(2,1)S(1)}, u32[]{:S(2)}, u32[]{:S(2)}) collective-permute-start(bf16[128,320]{0,1:T(8,128)(2,1)S(1)} %collective-permute-done.2), channel_id=1, source_target_pairs={{0,480},{32,0},{64,32},{96,64},{128,96},{160,128},{192,160},{224,1... | collective-permute-start | bytes 245768 | tf_op jit(solution)/shard_map/gather_sequence/ppermute | solution.py:32
  77.2 8.7 %collective-permute-start.10 = (bf16[128,320]{0,1:T(8,128)(2,1)S(1)}, bf16[128,320]{0,1:T(8,128)(2,1)S(1)}, u32[]{:S(2)}, u32[]{:S(2)}) collective-permute-start(bf16[128,320]{0,1:T(8,128)(2,1)S(1)} %collective-permute-done.9), channel_id=1, source_target_pairs={{0,32},{32,64},{64,96},{96,128},{128,160},{160,192},{192,224},{224... | collective-permute-start | bytes 245768 | tf_op jit(solution)/shard_map/gather_sequence/ppermute | solution.py:32
  79.8 8.7 %collective-permute-start.4 = (bf16[128,320]{0,1:T(8,128)(2,1)S(1)}, bf16[128,320]{0,1:T(8,128)(2,1)S(1)}, u32[]{:S(2)}, u32[]{:S(2)}) collective-permute-start(bf16[128,320]{0,1:T(8,128)(2,1)S(1)} %collective-permute-done.3), channel_id=1, source_target_pairs={{0,480},{32,0},{64,32},{96,64},{128,96},{160,128},{192,160},{224,1... | collective-permute-start | bytes 245768 | tf_op jit(solution)/shard_map/gather_sequence/ppermute | solution.py:32
  85.9 9.1 %collective-permute-start.11 = (bf16[128,320]{0,1:T(8,128)(2,1)S(1)}, bf16[128,320]{0,1:T(8,128)(2,1)S(1)}, u32[]{:S(2)}, u32[]{:S(2)}) collective-permute-start(bf16[128,320]{0,1:T(8,128)(2,1)S(1)} %collective-permute-done.10), channel_id=1, source_target_pairs={{0,32},{32,64},{64,96},{96,128},{128,160},{160,192},{192,224},{224... | collective-permute-start | bytes 245768 | tf_op jit(solution)/shard_map/gather_sequence/ppermute | solution.py:32
  88.4 9.1 %collective-permute-start.5 = (bf16[128,320]{0,1:T(8,128)(2,1)S(1)}, bf16[128,320]{0,1:T(8,128)(2,1)S(1)}, u32[]{:S(2)}, u32[]{:S(2)}) collective-permute-start(bf16[128,320]{0,1:T(8,128)(2,1)S(1)} %collective-permute-done.4), channel_id=1, source_target_pairs={{0,480},{32,0},{64,32},{96,64},{128,96},{160,128},{192,160},{224,1... | collective-permute-start | bytes 245768 | tf_op jit(solution)/shard_map/gather_sequence/ppermute | solution.py:32
  94.9 9.5 %collective-permute-start.12 = (bf16[128,320]{0,1:T(8,128)(2,1)S(1)}, bf16[128,320]{0,1:T(8,128)(2,1)S(1)}, u32[]{:S(2)}, u32[]{:S(2)}) collective-permute-start(bf16[128,320]{0,1:T(8,128)(2,1)S(1)} %collective-permute-done.11), channel_id=1, source_target_pairs={{0,32},{32,64},{64,96},{96,128},{128,160},{160,192},{192,224},{224... | collective-permute-start | bytes 245768 | tf_op jit(solution)/shard_map/gather_sequence/ppermute | solution.py:32
  97.5 18.9 %collective-permute-start.6 = (bf16[128,320]{0,1:T(8,128)(2,1)S(1)}, bf16[128,320]{0,1:T(8,128)(2,1)S(1)}, u32[]{:S(2)}, u32[]{:S(2)}) collective-permute-start(bf16[128,320]{0,1:T(8,128)(2,1)S(1)} %collective-permute-done.5), channel_id=1, source_target_pairs={{0,480},{32,0},{64,32},{96,64},{128,96},{160,128},{192,160},{224,1... | collective-permute-start | bytes 245768 | tf_op jit(solution)/shard_map/gather_sequence/ppermute | solution.py:32
  104.4 10.2 %collective-permute-start.13 = (bf16[128,320]{0,1:T(8,128)(2,1)S(1)}, bf16[128,320]{0,1:T(8,128)(2,1)S(1)}, u32[]{:S(2)}, u32[]{:S(2)}) collective-permute-start(bf16[128,320]{0,1:T(8,128)(2,1)S(1)} %collective-permute-done.12), channel_id=1, source_target_pairs={{0,32},{32,64},{64,96},{96,128},{128,160},{160,192},{192,224},{224... | collective-permute-start | bytes 245768 | tf_op jit(solution)/shard_map/gather_sequence/ppermute | solution.py:32
  114.6 8.9 %collective-permute-start.14 = (bf16[128,320]{0,1:T(8,128)(2,1)S(1)}, bf16[128,320]{0,1:T(8,128)(2,1)S(1)}, u32[]{:S(2)}, u32[]{:S(2)}) collective-permute-start(bf16[128,320]{0,1:T(8,128)(2,1)S(1)} %collective-permute-done.13), channel_id=1, source_target_pairs={{0,32},{32,64},{64,96},{96,128},{128,160},{160,192},{192,224},{224... | collective-permute-start | bytes 245768 | tf_op jit(solution)/shard_map/gather_sequence/ppermute | solution.py:32
  128.7 24.3 %collective-permute-start.15 = (bf16[2048,320]{0,1:T(8,128)(2,1)}, bf16[2048,320]{0,1:T(8,128)(2,1)}, u32[]{:S(2)}, u32[]{:S(2)}) collective-permute-start(bf16[2048,320]{0,1:T(8,128)(2,1)} %constant_dynamic-update-slice_fusion), channel_id=1, source_target_pairs={{0,8},{8,16},{16,24},{24,0},{1,9},{9,17},{17,25},{25,1},{2,10},{10... | collective-permute-start | bytes 3932168 | tf_op jit(solution)/shard_map/gather_sequence/ppermute | solution.py:32
  132.4 23.7 %collective-permute-start.16 = (bf16[2048,320]{0,1:T(8,128)(2,1)}, bf16[2048,320]{0,1:T(8,128)(2,1)}, u32[]{:S(2)}, u32[]{:S(2)}) collective-permute-start(bf16[2048,320]{0,1:T(8,128)(2,1)} %constant_dynamic-update-slice_fusion), channel_id=1, source_target_pairs={{0,24},{8,0},{16,8},{24,16},{1,25},{9,1},{17,9},{25,17},{2,26},{10... | collective-permute-start | bytes 3932168 | tf_op jit(solution)/shard_map/gather_sequence/ppermute | solution.py:32
  149.7 1.7 copy-start.8
  156.8 23.5 %all-to-all-start = ((f32[64,2,2,128]{3,2,1,0:T(2,128)}), f32[64,2,2,128]{3,2,1,0:T(2,128)}, u32[]{:S(2)}, u32[]{:S(2)}) async-start(f32[64,2,2,128]{3,2,1,0:T(2,128)} %broadcast_in_dim.87), calls=%async_computation | async-start | bytes 262144 | tf_op jit(solution)/shard_map/gather_row_stats/all_to_all | solution.py:163
  168.1 22.7 %collective-permute-start.17 = (bf16[1024,320]{0,1:T(8,128)(2,1)}, bf16[1024,320]{0,1:T(8,128)(2,1)}, u32[]{:S(2)}, u32[]{:S(2)}) collective-permute-start(bf16[1024,320]{0,1:T(8,128)(2,1)} %slice.137), channel_id=1, source_target_pairs={{0,8},{8,16},{16,24},{24,0},{1,9},{9,17},{17,25},{25,1},{2,10},{10... | collective-permute-start | bytes 1966088 | tf_op jit(solution)/shard_map/gather_row_stats/ppermute | solution.py:32
  172.6 19.5 %collective-permute-start.18 = (bf16[1024,320]{0,1:T(8,128)(2,1)}, bf16[1024,320]{0,1:T(8,128)(2,1)}, u32[]{:S(2)}, u32[]{:S(2)}) collective-permute-start(bf16[1024,320]{0,1:T(8,128)(2,1)} %slice.138), channel_id=1, source_target_pairs={{0,24},{8,0},{16,8},{24,16},{1,25},{9,1},{17,9},{25,17},{2,26},{10... | collective-permute-start | bytes 1966088 | tf_op jit(solution)/shard_map/gather_row_stats/ppermute | solution.py:32
  183.4 1.8 copy-start.3
  185.2 1.0 copy-start.11
  186.2 1.1 copy-start.2
  186.9 1.0 copy-start.10
  187.8 1.1 copy-start.4
  192.0 1.3 copy-start.9
  195.1 1.1 copy-start.5
  198.2 12.5 %copy-start.13 = (bf16[128,320]{0,1:T(8,128)(2,1)S(1)}, bf16[128,320]{0,1:T(8,128)(2,1)}, u32[]{:S(2)}) copy-start(bf16[128,320]{0,1:T(8,128)(2,1)} %param.11) | copy-start | bytes 245764
  198.2 12.5 %copy-start.14 = (bf16[128,320]{0,1:T(8,128)(2,1)S(1)}, bf16[128,320]{0,1:T(8,128)(2,1)}, u32[]{:S(2)}) copy-start(bf16[128,320]{0,1:T(8,128)(2,1)} %param.12) | copy-start | bytes 245764
Sparse Core Ops, SparseCore 0:
  37.0 92.5 all-gather.1

commit v17 on v16

--- a/solution.py
+++ b/solution.py
@@ -166,6 +166,7 @@
         piece_rows = qg_pieces[0].shape[0]
         stats_ordered = stats_all[qg_source]
         query_places = block_positions(offsets[qg_source], all_rows)
+        stats_rows = jnp.transpose(stats_ordered, (1, 2, 0, 3)).reshape(2, heads_here, all_rows)
         key_grad = jnp.zeros((row_count, heads_here, head_width), jnp.float32)
         value_grad = jnp.zeros((row_count, heads_here, head_width), jnp.float32)
         for ry, piece in enumerate(qg_pieces):
@@ -173,11 +174,9 @@
             query_part = piece[:, :cols].reshape(piece_rows, heads_here, head_width)
             grad_part = piece[:, cols:].reshape(piece_rows, heads_here, head_width)
             place = query_places[ry * piece_rows : (ry + 1) * piece_rows]
-            part_stats = stats_ordered[ry * z_size : (ry + 1) * z_size]
-            log_part = jnp.transpose(part_stats[:, 0], (1, 0, 2)).reshape(heads_here, piece_rows)
-            delta_part = jnp.transpose(part_stats[:, 1], (1, 0, 2)).reshape(
-                heads_here, piece_rows
-            )
+            rows_here = slice(ry * piece_rows, (ry + 1) * piece_rows)
+            log_part = stats_rows[0, :, rows_here]
+            delta_part = stats_rows[1, :, rows_here]
             scores_t = jnp.einsum(
                 "khd,qhd->hkq", key_heads, query_part, preferred_element_type=jnp.float32
             )

time: 221 us -> 221 us (level)
  no operation moved by 1% of the time
where the time goes in v17:
time: 221 us; the launch traced here: 218 us
  starting transfers between devices  76.6 us (35%)
  blocking collectives  40.2 us (18%)
  local copies, waits for them, and re-layouts  32 us (14%)
  waiting for transfers between devices  25.3 us (11%)
  matrix products  21.5 us (10%)
  between operations  14.8 us (7%)
  other arithmetic  7.99 us (4%)
    ppermute x19, starting transfers between devices, shift(): lax.ppermute(data, axis, [(i, (i + step) % size) for i in range(size)])  67.3 us
    ppermute x19, waiting for transfers between devices, shift(): lax.ppermute(data, axis, [(i, (i + step) % size) for i in range(size)])  24.2 us
    all_gather x1, blocking collectives, per_device(): kv_all = lax.all_gather(kv, 'y', axis=0, tiled=True)  14.6 us
    all_gather x1, blocking collectives, per_device(): gathered = lax.all_gather(both, 'tp', axis=1, tiled=True)  13.4 us
    all_to_all x1, blocking collectives, per_device(): received = lax.all_to_all(payload, 'tp', 0, 0, tiled=False)  12.3 us
    unnamed x50, local copies, waits for them, and re-layouts  11.4 us
    all_to_all x1, starting transfers between devices, per_device(): stats_all = lax.all_to_all(sent, ('z', 'y'), 0, 0, tiled=False)  9.32 us
    slice x3, local copies, waits for them, and re-layouts, per_device(): grad_part = piece[:, cols:].reshape(piece_rows, heads_here, head_width)  5.4 us
  transfers between devices with their start and end apart: 21, of which 11 were waited for; matrix products, arithmetic and copies ran while one was open for 23% of the time, Pallas kernels for 0%

profile of v17, /device:TPU:24, one launch (start us, length us, event | category | flops | bytes accessed | tf_op | source)
XLA Modules:
  0.0 218.4 jit_solution(18358014511435738756)
XLA Ops:
  6.5 1.0 pad_maximum_fusion.1
  7.5 13.4 %all_gather.9 = bf16[128,2560]{0,1:T(8,128)(2,1)S(1)} all-gather(bf16[128,640]{0,1:T(8,128)(2,1)S(1)} %pad_maximum_fusion.1), channel_id=1, replica_groups=mesh['z'=16,'y'=4,'tp'=4,'dp'=2] {'tp'}, dimensions={1}, use_global_device_ids=true | all-gather | bytes 819200 | tf_op jit(solution)/shard_map/gather_features/all_gather | solution.py:77
  22.3 14.6 %all_gather.10 = bf16[512,320]{0,1:T(8,128)(2,1)} all-gather(bf16[128,320]{0,1:T(8,128)(2,1)S(1)} %pad_maximum_fusion.2), channel_id=1, replica_groups=mesh['z'=16,'y'=4,'tp'=4,'dp'=2] {'y'}, dimensions={0}, use_global_device_ids=true | all-gather | bytes 409600 | tf_op jit(solution)/shard_map/gather_sequence/all_gather | solution.py:109
  38.2 8.9 %collective-permute-start = (bf16[128,320]{0,1:T(8,128)(2,1)S(1)}, bf16[128,320]{0,1:T(8,128)(2,1)S(1)}, u32[]{:S(2)}, u32[]{:S(2)}) collective-permute-start(bf16[128,320]{0,1:T(8,128)(2,1)S(1)} %get-tuple-element.59), channel_id=1, source_target_pairs={{0,480},{32,0},{64,32},{96,64},{128,96},{160,128},{192,160},{224,1... | collective-permute-start | bytes 245768 | tf_op jit(solution)/shard_map/gather_sequence/ppermute | solution.py:32
  47.1 1.9 collective-permute-start.7
  52.1 1.6 broadcast_compare_fusion.4
  53.7 5.1 %collective-permute-start.1 = (bf16[128,320]{0,1:T(8,128)(2,1)S(1)}, bf16[128,320]{0,1:T(8,128)(2,1)S(1)}, u32[]{:S(2)}, u32[]{:S(2)}) collective-permute-start(bf16[128,320]{0,1:T(8,128)(2,1)S(1)} %collective-permute-done), channel_id=1, source_target_pairs={{0,480},{32,0},{64,32},{96,64},{128,96},{160,128},{192,160},{224,1... | collective-permute-start | bytes 245768 | tf_op jit(solution)/shard_map/gather_sequence/ppermute | solution.py:32
  58.9 1.9 collective-permute-start.8
  61.7 4.9 %collective-permute-start.2 = (bf16[128,320]{0,1:T(8,128)(2,1)S(1)}, bf16[128,320]{0,1:T(8,128)(2,1)S(1)}, u32[]{:S(2)}, u32[]{:S(2)}) collective-permute-start(bf16[128,320]{0,1:T(8,128)(2,1)S(1)} %collective-permute-done.1), channel_id=1, source_target_pairs={{0,480},{32,0},{64,32},{96,64},{128,96},{160,128},{192,160},{224,1... | collective-permute-start | bytes 245768 | tf_op jit(solution)/shard_map/gather_sequence/ppermute | solution.py:32
  66.6 1.6 collective-permute-done.8
  68.2 1.9 collective-permute-start.9
  70.7 5.1 %collective-permute-start.3 = (bf16[128,320]{0,1:T(8,128)(2,1)S(1)}, bf16[128,320]{0,1:T(8,128)(2,1)S(1)}, u32[]{:S(2)}, u32[]{:S(2)}) collective-permute-start(bf16[128,320]{0,1:T(8,128)(2,1)S(1)} %collective-permute-done.2), channel_id=1, source_target_pairs={{0,480},{32,0},{64,32},{96,64},{128,96},{160,128},{192,160},{224,1... | collective-permute-start | bytes 245768 | tf_op jit(solution)/shard_map/gather_sequence/ppermute | solution.py:32
  75.9 1.3 collective-permute-done.9
  77.2 1.9 collective-permute-start.10
  79.8 5.2 %collective-permute-start.4 = (bf16[128,320]{0,1:T(8,128)(2,1)S(1)}, bf16[128,320]{0,1:T(8,128)(2,1)S(1)}, u32[]{:S(2)}, u32[]{:S(2)}) collective-permute-start(bf16[128,320]{0,1:T(8,128)(2,1)S(1)} %collective-permute-done.3), channel_id=1, source_target_pairs={{0,480},{32,0},{64,32},{96,64},{128,96},{160,128},{192,160},{224,1... | collective-permute-start | bytes 245768 | tf_op jit(solution)/shard_map/gather_sequence/ppermute | solution.py:32
  85.9 1.9 collective-permute-start.11
  88.4 5.5 %collective-permute-start.5 = (bf16[128,320]{0,1:T(8,128)(2,1)S(1)}, bf16[128,320]{0,1:T(8,128)(2,1)S(1)}, u32[]{:S(2)}, u32[]{:S(2)}) collective-permute-start(bf16[128,320]{0,1:T(8,128)(2,1)S(1)} %collective-permute-done.4), channel_id=1, source_target_pairs={{0,480},{32,0},{64,32},{96,64},{128,96},{160,128},{192,160},{224,1... | collective-permute-start | bytes 245768 | tf_op jit(solution)/shard_map/gather_sequence/ppermute | solution.py:32
  94.0 1.0 collective-permute-done.11
  94.9 1.9 collective-permute-start.12
  97.5 5.1 %collective-permute-start.6 = (bf16[128,320]{0,1:T(8,128)(2,1)S(1)}, bf16[128,320]{0,1:T(8,128)(2,1)S(1)}, u32[]{:S(2)}, u32[]{:S(2)}) collective-permute-start(bf16[128,320]{0,1:T(8,128)(2,1)S(1)} %collective-permute-done.5), channel_id=1, source_target_pairs={{0,480},{32,0},{64,32},{96,64},{128,96},{160,128},{192,160},{224,1... | collective-permute-start | bytes 245768 | tf_op jit(solution)/shard_map/gather_sequence/ppermute | solution.py:32
  102.7 1.7 collective-permute-done.12
  104.4 1.9 collective-permute-start.13
  107.0 7.6 %collective-permute-done.13 = bf16[128,320]{0,1:T(8,128)(2,1)S(1)} collective-permute-done((bf16[128,320]{0,1:T(8,128)(2,1)S(1)}, bf16[128,320]{0,1:T(8,128)(2,1)S(1)}, u32[]{:S(2)}, u32[]{:S(2)}) %collective-permute-start.13) | collective-permute-done | bytes 81952 | tf_op jit(solution)/shard_map/gather_sequence/ppermute | solution.py:32
  114.6 1.9 collective-permute-start.14
  117.1 6.3 %collective-permute-done.14 = bf16[128,320]{0,1:T(8,128)(2,1)S(1)} collective-permute-done((bf16[128,320]{0,1:T(8,128)(2,1)S(1)}, bf16[128,320]{0,1:T(8,128)(2,1)S(1)}, u32[]{:S(2)}, u32[]{:S(2)}) %collective-permute-start.14) | collective-permute-done | bytes 81952 | tf_op jit(solution)/shard_map/gather_sequence/ppermute | solution.py:32
  128.7 3.7 %collective-permute-start.15 = (bf16[2048,320]{0,1:T(8,128)(2,1)}, bf16[2048,320]{0,1:T(8,128)(2,1)}, u32[]{:S(2)}, u32[]{:S(2)}) collective-permute-start(bf16[2048,320]{0,1:T(8,128)(2,1)} %constant_dynamic-update-slice_fusion), channel_id=1, source_target_pairs={{0,8},{8,16},{16,24},{24,0},{1,9},{9,17},{17,25},{25,1},{2,10},{10... | collective-permute-start | bytes 3932168 | tf_op jit(solution)/shard_map/gather_sequence/ppermute | solution.py:32
  132.4 2.3 %collective-permute-start.16 = (bf16[2048,320]{0,1:T(8,128)(2,1)}, bf16[2048,320]{0,1:T(8,128)(2,1)}, u32[]{:S(2)}, u32[]{:S(2)}) collective-permute-start(bf16[2048,320]{0,1:T(8,128)(2,1)} %constant_dynamic-update-slice_fusion), channel_id=1, source_target_pairs={{0,24},{8,0},{16,8},{24,16},{1,25},{9,1},{17,9},{25,17},{2,26},{10... | collective-permute-start | bytes 3932168 | tf_op jit(solution)/shard_map/gather_sequence/ppermute | solution.py:32
  134.7 2.2 %fusion.52 = (bf16[2048,160]{0,1:T(8,128)(2,1)}, bf16[2048,160]{0,1:T(8,128)(2,1)S(1)}) fusion(bf16[2048,320]{0,1:T(8,128)(2,1)} %constant_dynamic-update-slice_fusion), kind=kLoop, calls=%fused_computation.130 | loop fusion | bytes 2621440 | tf_op jit(solution)/shard_map/key_pass/slice | solution.py:175
  137.0 3.0 %fusion.51 = (bf16[8192,160]{0,1:T(8,128)(2,1)S(1)}, bf16[8192,160]{0,1:T(8,128)(2,1)S(1)}) fusion(bf16[8192,320]{0,1:T(8,128)(2,1)} %all-gather.2.cloned.1.call-done), kind=kLoop, calls=%fused_computation.129 | loop fusion | bytes 10485760 | tf_op jit(solution)/shard_map/gather_sequence/slice | solution.py:114
  139.9 1.8 select_reduce_fusion.1
  141.7 2.5 %select_reduce_fusion = f32[2,128]{1,0:T(2,128)S(1)} fusion(f32[2,128,8192]{2,1,0:T(8,128)S(1)} %get-tuple-element.70, f32[2,128]{1,0:T(2,128)S(1)} %get-tuple-element.69, pred[128,8192]{1,0:T(8,128)(4,1)S(1)} %broadcast_compare_fusion), kind=kLoop, calls=%fused_computation.4 | loop fusion | flops 8388352 | bytes 9439232 | tf_op jit(solution)/shard_map/query_pass/reduce_sum | solution.py:137
  144.2 3.5 %fusion.57 = (f32[2,128]{1,0:T(2,128)S(1)}, bf16[2,128,8192]{2,1,0:T(8,128)(2,1)S(1)}) fusion(bf16[128,2,80]{0,2,1:T(8,128)(2,1)S(1)} %bitcast.166, bf16[8192,2,80]{0,2,1:T(8,128)(2,1)S(1)} %bitcast.152, f32[2,128,8192]{2,1,0:T(8,128)S(1)} %get-tuple-element.70, f32[2,128]{1,0:T(2,128)S(1)} %log_add_fusion, pred[128,8192]{1,0:T(8,128)(4,1)S(1)} %broadcast_compare_fusion), kind=kOutput, calls=%fused_computation.135 | convolution fusion | flops 346029824 | bytes 16295936 | tf_op jit(solution)/shard_map/query_pass/qhd,khd->hqk/dot_general | solution.py:140
  147.7 2.0 fusion.38
  149.7 1.5 fusion.28
  151.4 1.1 fusion.62
  152.9 3.2 %collective-permute-done.16 = bf16[2048,320]{0,1:T(8,128)(2,1)} collective-permute-done((bf16[2048,320]{0,1:T(8,128)(2,1)}, bf16[2048,320]{0,1:T(8,128)(2,1)}, u32[]{:S(2)}, u32[]{:S(2)}) %collective-permute-start.16) | collective-permute-done | bytes 1310752 | tf_op jit(solution)/shard_map/gather_sequence/ppermute | solution.py:32
  156.8 9.3 %all-to-all-start = ((f32[64,2,2,128]{3,2,1,0:T(2,128)}), f32[64,2,2,128]{3,2,1,0:T(2,128)}, u32[]{:S(2)}, u32[]{:S(2)}) async-start(f32[64,2,2,128]{3,2,1,0:T(2,128)} %broadcast_in_dim.87), calls=%async_computation | async-start | bytes 262144 | tf_op jit(solution)/shard_map/gather_row_stats/all_to_all | solution.py:163
  166.1 2.0 slice.125
  168.1 2.4 %collective-permute-start.17 = (bf16[1024,320]{0,1:T(8,128)(2,1)}, bf16[1024,320]{0,1:T(8,128)(2,1)}, u32[]{:S(2)}, u32[]{:S(2)}) collective-permute-start(bf16[1024,320]{0,1:T(8,128)(2,1)} %slice.125), channel_id=1, source_target_pairs={{0,8},{8,16},{16,24},{24,0},{1,9},{9,17},{17,25},{25,1},{2,10},{10... | collective-permute-start | bytes 1966088 | tf_op jit(solution)/shard_map/gather_row_stats/ppermute | solution.py:32
  170.6 2.0 slice.126
  172.6 3.6 %collective-permute-start.18 = (bf16[1024,320]{0,1:T(8,128)(2,1)}, bf16[1024,320]{0,1:T(8,128)(2,1)}, u32[]{:S(2)}, u32[]{:S(2)}) collective-permute-start(bf16[1024,320]{0,1:T(8,128)(2,1)} %slice.126), channel_id=1, source_target_pairs={{0,24},{8,0},{16,8},{24,16},{1,25},{9,1},{17,9},{25,17},{2,26},{10... | collective-permute-start | bytes 1966088 | tf_op jit(solution)/shard_map/gather_row_stats/ppermute | solution.py:32
  176.2 3.0 %fusion.53 = (bf16[2048,160]{0,1:T(8,128)(2,1)}, bf16[2048,160]{0,1:T(8,128)(2,1)S(1)}, bf16[2048,160]{0,1:T(8,128)(2,1)S(1)}, bf16[2048,160]{0,1:T(8,128)(2,1)}) fusion(bf16[2048,320]{0,1:T(8,128)(2,1)} %collective-permute-done.16, bf16[2048,320]{0,1:T(8,128)(2,1)} %collective-permute-done.15), kind=kLoop, calls=%fused_computation.131 | loop fusion | bytes 5242880 | tf_op jit(solution)/shard_map/key_pass/slice | solution.py:175
  179.2 1.1 all-to-all-done
  180.3 2.3 %gather_fusion.1 = f32[64,2,2,128]{3,2,1,0:T(2,128)} fusion(f32[64,2,2,128]{3,2,1,0:T(2,128)} %all-to-all-done, s32[1024]{0:T(1024)S(1)} %pad_clamp_fusion), kind=kCustom, calls=%fused_computation.1 | custom fusion | bytes 262400 | tf_op jit(solution)/shard_map/key_pass/gather | solution.py:167
  183.5 1.8 fusion.58
  191.0 1.1 constant_dynamic-update-slice_fusion.17
  192.1 1.2 constant_dynamic-update-slice_fusion.16
  198.4 12.3 %all_to_all.10 = f32[4,129,320]{2,1,0:T(8,128)S(1)} all-to-all(f32[4,129,320]{2,1,0:T(8,128)S(1)} %copy.35), channel_id=1, replica_groups=mesh['z'=16,'y'=4,'tp'=4,'dp'=2] {'tp'}, dimensions={0} | all-to-all | bytes 1320960 | tf_op jit(solution)/shard_map/back_projection/all_to_all | solution.py:217
  (127 shorter events, 29.5 us)
Async XLA Ops:
  6.5 15.1 %copy-start = (bf16[160,1280]{1,0:T(8,128)(2,1)S(1)}, bf16[160,1280]{1,0:T(8,128)(2,1)}, u32[]{:S(2)}) copy-start(bf16[160,1280]{1,0:T(8,128)(2,1)} %param.16) | copy-start | bytes 1228804
  6.5 130.4 %all-gather.2.cloned.1.call-start = ((), (), s32[]{:S(2)}) async-start(), calls=%async_computation.2 | async-start | bytes 5570560 | tf_op jit(solution)/shard_map/gather_sequence/all_gather | solution.py:110
  7.5 13.9 %copy-start.15 = (f32[1280]{0:T(1024)S(1)}, f32[1280]{0:T(1024)}, u32[]{:S(2)}) copy-start(f32[1280]{0:T(1024)} %param.13) | copy-start | bytes 15364
  21.0 1.0 copy-start.6
  21.2 15.7 %copy-start.16 = (f32[80]{0:T(128)S(1)}, f32[80]{0:T(128)}, u32[]{:S(2)}) copy-start(f32[80]{0:T(128)} %param.18) | copy-start | bytes 964
  21.2 15.8 %copy-start.12 = (bf16[160,1280]{1,0:T(8,128)(2,1)S(1)}, bf16[160,1280]{1,0:T(8,128)(2,1)}, u32[]{:S(2)}) copy-start(bf16[160,1280]{1,0:T(8,128)(2,1)} %param.17) | copy-start | bytes 1228804
  21.5 15.8 %copy-start.7 = (bf16[160,1280]{1,0:T(8,128)(2,1)S(1)}, bf16[160,1280]{1,0:T(8,128)(2,1)}, u32[]{:S(2)}) copy-start(bf16[160,1280]{1,0:T(8,128)(2,1)} %param.14) | copy-start | bytes 1228804
  21.6 27.6 %copy-start.1 = (s32[64]{0:T(128)S(1)}, s32[64]{0:T(128)}, u32[]{:S(2)}) copy-start(s32[64]{0:T(128)} %param.19) | copy-start | bytes 772
  38.2 15.5 %collective-permute-start = (bf16[128,320]{0,1:T(8,128)(2,1)S(1)}, bf16[128,320]{0,1:T(8,128)(2,1)S(1)}, u32[]{:S(2)}, u32[]{:S(2)}) collective-permute-start(bf16[128,320]{0,1:T(8,128)(2,1)S(1)} %get-tuple-element.59), channel_id=1, source_target_pairs={{0,480},{32,0},{64,32},{96,64},{128,96},{160,128},{192,160},{224,1... | collective-permute-start | bytes 245768 | tf_op jit(solution)/shard_map/gather_sequence/ppermute | solution.py:32
  47.1 11.7 %collective-permute-start.7 = (bf16[128,320]{0,1:T(8,128)(2,1)S(1)}, bf16[128,320]{0,1:T(8,128)(2,1)S(1)}, u32[]{:S(2)}, u32[]{:S(2)}) collective-permute-start(bf16[128,320]{0,1:T(8,128)(2,1)S(1)} %get-tuple-element.59), channel_id=1, source_target_pairs={{0,32},{32,64},{64,96},{96,128},{128,160},{160,192},{192,224},{224... | collective-permute-start | bytes 245768 | tf_op jit(solution)/shard_map/gather_sequence/ppermute | solution.py:32
  53.7 7.9 %collective-permute-start.1 = (bf16[128,320]{0,1:T(8,128)(2,1)S(1)}, bf16[128,320]{0,1:T(8,128)(2,1)S(1)}, u32[]{:S(2)}, u32[]{:S(2)}) collective-permute-start(bf16[128,320]{0,1:T(8,128)(2,1)S(1)} %collective-permute-done), channel_id=1, source_target_pairs={{0,480},{32,0},{64,32},{96,64},{128,96},{160,128},{192,160},{224,1... | collective-permute-start | bytes 245768 | tf_op jit(solution)/shard_map/gather_sequence/ppermute | solution.py:32
  58.9 9.3 %collective-permute-start.8 = (bf16[128,320]{0,1:T(8,128)(2,1)S(1)}, bf16[128,320]{0,1:T(8,128)(2,1)S(1)}, u32[]{:S(2)}, u32[]{:S(2)}) collective-permute-start(bf16[128,320]{0,1:T(8,128)(2,1)S(1)} %collective-permute-done.7), channel_id=1, source_target_pairs={{0,32},{32,64},{64,96},{96,128},{128,160},{160,192},{192,224},{224... | collective-permute-start | bytes 245768 | tf_op jit(solution)/shard_map/gather_sequence/ppermute | solution.py:32
  61.7 9.1 %collective-permute-start.2 = (bf16[128,320]{0,1:T(8,128)(2,1)S(1)}, bf16[128,320]{0,1:T(8,128)(2,1)S(1)}, u32[]{:S(2)}, u32[]{:S(2)}) collective-permute-start(bf16[128,320]{0,1:T(8,128)(2,1)S(1)} %collective-permute-done.1), channel_id=1, source_target_pairs={{0,480},{32,0},{64,32},{96,64},{128,96},{160,128},{192,160},{224,1... | collective-permute-start | bytes 245768 | tf_op jit(solution)/shard_map/gather_sequence/ppermute | solution.py:32
  68.2 9.0 %collective-permute-start.9 = (bf16[128,320]{0,1:T(8,128)(2,1)S(1)}, bf16[128,320]{0,1:T(8,128)(2,1)S(1)}, u32[]{:S(2)}, u32[]{:S(2)}) collective-permute-start(bf16[128,320]{0,1:T(8,128)(2,1)S(1)} %collective-permute-done.8), channel_id=1, source_target_pairs={{0,32},{32,64},{64,96},{96,128},{128,160},{160,192},{192,224},{224... | collective-permute-start | bytes 245768 | tf_op jit(solution)/shard_map/gather_sequence/ppermute | solution.py:32
  70.7 9.0 %collective-permute-start.3 = (bf16[128,320]{0,1:T(8,128)(2,1)S(1)}, bf16[128,320]{0,1:T(8,128)(2,1)S(1)}, u32[]{:S(2)}, u32[]{:S(2)}) collective-permute-start(bf16[128,320]{0,1:T(8,128)(2,1)S(1)} %collective-permute-done.2), channel_id=1, source_target_pairs={{0,480},{32,0},{64,32},{96,64},{128,96},{160,128},{192,160},{224,1... | collective-permute-start | bytes 245768 | tf_op jit(solution)/shard_map/gather_sequence/ppermute | solution.py:32
  77.2 8.7 %collective-permute-start.10 = (bf16[128,320]{0,1:T(8,128)(2,1)S(1)}, bf16[128,320]{0,1:T(8,128)(2,1)S(1)}, u32[]{:S(2)}, u32[]{:S(2)}) collective-permute-start(bf16[128,320]{0,1:T(8,128)(2,1)S(1)} %collective-permute-done.9), channel_id=1, source_target_pairs={{0,32},{32,64},{64,96},{96,128},{128,160},{160,192},{192,224},{224... | collective-permute-start | bytes 245768 | tf_op jit(solution)/shard_map/gather_sequence/ppermute | solution.py:32
  79.8 8.7 %collective-permute-start.4 = (bf16[128,320]{0,1:T(8,128)(2,1)S(1)}, bf16[128,320]{0,1:T(8,128)(2,1)S(1)}, u32[]{:S(2)}, u32[]{:S(2)}) collective-permute-start(bf16[128,320]{0,1:T(8,128)(2,1)S(1)} %collective-permute-done.3), channel_id=1, source_target_pairs={{0,480},{32,0},{64,32},{96,64},{128,96},{160,128},{192,160},{224,1... | collective-permute-start | bytes 245768 | tf_op jit(solution)/shard_map/gather_sequence/ppermute | solution.py:32
  85.9 9.1 %collective-permute-start.11 = (bf16[128,320]{0,1:T(8,128)(2,1)S(1)}, bf16[128,320]{0,1:T(8,128)(2,1)S(1)}, u32[]{:S(2)}, u32[]{:S(2)}) collective-permute-start(bf16[128,320]{0,1:T(8,128)(2,1)S(1)} %collective-permute-done.10), channel_id=1, source_target_pairs={{0,32},{32,64},{64,96},{96,128},{128,160},{160,192},{192,224},{224... | collective-permute-start | bytes 245768 | tf_op jit(solution)/shard_map/gather_sequence/ppermute | solution.py:32
  88.4 9.1 %collective-permute-start.5 = (bf16[128,320]{0,1:T(8,128)(2,1)S(1)}, bf16[128,320]{0,1:T(8,128)(2,1)S(1)}, u32[]{:S(2)}, u32[]{:S(2)}) collective-permute-start(bf16[128,320]{0,1:T(8,128)(2,1)S(1)} %collective-permute-done.4), channel_id=1, source_target_pairs={{0,480},{32,0},{64,32},{96,64},{128,96},{160,128},{192,160},{224,1... | collective-permute-start | bytes 245768 | tf_op jit(solution)/shard_map/gather_sequence/ppermute | solution.py:32
  94.9 9.5 %collective-permute-start.12 = (bf16[128,320]{0,1:T(8,128)(2,1)S(1)}, bf16[128,320]{0,1:T(8,128)(2,1)S(1)}, u32[]{:S(2)}, u32[]{:S(2)}) collective-permute-start(bf16[128,320]{0,1:T(8,128)(2,1)S(1)} %collective-permute-done.11), channel_id=1, source_target_pairs={{0,32},{32,64},{64,96},{96,128},{128,160},{160,192},{192,224},{224... | collective-permute-start | bytes 245768 | tf_op jit(solution)/shard_map/gather_sequence/ppermute | solution.py:32
  97.5 18.9 %collective-permute-start.6 = (bf16[128,320]{0,1:T(8,128)(2,1)S(1)}, bf16[128,320]{0,1:T(8,128)(2,1)S(1)}, u32[]{:S(2)}, u32[]{:S(2)}) collective-permute-start(bf16[128,320]{0,1:T(8,128)(2,1)S(1)} %collective-permute-done.5), channel_id=1, source_target_pairs={{0,480},{32,0},{64,32},{96,64},{128,96},{160,128},{192,160},{224,1... | collective-permute-start | bytes 245768 | tf_op jit(solution)/shard_map/gather_sequence/ppermute | solution.py:32
  104.4 10.2 %collective-permute-start.13 = (bf16[128,320]{0,1:T(8,128)(2,1)S(1)}, bf16[128,320]{0,1:T(8,128)(2,1)S(1)}, u32[]{:S(2)}, u32[]{:S(2)}) collective-permute-start(bf16[128,320]{0,1:T(8,128)(2,1)S(1)} %collective-permute-done.12), channel_id=1, source_target_pairs={{0,32},{32,64},{64,96},{96,128},{128,160},{160,192},{192,224},{224... | collective-permute-start | bytes 245768 | tf_op jit(solution)/shard_map/gather_sequence/ppermute | solution.py:32
  114.6 8.9 %collective-permute-start.14 = (bf16[128,320]{0,1:T(8,128)(2,1)S(1)}, bf16[128,320]{0,1:T(8,128)(2,1)S(1)}, u32[]{:S(2)}, u32[]{:S(2)}) collective-permute-start(bf16[128,320]{0,1:T(8,128)(2,1)S(1)} %collective-permute-done.13), channel_id=1, source_target_pairs={{0,32},{32,64},{64,96},{96,128},{128,160},{160,192},{192,224},{224... | collective-permute-start | bytes 245768 | tf_op jit(solution)/shard_map/gather_sequence/ppermute | solution.py:32
  128.7 24.3 %collective-permute-start.15 = (bf16[2048,320]{0,1:T(8,128)(2,1)}, bf16[2048,320]{0,1:T(8,128)(2,1)}, u32[]{:S(2)}, u32[]{:S(2)}) collective-permute-start(bf16[2048,320]{0,1:T(8,128)(2,1)} %constant_dynamic-update-slice_fusion), channel_id=1, source_target_pairs={{0,8},{8,16},{16,24},{24,0},{1,9},{9,17},{17,25},{25,1},{2,10},{10... | collective-permute-start | bytes 3932168 | tf_op jit(solution)/shard_map/gather_sequence/ppermute | solution.py:32
  132.4 23.7 %collective-permute-start.16 = (bf16[2048,320]{0,1:T(8,128)(2,1)}, bf16[2048,320]{0,1:T(8,128)(2,1)}, u32[]{:S(2)}, u32[]{:S(2)}) collective-permute-start(bf16[2048,320]{0,1:T(8,128)(2,1)} %constant_dynamic-update-slice_fusion), channel_id=1, source_target_pairs={{0,24},{8,0},{16,8},{24,16},{1,25},{9,1},{17,9},{25,17},{2,26},{10... | collective-permute-start | bytes 3932168 | tf_op jit(solution)/shard_map/gather_sequence/ppermute | solution.py:32
  149.7 1.7 copy-start.8
  156.8 23.5 %all-to-all-start = ((f32[64,2,2,128]{3,2,1,0:T(2,128)}), f32[64,2,2,128]{3,2,1,0:T(2,128)}, u32[]{:S(2)}, u32[]{:S(2)}) async-start(f32[64,2,2,128]{3,2,1,0:T(2,128)} %broadcast_in_dim.87), calls=%async_computation | async-start | bytes 262144 | tf_op jit(solution)/shard_map/gather_row_stats/all_to_all | solution.py:163
  168.1 22.8 %collective-permute-start.17 = (bf16[1024,320]{0,1:T(8,128)(2,1)}, bf16[1024,320]{0,1:T(8,128)(2,1)}, u32[]{:S(2)}, u32[]{:S(2)}) collective-permute-start(bf16[1024,320]{0,1:T(8,128)(2,1)} %slice.125), channel_id=1, source_target_pairs={{0,8},{8,16},{16,24},{24,0},{1,9},{9,17},{17,25},{25,1},{2,10},{10... | collective-permute-start | bytes 1966088 | tf_op jit(solution)/shard_map/gather_row_stats/ppermute | solution.py:32
  172.6 19.6 %collective-permute-start.18 = (bf16[1024,320]{0,1:T(8,128)(2,1)}, bf16[1024,320]{0,1:T(8,128)(2,1)}, u32[]{:S(2)}, u32[]{:S(2)}) collective-permute-start(bf16[1024,320]{0,1:T(8,128)(2,1)} %slice.126), channel_id=1, source_target_pairs={{0,24},{8,0},{16,8},{24,16},{1,25},{9,1},{17,9},{25,17},{2,26},{10... | collective-permute-start | bytes 1966088 | tf_op jit(solution)/shard_map/gather_row_stats/ppermute | solution.py:32
  183.5 1.8 copy-start.3
  185.3 1.0 copy-start.11
  186.3 1.1 copy-start.2
  187.1 1.0 copy-start.10
  187.9 1.1 copy-start.4
  192.1 1.3 copy-start.9
  195.2 1.1 copy-start.5
  198.3 12.5 %copy-start.13 = (bf16[128,320]{0,1:T(8,128)(2,1)S(1)}, bf16[128,320]{0,1:T(8,128)(2,1)}, u32[]{:S(2)}) copy-start(bf16[128,320]{0,1:T(8,128)(2,1)} %param.11) | copy-start | bytes 245764
  198.4 12.5 %copy-start.14 = (bf16[128,320]{0,1:T(8,128)(2,1)S(1)}, bf16[128,320]{0,1:T(8,128)(2,1)}, u32[]{:S(2)}) copy-start(bf16[128,320]{0,1:T(8,128)(2,1)} %param.12) | copy-start | bytes 245764
Sparse Core Ops, SparseCore 0:
  37.0 92.5 all-gather.1

commit v18 on v16

--- a/solution.py
+++ b/solution.py
@@ -168,7 +168,8 @@
         query_places = block_positions(offsets[qg_source], all_rows)
         key_grad = jnp.zeros((row_count, heads_here, head_width), jnp.float32)
         value_grad = jnp.zeros((row_count, heads_here, head_width), jnp.float32)
-        for ry, piece in enumerate(qg_pieces):
+        for ry in (0, 1, 3, 2):
+            piece = qg_pieces[ry]
             source = qg_source[ry * z_size : (ry + 1) * z_size]
             query_part = piece[:, :cols].reshape(piece_rows, heads_here, head_width)
             grad_part = piece[:, cols:].reshape(piece_rows, heads_here, head_width)

time: 221 us -> 221 us (level)
  transfers between devices with their start and end apart: 21 -> 21, of which waited for: 11 -> 11; matrix products, arithmetic and copies ran while one was open for 23% -> 24% of each run, Pallas kernels for 0% -> 0%
where the time goes in v18:
time: 221 us; the launch traced here: 219 us
  starting transfers between devices  76.9 us (35%)
  blocking collectives  41 us (19%)
  local copies, waits for them, and re-layouts  31.9 us (14%)
  waiting for transfers between devices  24.6 us (11%)
  matrix products  21.5 us (10%)
  between operations  14.8 us (7%)
  other arithmetic  7.98 us (4%)
    ppermute x19, starting transfers between devices, shift(): lax.ppermute(data, axis, [(i, (i + step) % size) for i in range(size)])  67.8 us
    ppermute x19, waiting for transfers between devices, shift(): lax.ppermute(data, axis, [(i, (i + step) % size) for i in range(size)])  23.5 us
    all_gather x1, blocking collectives, per_device(): kv_all = lax.all_gather(kv, 'y', axis=0, tiled=True)  14.6 us
    all_gather x1, blocking collectives, per_device(): gathered = lax.all_gather(both, 'tp', axis=1, tiled=True)  13.4 us
    all_to_all x1, blocking collectives, per_device(): received = lax.all_to_all(payload, 'tp', 0, 0, tiled=False)  13.1 us
    unnamed x50, local copies, waits for them, and re-layouts  11.4 us
    all_to_all x1, starting transfers between devices, per_device(): stats_all = lax.all_to_all(sent, ('z', 'y'), 0, 0, tiled=False)  9.12 us
    slice x3, local copies, waits for them, and re-layouts, per_device(): grad_part = piece[:, cols:].reshape(piece_rows, heads_here, head_width)  5.4 us
  transfers between devices with their start and end apart: 21, of which 11 were waited for; matrix products, arithmetic and copies ran while one was open for 24% of the time, Pallas kernels for 0%

profile of v18, /device:TPU:24, one launch (start us, length us, event | category | flops | bytes accessed | tf_op | source)
XLA Modules:
  0.0 218.7 jit_solution(17042509806322357513)
XLA Ops:
  6.5 1.0 pad_maximum_fusion.1
  7.5 13.4 %all_gather.9 = bf16[128,2560]{0,1:T(8,128)(2,1)S(1)} all-gather(bf16[128,640]{0,1:T(8,128)(2,1)S(1)} %pad_maximum_fusion.1), channel_id=1, replica_groups=mesh['z'=16,'y'=4,'tp'=4,'dp'=2] {'tp'}, dimensions={1}, use_global_device_ids=true | all-gather | bytes 819200 | tf_op jit(solution)/shard_map/gather_features/all_gather | solution.py:77
  22.3 14.6 %all_gather.10 = bf16[512,320]{0,1:T(8,128)(2,1)} all-gather(bf16[128,320]{0,1:T(8,128)(2,1)S(1)} %pad_maximum_fusion.2), channel_id=1, replica_groups=mesh['z'=16,'y'=4,'tp'=4,'dp'=2] {'y'}, dimensions={0}, use_global_device_ids=true | all-gather | bytes 409600 | tf_op jit(solution)/shard_map/gather_sequence/all_gather | solution.py:109
  38.2 8.9 %collective-permute-start = (bf16[128,320]{0,1:T(8,128)(2,1)S(1)}, bf16[128,320]{0,1:T(8,128)(2,1)S(1)}, u32[]{:S(2)}, u32[]{:S(2)}) collective-permute-start(bf16[128,320]{0,1:T(8,128)(2,1)S(1)} %get-tuple-element.59), channel_id=1, source_target_pairs={{0,480},{32,0},{64,32},{96,64},{128,96},{160,128},{192,160},{224,1... | collective-permute-start | bytes 245768 | tf_op jit(solution)/shard_map/gather_sequence/ppermute | solution.py:32
  47.1 1.9 collective-permute-start.7
  52.1 1.6 broadcast_compare_fusion.1
  53.7 5.1 %collective-permute-start.1 = (bf16[128,320]{0,1:T(8,128)(2,1)S(1)}, bf16[128,320]{0,1:T(8,128)(2,1)S(1)}, u32[]{:S(2)}, u32[]{:S(2)}) collective-permute-start(bf16[128,320]{0,1:T(8,128)(2,1)S(1)} %collective-permute-done), channel_id=1, source_target_pairs={{0,480},{32,0},{64,32},{96,64},{128,96},{160,128},{192,160},{224,1... | collective-permute-start | bytes 245768 | tf_op jit(solution)/shard_map/gather_sequence/ppermute | solution.py:32
  58.9 1.9 collective-permute-start.8
  61.7 4.9 %collective-permute-start.2 = (bf16[128,320]{0,1:T(8,128)(2,1)S(1)}, bf16[128,320]{0,1:T(8,128)(2,1)S(1)}, u32[]{:S(2)}, u32[]{:S(2)}) collective-permute-start(bf16[128,320]{0,1:T(8,128)(2,1)S(1)} %collective-permute-done.1), channel_id=1, source_target_pairs={{0,480},{32,0},{64,32},{96,64},{128,96},{160,128},{192,160},{224,1... | collective-permute-start | bytes 245768 | tf_op jit(solution)/shard_map/gather_sequence/ppermute | solution.py:32
  66.6 1.6 collective-permute-done.8
  68.1 1.9 collective-permute-start.9
  70.7 5.1 %collective-permute-start.3 = (bf16[128,320]{0,1:T(8,128)(2,1)S(1)}, bf16[128,320]{0,1:T(8,128)(2,1)S(1)}, u32[]{:S(2)}, u32[]{:S(2)}) collective-permute-start(bf16[128,320]{0,1:T(8,128)(2,1)S(1)} %collective-permute-done.2), channel_id=1, source_target_pairs={{0,480},{32,0},{64,32},{96,64},{128,96},{160,128},{192,160},{224,1... | collective-permute-start | bytes 245768 | tf_op jit(solution)/shard_map/gather_sequence/ppermute | solution.py:32
  75.9 1.3 collective-permute-done.9
  77.2 1.9 collective-permute-start.10
  79.8 5.2 %collective-permute-start.4 = (bf16[128,320]{0,1:T(8,128)(2,1)S(1)}, bf16[128,320]{0,1:T(8,128)(2,1)S(1)}, u32[]{:S(2)}, u32[]{:S(2)}) collective-permute-start(bf16[128,320]{0,1:T(8,128)(2,1)S(1)} %collective-permute-done.3), channel_id=1, source_target_pairs={{0,480},{32,0},{64,32},{96,64},{128,96},{160,128},{192,160},{224,1... | collective-permute-start | bytes 245768 | tf_op jit(solution)/shard_map/gather_sequence/ppermute | solution.py:32
  85.0 0.9 collective-permute-done.10
  85.9 1.9 collective-permute-start.11
  88.5 5.5 %collective-permute-start.5 = (bf16[128,320]{0,1:T(8,128)(2,1)S(1)}, bf16[128,320]{0,1:T(8,128)(2,1)S(1)}, u32[]{:S(2)}, u32[]{:S(2)}) collective-permute-start(bf16[128,320]{0,1:T(8,128)(2,1)S(1)} %collective-permute-done.4), channel_id=1, source_target_pairs={{0,480},{32,0},{64,32},{96,64},{128,96},{160,128},{192,160},{224,1... | collective-permute-start | bytes 245768 | tf_op jit(solution)/shard_map/gather_sequence/ppermute | solution.py:32
  94.9 1.9 collective-permute-start.12
  97.5 5.1 %collective-permute-start.6 = (bf16[128,320]{0,1:T(8,128)(2,1)S(1)}, bf16[128,320]{0,1:T(8,128)(2,1)S(1)}, u32[]{:S(2)}, u32[]{:S(2)}) collective-permute-start(bf16[128,320]{0,1:T(8,128)(2,1)S(1)} %collective-permute-done.5), channel_id=1, source_target_pairs={{0,480},{32,0},{64,32},{96,64},{128,96},{160,128},{192,160},{224,1... | collective-permute-start | bytes 245768 | tf_op jit(solution)/shard_map/gather_sequence/ppermute | solution.py:32
  102.6 1.7 collective-permute-done.12
  104.3 1.9 collective-permute-start.13
  106.9 7.1 %collective-permute-done.13 = bf16[128,320]{0,1:T(8,128)(2,1)S(1)} collective-permute-done((bf16[128,320]{0,1:T(8,128)(2,1)S(1)}, bf16[128,320]{0,1:T(8,128)(2,1)S(1)}, u32[]{:S(2)}, u32[]{:S(2)}) %collective-permute-start.13) | collective-permute-done | bytes 81952 | tf_op jit(solution)/shard_map/gather_sequence/ppermute | solution.py:32
  113.9 1.9 collective-permute-start.14
  116.5 6.2 %collective-permute-done.14 = bf16[128,320]{0,1:T(8,128)(2,1)S(1)} collective-permute-done((bf16[128,320]{0,1:T(8,128)(2,1)S(1)}, bf16[128,320]{0,1:T(8,128)(2,1)S(1)}, u32[]{:S(2)}, u32[]{:S(2)}) %collective-permute-start.14) | collective-permute-done | bytes 81952 | tf_op jit(solution)/shard_map/gather_sequence/ppermute | solution.py:32
  127.9 4.4 %collective-permute-start.15 = (bf16[2048,320]{0,1:T(8,128)(2,1)}, bf16[2048,320]{0,1:T(8,128)(2,1)}, u32[]{:S(2)}, u32[]{:S(2)}) collective-permute-start(bf16[2048,320]{0,1:T(8,128)(2,1)} %constant_dynamic-update-slice_fusion), channel_id=1, source_target_pairs={{0,8},{8,16},{16,24},{24,0},{1,9},{9,17},{17,25},{25,1},{2,10},{10... | collective-permute-start | bytes 3932168 | tf_op jit(solution)/shard_map/gather_sequence/ppermute | solution.py:32
  132.4 2.1 collective-permute-start.16
  134.5 2.2 %fusion.51 = (bf16[2048,160]{0,1:T(8,128)(2,1)}, bf16[2048,160]{0,1:T(8,128)(2,1)S(1)}) fusion(bf16[2048,320]{0,1:T(8,128)(2,1)} %constant_dynamic-update-slice_fusion), kind=kLoop, calls=%fused_computation.130 | loop fusion | bytes 2621440 | tf_op jit(solution)/shard_map/key_pass/slice | solution.py:175
  136.7 3.0 %fusion.49 = (bf16[8192,160]{0,1:T(8,128)(2,1)S(1)}, bf16[8192,160]{0,1:T(8,128)(2,1)S(1)}) fusion(bf16[8192,320]{0,1:T(8,128)(2,1)} %all-gather.2.cloned.1.call-done), kind=kLoop, calls=%fused_computation.128 | loop fusion | bytes 10485760 | tf_op jit(solution)/shard_map/gather_sequence/slice | solution.py:114
  139.7 1.8 select_reduce_fusion.1
  141.5 2.5 %select_reduce_fusion = f32[2,128]{1,0:T(2,128)S(1)} fusion(f32[2,128,8192]{2,1,0:T(8,128)S(1)} %get-tuple-element.70, f32[2,128]{1,0:T(2,128)S(1)} %get-tuple-element.69, pred[128,8192]{1,0:T(8,128)(4,1)S(1)} %broadcast_compare_fusion), kind=kLoop, calls=%fused_computation.4 | loop fusion | flops 8388352 | bytes 9439232 | tf_op jit(solution)/shard_map/query_pass/reduce_sum | solution.py:137
  144.0 3.5 %fusion.55 = (f32[2,128]{1,0:T(2,128)S(1)}, bf16[2,128,8192]{2,1,0:T(8,128)(2,1)S(1)}) fusion(bf16[128,2,80]{0,2,1:T(8,128)(2,1)S(1)} %bitcast.192, bf16[8192,2,80]{0,2,1:T(8,128)(2,1)S(1)} %bitcast.178, f32[2,128,8192]{2,1,0:T(8,128)S(1)} %get-tuple-element.70, f32[2,128]{1,0:T(2,128)S(1)} %log_add_fusion, pred[128,8192]{1,0:T(8,128)(4,1)S(1)} %broadcast_compare_fusion), kind=kOutput, calls=%fused_computation.134 | convolution fusion | flops 346029824 | bytes 16295936 | tf_op jit(solution)/shard_map/query_pass/qhd,khd->hqk/dot_general | solution.py:140
  147.5 2.0 fusion.36
  149.5 1.5 fusion.28
  151.1 1.1 fusion.60
  152.7 3.2 %collective-permute-done.16 = bf16[2048,320]{0,1:T(8,128)(2,1)} collective-permute-done((bf16[2048,320]{0,1:T(8,128)(2,1)}, bf16[2048,320]{0,1:T(8,128)(2,1)}, u32[]{:S(2)}, u32[]{:S(2)}) %collective-permute-start.16) | collective-permute-done | bytes 1310752 | tf_op jit(solution)/shard_map/gather_sequence/ppermute | solution.py:32
  156.6 9.1 %all-to-all-start = ((f32[64,2,2,128]{3,2,1,0:T(2,128)}), f32[64,2,2,128]{3,2,1,0:T(2,128)}, u32[]{:S(2)}, u32[]{:S(2)}) async-start(f32[64,2,2,128]{3,2,1,0:T(2,128)} %broadcast_in_dim.87), calls=%async_computation | async-start | bytes 262144 | tf_op jit(solution)/shard_map/gather_row_stats/all_to_all | solution.py:163
  165.7 2.0 slice.142
  167.7 2.4 %collective-permute-start.17 = (bf16[1024,320]{0,1:T(8,128)(2,1)}, bf16[1024,320]{0,1:T(8,128)(2,1)}, u32[]{:S(2)}, u32[]{:S(2)}) collective-permute-start(bf16[1024,320]{0,1:T(8,128)(2,1)} %slice.142), channel_id=1, source_target_pairs={{0,8},{8,16},{16,24},{24,0},{1,9},{9,17},{17,25},{25,1},{2,10},{10... | collective-permute-start | bytes 1966088 | tf_op jit(solution)/shard_map/gather_row_stats/ppermute | solution.py:32
  170.1 2.0 slice.143
  172.1 3.6 %collective-permute-start.18 = (bf16[1024,320]{0,1:T(8,128)(2,1)}, bf16[1024,320]{0,1:T(8,128)(2,1)}, u32[]{:S(2)}, u32[]{:S(2)}) collective-permute-start(bf16[1024,320]{0,1:T(8,128)(2,1)} %slice.143), channel_id=1, source_target_pairs={{0,24},{8,0},{16,8},{24,16},{1,25},{9,1},{17,9},{25,17},{2,26},{10... | collective-permute-start | bytes 1966088 | tf_op jit(solution)/shard_map/gather_row_stats/ppermute | solution.py:32
  175.8 3.0 %fusion.52 = (bf16[2048,160]{0,1:T(8,128)(2,1)}, bf16[2048,160]{0,1:T(8,128)(2,1)S(1)}, bf16[2048,160]{0,1:T(8,128)(2,1)S(1)}, bf16[2048,160]{0,1:T(8,128)(2,1)}) fusion(bf16[2048,320]{0,1:T(8,128)(2,1)} %collective-permute-done.16, bf16[2048,320]{0,1:T(8,128)(2,1)} %collective-permute-done.15), kind=kLoop, calls=%fused_computation.131 | loop fusion | bytes 5242880 | tf_op jit(solution)/shard_map/key_pass/slice | solution.py:175
  178.8 1.1 all-to-all-done
  179.8 2.3 %gather_fusion.1 = f32[64,2,2,128]{3,2,1,0:T(2,128)} fusion(f32[64,2,2,128]{3,2,1,0:T(2,128)} %all-to-all-done, s32[1024]{0:T(1024)S(1)} %pad_clamp_fusion), kind=kCustom, calls=%fused_computation.1 | custom fusion | bytes 262400 | tf_op jit(solution)/shard_map/key_pass/gather | solution.py:167
  183.0 1.8 fusion.56
  191.4 1.1 constant_dynamic-update-slice_fusion.17
  192.6 1.2 constant_dynamic-update-slice_fusion.16
  197.8 13.1 %all_to_all.10 = f32[4,129,320]{2,1,0:T(8,128)S(1)} all-to-all(f32[4,129,320]{2,1,0:T(8,128)S(1)} %copy.31), channel_id=1, replica_groups=mesh['z'=16,'y'=4,'tp'=4,'dp'=2] {'tp'}, dimensions={0} | all-to-all | bytes 1320960 | tf_op jit(solution)/shard_map/back_projection/all_to_all | solution.py:219
  (126 shorter events, 29.4 us)
Async XLA Ops:
  6.5 15.1 %copy-start = (bf16[160,1280]{1,0:T(8,128)(2,1)S(1)}, bf16[160,1280]{1,0:T(8,128)(2,1)}, u32[]{:S(2)}) copy-start(bf16[160,1280]{1,0:T(8,128)(2,1)} %param.16) | copy-start | bytes 1228804
  6.5 130.2 %all-gather.2.cloned.1.call-start = ((), (), s32[]{:S(2)}) async-start(), calls=%async_computation.2 | async-start | bytes 5570560 | tf_op jit(solution)/shard_map/gather_sequence/all_gather | solution.py:110
  7.5 13.9 %copy-start.15 = (f32[1280]{0:T(1024)S(1)}, f32[1280]{0:T(1024)}, u32[]{:S(2)}) copy-start(f32[1280]{0:T(1024)} %param.13) | copy-start | bytes 15364
  21.0 1.0 copy-start.6
  21.2 15.7 %copy-start.16 = (f32[80]{0:T(128)S(1)}, f32[80]{0:T(128)}, u32[]{:S(2)}) copy-start(f32[80]{0:T(128)} %param.18) | copy-start | bytes 964
  21.2 15.8 %copy-start.12 = (bf16[160,1280]{1,0:T(8,128)(2,1)S(1)}, bf16[160,1280]{1,0:T(8,128)(2,1)}, u32[]{:S(2)}) copy-start(bf16[160,1280]{1,0:T(8,128)(2,1)} %param.17) | copy-start | bytes 1228804
  21.5 15.8 %copy-start.7 = (bf16[160,1280]{1,0:T(8,128)(2,1)S(1)}, bf16[160,1280]{1,0:T(8,128)(2,1)}, u32[]{:S(2)}) copy-start(bf16[160,1280]{1,0:T(8,128)(2,1)} %param.14) | copy-start | bytes 1228804
  21.6 27.6 %copy-start.1 = (s32[64]{0:T(128)S(1)}, s32[64]{0:T(128)}, u32[]{:S(2)}) copy-start(s32[64]{0:T(128)} %param.19) | copy-start | bytes 772
  38.2 15.5 %collective-permute-start = (bf16[128,320]{0,1:T(8,128)(2,1)S(1)}, bf16[128,320]{0,1:T(8,128)(2,1)S(1)}, u32[]{:S(2)}, u32[]{:S(2)}) collective-permute-start(bf16[128,320]{0,1:T(8,128)(2,1)S(1)} %get-tuple-element.59), channel_id=1, source_target_pairs={{0,480},{32,0},{64,32},{96,64},{128,96},{160,128},{192,160},{224,1... | collective-permute-start | bytes 245768 | tf_op jit(solution)/shard_map/gather_sequence/ppermute | solution.py:32
  47.1 11.7 %collective-permute-start.7 = (bf16[128,320]{0,1:T(8,128)(2,1)S(1)}, bf16[128,320]{0,1:T(8,128)(2,1)S(1)}, u32[]{:S(2)}, u32[]{:S(2)}) collective-permute-start(bf16[128,320]{0,1:T(8,128)(2,1)S(1)} %get-tuple-element.59), channel_id=1, source_target_pairs={{0,32},{32,64},{64,96},{96,128},{128,160},{160,192},{192,224},{224... | collective-permute-start | bytes 245768 | tf_op jit(solution)/shard_map/gather_sequence/ppermute | solution.py:32
  53.7 7.9 %collective-permute-start.1 = (bf16[128,320]{0,1:T(8,128)(2,1)S(1)}, bf16[128,320]{0,1:T(8,128)(2,1)S(1)}, u32[]{:S(2)}, u32[]{:S(2)}) collective-permute-start(bf16[128,320]{0,1:T(8,128)(2,1)S(1)} %collective-permute-done), channel_id=1, source_target_pairs={{0,480},{32,0},{64,32},{96,64},{128,96},{160,128},{192,160},{224,1... | collective-permute-start | bytes 245768 | tf_op jit(solution)/shard_map/gather_sequence/ppermute | solution.py:32
  58.9 9.3 %collective-permute-start.8 = (bf16[128,320]{0,1:T(8,128)(2,1)S(1)}, bf16[128,320]{0,1:T(8,128)(2,1)S(1)}, u32[]{:S(2)}, u32[]{:S(2)}) collective-permute-start(bf16[128,320]{0,1:T(8,128)(2,1)S(1)} %collective-permute-done.7), channel_id=1, source_target_pairs={{0,32},{32,64},{64,96},{96,128},{128,160},{160,192},{192,224},{224... | collective-permute-start | bytes 245768 | tf_op jit(solution)/shard_map/gather_sequence/ppermute | solution.py:32
  61.7 9.1 %collective-permute-start.2 = (bf16[128,320]{0,1:T(8,128)(2,1)S(1)}, bf16[128,320]{0,1:T(8,128)(2,1)S(1)}, u32[]{:S(2)}, u32[]{:S(2)}) collective-permute-start(bf16[128,320]{0,1:T(8,128)(2,1)S(1)} %collective-permute-done.1), channel_id=1, source_target_pairs={{0,480},{32,0},{64,32},{96,64},{128,96},{160,128},{192,160},{224,1... | collective-permute-start | bytes 245768 | tf_op jit(solution)/shard_map/gather_sequence/ppermute | solution.py:32
  68.1 9.0 %collective-permute-start.9 = (bf16[128,320]{0,1:T(8,128)(2,1)S(1)}, bf16[128,320]{0,1:T(8,128)(2,1)S(1)}, u32[]{:S(2)}, u32[]{:S(2)}) collective-permute-start(bf16[128,320]{0,1:T(8,128)(2,1)S(1)} %collective-permute-done.8), channel_id=1, source_target_pairs={{0,32},{32,64},{64,96},{96,128},{128,160},{160,192},{192,224},{224... | collective-permute-start | bytes 245768 | tf_op jit(solution)/shard_map/gather_sequence/ppermute | solution.py:32
  70.7 9.0 %collective-permute-start.3 = (bf16[128,320]{0,1:T(8,128)(2,1)S(1)}, bf16[128,320]{0,1:T(8,128)(2,1)S(1)}, u32[]{:S(2)}, u32[]{:S(2)}) collective-permute-start(bf16[128,320]{0,1:T(8,128)(2,1)S(1)} %collective-permute-done.2), channel_id=1, source_target_pairs={{0,480},{32,0},{64,32},{96,64},{128,96},{160,128},{192,160},{224,1... | collective-permute-start | bytes 245768 | tf_op jit(solution)/shard_map/gather_sequence/ppermute | solution.py:32
  77.2 8.7 %collective-permute-start.10 = (bf16[128,320]{0,1:T(8,128)(2,1)S(1)}, bf16[128,320]{0,1:T(8,128)(2,1)S(1)}, u32[]{:S(2)}, u32[]{:S(2)}) collective-permute-start(bf16[128,320]{0,1:T(8,128)(2,1)S(1)} %collective-permute-done.9), channel_id=1, source_target_pairs={{0,32},{32,64},{64,96},{96,128},{128,160},{160,192},{192,224},{224... | collective-permute-start | bytes 245768 | tf_op jit(solution)/shard_map/gather_sequence/ppermute | solution.py:32
  79.8 8.7 %collective-permute-start.4 = (bf16[128,320]{0,1:T(8,128)(2,1)S(1)}, bf16[128,320]{0,1:T(8,128)(2,1)S(1)}, u32[]{:S(2)}, u32[]{:S(2)}) collective-permute-start(bf16[128,320]{0,1:T(8,128)(2,1)S(1)} %collective-permute-done.3), channel_id=1, source_target_pairs={{0,480},{32,0},{64,32},{96,64},{128,96},{160,128},{192,160},{224,1... | collective-permute-start | bytes 245768 | tf_op jit(solution)/shard_map/gather_sequence/ppermute | solution.py:32
  85.9 9.0 %collective-permute-start.11 = (bf16[128,320]{0,1:T(8,128)(2,1)S(1)}, bf16[128,320]{0,1:T(8,128)(2,1)S(1)}, u32[]{:S(2)}, u32[]{:S(2)}) collective-permute-start(bf16[128,320]{0,1:T(8,128)(2,1)S(1)} %collective-permute-done.10), channel_id=1, source_target_pairs={{0,32},{32,64},{64,96},{96,128},{128,160},{160,192},{192,224},{224... | collective-permute-start | bytes 245768 | tf_op jit(solution)/shard_map/gather_sequence/ppermute | solution.py:32
  88.5 9.0 %collective-permute-start.5 = (bf16[128,320]{0,1:T(8,128)(2,1)S(1)}, bf16[128,320]{0,1:T(8,128)(2,1)S(1)}, u32[]{:S(2)}, u32[]{:S(2)}) collective-permute-start(bf16[128,320]{0,1:T(8,128)(2,1)S(1)} %collective-permute-done.4), channel_id=1, source_target_pairs={{0,480},{32,0},{64,32},{96,64},{128,96},{160,128},{192,160},{224,1... | collective-permute-start | bytes 245768 | tf_op jit(solution)/shard_map/gather_sequence/ppermute | solution.py:32
  94.9 9.4 %collective-permute-start.12 = (bf16[128,320]{0,1:T(8,128)(2,1)S(1)}, bf16[128,320]{0,1:T(8,128)(2,1)S(1)}, u32[]{:S(2)}, u32[]{:S(2)}) collective-permute-start(bf16[128,320]{0,1:T(8,128)(2,1)S(1)} %collective-permute-done.11), channel_id=1, source_target_pairs={{0,32},{32,64},{64,96},{96,128},{128,160},{160,192},{192,224},{224... | collective-permute-start | bytes 245768 | tf_op jit(solution)/shard_map/gather_sequence/ppermute | solution.py:32
  97.5 18.3 %collective-permute-start.6 = (bf16[128,320]{0,1:T(8,128)(2,1)S(1)}, bf16[128,320]{0,1:T(8,128)(2,1)S(1)}, u32[]{:S(2)}, u32[]{:S(2)}) collective-permute-start(bf16[128,320]{0,1:T(8,128)(2,1)S(1)} %collective-permute-done.5), channel_id=1, source_target_pairs={{0,480},{32,0},{64,32},{96,64},{128,96},{160,128},{192,160},{224,1... | collective-permute-start | bytes 245768 | tf_op jit(solution)/shard_map/gather_sequence/ppermute | solution.py:32
  104.3 9.6 %collective-permute-start.13 = (bf16[128,320]{0,1:T(8,128)(2,1)S(1)}, bf16[128,320]{0,1:T(8,128)(2,1)S(1)}, u32[]{:S(2)}, u32[]{:S(2)}) collective-permute-start(bf16[128,320]{0,1:T(8,128)(2,1)S(1)} %collective-permute-done.12), channel_id=1, source_target_pairs={{0,32},{32,64},{64,96},{96,128},{128,160},{160,192},{192,224},{224... | collective-permute-start | bytes 245768 | tf_op jit(solution)/shard_map/gather_sequence/ppermute | solution.py:32
  113.9 8.8 %collective-permute-start.14 = (bf16[128,320]{0,1:T(8,128)(2,1)S(1)}, bf16[128,320]{0,1:T(8,128)(2,1)S(1)}, u32[]{:S(2)}, u32[]{:S(2)}) collective-permute-start(bf16[128,320]{0,1:T(8,128)(2,1)S(1)} %collective-permute-done.13), channel_id=1, source_target_pairs={{0,32},{32,64},{64,96},{96,128},{128,160},{160,192},{192,224},{224... | collective-permute-start | bytes 245768 | tf_op jit(solution)/shard_map/gather_sequence/ppermute | solution.py:32
  127.9 24.7 %collective-permute-start.15 = (bf16[2048,320]{0,1:T(8,128)(2,1)}, bf16[2048,320]{0,1:T(8,128)(2,1)}, u32[]{:S(2)}, u32[]{:S(2)}) collective-permute-start(bf16[2048,320]{0,1:T(8,128)(2,1)} %constant_dynamic-update-slice_fusion), channel_id=1, source_target_pairs={{0,8},{8,16},{16,24},{24,0},{1,9},{9,17},{17,25},{25,1},{2,10},{10... | collective-permute-start | bytes 3932168 | tf_op jit(solution)/shard_map/gather_sequence/ppermute | solution.py:32
  132.4 23.5 %collective-permute-start.16 = (bf16[2048,320]{0,1:T(8,128)(2,1)}, bf16[2048,320]{0,1:T(8,128)(2,1)}, u32[]{:S(2)}, u32[]{:S(2)}) collective-permute-start(bf16[2048,320]{0,1:T(8,128)(2,1)} %constant_dynamic-update-slice_fusion), channel_id=1, source_target_pairs={{0,24},{8,0},{16,8},{24,16},{1,25},{9,1},{17,9},{25,17},{2,26},{10... | collective-permute-start | bytes 3932168 | tf_op jit(solution)/shard_map/gather_sequence/ppermute | solution.py:32
  149.5 1.7 copy-start.8
  156.6 23.3 %all-to-all-start = ((f32[64,2,2,128]{3,2,1,0:T(2,128)}), f32[64,2,2,128]{3,2,1,0:T(2,128)}, u32[]{:S(2)}, u32[]{:S(2)}) async-start(f32[64,2,2,128]{3,2,1,0:T(2,128)} %broadcast_in_dim.87), calls=%async_computation | async-start | bytes 262144 | tf_op jit(solution)/shard_map/gather_row_stats/all_to_all | solution.py:163
  167.7 23.7 %collective-permute-start.17 = (bf16[1024,320]{0,1:T(8,128)(2,1)}, bf16[1024,320]{0,1:T(8,128)(2,1)}, u32[]{:S(2)}, u32[]{:S(2)}) collective-permute-start(bf16[1024,320]{0,1:T(8,128)(2,1)} %slice.142), channel_id=1, source_target_pairs={{0,8},{8,16},{16,24},{24,0},{1,9},{9,17},{17,25},{25,1},{2,10},{10... | collective-permute-start | bytes 1966088 | tf_op jit(solution)/shard_map/gather_row_stats/ppermute | solution.py:32
  172.1 20.4 %collective-permute-start.18 = (bf16[1024,320]{0,1:T(8,128)(2,1)}, bf16[1024,320]{0,1:T(8,128)(2,1)}, u32[]{:S(2)}, u32[]{:S(2)}) collective-permute-start(bf16[1024,320]{0,1:T(8,128)(2,1)} %slice.143), channel_id=1, source_target_pairs={{0,24},{8,0},{16,8},{24,16},{1,25},{9,1},{17,9},{25,17},{2,26},{10... | collective-permute-start | bytes 1966088 | tf_op jit(solution)/shard_map/gather_row_stats/ppermute | solution.py:32
  183.0 1.8 copy-start.3
  184.7 1.0 copy-start.11
  185.7 1.1 copy-start.2
  186.8 1.0 copy-start.10
  187.8 1.1 copy-start.4
  192.6 1.3 copy-start.9
  194.7 1.1 copy-start.5
  197.8 13.3 %copy-start.13 = (bf16[128,320]{0,1:T(8,128)(2,1)S(1)}, bf16[128,320]{0,1:T(8,128)(2,1)}, u32[]{:S(2)}) copy-start(bf16[128,320]{0,1:T(8,128)(2,1)} %param.11) | copy-start | bytes 245764
  197.8 13.3 %copy-start.14 = (bf16[128,320]{0,1:T(8,128)(2,1)S(1)}, bf16[128,320]{0,1:T(8,128)(2,1)}, u32[]{:S(2)}) copy-start(bf16[128,320]{0,1:T(8,128)(2,1)} %param.12) | copy-start | bytes 245764
Sparse Core Ops, SparseCore 0:
  37.0 92.6 all-gather.1
